TPU v7x, 32 devices: a whole 2x2x4 slice. The times are simulated.
32 devices in a mesh: ctx: 8 (over z, x), tp: 4 (over y, core).
Axes of the slice: x: 2, y: 2, z: 4, core: 2. Of those that a mesh axis runs over, the one named last changes fastest.
Arguments:
- inner_input: bfloat16 [4096, 8192], P('ctx', 'tp'), may hold values from -6 to 6
- state_input: bfloat16 [4096, 2, 1024], P('ctx', None, 'tp'), may hold values from -6 to 6
- gate_input: bfloat16 [4096, 8192], P('ctx', 'tp'), may hold values from -40 to 40
- step_logits: float32 [4096, 128], P('ctx', 'tp'), may hold values from -20 to 1
- conv_inner: bfloat16 [4, 8192], P(None, 'tp'), may hold values from -3 to 3
- conv_states: bfloat16 [4, 2, 1024], P(None, None, 'tp'), may hold values from -3 to 3
- bias_inner: bfloat16 [8192], P('tp'), may hold values from -0.5 to 0.5
- bias_states: bfloat16 [2, 1024], P(None, 'tp'), may hold values from -0.5 to 0.5
- decay_log: float32 [128], P('tp'), may hold values from -0.7 to 0.7
- skip_gain: float32 [128], P('tp'), may hold values from 0.5 to 1.5
- norm_gain: bfloat16 [8192], P('tp'), may hold values from 0.5 to 1.5
- out_weight: bfloat16 [8192, 4096], P('tp'), may hold values from -0.0625 to 0.0625
Outputs:
- layer_out: bfloat16 [4096, 4096], P(('ctx', 'tp'))
All inputs are finite; a program needn't handle non-finite values.
Results may differ from a plain program's by a relative error of at most 0.009.
Values may be sent and summed in bfloat16 or wider, within the bound.
No kernel may reach another device: no remote copies, remote signals or barrier semaphores. Data moves between devices by JAX's collectives and lax.ppermute only.
A program may use at most 128 MiB of HBM per device.

v0:
```python
import jax
import jax.numpy as jnp
from jax import lax
from jax.sharding import PartitionSpec as P

SSM_HEAD_COUNT = 128
HEAD_DIM = 64
STATE = 128
GROUPS = 8
CONV = 4
BLK = 512


epsilon = 1e-05


def shifted(value, axis, by):
    count = lax.axis_size(axis)
    pairs = [(i, i + by) for i in range(count) if 0 <= i + by < count]
    return lax.ppermute(value, axis, pairs)


def conv_silu(padded, weight, offsets, row_count):
    summed = offsets.astype(jnp.float32)
    for k in range(CONV):
        summed = summed + weight[k].astype(jnp.float32) * padded[k : k + row_count].astype(
            jnp.float32
        )
    return lax.optimization_barrier(jax.nn.silu(summed).astype(jnp.bfloat16))


def block_local(carried_in, inputs_block):
    local_state, entry_decay = carried_in
    inner_block, b_block, c_block, step_sizes, log_rates = inputs_block
    length = inner_block.shape[0]
    cumulative = jnp.cumsum(log_rates, axis=0)
    along = jnp.transpose(cumulative, (1, 2, 0))
    causal = lax.broadcasted_iota(jnp.int32, (length, length), 0) >= lax.broadcasted_iota(
        jnp.int32, (length, length), 1
    )
    decays = jnp.exp(jnp.where(causal, along[:, :, :, None] - along[:, :, None, :], -jnp.inf))
    scores = jnp.einsum("ign,jgn->gij", c_block, b_block, preferred_element_type=jnp.float32)
    mixing = (
        decays * scores[:, None] * jnp.transpose(step_sizes, (1, 2, 0))[:, :, None, :]
    ).astype(jnp.bfloat16)
    diagonal = jnp.einsum(
        "ghij,jghp->ighp", mixing, inner_block, preferred_element_type=jnp.float32
    )
    within = jnp.exp(cumulative)
    carried = within[..., None] * jnp.einsum(
        "ign,ghpn->ighp", c_block.astype(jnp.float32), local_state, precision=lax.Precision.HIGHEST
    )
    tail_weight = jnp.exp(cumulative[-1][None] - cumulative) * step_sizes
    weighted = (inner_block * tail_weight[..., None]).astype(jnp.bfloat16)
    block_state = jnp.einsum(
        "jghp,jgn->ghpn", weighted, b_block, preferred_element_type=jnp.float32
    )
    block_decay = jnp.exp(cumulative[-1])
    new_state = block_decay[..., None, None] * local_state + block_state
    return (
        (new_state, entry_decay * block_decay),
        (diagonal + carried, within * entry_decay[None]),
    )


def body(
    inner_input,
    state_input,
    gate_input,
    step_logits,
    conv_inner,
    conv_states,
    bias_inner,
    bias_states,
    decay_log,
    skip_gain,
    norm_gain,
    out_weight,
):
    tokens = inner_input.shape[0]
    margin = CONV - 1
    previous = shifted((inner_input[tokens - margin :], state_input[tokens - margin :]), "ctx", 1)
    inner_conv = conv_silu(
        jnp.concatenate([previous[0], inner_input], axis=0), conv_inner, bias_inner, tokens
    )
    state_conv = conv_silu(
        jnp.concatenate([previous[1], state_input], axis=0), conv_states, bias_states, tokens
    )
    groups_here = state_input.shape[2] // STATE
    per_group = SSM_HEAD_COUNT // GROUPS
    blocks = tokens // BLK
    step_sizes = jax.nn.softplus(step_logits)
    log_rates = -step_sizes * jnp.exp(decay_log)[None]
    c_all = state_conv[:, 1].reshape(blocks, BLK, groups_here, STATE)
    inputs_all = (
        inner_conv.reshape(blocks, BLK, groups_here, per_group, HEAD_DIM),
        state_conv[:, 0].reshape(blocks, BLK, groups_here, STATE),
        c_all,
        step_sizes.reshape(blocks, BLK, groups_here, per_group),
        log_rates.reshape(blocks, BLK, groups_here, per_group),
    )
    start_state = jnp.zeros((groups_here, per_group, HEAD_DIM, STATE), jnp.float32)
    start_decay = jnp.ones((groups_here, per_group), jnp.float32)
    (local_state, device_decay), (partial_heads, factors) = lax.scan(
        block_local, (start_state, start_decay), inputs_all
    )
    own_total = jnp.sum(log_rates, axis=0).reshape(1, groups_here, per_group)
    totals = lax.all_gather(own_total, "ctx", axis=0, tiled=True)
    through = jnp.cumsum(totals, axis=0)
    position = lax.axis_index("ctx")
    before = lax.dynamic_index_in_dim(through - totals, position, 0, keepdims=False)
    shards = lax.all_gather(local_state[None], "ctx", axis=0, tiled=True)
    amount = shards.shape[0]
    anchor = lax.broadcasted_iota(jnp.int32, (amount, 1, 1), 0)
    earlier = anchor < position
    weights_far = jnp.where(earlier, jnp.exp(jnp.where(earlier, before[None] - through, 0.0)), 0.0)
    state_in = jnp.einsum("kgh,kghpn->ghpn", weights_far, shards, precision=lax.Precision.HIGHEST)
    correction = factors[..., None] * jnp.einsum(
        "bign,ghpn->bighp", c_all.astype(jnp.float32), state_in, precision=lax.Precision.HIGHEST
    )
    width_here = groups_here * per_group * HEAD_DIM
    mixed_heads = (partial_heads + correction).reshape(tokens, width_here) + jnp.repeat(
        skip_gain, HEAD_DIM
    )[None] * inner_conv.astype(jnp.float32)
    gated_out = mixed_heads * jax.nn.silu(gate_input.astype(jnp.float32))
    grouped = gated_out.reshape(tokens, groups_here, width_here // groups_here)
    normed = grouped * lax.rsqrt(jnp.mean(grouped * grouped, axis=-1, keepdims=True) + epsilon)
    normed = (normed.reshape(tokens, width_here) * norm_gain.astype(jnp.float32)).astype(
        jnp.bfloat16
    )
    return lax.psum_scatter(
        jnp.dot(normed, out_weight, preferred_element_type=jnp.float32).astype(jnp.bfloat16),
        "tp",
        scatter_dimension=0,
        tiled=True,
    )


def solution(mesh):
    placed = (
        P("ctx", "tp"),
        P("ctx", None, "tp"),
        P("ctx", "tp"),
        P("ctx", "tp"),
        P(None, "tp"),
        P(None, None, "tp"),
        P("tp"),
        P(None, "tp"),
        P("tp"),
        P("tp"),
        P("tp"),
        P("tp", None),
    )
    return jax.shard_map(
        body, mesh=mesh, in_specs=placed, out_specs=P(("ctx", "tp"), None), check_vma=False
    )
```

profile of v0, /device:TPU:0, one launch (start us, length us, event | category | flops | bytes accessed | tf_op | source)
XLA Modules:
  0.0 249.1 jit_solution(14708655856131833193)
XLA Ops:
  6.5 0.8 slice.66
  7.4 0.3 copy.54
  7.7 4.9 %collective-permute-start = (bf16[3,2048]{0,1:T(8,128)(2,1)S(1)}, bf16[3,2048]{0,1:T(8,128)(2,1)S(1)}, u32[]{:S(2)}, u32[]{:S(2)}) collective-permute-start(bf16[3,2048]{0,1:T(8,128)(2,1)S(1)} %copy.54), channel_id=1, source_target_pairs={{0,4},{4,8},{8,12},{12,16},{16,20},{20,24},{24,28},{1,5},{5,9},{9,... | collective-permute-start | bytes 36872 | tf_op jit(solution)/shard_map/ppermute | solution.py:20
  12.6 0.7 slice.76
  13.3 0.2 copy.61
  13.5 3.4 %collective-permute-start.1 = (bf16[3,2,256]{0,2,1:T(8,128)(2,1)S(1)}, bf16[3,2,256]{0,2,1:T(8,128)(2,1)S(1)}, u32[]{:S(2)}, u32[]{:S(2)}) collective-permute-start(bf16[3,2,256]{0,2,1:T(8,128)(2,1)S(1)} %copy.61), channel_id=1, source_target_pairs={{0,4},{4,8},{8,12},{12,16},{16,20},{20,24},{24,28},{1,5},{5,9},{9,... | collective-permute-start | bytes 9224 | tf_op jit(solution)/shard_map/ppermute | solution.py:20
  16.9 0.7 exp.43
  17.6 1.0 fusion.26
  18.6 2.3 reduce-window.6
  21.0 0.1 copy.58
  21.2 0.2 slice_reduce_fusion
  21.4 0.9 slice_convert_fusion.3
  22.3 0.7 bitcast_convert_fusion.3
  23.1 3.9 %copy.55 = bf16[512,2048]{0,1:T(8,128)(2,1)} copy(bf16[512,2048]{1,0:T(8,128)(2,1)} %param.12) | data formatting | bytes 4194304 | tf_op args[0]
  27.1 0.7 copy.62
  27.9 1.3 multiply_convert_fusion.7
  29.3 9.5 %multiply_convert_fusion.3 = bf16[512,2048]{0,1:T(8,128)(2,1)S(1)} fusion(bf16[512,2048]{0,1:T(8,128)(2,1)} %copy.55, bf16[3,2048]{0,1:T(8,128)(2,1)S(1)} %collective-permute-done, f32[2048]{0:T(1024)S(1)} %bitcast.120, f32[2048]{0:T(1024)S(1)} %bitcast.121, f32[2048]{0:T(1024)S(1)} %bitcast.119, f32[2048]{0:T(1024)S(1)} %bitcast.118, ...), kind=kLoop, calls=%fused_computation.22 | loop fusion | flops 27262976 | bytes 4247552 | tf_op jit(solution)/shard_map/convert_element_type | solution.py:29
  38.8 1.7 fusion.16
  40.7 20.8 %all_gather.6 = f32[8,2,16]{2,1,0:T(2,128)S(1)} all-gather(f32[1,2,16]{2,1,0:T(2,128)S(1)} %reshape.66), channel_id=1, replica_groups=mesh['ctx'=8,'tp'=4] {'ctx'}, dimensions={0}, use_global_device_ids=true | all-gather | bytes 1152 | tf_op jit(solution)/shard_map/all_gather | solution.py:108
  61.7 3.9 %copy.69 = bf16[512,2048]{0,1:T(8,128)(2,1)} copy(bf16[512,2048]{1,0:T(8,128)(2,1)} %param.14) | data formatting | bytes 4194304 | tf_op args[2]
  65.8 0.5 fusion.29
  66.3 3.7 %fusion.19 = f32[2,16,64,512]{3,2,1,0:T(8,128)} fusion(bf16[512,2,128,1]{0,2,3,1:T(8,128)(2,1)S(1)} %bitcast.109), kind=kOutput, calls=%fused_computation.42 | convolution fusion | flops 1610612736 | bytes 4456448 | tf_op jit(solution)/shard_map/while/body/eval_jaxpr/ign,ghpn->ighp/dot_general | solution.py:50
  70.1 10.4 %fusion = f32[2,16,64,512]{3,2,1,0:T(8,128)} fusion(bf16[512,2,16,64]{0,3,2,1:T(8,128)(2,1)S(1)} %bitcast.106, f32[2,16,512]{2,1,0:T(8,128)S(1)} %bitcast.116, f32[2,512,512]{2,1,0:T(8,128)S(1)} %fusion.29, f32[2,16,512]{2,1,0:T(8,128)S(1)} %get-tuple-element.44, pred[512,512]{1,0:T(8,128)(4,1)S(1)} %iota_compare_fusion), kind=kOutput, calls=%fused_computation.1 | convolution fusion | flops 1115684864 | bytes 8781824 | tf_op jit(solution)/shard_map/while/body/eval_jaxpr/ghij,jghp->ighp/dot_general | solution.py:46
  80.5 86.0 %all-gather.3.cloned.1.call-done = f32[16,16,64,128]{3,2,1,0:T(8,128)} async-done(((f32[2,16,64,128]{3,2,1,0:T(8,128)}), f32[16,16,64,128]{3,2,1,0:T(8,128)}) %all-gather.3.cloned.1.call-update) | async-done | bytes 8388624 | tf_op jit(solution)/shard_map/all_gather | solution.py:112
  166.5 15.7 %fusion.2 = f32[2,16,1,64,128]{4,2,3,1,0:T(1,128)S(1)} fusion(f32[8,2,16,1,1]{0,3,4,2,1:T(1,128)S(1)} %copy.74, f32[8,2,16,64,128]{4,3,2,1,0:T(8,128)} %bitcast.107), kind=kOutput, calls=%fused_computation.3 | convolution fusion | flops 25165824 | bytes 9438208 | tf_op jit(solution)/shard_map/kgh,kghpn->ghpn/dot_general | solution.py:117
  182.3 2.1 fusion.8
  184.4 2.1 bitcast_reduce_fusion
  186.5 0.4 fusion.10
  187.0 0.7 slice-done.2
  187.7 1.2 slice-done.3
  188.9 10.6 %convolution_convert_fusion = bf16[512,4096]{1,0:T(8,128)(2,1)} fusion(bf16[512,2048]{0,1:T(8,128)(2,1)S(1)} %fusion.10, bf16[2048,4096]{1,0:T(8,128)(2,1)S(1)} %bitcast.124), kind=kOutput, calls=%fused_computation.5 | convolution fusion | flops 8592031744 | bytes 23068672 | tf_op jit(solution)/shard_map/dot_general | solution.py:132
  199.5 42.8 %reduce-scatter.2.cloned.1.call-done = bf16[128,4096]{1,0:T(8,128)(2,1)} async-done(((bf16[512,4096]{1,0:T(8,128)(2,1)}), bf16[128,4096]{1,0:T(8,128)(2,1)}) %reduce-scatter.2.cloned.1.call-update) | async-done | bytes 1048592 | tf_op jit(solution)/shard_map/reduce_scatter | solution.py:131
  (51 shorter events, 1.0 us)
Async XLA Ops:
  6.5 20.5 %copy-start.3 = (bf16[512,2,256]{2,1,0:T(2,128)(2,1)S(1)}, bf16[512,2,256]{2,1,0:T(2,128)(2,1)}, u32[]{:S(2)}) copy-start(bf16[512,2,256]{2,1,0:T(2,128)(2,1)} %param.13) | copy-start | bytes 1572868
  6.5 21.3 %copy-start.4 = (bf16[2048]{0:T(1024)(128)(2,1)S(1)}, bf16[2048]{0:T(1024)(128)(2,1)}, u32[]{:S(2)}) copy-start(bf16[2048]{0:T(1024)(128)(2,1)} %param.18) | copy-start | bytes 12292
  6.5 21.3 %copy-start.6 = (bf16[2,256]{1,0:T(2,128)(2,1)S(1)}, bf16[2,256]{1,0:T(2,128)(2,1)}, u32[]{:S(2)}) copy-start(bf16[2,256]{1,0:T(2,128)(2,1)} %param.19) | copy-start | bytes 3076
  6.5 160.0 %all-gather.3.cloned.1.call-start = ((), (), s32[]{:S(2)}) async-start(), calls=%async_computation.2 | async-start | bytes 9437184 | tf_op jit(solution)/shard_map/all_gather | solution.py:112
  7.7 21.6 %collective-permute-start = (bf16[3,2048]{0,1:T(8,128)(2,1)S(1)}, bf16[3,2048]{0,1:T(8,128)(2,1)S(1)}, u32[]{:S(2)}, u32[]{:S(2)}) collective-permute-start(bf16[3,2048]{0,1:T(8,128)(2,1)S(1)} %copy.54), channel_id=1, source_target_pairs={{0,4},{4,8},{8,12},{12,16},{16,20},{20,24},{24,28},{1,5},{5,9},{9,... | collective-permute-start | bytes 36872 | tf_op jit(solution)/shard_map/ppermute | solution.py:20
  13.5 14.4 %collective-permute-start.1 = (bf16[3,2,256]{0,2,1:T(8,128)(2,1)S(1)}, bf16[3,2,256]{0,2,1:T(8,128)(2,1)S(1)}, u32[]{:S(2)}, u32[]{:S(2)}) collective-permute-start(bf16[3,2,256]{0,2,1:T(8,128)(2,1)S(1)} %copy.61), channel_id=1, source_target_pairs={{0,4},{4,8},{8,12},{12,16},{16,20},{20,24},{24,28},{1,5},{5,9},{9,... | collective-permute-start | bytes 9224 | tf_op jit(solution)/shard_map/ppermute | solution.py:20
  38.8 26.8 %copy-start.7 = (f32[32]{0:T(128)S(1)}, f32[32]{0:T(128)}, u32[]{:S(2)}) copy-start(f32[32]{0:T(128)} %param.21) | copy-start | bytes 388
  38.8 26.9 %copy-start.5 = (bf16[2048]{0:T(1024)(128)(2,1)S(1)}, bf16[2048]{0:T(1024)(128)(2,1)}, u32[]{:S(2)}) copy-start(bf16[2048]{0:T(1024)(128)(2,1)} %param.22) | copy-start | bytes 12292
  40.6 201.7 %reduce-scatter.2.cloned.1.call-start = ((), (), s32[]{:S(2)}) async-start(), calls=%async_computation.1 | async-start | bytes 5242880 | tf_op jit(solution)/shard_map/reduce_scatter | solution.py:131
  166.5 15.7 %copy-start = (f32[2,16,64,512]{3,2,1,0:T(8,128)S(1)}, f32[2,16,64,512]{3,2,1,0:T(8,128)}, u32[]{:S(2)}) copy-start(f32[2,16,64,512]{3,2,1,0:T(8,128)} %fusion.19) | copy-start | bytes 12582916
  166.5 15.7 %copy-start.2 = (f32[2,16,64,512]{3,2,1,0:T(8,128)S(1)}, f32[2,16,64,512]{3,2,1,0:T(8,128)}, u32[]{:S(2)}) copy-start(f32[2,16,64,512]{3,2,1,0:T(8,128)} %fusion) | copy-start | bytes 12582916
  182.2 2.2 copy-start.1
  182.2 4.7 %slice-start = ((s8[16777216]{0:T(1024)(128)(4,1)}), s8[4194304]{0:T(1024)(128)(4,1)S(1)}, s32[]{:S(2)}) async-start(s8[16777216]{0:T(1024)(128)(4,1)} %bitcast.123), calls=%async_computation.3 | async-start | bytes 8388608
  182.2 4.7 %slice-start.1 = ((s8[16777216]{0:T(1024)(128)(4,1)}), s8[4194304]{0:T(1024)(128)(4,1)S(1)}, s32[]{:S(2)}) async-start(s8[16777216]{0:T(1024)(128)(4,1)} %bitcast.123), calls=%async_computation.4 | async-start | bytes 8388608
  184.4 3.3 %slice-start.2 = ((s8[16777216]{0:T(1024)(128)(4,1)}), s8[4194304]{0:T(1024)(128)(4,1)S(1)}, s32[]{:S(2)}) async-start(s8[16777216]{0:T(1024)(128)(4,1)} %bitcast.123), calls=%async_computation.5 | async-start | bytes 8388608
  184.4 4.4 %slice-start.3 = ((s8[16777216]{0:T(1024)(128)(4,1)}), s8[4194304]{0:T(1024)(128)(4,1)S(1)}, s32[]{:S(2)}) async-start(s8[16777216]{0:T(1024)(128)(4,1)} %bitcast.123), calls=%async_computation.6 | async-start | bytes 8388608
Sparse Core Ops, SparseCore 0:
  40.7 125.7 all-gather.2
  199.6 42.6 reduce-scatter.1
where the time goes:
time: 250 us; the launch traced here: 249 us
  waiting for transfers between devices  129 us (52%)
  matrix products  44.7 us (18%)
  blocking collectives  20.8 us (8%)
  other arithmetic  18.7 us (7%)
  local copies, waits for them, and re-layouts  13.9 us (6%)
  between operations  13.7 us (5%)
  starting transfers between devices  8.35 us (3%)
    all_gather x1, waiting for transfers between devices, body(): shards = lax.all_gather(local_state[None], 'ctx', axis=0, tiled=True)  86 us
    reduce_scatter x1, waiting for transfers between devices, body(): lax.psum_scatter(jnp.dot(normed, out_weight, preferred_element_type=jnp.f...  42.8 us
    all_gather x1, blocking collectives, body(): totals = lax.all_gather(own_total, 'ctx', axis=0, tiled=True)  20.8 us
    dot_general x1, matrix products, body(): jnp.einsum('kgh,kghpn->ghpn', weights_far, shards, precision=lax.Precisio...  15.7 us
    convert_element_type x2, other arithmetic, conv_silu(): return lax.optimization_barrier(jax.nn.silu(summed).astype(jnp.bfloat16))  10.9 us
    dot_general x1, matrix products, body(): jnp.dot(normed, out_weight, preferred_element_type=jnp.float32)  10.6 us
    unnamed x27, local copies, waits for them, and re-layouts  10.5 us
    dot_general x1, matrix products, block_local(): jnp.einsum('ghij,jghp->ighp', mixing, inner_block, preferred_element_type...  10.4 us
  transfers between devices with their start and end apart: 4, of which 2 were waited for; matrix products, arithmetic and copies ran while one was open for 13% of the time, Pallas kernels for 0%

commit v1 on v0

--- a/solution.py
+++ b/solution.py
@@ -29,9 +29,7 @@
     return lax.optimization_barrier(jax.nn.silu(summed).astype(jnp.bfloat16))
 
 
-def block_local(carried_in, inputs_block):
-    local_state, entry_decay = carried_in
-    inner_block, b_block, c_block, step_sizes, log_rates = inputs_block
+def block_parts(inner_block, b_block, c_block, step_sizes, log_rates):
     length = inner_block.shape[0]
     cumulative = jnp.cumsum(log_rates, axis=0)
     along = jnp.transpose(cumulative, (1, 2, 0))
@@ -46,21 +44,42 @@
     diagonal = jnp.einsum(
         "ghij,jghp->ighp", mixing, inner_block, preferred_element_type=jnp.float32
     )
-    within = jnp.exp(cumulative)
-    carried = within[..., None] * jnp.einsum(
-        "ign,ghpn->ighp", c_block.astype(jnp.float32), local_state, precision=lax.Precision.HIGHEST
-    )
     tail_weight = jnp.exp(cumulative[-1][None] - cumulative) * step_sizes
     weighted = (inner_block * tail_weight[..., None]).astype(jnp.bfloat16)
     block_state = jnp.einsum(
         "jghp,jgn->ghpn", weighted, b_block, preferred_element_type=jnp.float32
     )
-    block_decay = jnp.exp(cumulative[-1])
-    new_state = block_decay[..., None, None] * local_state + block_state
+    return diagonal, cumulative, block_state
+
+
+def apply_state(c_block, state, cumulative):
+    return jnp.exp(cumulative)[..., None] * jnp.einsum(
+        "ign,ghpn->ighp", c_block.astype(jnp.float32), state, precision=lax.Precision.HIGHEST
+    )
+
+
+def block_local(carried_in, inputs_block):
+    local_state, entry_total = carried_in
+    inner_block, b_block, c_block, step_sizes, log_rates = inputs_block
+    diagonal, cumulative, block_state = block_parts(*inputs_block)
+    carried = apply_state(c_block, local_state, cumulative)
+    new_state = jnp.exp(cumulative[-1])[..., None, None] * local_state + block_state
     return (
-        (new_state, entry_decay * block_decay),
-        (diagonal + carried, within * entry_decay[None]),
+        (new_state, entry_total + cumulative[-1]),
+        (diagonal + carried, cumulative + entry_total[None]),
     )
+
+
+def entering_state(total, state, axis):
+    count = lax.axis_size(axis)
+    total, state = shifted((total, state), axis, 1)
+    span = 1
+    while span < count - 1:
+        far_total, far_state = shifted((total, state), axis, span)
+        state = jnp.exp(total)[..., None, None] * far_state + state
+        total = total + far_total
+        span *= 2
+    return state
 
 
 def body(
@@ -99,25 +118,19 @@
         step_sizes.reshape(blocks, BLK, groups_here, per_group),
         log_rates.reshape(blocks, BLK, groups_here, per_group),
     )
-    start_state = jnp.zeros((groups_here, per_group, HEAD_DIM, STATE), jnp.float32)
-    start_decay = jnp.ones((groups_here, per_group), jnp.float32)
-    (local_state, device_decay), (partial_heads, factors) = lax.scan(
-        block_local, (start_state, start_decay), inputs_all
-    )
-    own_total = jnp.sum(log_rates, axis=0).reshape(1, groups_here, per_group)
-    totals = lax.all_gather(own_total, "ctx", axis=0, tiled=True)
-    through = jnp.cumsum(totals, axis=0)
-    position = lax.axis_index("ctx")
-    before = lax.dynamic_index_in_dim(through - totals, position, 0, keepdims=False)
-    shards = lax.all_gather(local_state[None], "ctx", axis=0, tiled=True)
-    amount = shards.shape[0]
-    anchor = lax.broadcasted_iota(jnp.int32, (amount, 1, 1), 0)
-    earlier = anchor < position
-    weights_far = jnp.where(earlier, jnp.exp(jnp.where(earlier, before[None] - through, 0.0)), 0.0)
-    state_in = jnp.einsum("kgh,kghpn->ghpn", weights_far, shards, precision=lax.Precision.HIGHEST)
-    correction = factors[..., None] * jnp.einsum(
-        "bign,ghpn->bighp", c_all.astype(jnp.float32), state_in, precision=lax.Precision.HIGHEST
-    )
+    if blocks == 1:
+        diagonal, cumulative, local_state = block_parts(*(x[0] for x in inputs_all))
+        partial_heads = diagonal[None]
+        factors = cumulative[None]
+        device_total = cumulative[-1]
+    else:
+        start_state = jnp.zeros((groups_here, per_group, HEAD_DIM, STATE), jnp.float32)
+        start_total = jnp.zeros((groups_here, per_group), jnp.float32)
+        (local_state, device_total), (partial_heads, factors) = lax.scan(
+            block_local, (start_state, start_total), inputs_all
+        )
+    state_in = entering_state(device_total, local_state, "ctx")
+    correction = jax.vmap(apply_state, in_axes=(0, None, 0))(c_all, state_in, factors)
     width_here = groups_here * per_group * HEAD_DIM
     mixed_heads = (partial_heads + correction).reshape(tokens, width_here) + jnp.repeat(
         skip_gain, HEAD_DIM

time: 250 us -> 240 us (0.960)
  starting transfers between devices: 8.35 us -> 41.1 us
  blocking collectives: 20.8 us -> 0 us
  matrix products: 44.7 us -> 24.5 us
  waiting for transfers between devices: 129 us -> 124 us
  other arithmetic: 18.7 us -> 23.1 us
    all_gather x1 -> x0, waiting for transfers between devices: 86 us -> none  [body(): shards = lax.all_gather(local_state[None], 'ctx', axis=0, tiled=True)]
    ppermute x2 -> x9, waiting for transfers between devices: 0.01 us -> 57.1 us  [shifted(): return lax.ppermute(value, axis, pairs)]
    ppermute x2 -> x9, starting transfers between devices: 8.31 us -> 41.1 us  [shifted(): return lax.ppermute(value, axis, pairs)]
    reduce_scatter x1, waiting for transfers between devices: 42.8 us -> 66.9 us  [body(): lax.psum_scatter(jnp.dot(normed, out_weight, preferred_element_type=jnp.f...]
    all_gather x1 -> x0, blocking collectives: 20.8 us -> none  [body(): totals = lax.all_gather(own_total, 'ctx', axis=0, tiled=True)]
    dot_general x6 -> x4, matrix products: 34.2 us -> 13.6 us  [the longest x1 9.45 us: block_parts(): jnp.einsum('ghij,jghp->ighp', mixing, inner_block, preferred_element_type...]
    unnamed x27 -> x25, local copies, waits for them, and re-layouts: 10.5 us -> 8.68 us
  transfers between devices with their start and end apart: 4 -> 10, of which waited for: 2 -> 6; matrix products, arithmetic and copies ran while one was open for 13% -> 13% of each run, Pallas kernels for 0% -> 0%
where the time goes in v1:
time: 240 us
  waiting for transfers between devices  124 us (52%)
  starting transfers between devices  41.1 us (17%)
  matrix products  24.5 us (10%)
  other arithmetic  23.1 us (10%)
  between operations  13.8 us (6%)
  local copies, waits for them, and re-layouts  13.2 us (6%)
    reduce_scatter x1, waiting for transfers between devices, body(): lax.psum_scatter(jnp.dot(normed, out_weight, preferred_element_type=jnp.f...  66.9 us
    ppermute x9, waiting for transfers between devices, shifted(): return lax.ppermute(value, axis, pairs)  57.1 us
    ppermute x9, starting transfers between devices, shifted(): return lax.ppermute(value, axis, pairs)  41.1 us
    convert_element_type x2, other arithmetic, conv_silu(): return lax.optimization_barrier(jax.nn.silu(summed).astype(jnp.bfloat16))  11.3 us
    dot_general x1, matrix products, body(): jnp.dot(normed, out_weight, preferred_element_type=jnp.float32)  11 us
    dot_general x1, matrix products, block_parts(): jnp.einsum('ghij,jghp->ighp', mixing, inner_block, preferred_element_type...  9.45 us
    unnamed x25, local copies, waits for them, and re-layouts  8.68 us
  transfers between devices with their start and end apart: 10, of which 6 were waited for; matrix products, arithmetic and copies ran while one was open for 13% of the time, Pallas kernels for 0%

profile of v1, /device:TPU:0, one launch (start us, length us, event | category | flops | bytes accessed | tf_op | source)
XLA Modules:
  0.0 239.6 jit_solution(11391875637520399085)
XLA Ops:
  6.5 0.8 slice.65
  7.7 4.9 %collective-permute-start = (bf16[3,2048]{0,1:T(8,128)(2,1)S(1)}, bf16[3,2048]{0,1:T(8,128)(2,1)S(1)}, u32[]{:S(2)}, u32[]{:S(2)}) collective-permute-start(bf16[3,2048]{0,1:T(8,128)(2,1)S(1)} %copy.36), channel_id=1, source_target_pairs={{0,4},{4,8},{8,12},{12,16},{16,20},{20,24},{24,28},{1,5},{5,9},{9,... | collective-permute-start | bytes 36872 | tf_op jit(solution)/shard_map/ppermute | solution.py:20
  13.5 3.4 %collective-permute-start.1 = (bf16[3,2,256]{0,2,1:T(8,128)(2,1)S(1)}, bf16[3,2,256]{0,2,1:T(8,128)(2,1)S(1)}, u32[]{:S(2)}, u32[]{:S(2)}) collective-permute-start(bf16[3,2,256]{0,2,1:T(8,128)(2,1)S(1)} %copy.43), channel_id=1, source_target_pairs={{0,4},{4,8},{8,12},{12,16},{16,20},{20,24},{24,28},{1,5},{5,9},{9,... | collective-permute-start | bytes 9224 | tf_op jit(solution)/shard_map/ppermute | solution.py:20
  17.6 0.9 negate_multiply_fusion
  18.5 2.3 reduce-window.6
  21.0 0.7 bitcast_bitcast_fusion
  21.9 0.9 slice_convert_fusion.3
  22.9 0.7 bitcast_convert_fusion.3
  23.7 3.9 %copy.37 = bf16[512,2048]{0,1:T(8,128)(2,1)} copy(bf16[512,2048]{1,0:T(8,128)(2,1)} %param.12) | data formatting | bytes 4194304 | tf_op args[0]
  27.6 0.7 copy.44
  28.4 1.3 multiply_convert_fusion.5
  29.8 9.9 %multiply_convert_fusion.3 = bf16[512,2048]{0,1:T(8,128)(2,1)S(1)} fusion(bf16[512,2048]{0,1:T(8,128)(2,1)} %copy.37, bf16[3,2048]{0,1:T(8,128)(2,1)S(1)} %collective-permute-done, f32[2048]{0:T(1024)S(1)} %bitcast.99, f32[2048]{0:T(1024)S(1)} %bitcast.100, f32[2048]{0:T(1024)S(1)} %bitcast.98, f32[2048]{0:T(1024)S(1)} %bitcast.97, ...), kind=kLoop, calls=%fused_computation.18 | loop fusion | flops 27262976 | bytes 4247552 | tf_op jit(solution)/shard_map/convert_element_type | solution.py:29
  40.5 3.5 %collective-permute-start.5 = (f32[2,16,64,128]{3,2,1,0:T(8,128)S(1)}, f32[2,16,64,128]{3,2,1,0:T(8,128)S(1)}, u32[]{:S(2)}, u32[]{:S(2)}) collective-permute-start(f32[2,16,64,128]{3,2,1,0:T(8,128)S(1)} %fusion.11), channel_id=1, source_target_pairs={{0,4},{4,8},{8,12},{12,16},{16,20},{20,24},{24,28},{1,5},{5,9},{9,... | collective-permute-start | bytes 3145736 | tf_op jit(solution)/shard_map/ppermute | solution.py:20
  43.9 21.8 %collective-permute-done.5 = f32[2,16,64,128]{3,2,1,0:T(8,128)S(1)} collective-permute-done((f32[2,16,64,128]{3,2,1,0:T(8,128)S(1)}, f32[2,16,64,128]{3,2,1,0:T(8,128)S(1)}, u32[]{:S(2)}, u32[]{:S(2)}) %collective-permute-start.5) | collective-permute-done | bytes 1048608 | tf_op jit(solution)/shard_map/ppermute | solution.py:20
  65.7 4.4 %collective-permute-start.6 = (f32[2,16,64,128]{3,2,1,0:T(8,128)S(1)}, f32[2,16,64,128]{3,2,1,0:T(8,128)S(1)}, u32[]{:S(2)}, u32[]{:S(2)}) collective-permute-start(f32[2,16,64,128]{3,2,1,0:T(8,128)S(1)} %collective-permute-done.5), channel_id=1, source_target_pairs={{0,4},{4,8},{8,12},{12,16},{16,20},{20,24},{24,28},{1,5},{5,9},{9,... | collective-permute-start | bytes 3145736 | tf_op jit(solution)/shard_map/ppermute | solution.py:20
  70.2 4.3 %collective-permute-start.2 = (f32[2,16]{1,0:T(2,128)S(1)}, f32[2,16]{1,0:T(2,128)S(1)}, u32[]{:S(2)}, u32[]{:S(2)}) collective-permute-start(f32[2,16]{1,0:T(2,128)S(1)} %slice_reduce_fusion), channel_id=1, source_target_pairs={{0,4},{4,8},{8,12},{12,16},{16,20},{20,24},{24,28},{1,5},{5,9},{9,... | collective-permute-start | bytes 392 | tf_op jit(solution)/shard_map/ppermute | solution.py:20
  74.5 16.6 %collective-permute-done.2 = f32[2,16]{1,0:T(2,128)S(1)} collective-permute-done((f32[2,16]{1,0:T(2,128)S(1)}, f32[2,16]{1,0:T(2,128)S(1)}, u32[]{:S(2)}, u32[]{:S(2)}) %collective-permute-start.2) | collective-permute-done | bytes 160 | tf_op jit(solution)/shard_map/ppermute | solution.py:20
  91.1 4.4 %collective-permute-start.3 = (f32[2,16]{1,0:T(2,128)S(1)}, f32[2,16]{1,0:T(2,128)S(1)}, u32[]{:S(2)}, u32[]{:S(2)}) collective-permute-start(f32[2,16]{1,0:T(2,128)S(1)} %collective-permute-done.2), channel_id=1, source_target_pairs={{0,4},{4,8},{8,12},{12,16},{16,20},{20,24},{24,28},{1,5},{5,9},{9,... | collective-permute-start | bytes 392 | tf_op jit(solution)/shard_map/ppermute | solution.py:20
  95.5 1.3 collective-permute-done.3
  97.5 7.9 %collective-permute-start.7 = (f32[2,16,64,128]{3,2,1,0:T(8,128)S(1)}, f32[2,16,64,128]{3,2,1,0:T(8,128)}, u32[]{:S(2)}, u32[]{:S(2)}) collective-permute-start(f32[2,16,64,128]{3,2,1,0:T(8,128)S(1)} %multiply_add_fusion.1), channel_id=1, source_target_pairs={{0,8},{4,12},{8,16},{12,20},{16,24},{20,28},{1,9},{5,13},{9,17},{1... | collective-permute-start | bytes 3145736 | tf_op jit(solution)/shard_map/ppermute | solution.py:20
  105.5 3.9 %copy.50 = bf16[512,2048]{0,1:T(8,128)(2,1)} copy(bf16[512,2048]{1,0:T(8,128)(2,1)} %param.14) | data formatting | bytes 4194304 | tf_op args[2]
  110.9 2.5 %collective-permute-start.4 = (f32[2,16]{1,0:T(2,128)}, f32[2,16]{1,0:T(2,128)S(1)}, u32[]{:S(2)}, u32[]{:S(2)}) collective-permute-start(f32[2,16]{1,0:T(2,128)} %get-tuple-element.8), channel_id=1, source_target_pairs={{0,8},{4,12},{8,16},{12,20},{16,24},{20,28},{1,9},{5,13},{9,17},{1... | collective-permute-start | bytes 392 | tf_op jit(solution)/shard_map/ppermute | solution.py:20
  114.1 9.2 %collective-permute-done.4 = f32[2,16]{1,0:T(2,128)S(1)} collective-permute-done((f32[2,16]{1,0:T(2,128)}, f32[2,16]{1,0:T(2,128)S(1)}, u32[]{:S(2)}, u32[]{:S(2)}) %collective-permute-start.4) | collective-permute-done | bytes 160 | tf_op jit(solution)/shard_map/ppermute | solution.py:20
  124.0 1.4 fusion.23
  125.5 1.4 multiply_add_fusion
  126.9 5.7 %collective-permute-start.8 = (f32[2,16,64,128]{3,2,1,0:T(8,128)S(1)}, f32[2,16,64,128]{3,2,1,0:T(8,128)S(1)}, u32[]{:S(2)}, u32[]{:S(2)}) collective-permute-start(f32[2,16,64,128]{3,2,1,0:T(8,128)S(1)} %multiply_add_fusion), channel_id=1, source_target_pairs={{0,16},{4,20},{8,24},{12,28},{1,17},{5,21},{9,25},{13,29},{2,18},{... | collective-permute-start | bytes 3145736 | tf_op jit(solution)/shard_map/ppermute | solution.py:20
  132.6 9.5 %fusion = f32[2,16,64,512]{3,2,1,0:T(8,128)S(1)} fusion(bf16[512,2,16,64]{0,3,2,1:T(8,128)(2,1)S(1)} %bitcast.88, f32[2,16,512]{2,1,0:T(8,128)S(1)} %bitcast.95, f32[2,512,512]{2,1,0:T(8,128)S(1)} %fusion.23, f32[2,16,512]{2,1,0:T(8,128)S(1)} %copy-done.3, pred[512,512]{1,0:T(8,128)(4,1)S(1)} %iota_compare_fusion), kind=kOutput, calls=%fused_computation.1 | convolution fusion | flops 1115684864 | bytes 8781824 | tf_op jit(solution)/shard_map/ghij,jghp->ighp/dot_general | solution.py:44
  142.1 8.2 %collective-permute-done.8 = f32[2,16,64,128]{3,2,1,0:T(8,128)S(1)} collective-permute-done((f32[2,16,64,128]{3,2,1,0:T(8,128)S(1)}, f32[2,16,64,128]{3,2,1,0:T(8,128)S(1)}, u32[]{:S(2)}, u32[]{:S(2)}) %collective-permute-start.8) | collective-permute-done | bytes 1048608 | tf_op jit(solution)/shard_map/ppermute | solution.py:20
  150.3 2.0 fusion.6
  152.3 2.1 bitcast_reduce_fusion
  154.9 11.0 %convolution_convert_fusion = bf16[512,4096]{1,0:T(8,128)(2,1)} fusion(bf16[512,2048]{0,1:T(8,128)(2,1)S(1)} %fusion.8, bf16[2048,4096]{1,0:T(8,128)(2,1)S(1)} %bitcast.103), kind=kOutput, calls=%fused_computation.3 | convolution fusion | flops 8592031744 | bytes 23068672 | tf_op jit(solution)/shard_map/dot_general | solution.py:145
  165.8 66.9 %reduce-scatter.2.cloned.1.call-done = bf16[128,4096]{1,0:T(8,128)(2,1)} async-done(((bf16[512,4096]{1,0:T(8,128)(2,1)}), bf16[128,4096]{1,0:T(8,128)(2,1)}) %reduce-scatter.2.cloned.1.call-update) | async-done | bytes 1048592 | tf_op jit(solution)/shard_map/reduce_scatter | solution.py:144
  (54 shorter events, 7.2 us)
Async XLA Ops:
  6.5 21.1 %copy-start.2 = (bf16[512,2,256]{2,1,0:T(2,128)(2,1)S(1)}, bf16[512,2,256]{2,1,0:T(2,128)(2,1)}, u32[]{:S(2)}) copy-start(bf16[512,2,256]{2,1,0:T(2,128)(2,1)} %param.13) | copy-start | bytes 1572868
  6.5 21.8 %copy-start.5 = (bf16[2048]{0:T(1024)(128)(2,1)S(1)}, bf16[2048]{0:T(1024)(128)(2,1)}, u32[]{:S(2)}) copy-start(bf16[2048]{0:T(1024)(128)(2,1)} %param.18) | copy-start | bytes 12292
  6.5 21.8 %copy-start.6 = (bf16[2,256]{1,0:T(2,128)(2,1)S(1)}, bf16[2,256]{1,0:T(2,128)(2,1)}, u32[]{:S(2)}) copy-start(bf16[2,256]{1,0:T(2,128)(2,1)} %param.19) | copy-start | bytes 3076
  6.5 226.2 %reduce-scatter.2.cloned.1.call-start = ((), (), s32[]{:S(2)}) async-start(), calls=%async_computation.1 | async-start | bytes 5242880 | tf_op jit(solution)/shard_map/reduce_scatter | solution.py:144
  7.7 22.1 %collective-permute-start = (bf16[3,2048]{0,1:T(8,128)(2,1)S(1)}, bf16[3,2048]{0,1:T(8,128)(2,1)S(1)}, u32[]{:S(2)}, u32[]{:S(2)}) collective-permute-start(bf16[3,2048]{0,1:T(8,128)(2,1)S(1)} %copy.36), channel_id=1, source_target_pairs={{0,4},{4,8},{8,12},{12,16},{16,20},{20,24},{24,28},{1,5},{5,9},{9,... | collective-permute-start | bytes 36872 | tf_op jit(solution)/shard_map/ppermute | solution.py:20
  13.5 14.9 %collective-permute-start.1 = (bf16[3,2,256]{0,2,1:T(8,128)(2,1)S(1)}, bf16[3,2,256]{0,2,1:T(8,128)(2,1)S(1)}, u32[]{:S(2)}, u32[]{:S(2)}) collective-permute-start(bf16[3,2,256]{0,2,1:T(8,128)(2,1)S(1)} %copy.43), channel_id=1, source_target_pairs={{0,4},{4,8},{8,12},{12,16},{16,20},{20,24},{24,28},{1,5},{5,9},{9,... | collective-permute-start | bytes 9224 | tf_op jit(solution)/shard_map/ppermute | solution.py:20
  29.8 67.7 %copy-start.1 = (bf16[512,1,256]{0,2,1:T(8,128)(2,1)}, bf16[512,1,256]{0,2,1:T(8,128)(2,1)S(1)}, u32[]{:S(2)}) copy-start(bf16[512,1,256]{0,2,1:T(8,128)(2,1)S(1)} %get-tuple-element.9) | copy-start | bytes 786436
  40.5 25.2 %collective-permute-start.5 = (f32[2,16,64,128]{3,2,1,0:T(8,128)S(1)}, f32[2,16,64,128]{3,2,1,0:T(8,128)S(1)}, u32[]{:S(2)}, u32[]{:S(2)}) collective-permute-start(f32[2,16,64,128]{3,2,1,0:T(8,128)S(1)} %fusion.11), channel_id=1, source_target_pairs={{0,4},{4,8},{8,12},{12,16},{16,20},{20,24},{24,28},{1,5},{5,9},{9,... | collective-permute-start | bytes 3145736 | tf_op jit(solution)/shard_map/ppermute | solution.py:20
  65.7 31.6 %collective-permute-start.6 = (f32[2,16,64,128]{3,2,1,0:T(8,128)S(1)}, f32[2,16,64,128]{3,2,1,0:T(8,128)S(1)}, u32[]{:S(2)}, u32[]{:S(2)}) collective-permute-start(f32[2,16,64,128]{3,2,1,0:T(8,128)S(1)} %collective-permute-done.5), channel_id=1, source_target_pairs={{0,4},{4,8},{8,12},{12,16},{16,20},{20,24},{24,28},{1,5},{5,9},{9,... | collective-permute-start | bytes 3145736 | tf_op jit(solution)/shard_map/ppermute | solution.py:20
  70.2 20.9 %collective-permute-start.2 = (f32[2,16]{1,0:T(2,128)S(1)}, f32[2,16]{1,0:T(2,128)S(1)}, u32[]{:S(2)}, u32[]{:S(2)}) collective-permute-start(f32[2,16]{1,0:T(2,128)S(1)} %slice_reduce_fusion), channel_id=1, source_target_pairs={{0,4},{4,8},{8,12},{12,16},{16,20},{20,24},{24,28},{1,5},{5,9},{9,... | collective-permute-start | bytes 392 | tf_op jit(solution)/shard_map/ppermute | solution.py:20
  91.1 5.7 %collective-permute-start.3 = (f32[2,16]{1,0:T(2,128)S(1)}, f32[2,16]{1,0:T(2,128)S(1)}, u32[]{:S(2)}, u32[]{:S(2)}) collective-permute-start(f32[2,16]{1,0:T(2,128)S(1)} %collective-permute-done.2), channel_id=1, source_target_pairs={{0,4},{4,8},{8,12},{12,16},{16,20},{20,24},{24,28},{1,5},{5,9},{9,... | collective-permute-start | bytes 392 | tf_op jit(solution)/shard_map/ppermute | solution.py:20
  97.5 27.9 %collective-permute-start.7 = (f32[2,16,64,128]{3,2,1,0:T(8,128)S(1)}, f32[2,16,64,128]{3,2,1,0:T(8,128)}, u32[]{:S(2)}, u32[]{:S(2)}) collective-permute-start(f32[2,16,64,128]{3,2,1,0:T(8,128)S(1)} %multiply_add_fusion.1), channel_id=1, source_target_pairs={{0,8},{4,12},{8,16},{12,20},{16,24},{20,28},{1,9},{5,13},{9,17},{1... | collective-permute-start | bytes 3145736 | tf_op jit(solution)/shard_map/ppermute | solution.py:20
  110.8 21.8 %copy-start.3 = (f32[2,16,512]{2,1,0:T(8,128)S(1)}, f32[2,16,512]{2,1,0:T(8,128)}, u32[]{:S(2)}) copy-start(f32[2,16,512]{2,1,0:T(8,128)} %get-tuple-element.14) | copy-start | bytes 196612
  110.9 12.4 %collective-permute-start.4 = (f32[2,16]{1,0:T(2,128)}, f32[2,16]{1,0:T(2,128)S(1)}, u32[]{:S(2)}, u32[]{:S(2)}) collective-permute-start(f32[2,16]{1,0:T(2,128)} %get-tuple-element.8), channel_id=1, source_target_pairs={{0,8},{4,12},{8,16},{12,20},{16,24},{20,28},{1,9},{5,13},{9,17},{1... | collective-permute-start | bytes 392 | tf_op jit(solution)/shard_map/ppermute | solution.py:20
  126.9 23.4 %collective-permute-start.8 = (f32[2,16,64,128]{3,2,1,0:T(8,128)S(1)}, f32[2,16,64,128]{3,2,1,0:T(8,128)S(1)}, u32[]{:S(2)}, u32[]{:S(2)}) collective-permute-start(f32[2,16,64,128]{3,2,1,0:T(8,128)S(1)} %multiply_add_fusion), channel_id=1, source_target_pairs={{0,16},{4,20},{8,24},{12,28},{1,17},{5,21},{9,25},{13,29},{2,18},{... | collective-permute-start | bytes 3145736 | tf_op jit(solution)/shard_map/ppermute | solution.py:20
  132.6 22.2 %slice-start = ((s8[16777216]{0:T(1024)(128)(4,1)}), s8[4194304]{0:T(1024)(128)(4,1)S(1)}, s32[]{:S(2)}) async-start(s8[16777216]{0:T(1024)(128)(4,1)} %bitcast.102), calls=%async_computation.2 | async-start | bytes 8388608
  132.6 22.2 %slice-start.1 = ((s8[16777216]{0:T(1024)(128)(4,1)}), s8[4194304]{0:T(1024)(128)(4,1)S(1)}, s32[]{:S(2)}) async-start(s8[16777216]{0:T(1024)(128)(4,1)} %bitcast.102), calls=%async_computation.3 | async-start | bytes 8388608
  132.6 22.2 %slice-start.2 = ((s8[16777216]{0:T(1024)(128)(4,1)}), s8[4194304]{0:T(1024)(128)(4,1)S(1)}, s32[]{:S(2)}) async-start(s8[16777216]{0:T(1024)(128)(4,1)} %bitcast.102), calls=%async_computation.4 | async-start | bytes 8388608
  150.3 2.0 copy-start
  150.3 2.0 copy-start.4
  150.3 4.6 %slice-start.3 = ((s8[16777216]{0:T(1024)(128)(4,1)}), s8[4194304]{0:T(1024)(128)(4,1)S(1)}, s32[]{:S(2)}) async-start(s8[16777216]{0:T(1024)(128)(4,1)} %bitcast.102), calls=%async_computation.5 | async-start | bytes 8388608
Sparse Core Ops, SparseCore 0:
  166.0 66.7 reduce-scatter.1

commit v2 on v1

--- a/solution.py
+++ b/solution.py
@@ -1,7 +1,7 @@
 import jax
 import jax.numpy as jnp
 from jax import lax
-from jax.sharding import PartitionSpec as P
+from jax.sharding import Mesh, PartitionSpec as P
 
 SSM_HEAD_COUNT = 128
 HEAD_DIM = 64
@@ -70,16 +70,50 @@
     )
 
 
+def pack(weight, state):
+    rows = state.reshape(-1, state.shape[-1])
+    high = weight.astype(jnp.bfloat16)
+    low = (weight - high.astype(jnp.float32)).astype(jnp.bfloat16)
+    lanes = rows.shape[-1]
+    flat = jnp.concatenate([high.reshape(-1), low.reshape(-1)])
+    pad = (-flat.shape[0]) % (16 * lanes)
+    tail = jnp.pad(flat, (0, pad)).reshape(-1, lanes)
+    return jnp.concatenate([rows.astype(jnp.bfloat16), tail], axis=0)
+
+
+def unpack(packed, weight_shape, state_shape):
+    count = 1
+    for size in state_shape[:-1]:
+        count *= size
+    state = packed[:count].astype(jnp.float32).reshape(state_shape)
+    flat = packed[count:].reshape(-1).astype(jnp.float32)
+    size = 1
+    for s in weight_shape:
+        size *= s
+    weight = (flat[:size] + flat[size : 2 * size]).reshape(weight_shape)
+    return weight, state
+
+
 def entering_state(total, state, axis):
     count = lax.axis_size(axis)
-    total, state = shifted((total, state), axis, 1)
-    span = 1
-    while span < count - 1:
-        far_total, far_state = shifted((total, state), axis, span)
-        state = jnp.exp(total)[..., None, None] * far_state + state
-        total = total + far_total
+    weight = jnp.exp(total)
+    if count == 1:
+        return jnp.zeros_like(state)
+    own = pack(weight, state)
+    near_w, near_s = unpack(shifted(own, axis, 1), weight.shape, state.shape)
+    if count == 2:
+        return near_s
+    far_w, far_s = unpack(shifted(own, axis, 2), weight.shape, state.shape)
+    state = near_w[..., None, None] * far_s + near_s
+    weight = near_w * far_w
+    span = 2
+    while 2 * span < count:
+        far_w, far_s = unpack(shifted(pack(weight, state), axis, span), weight.shape, state.shape)
+        state = weight[..., None, None] * far_s + state
+        weight = weight * far_w
         span *= 2
-    return state
+    far = shifted(state.astype(jnp.bfloat16), axis, span).astype(jnp.float32)
+    return weight[..., None, None] * far + state
 
 
 def body(
@@ -98,12 +132,19 @@
 ):
     tokens = inner_input.shape[0]
     margin = CONV - 1
-    previous = shifted((inner_input[tokens - margin :], state_input[tokens - margin :]), "ctx", 1)
+    inner_width = inner_input.shape[1]
+    halo = jnp.concatenate(
+        [inner_input[tokens - margin :], state_input[tokens - margin :].reshape(margin, -1)], axis=1
+    )
+    halo = shifted(halo, "ctx", 1)
     inner_conv = conv_silu(
-        jnp.concatenate([previous[0], inner_input], axis=0), conv_inner, bias_inner, tokens
+        jnp.concatenate([halo[:, :inner_width], inner_input], axis=0), conv_inner, bias_inner, tokens
     )
     state_conv = conv_silu(
-        jnp.concatenate([previous[1], state_input], axis=0), conv_states, bias_states, tokens
+        jnp.concatenate([halo[:, inner_width:].reshape((margin,) + state_input.shape[1:]), state_input], axis=0),
+        conv_states,
+        bias_states,
+        tokens,
     )
     groups_here = state_input.shape[2] // STATE
     per_group = SSM_HEAD_COUNT // GROUPS
@@ -141,29 +182,37 @@
     normed = (normed.reshape(tokens, width_here) * norm_gain.astype(jnp.float32)).astype(
         jnp.bfloat16
     )
-    return lax.psum_scatter(
-        jnp.dot(normed, out_weight, preferred_element_type=jnp.float32).astype(jnp.bfloat16),
-        "tp",
-        scatter_dimension=0,
-        tiled=True,
-    )
+    projected = jnp.dot(normed, out_weight, preferred_element_type=jnp.float32).astype(jnp.bfloat16)
+    outer = lax.axis_size("ty")
+    inner = lax.axis_size("tc")
+    piece = tokens // (outer * inner)
+    projected = projected.reshape(outer, inner, piece, -1).transpose(1, 0, 2, 3)
+    projected = lax.psum_scatter(projected, "tc", scatter_dimension=0, tiled=True)
+    projected = lax.psum_scatter(projected[0], "ty", scatter_dimension=0, tiled=True)
+    return projected.reshape(piece, -1)
 
 
 def solution(mesh):
+    cores = 2
+    split = Mesh(
+        mesh.devices.reshape(mesh.shape["ctx"], mesh.shape["tp"] // cores, cores),
+        ("ctx", "ty", "tc"),
+    )
+    tp = ("ty", "tc")
     placed = (
-        P("ctx", "tp"),
-        P("ctx", None, "tp"),
-        P("ctx", "tp"),
-        P("ctx", "tp"),
-        P(None, "tp"),
-        P(None, None, "tp"),
-        P("tp"),
-        P(None, "tp"),
-        P("tp"),
-        P("tp"),
-        P("tp"),
-        P("tp", None),
+        P("ctx", tp),
+        P("ctx", None, tp),
+        P("ctx", tp),
+        P("ctx", tp),
+        P(None, tp),
+        P(None, None, tp),
+        P(tp),
+        P(None, tp),
+        P(tp),
+        P(tp),
+        P(tp),
+        P(tp, None),
     )
     return jax.shard_map(
-        body, mesh=mesh, in_specs=placed, out_specs=P(("ctx", "tp"), None), check_vma=False
-    )
+        body, mesh=split, in_specs=placed, out_specs=P(("ctx",) + tp, None), check_vma=False
+    )

time: 240 us -> 189 us (0.79)
  waiting for transfers between devices: 124 us -> 77.6 us
  starting transfers between devices: 41.1 us -> 22.9 us
  matrix products: 24.5 us -> 30.8 us
  other arithmetic: 23.1 us -> 27.2 us
  local copies, waits for them, and re-layouts: 13.2 us -> 15.8 us
    ppermute x9 -> x5, waiting for transfers between devices: 57.1 us -> 11.3 us  [shifted(): return lax.ppermute(value, axis, pairs)]
    ppermute x9 -> x5, starting transfers between devices: 41.1 us -> 22.9 us  [shifted(): return lax.ppermute(value, axis, pairs)]
    convert_element_type x0 -> x9, other arithmetic: none -> 4.93 us  [the longest x1 1.38 us: pack(): return jnp.concatenate([rows.astype(jnp.bfloat16), tail], axis=0)]
    reshape x1 -> x4, local copies, waits for them, and re-layouts: 0.01 us -> 2.63 us  [the longest x1 2.45 us: body(): projected = projected.reshape(outer, inner, piece, -1).transpose(1, 0, 2, 3)]
    unnamed x25 -> x35, local copies, waits for them, and re-layouts: 8.68 us -> 9.4 us
    reduce_scatter x1 -> x2, waiting for transfers between devices: 66.9 us -> 66.2 us  [the longest x1 35.4 us: body(): lax.psum_scatter(projected[0], 'ty', scatter_dimension=0, tiled=True)]
  transfers between devices with their start and end apart: 10 -> 7, of which waited for: 6 -> 4; matrix products, arithmetic and copies ran while one was open for 13% -> 17% of each run, Pallas kernels for 0% -> 0%
where the time goes in v2:
time: 189 us; the launch traced here: 188 us
  waiting for transfers between devices  77.6 us (41%)
  matrix products  30.8 us (16%)
  other arithmetic  27.2 us (14%)
  starting transfers between devices  22.9 us (12%)
  local copies, waits for them, and re-layouts  15.8 us (8%)
  between operations  13.8 us (7%)
    reduce_scatter x1, waiting for transfers between devices, body(): lax.psum_scatter(projected[0], 'ty', scatter_dimension=0, tiled=True)  35.4 us
    reduce_scatter x1, waiting for transfers between devices, body(): lax.psum_scatter(projected, 'tc', scatter_dimension=0, tiled=True)  30.8 us
    ppermute x5, starting transfers between devices, shifted(): return lax.ppermute(value, axis, pairs)  22.9 us
    dot_general x1, matrix products, body(): jnp.dot(normed, out_weight, preferred_element_type=jnp.float32)  12.6 us
    ppermute x5, waiting for transfers between devices, shifted(): return lax.ppermute(value, axis, pairs)  11.3 us
    convert_element_type x2, other arithmetic, conv_silu(): return lax.optimization_barrier(jax.nn.silu(summed).astype(jnp.bfloat16))  11 us
    dot_general x1, matrix products, block_parts(): jnp.einsum('ghij,jghp->ighp', mixing, inner_block, preferred_element_type...  10.5 us
    unnamed x35, local copies, waits for them, and re-layouts  9.4 us
  transfers between devices with their start and end apart: 7, of which 4 were waited for; matrix products, arithmetic and copies ran while one was open for 17% of the time, Pallas kernels for 0%

profile of v2, /device:TPU:0, one launch (start us, length us, event | category | flops | bytes accessed | tf_op | source)
XLA Modules:
  0.0 188.1 jit_solution(1726278995932472996)
XLA Ops:
  6.5 0.8 slice.131
  8.1 4.8 %collective-permute-start = (bf16[3,2560]{1,0:T(4,128)(2,1)S(1)}, bf16[3,2560]{1,0:T(4,128)(2,1)S(1)}, u32[]{:S(2)}, u32[]{:S(2)}) collective-permute-start(bf16[3,2560]{1,0:T(4,128)(2,1)S(1)} %pad_maximum_fusion.4), channel_id=1, source_target_pairs={{0,4},{4,8},{8,12},{12,16},{16,20},{20,24},{24,28},{1,5},{5,9},{9,... | collective-permute-start | bytes 46088 | tf_op jit(solution)/shard_map/ppermute | solution.py:20
  13.6 0.9 negate_multiply_fusion
  14.5 2.3 %reduce-window.6 = f32[16,2,4,128]{3,0,1,2:T(8,128)S(1)} reduce-window(f32[16,2,4,128]{3,0,1,2:T(8,128)S(1)} %bitcast.126, f32[]{:T(128)} %constant.18.clone.1), window={size=1x1x1x128 pad=0_0x0_0x0_0x127_0}, to_apply=%region_0.1 | reduce-window | flops 2080768 | bytes 131076 | tf_op jit(solution)/shard_map/reduce-window
  18.0 0.9 slice_convert_fusion.5
  18.9 0.7 bitcast_convert_fusion.3
  20.5 3.9 %copy.55 = bf16[512,2048]{0,1:T(8,128)(2,1)} copy(bf16[512,2048]{1,0:T(8,128)(2,1)} %param.12) | data formatting | bytes 4194304 | tf_op args[0]
  24.4 0.7 copy.62
  25.6 9.7 %multiply_convert_fusion.3 = bf16[512,2048]{0,1:T(8,128)(2,1)S(1)} fusion(bf16[512,2048]{0,1:T(8,128)(2,1)} %copy.55, bf16[3,2048]{0,1:T(8,128)(2,1)S(1)} %copy.54, f32[2048]{0:T(1024)S(1)} %bitcast.129, f32[2048]{0:T(1024)S(1)} %bitcast.130, f32[2048]{0:T(1024)S(1)} %bitcast.128, f32[2048]{0:T(1024)S(1)} %bitcast.127, f32[2048]{0:T(1024)S(1)} %convert_element_type.150), kind=kLoop, calls=%fused_computation.19 | loop fusion | flops 27262976 | bytes 4247552 | tf_op jit(solution)/shard_map/convert_element_type | solution.py:29
  35.4 1.3 multiply_convert_fusion.7
  36.8 1.6 fusion.13
  38.4 0.8 pad_maximum_fusion.1
  39.2 3.5 %collective-permute-start.1 = (bf16[2064,128]{1,0:T(8,128)(2,1)}, bf16[2064,128]{1,0:T(8,128)(2,1)S(1)}, u32[]{:S(2)}, u32[]{:S(2)}) collective-permute-start(bf16[2064,128]{1,0:T(8,128)(2,1)} %pad_maximum_fusion.1), channel_id=1, source_target_pairs={{0,4},{4,8},{8,12},{12,16},{16,20},{20,24},{24,28},{1,5},{5,9},{9,... | collective-permute-start | bytes 1585160 | tf_op jit(solution)/shard_map/ppermute | solution.py:20
  42.7 4.3 %collective-permute-start.2 = (bf16[2064,128]{1,0:T(8,128)(2,1)}, bf16[2064,128]{1,0:T(8,128)(2,1)}, u32[]{:S(2)}, u32[]{:S(2)}) collective-permute-start(bf16[2064,128]{1,0:T(8,128)(2,1)} %pad_maximum_fusion.1), channel_id=1, source_target_pairs={{0,8},{4,12},{8,16},{12,20},{16,24},{20,28},{1,9},{5,13},{9,17},{1... | collective-permute-start | bytes 1585160 | tf_op jit(solution)/shard_map/ppermute | solution.py:20
  47.0 0.8 iota_compare_fusion
  47.8 4.0 %copy.68 = bf16[512,2048]{0,1:T(8,128)(2,1)} copy(bf16[512,2048]{1,0:T(8,128)(2,1)} %param.14) | data formatting | bytes 4194304 | tf_op args[2]
  52.5 1.8 fusion.39
  54.4 2.8 %collective-permute-done.2 = bf16[2064,128]{1,0:T(8,128)(2,1)} collective-permute-done((bf16[2064,128]{1,0:T(8,128)(2,1)}, bf16[2064,128]{1,0:T(8,128)(2,1)}, u32[]{:S(2)}, u32[]{:S(2)}) %collective-permute-start.2) | collective-permute-done | bytes 528416 | tf_op jit(solution)/shard_map/ppermute | solution.py:20
  58.4 1.4 add_convert_fusion
  59.8 4.7 %collective-permute-start.3 = (bf16[2064,128]{1,0:T(8,128)(2,1)S(1)}, bf16[2064,128]{1,0:T(8,128)(2,1)S(1)}, u32[]{:S(2)}, u32[]{:S(2)}) collective-permute-start(bf16[2064,128]{1,0:T(8,128)(2,1)S(1)} %pad_maximum_fusion.2), channel_id=1, source_target_pairs={{0,8},{4,12},{8,16},{12,20},{16,24},{20,28},{1,9},{5,13},{9,17},{1... | collective-permute-start | bytes 1585160 | tf_op jit(solution)/shard_map/ppermute | solution.py:20
  64.5 1.1 slice_convert_fusion.1
  65.7 8.5 %collective-permute-done.3 = bf16[2064,128]{1,0:T(8,128)(2,1)S(1)} collective-permute-done((bf16[2064,128]{1,0:T(8,128)(2,1)S(1)}, bf16[2064,128]{1,0:T(8,128)(2,1)S(1)}, u32[]{:S(2)}, u32[]{:S(2)}) %collective-permute-start.3) | collective-permute-done | bytes 528416 | tf_op jit(solution)/shard_map/ppermute | solution.py:20
  74.3 1.1 fusion.22
  75.4 5.6 %collective-permute-start.4 = (bf16[2,16,64,128]{3,2,1,0:T(8,128)(2,1)}, bf16[2,16,64,128]{3,2,1,0:T(8,128)(2,1)S(1)}, u32[]{:S(2)}, u32[]{:S(2)}) collective-permute-start(bf16[2,16,64,128]{3,2,1,0:T(8,128)(2,1)} %fusion.22), channel_id=1, source_target_pairs={{0,16},{4,20},{8,24},{12,28},{1,17},{5,21},{9,25},{13,29},{2,18},{... | collective-permute-start | bytes 1572872 | tf_op jit(solution)/shard_map/ppermute | solution.py:20
  81.1 10.5 %fusion = f32[2,16,64,512]{3,2,1,0:T(8,128)} fusion(bf16[512,2,16,64]{0,3,2,1:T(8,128)(2,1)S(1)} %bitcast.112, f32[2,16,512]{2,1,0:T(8,128)S(1)} %bitcast.125, f32[2,512,512]{2,1,0:T(8,128)S(1)} %copy-done.4, f32[2,16,512]{2,1,0:T(8,128)S(1)} %copy-done.7, pred[512,512]{1,0:T(8,128)(4,1)S(1)} %copy-done.6), kind=kOutput, calls=%fused_computation.1 | convolution fusion | flops 1115684864 | bytes 8781824 | tf_op jit(solution)/shard_map/ghij,jghp->ighp/dot_general | solution.py:44
  92.2 0.8 reshape.163
  93.0 4.3 %fusion.6 = f32[1,512,2,16,64]{1,4,3,2,0:T(8,128)S(1)} fusion(f32[2,16,64,512]{3,2,1,0:T(8,128)} %fusion, bf16[512,2,128,1]{0,2,3,1:T(8,128)(2,1)S(1)} %bitcast.117, f32[512,2,16]{0,2,1:T(8,128)S(1)} %get-tuple-element.16, bf16[2,16,64,128]{3,2,1,0:T(8,128)(2,1)S(1)} %collective-permute-done.4, f32[2,16]{1,0:T(2,128)S(1)} %fusion.31, ...), kind=kOutput, calls=%fused_computation.11 | convolution fusion | flops 1614807040 | bytes 11862400 | tf_op jit(solution)/shard_map/vmap(ign,ghpn->ighp)/dot_general | solution.py:56
  97.4 2.1 %bitcast_reduce_fusion = (f32[512,2]{0,1:T(2,128)S(1)}, f32[512,2048]{0,1:T(8,128)S(1)}) fusion(bf16[512,2048]{0,1:T(8,128)(2,1)S(1)} %copy-done.3, bf16[512,2048]{0,1:T(8,128)(2,1)S(1)} %copy-done.2, f32[2048]{0:T(1024)S(1)} %mul.292, f32[1,512,2,16,64]{1,4,3,2,0:T(8,128)S(1)} %fusion.6), kind=kLoop, calls=%fused_computation.15 | loop fusion | flops 11533312 | bytes 12595200 | tf_op jit(solution)/shard_map/reduce_sum | solution.py:181
  99.9 12.6 %convolution_convert_fusion = bf16[512,4096]{1,0:T(8,128)(2,1)S(1)} fusion(bf16[512,2048]{0,1:T(8,128)(2,1)S(1)} %fusion.8, bf16[2048,4096]{1,0:T(8,128)(2,1)} %param.23), kind=kOutput, calls=%fused_computation.3 | convolution fusion | flops 8592031744 | bytes 23068672 | tf_op jit(solution)/shard_map/dot_general | solution.py:185
  112.5 2.5 %copy.89 = bf16[2,2,128,4096]{3,2,0,1:T(8,128)(2,1)} copy(bf16[2,2,128,4096]{3,2,1,0:T(8,128)(2,1)S(1)} %bitcast.115) | data formatting | bytes 8388608 | tf_op jit(solution)/shard_map/reshape | solution.py:189
  115.0 30.8 %reduce-scatter.3.cloned.1.call-done = bf16[1,2,128,4096]{3,2,1,0:T(8,128)(2,1)} async-done(((bf16[2,2,128,4096]{3,2,1,0:T(8,128)(2,1)}), bf16[1,2,128,4096]{3,2,1,0:T(8,128)(2,1)}) %reduce-scatter.3.cloned.1.call-update) | async-done | bytes 2097168 | tf_op jit(solution)/shard_map/reduce_scatter | solution.py:190
  145.8 35.4 %reduce-scatter.5.cloned.1.call-done = bf16[1,128,4096]{2,1,0:T(8,128)(2,1)} async-done(((bf16[2,128,4096]{2,1,0:T(8,128)(2,1)}), bf16[1,128,4096]{2,1,0:T(8,128)(2,1)}) %reduce-scatter.5.cloned.1.call-update) | async-done | bytes 1048592 | tf_op jit(solution)/shard_map/reduce_scatter | solution.py:191
  (80 shorter events, 7.3 us)
Async XLA Ops:
  6.5 17.9 %copy-start.5 = (bf16[512,2,256]{2,1,0:T(2,128)(2,1)S(1)}, bf16[512,2,256]{2,1,0:T(2,128)(2,1)}, u32[]{:S(2)}) copy-start(bf16[512,2,256]{2,1,0:T(2,128)(2,1)} %param.13) | copy-start | bytes 1572868
  6.5 18.6 %copy-start.11 = (bf16[2048]{0:T(1024)(128)(2,1)S(1)}, bf16[2048]{0:T(1024)(128)(2,1)}, u32[]{:S(2)}) copy-start(bf16[2048]{0:T(1024)(128)(2,1)} %param.18) | copy-start | bytes 12292
  6.5 18.7 %copy-start.13 = (bf16[2,256]{1,0:T(2,128)(2,1)S(1)}, bf16[2,256]{1,0:T(2,128)(2,1)}, u32[]{:S(2)}) copy-start(bf16[2,256]{1,0:T(2,128)(2,1)} %param.19) | copy-start | bytes 3076
  6.5 139.2 %reduce-scatter.3.cloned.1.call-start = ((), (), s32[]{:S(2)}) async-start(), calls=%async_computation.2 | async-start | bytes 6291456 | tf_op jit(solution)/shard_map/reduce_scatter | solution.py:190
  8.1 17.1 %collective-permute-start = (bf16[3,2560]{1,0:T(4,128)(2,1)S(1)}, bf16[3,2560]{1,0:T(4,128)(2,1)S(1)}, u32[]{:S(2)}, u32[]{:S(2)}) collective-permute-start(bf16[3,2560]{1,0:T(4,128)(2,1)S(1)} %pad_maximum_fusion.4), channel_id=1, source_target_pairs={{0,4},{4,8},{8,12},{12,16},{16,20},{20,24},{24,28},{1,5},{5,9},{9,... | collective-permute-start | bytes 46088 | tf_op jit(solution)/shard_map/ppermute | solution.py:20
  35.2 16.5 %copy-start = (bf16[512,2048]{0,1:T(8,128)(2,1)}, bf16[512,2048]{0,1:T(8,128)(2,1)S(1)}, u32[]{:S(2)}) copy-start(bf16[512,2048]{0,1:T(8,128)(2,1)S(1)} %multiply_convert_fusion.3) | copy-start | bytes 6291460
  36.8 15.0 %copy-start.14 = (f32[32]{0:T(128)S(1)}, f32[32]{0:T(128)}, u32[]{:S(2)}) copy-start(f32[32]{0:T(128)} %param.21) | copy-start | bytes 388
  36.8 15.1 %copy-start.12 = (bf16[2048]{0:T(1024)(128)(2,1)S(1)}, bf16[2048]{0:T(1024)(128)(2,1)}, u32[]{:S(2)}) copy-start(bf16[2048]{0:T(1024)(128)(2,1)} %param.22) | copy-start | bytes 12292
  39.2 15.1 %collective-permute-start.1 = (bf16[2064,128]{1,0:T(8,128)(2,1)}, bf16[2064,128]{1,0:T(8,128)(2,1)S(1)}, u32[]{:S(2)}, u32[]{:S(2)}) collective-permute-start(bf16[2064,128]{1,0:T(8,128)(2,1)} %pad_maximum_fusion.1), channel_id=1, source_target_pairs={{0,4},{4,8},{8,12},{12,16},{16,20},{20,24},{24,28},{1,5},{5,9},{9,... | collective-permute-start | bytes 1585160 | tf_op jit(solution)/shard_map/ppermute | solution.py:20
  42.7 14.5 %collective-permute-start.2 = (bf16[2064,128]{1,0:T(8,128)(2,1)}, bf16[2064,128]{1,0:T(8,128)(2,1)}, u32[]{:S(2)}, u32[]{:S(2)}) collective-permute-start(bf16[2064,128]{1,0:T(8,128)(2,1)} %pad_maximum_fusion.1), channel_id=1, source_target_pairs={{0,8},{4,12},{8,16},{12,20},{16,24},{20,28},{1,9},{5,13},{9,17},{1... | collective-permute-start | bytes 1585160 | tf_op jit(solution)/shard_map/ppermute | solution.py:20
  58.0 16.3 %copy-start.9 = (f32[2,16]{1,0:T(2,128)}, f32[2,16]{1,0:T(2,128)S(1)}, u32[]{:S(2)}) copy-start(f32[2,16]{1,0:T(2,128)S(1)} %get-tuple-element.11) | copy-start | bytes 388
  59.8 21.3 %copy-start.1 = (bf16[512,2048]{0,1:T(8,128)(2,1)S(1)}, bf16[512,2048]{0,1:T(8,128)(2,1)}, u32[]{:S(2)}) copy-start(bf16[512,2048]{0,1:T(8,128)(2,1)} %copy-done) | copy-start | bytes 6291460
  59.8 21.3 %copy-start.4 = (f32[2,512,512]{2,1,0:T(8,128)S(1)}, f32[2,512,512]{2,1,0:T(8,128)}, u32[]{:S(2)}) copy-start(f32[2,512,512]{2,1,0:T(8,128)} %fusion.39) | copy-start | bytes 6291460
  59.8 21.3 %copy-start.6 = (pred[512,512]{1,0:T(8,128)(4,1)S(1)}, pred[512,512]{1,0:T(8,128)(4,1)}, u32[]{:S(2)}) copy-start(pred[512,512]{1,0:T(8,128)(4,1)} %iota_compare_fusion) | copy-start | bytes 786436
  59.8 21.3 %copy-start.7 = (f32[2,16,512]{2,1,0:T(8,128)S(1)}, f32[2,16,512]{2,1,0:T(8,128)}, u32[]{:S(2)}) copy-start(f32[2,16,512]{2,1,0:T(8,128)} %get-tuple-element.18) | copy-start | bytes 196612
  59.8 14.4 %collective-permute-start.3 = (bf16[2064,128]{1,0:T(8,128)(2,1)S(1)}, bf16[2064,128]{1,0:T(8,128)(2,1)S(1)}, u32[]{:S(2)}, u32[]{:S(2)}) collective-permute-start(bf16[2064,128]{1,0:T(8,128)(2,1)S(1)} %pad_maximum_fusion.2), channel_id=1, source_target_pairs={{0,8},{4,12},{8,16},{12,20},{16,24},{20,28},{1,9},{5,13},{9,17},{1... | collective-permute-start | bytes 1585160 | tf_op jit(solution)/shard_map/ppermute | solution.py:20
  75.4 17.6 %collective-permute-start.4 = (bf16[2,16,64,128]{3,2,1,0:T(8,128)(2,1)}, bf16[2,16,64,128]{3,2,1,0:T(8,128)(2,1)S(1)}, u32[]{:S(2)}, u32[]{:S(2)}) collective-permute-start(bf16[2,16,64,128]{3,2,1,0:T(8,128)(2,1)} %fusion.22), channel_id=1, source_target_pairs={{0,16},{4,20},{8,24},{12,28},{1,17},{5,21},{9,25},{13,29},{2,18},{... | collective-permute-start | bytes 1572872 | tf_op jit(solution)/shard_map/ppermute | solution.py:20
  81.1 11.9 %copy-start.10 = (f32[2,16]{1,0:T(2,128)S(1)}, f32[2,16]{1,0:T(2,128)}, u32[]{:S(2)}) copy-start(f32[2,16]{1,0:T(2,128)} %copy-done.9) | copy-start | bytes 388
  93.0 4.4 %copy-start.2 = (bf16[512,2048]{0,1:T(8,128)(2,1)S(1)}, bf16[512,2048]{0,1:T(8,128)(2,1)}, u32[]{:S(2)}) copy-start(bf16[512,2048]{0,1:T(8,128)(2,1)} %copy-done) | copy-start | bytes 6291460
  93.0 4.4 %copy-start.3 = (bf16[512,2048]{0,1:T(8,128)(2,1)S(1)}, bf16[512,2048]{0,1:T(8,128)(2,1)}, u32[]{:S(2)}) copy-start(bf16[512,2048]{0,1:T(8,128)(2,1)} %copy.68) | copy-start | bytes 6291460
  97.4 2.1 %copy-start.8 = (f32[2048]{0:T(1024)S(1)}, f32[2048]{0:T(1024)}, u32[]{:S(2)}) copy-start(f32[2048]{0:T(1024)} %convert_element_type.186) | copy-start | bytes 24580
  114.9 66.3 %reduce-scatter.5.cloned.1.call-start = ((), (), s32[]{:S(2)}) async-start(), calls=%async_computation.3 | async-start | bytes 3145728 | tf_op jit(solution)/shard_map/reduce_scatter | solution.py:191
Sparse Core Ops, SparseCore 0:
  115.1 30.6 reduce-scatter.2
  148.1 33.0 reduce-scatter.4

commit v3 on v2

--- a/solution.py
+++ b/solution.py
@@ -182,14 +182,48 @@
     normed = (normed.reshape(tokens, width_here) * norm_gain.astype(jnp.float32)).astype(
         jnp.bfloat16
     )
-    projected = jnp.dot(normed, out_weight, preferred_element_type=jnp.float32).astype(jnp.bfloat16)
+    return reduce_rows(normed, out_weight)
+
+
+def swap(value, axis):
+    return lax.ppermute(value, axis, [(0, 1), (1, 0)])
+
+
+def reduce_rows(normed, out_weight):
+    tokens = normed.shape[0]
     outer = lax.axis_size("ty")
     inner = lax.axis_size("tc")
     piece = tokens // (outer * inner)
-    projected = projected.reshape(outer, inner, piece, -1).transpose(1, 0, 2, 3)
-    projected = lax.psum_scatter(projected, "tc", scatter_dimension=0, tiled=True)
-    projected = lax.psum_scatter(projected[0], "ty", scatter_dimension=0, tiled=True)
-    return projected.reshape(piece, -1)
+    ty = lax.axis_index("ty")
+    tc = lax.axis_index("tc")
+    rows = normed.reshape(outer, inner, piece, -1)
+
+    def project(block):
+        partial = jnp.dot(block, out_weight, preferred_element_type=jnp.float32)
+        return partial.astype(jnp.bfloat16)
+
+    def quarter(a, b):
+        block = lax.dynamic_index_in_dim(rows, a, 0, keepdims=False)
+        return lax.dynamic_index_in_dim(block, b, 0, keepdims=False)
+
+    if inner != 2:
+        projected = project(normed).reshape(outer, inner, piece, -1).reshape(outer * inner, piece, -1)
+        return lax.psum_scatter(projected, ("ty", "tc"), scatter_dimension=0, tiled=True)[0]
+    other = 1 - tc
+    if outer == 2:
+        far = 1 - ty
+        sent_far = swap(project(quarter(far, other)), "tc")
+        sent_near = swap(project(quarter(ty, other)), "tc")
+        half = project(quarter(far, tc)).astype(jnp.float32) + sent_far.astype(jnp.float32)
+        across = lax.ppermute(half.astype(jnp.bfloat16), "ty", [(0, 1), (1, 0)])
+        mine = project(quarter(ty, tc)).astype(jnp.float32) + sent_near.astype(jnp.float32)
+        return (mine + across.astype(jnp.float32)).astype(jnp.bfloat16)
+    block = lax.dynamic_index_in_dim(rows, other, 1, keepdims=False)
+    sent = swap(project(block.reshape(outer * piece, -1)), "tc")
+    block = lax.dynamic_index_in_dim(rows, tc, 1, keepdims=False)
+    half = project(block.reshape(outer * piece, -1)).astype(jnp.float32) + sent.astype(jnp.float32)
+    half = half.astype(jnp.bfloat16).reshape(outer, piece, -1)
+    return lax.psum_scatter(half, "ty", scatter_dimension=0, tiled=True)[0]
 
 
 def solution(mesh):

time: 189 us -> 168 us (0.89)
  the two profiles are of different devices: /device:TPU:0 before, /device:TPU:30 now
where the time goes in v3:
time: 168 us; the launch traced here: 167 us
  waiting for transfers between devices  65.2 us (39%)
  matrix products  45.6 us (27%)
  other arithmetic  31.2 us (19%)
  local copies, waits for them, and re-layouts  16.5 us (10%)
  starting transfers between devices  8.15 us (5%)
    ppermute x5, waiting for transfers between devices, shifted(): return lax.ppermute(value, axis, pairs)  43.2 us
    dot_general x4, matrix products, project(): partial = jnp.dot(block, out_weight, preferred_element_type=jnp.float32)  28.2 us
    ppermute x1, waiting for transfers between devices, reduce_rows(): across = lax.ppermute(half.astype(jnp.bfloat16), 'ty', [(0, 1), (1, 0)])  22 us
    convert_element_type x2, other arithmetic, conv_silu(): return lax.optimization_barrier(jax.nn.silu(summed).astype(jnp.bfloat16))  11.8 us
    dot_general x1, matrix products, block_parts(): jnp.einsum('ghij,jghp->ighp', mixing, inner_block, preferred_element_type...  10.6 us
    unnamed x47, local copies, waits for them, and re-layouts  9.42 us
    ppermute x5, starting transfers between devices, shifted(): return lax.ppermute(value, axis, pairs)  7.01 us
    dot_general x1, matrix products, apply_state(): jnp.einsum('ign,ghpn->ighp', c_block.astype(jnp.float32), state, precisio...  4.34 us
  transfers between devices with their start and end apart: 8, of which 5 were waited for; matrix products, arithmetic and copies ran while one was open for 31% of the time, Pallas kernels for 0%

profile of v3, /device:TPU:30, one launch (start us, length us, event | category | flops | bytes accessed | tf_op | source)
XLA Modules:
  0.0 167.2 jit_solution(13372718617220681002)
XLA Ops:
  1.6 1.3 collective-permute-start
  3.5 0.9 negate_multiply_fusion
  4.4 2.3 %reduce-window.6 = f32[16,2,4,128]{3,0,1,2:T(8,128)S(1)} reduce-window(f32[16,2,4,128]{3,0,1,2:T(8,128)S(1)} %bitcast.140, f32[]{:T(128)} %constant.126.clone.1), window={size=1x1x1x128 pad=0_0x0_0x0_0x127_0}, to_apply=%region_0.1 | reduce-window | flops 2080768 | bytes 131076 | tf_op jit(solution)/shard_map/reduce-window
  7.9 0.9 slice_convert_fusion.5
  8.8 1.3 bitcast_convert_fusion.3
  10.4 3.9 %copy.56 = bf16[512,2048]{0,1:T(8,128)(2,1)} copy(bf16[512,2048]{1,0:T(8,128)(2,1)} %param.12) | data formatting | bytes 4194304 | tf_op args[0]
  15.4 9.7 %multiply_convert_fusion.3 = bf16[512,2048]{0,1:T(8,128)(2,1)S(1)} fusion(bf16[512,2048]{0,1:T(8,128)(2,1)} %copy.56, bf16[3,2048]{0,1:T(8,128)(2,1)S(1)} %copy.55, f32[2048]{0:T(1024)S(1)} %bitcast.143, f32[2048]{0:T(1024)S(1)} %bitcast.144, f32[2048]{0:T(1024)S(1)} %bitcast.142, f32[2048]{0:T(1024)S(1)} %bitcast.141, f32[2048]{0:T(1024)S(1)} %convert_element_type.180), kind=kLoop, calls=%fused_computation.23 | loop fusion | flops 27262976 | bytes 4247552 | tf_op jit(solution)/shard_map/convert_element_type | solution.py:29
  25.3 2.1 %multiply_convert_fusion.7 = bf16[512,2,256]{0,2,1:T(8,128)(2,1)S(1)} fusion(bf16[512,2,256]{0,2,1:T(8,128)(2,1)S(1)} %copy.63, bf16[3,2,256]{0,2,1:T(8,128)(2,1)S(1)} %bitcast.135, f32[2,256]{1,0:T(2,128)} %get-tuple-element.27, f32[2,256]{1,0:T(2,128)} %get-tuple-element.28, f32[2,256]{1,0:T(2,128)S(1)} %get-tuple-element.26, ...), kind=kLoop, calls=%fused_computation.42 | loop fusion | flops 6815744 | bytes 1061888 | tf_op jit(solution)/shard_map/convert_element_type | solution.py:29
  29.1 1.4 collective-permute-start.1
  30.5 1.3 collective-permute-start.2
  32.6 4.0 %copy.69 = bf16[512,2048]{0,1:T(8,128)(2,1)} copy(bf16[512,2048]{1,0:T(8,128)(2,1)} %param.14) | data formatting | bytes 4194304 | tf_op args[2]
  37.3 1.8 %fusion.55 = f32[2,512,512]{2,1,0:T(8,128)} fusion(bf16[512,2,128]{0,2,1:T(8,128)(2,1)S(1)} %bitcast.131, bf16[512,2,128]{0,2,1:T(8,128)(2,1)S(1)} %bitcast.134), kind=kOutput, calls=%fused_computation.112 | convolution fusion | flops 134217728 | bytes 2621440 | tf_op jit(solution)/shard_map/ign,jgn->gij/dot_general | solution.py:40
  39.1 6.5 %collective-permute-done.1 = bf16[2064,128]{1,0:T(8,128)(2,1)S(1)} collective-permute-done((bf16[2064,128]{1,0:T(8,128)(2,1)}, bf16[2064,128]{1,0:T(8,128)(2,1)S(1)}, u32[]{:S(2)}, u32[]{:S(2)}) %collective-permute-start.1) | collective-permute-done | bytes 528416 | tf_op jit(solution)/shard_map/ppermute | solution.py:20
  45.8 12.5 %collective-permute-done.2 = bf16[2064,128]{1,0:T(8,128)(2,1)} collective-permute-done((bf16[2064,128]{1,0:T(8,128)(2,1)}, bf16[2064,128]{1,0:T(8,128)(2,1)}, u32[]{:S(2)}, u32[]{:S(2)}) %collective-permute-start.2) | collective-permute-done | bytes 528416 | tf_op jit(solution)/shard_map/ppermute | solution.py:20
  60.0 1.4 add_convert_fusion.2
  61.5 1.6 collective-permute-start.3
  63.0 1.1 slice_convert_fusion.1
  64.2 12.0 %collective-permute-done.3 = bf16[2064,128]{1,0:T(8,128)(2,1)S(1)} collective-permute-done((bf16[2064,128]{1,0:T(8,128)(2,1)S(1)}, bf16[2064,128]{1,0:T(8,128)(2,1)S(1)}, u32[]{:S(2)}, u32[]{:S(2)}) %collective-permute-start.3) | collective-permute-done | bytes 528416 | tf_op jit(solution)/shard_map/ppermute | solution.py:20
  76.2 1.1 fusion.34
  77.3 1.5 collective-permute-start.4
  78.8 10.6 %fusion = f32[2,16,64,512]{3,2,1,0:T(8,128)} fusion(bf16[512,2,16,64]{0,3,2,1:T(8,128)(2,1)S(1)} %bitcast.124, f32[2,16,512]{2,1,0:T(8,128)S(1)} %bitcast.139, f32[2,512,512]{2,1,0:T(8,128)S(1)} %copy-done.4, f32[2,16,512]{2,1,0:T(8,128)S(1)} %copy-done.9, pred[512,512]{1,0:T(8,128)(4,1)S(1)} %copy-done.8), kind=kOutput, calls=%fused_computation.1 | convolution fusion | flops 1115684864 | bytes 8781824 | tf_op jit(solution)/shard_map/ghij,jghp->ighp/dot_general | solution.py:44
  90.8 12.2 %collective-permute-done.4 = bf16[2,16,64,128]{3,2,1,0:T(8,128)(2,1)S(1)} collective-permute-done((bf16[2,16,64,128]{3,2,1,0:T(8,128)(2,1)}, bf16[2,16,64,128]{3,2,1,0:T(8,128)(2,1)S(1)}, u32[]{:S(2)}, u32[]{:S(2)}) %collective-permute-start.4) | collective-permute-done | bytes 524320 | tf_op jit(solution)/shard_map/ppermute | solution.py:20
  103.0 4.3 %fusion.8 = f32[1,512,2,16,64]{1,4,3,2,0:T(8,128)S(1)} fusion(f32[2,16,64,512]{3,2,1,0:T(8,128)} %fusion, bf16[512,2,128,1]{0,2,3,1:T(8,128)(2,1)S(1)} %bitcast.132, f32[512,2,16]{0,2,1:T(8,128)S(1)} %get-tuple-element.16, bf16[2,16,64,128]{3,2,1,0:T(8,128)(2,1)S(1)} %collective-permute-done.4, f32[2,16]{1,0:T(2,128)S(1)} %fusion.43, ...), kind=kOutput, calls=%fused_computation.16 | convolution fusion | flops 1614807040 | bytes 11862400 | tf_op jit(solution)/shard_map/vmap(ign,ghpn->ighp)/dot_general | solution.py:56
  107.4 2.1 %bitcast_reduce_fusion = (f32[512,2]{0,1:T(2,128)S(1)}, f32[512,2048]{0,1:T(8,128)S(1)}) fusion(bf16[512,2048]{0,1:T(8,128)(2,1)S(1)} %copy-done.3, bf16[512,2048]{0,1:T(8,128)(2,1)S(1)} %copy-done.2, f32[2048]{0:T(1024)S(1)} %mul.292, f32[1,512,2,16,64]{1,4,3,2,0:T(8,128)S(1)} %fusion.8), kind=kLoop, calls=%fused_computation.20 | loop fusion | flops 11533312 | bytes 12595200 | tf_op jit(solution)/shard_map/reduce_sum | solution.py:181
  109.5 1.8 %fusion.10 = bf16[512,2048]{0,1:T(8,128)(2,1)} fusion(f32[512,2048]{0,1:T(8,128)S(1)} %get-tuple-element.8, f32[2048]{0:T(1024)S(1)} %copy-done.10, f32[512,2]{0,1:T(2,128)S(1)} %add_rsqrt_fusion), kind=kLoop, calls=%fused_computation.19 | loop fusion | flops 3145728 | bytes 6303744 | tf_op jit(solution)/shard_map/convert_element_type | solution.py:182
  111.2 3.1 %copy.82 = bf16[512,2048]{1,0:T(8,128)(2,1)S(1)} copy(bf16[512,2048]{0,1:T(8,128)(2,1)} %fusion.10) | data formatting | bytes 4194304 | tf_op jit(solution)/shard_map/reshape | solution.py:199
  114.4 9.1 %convolution_convert_fusion = bf16[128,4096]{1,0:T(8,128)(2,1)} fusion(bf16[2048,4096]{1,0:T(8,128)(2,1)} %param.23, bf16[2,2,128,2048]{3,2,1,0:T(8,128)(2,1)S(1)} %bitcast.125, s32[]{:T(128)S(6)} %select_n.43, s32[]{:T(128)S(6)} %select_n.41), kind=kOutput, calls=%fused_computation.5 | convolution fusion | flops 2148007936 | bytes 18350088 | tf_op jit(solution)/shard_map/dot_general | solution.py:202
  123.5 8.3 %convolution_convert_fusion.2 = bf16[128,4096]{1,0:T(8,128)(2,1)S(1)} fusion(bf16[2048,4096]{1,0:T(8,128)(2,1)} %param.23, bf16[2,2,128,2048]{3,2,1,0:T(8,128)(2,1)S(1)} %bitcast.126, s32[]{:T(128)S(6)} %select_n.37, s32[]{:T(128)S(6)} %select_n.41), kind=kOutput, calls=%fused_computation.8 | convolution fusion | flops 2148007936 | bytes 18350088 | tf_op jit(solution)/shard_map/dot_general | solution.py:202
  132.4 8.4 %add_convert_fusion.1 = bf16[128,4096]{1,0:T(8,128)(2,1)S(1)} fusion(bf16[128,4096]{1,0:T(8,128)(2,1)S(1)} %collective-permute-done.6, bf16[2048,4096]{1,0:T(8,128)(2,1)} %param.23, bf16[2,2,128,2048]{3,2,1,0:T(8,128)(2,1)S(1)} %bitcast.127, s32[]{:T(128)S(6)} %select_n.43, s32[]{:T(128)S(6)} %select_n.39), kind=kOutput, calls=%fused_computation.33 | convolution fusion | flops 2150105088 | bytes 19398664 | tf_op jit(solution)/shard_map/dot_general | solution.py:202
  141.3 2.4 %fusion.3 = f32[128,4096]{1,0:T(8,128)S(1)} fusion(bf16[2048,4096]{1,0:T(8,128)(2,1)S(1)} %bitcast.118, bf16[2,2,128,2048]{3,2,1,0:T(8,128)(2,1)S(1)} %bitcast.128, s32[]{:T(128)S(6)} %select_n.37, s32[]{:T(128)S(6)} %select_n.39), kind=kOutput, calls=%fused_computation.10 | convolution fusion | flops 2148532224 | bytes 19398664 | tf_op jit(solution)/shard_map/dot_general | solution.py:202
  143.8 22.0 %collective-permute-done.7 = bf16[128,4096]{1,0:T(8,128)(2,1)S(1)} collective-permute-done((bf16[128,4096]{1,0:T(8,128)(2,1)S(1)}, bf16[128,4096]{1,0:T(8,128)(2,1)S(1)}, u32[]{:S(2)}, u32[]{:S(2)}) %collective-permute-start.7) | collective-permute-done | bytes 1048608 | tf_op jit(solution)/shard_map/ppermute | solution.py:218
  165.8 1.4 add_convert_fusion
  (97 shorter events, 12.5 us)
Async XLA Ops:
  0.0 14.3 %copy-start.7 = (bf16[512,2,256]{2,1,0:T(2,128)(2,1)S(1)}, bf16[512,2,256]{2,1,0:T(2,128)(2,1)}, u32[]{:S(2)}) copy-start(bf16[512,2,256]{2,1,0:T(2,128)(2,1)} %param.13) | copy-start | bytes 1572868
  0.0 15.0 %copy-start.13 = (bf16[2048]{0:T(1024)(128)(2,1)S(1)}, bf16[2048]{0:T(1024)(128)(2,1)}, u32[]{:S(2)}) copy-start(bf16[2048]{0:T(1024)(128)(2,1)} %param.18) | copy-start | bytes 12292
  0.0 15.0 %copy-start.15 = (bf16[2,256]{1,0:T(2,128)(2,1)S(1)}, bf16[2,256]{1,0:T(2,128)(2,1)}, u32[]{:S(2)}) copy-start(bf16[2,256]{1,0:T(2,128)(2,1)} %param.19) | copy-start | bytes 3076
  1.6 13.5 %collective-permute-start = (bf16[3,2560]{1,0:T(4,128)(2,1)S(1)}, bf16[3,2560]{1,0:T(4,128)(2,1)S(1)}, u32[]{:S(2)}, u32[]{:S(2)}) collective-permute-start(bf16[3,2560]{1,0:T(4,128)(2,1)S(1)} %pad_maximum_fusion.4), channel_id=1, source_target_pairs={{0,4},{4,8},{8,12},{12,16},{16,20},{20,24},{24,28},{1,5},{5,9},{9,... | collective-permute-start | bytes 46088 | tf_op jit(solution)/shard_map/ppermute | solution.py:20
  25.1 11.4 %copy-start = (bf16[512,2048]{0,1:T(8,128)(2,1)}, bf16[512,2048]{0,1:T(8,128)(2,1)S(1)}, u32[]{:S(2)}) copy-start(bf16[512,2048]{0,1:T(8,128)(2,1)S(1)} %multiply_convert_fusion.3) | copy-start | bytes 6291460
  27.5 0.8 copy-start.5
  27.5 9.1 %copy-start.16 = (f32[32]{0:T(128)S(1)}, f32[32]{0:T(128)}, u32[]{:S(2)}) copy-start(f32[32]{0:T(128)} %param.21) | copy-start | bytes 388
  27.5 9.2 %copy-start.14 = (bf16[2048]{0:T(1024)(128)(2,1)S(1)}, bf16[2048]{0:T(1024)(128)(2,1)}, u32[]{:S(2)}) copy-start(bf16[2048]{0:T(1024)(128)(2,1)} %param.22) | copy-start | bytes 12292
  29.1 8.3 %copy-start.6 = (bf16[512,1,256]{0,2,1:T(8,128)(2,1)S(1)}, bf16[512,1,256]{0,2,1:T(8,128)(2,1)}, u32[]{:S(2)}) copy-start(bf16[512,1,256]{0,2,1:T(8,128)(2,1)} %copy-done.5) | copy-start | bytes 786436
  29.1 16.6 %collective-permute-start.1 = (bf16[2064,128]{1,0:T(8,128)(2,1)}, bf16[2064,128]{1,0:T(8,128)(2,1)S(1)}, u32[]{:S(2)}, u32[]{:S(2)}) collective-permute-start(bf16[2064,128]{1,0:T(8,128)(2,1)} %pad_maximum_fusion.1), channel_id=1, source_target_pairs={{0,4},{4,8},{8,12},{12,16},{16,20},{20,24},{24,28},{1,5},{5,9},{9,... | collective-permute-start | bytes 1585160 | tf_op jit(solution)/shard_map/ppermute | solution.py:20
  30.5 27.8 %collective-permute-start.2 = (bf16[2064,128]{1,0:T(8,128)(2,1)}, bf16[2064,128]{1,0:T(8,128)(2,1)}, u32[]{:S(2)}, u32[]{:S(2)}) collective-permute-start(bf16[2064,128]{1,0:T(8,128)(2,1)} %pad_maximum_fusion.1), channel_id=1, source_target_pairs={{0,8},{4,12},{8,16},{12,20},{16,24},{20,28},{1,9},{5,13},{9,17},{1... | collective-permute-start | bytes 1585160 | tf_op jit(solution)/shard_map/ppermute | solution.py:20
  59.9 16.3 %copy-start.11 = (f32[2,16]{1,0:T(2,128)S(1)}, f32[2,16]{1,0:T(2,128)}, u32[]{:S(2)}) copy-start(f32[2,16]{1,0:T(2,128)} %get-tuple-element.11) | copy-start | bytes 388
  61.4 17.4 %copy-start.1 = (bf16[512,2048]{0,1:T(8,128)(2,1)S(1)}, bf16[512,2048]{0,1:T(8,128)(2,1)}, u32[]{:S(2)}) copy-start(bf16[512,2048]{0,1:T(8,128)(2,1)} %copy-done) | copy-start | bytes 6291460
  61.4 17.4 %copy-start.4 = (f32[2,512,512]{2,1,0:T(8,128)S(1)}, f32[2,512,512]{2,1,0:T(8,128)}, u32[]{:S(2)}) copy-start(f32[2,512,512]{2,1,0:T(8,128)} %fusion.55) | copy-start | bytes 6291460
  61.4 17.4 %copy-start.8 = (pred[512,512]{1,0:T(8,128)(4,1)S(1)}, pred[512,512]{1,0:T(8,128)(4,1)}, u32[]{:S(2)}) copy-start(pred[512,512]{1,0:T(8,128)(4,1)} %iota_compare_fusion) | copy-start | bytes 786436
  61.4 17.4 %copy-start.9 = (f32[2,16,512]{2,1,0:T(8,128)S(1)}, f32[2,16,512]{2,1,0:T(8,128)}, u32[]{:S(2)}) copy-start(f32[2,16,512]{2,1,0:T(8,128)} %get-tuple-element.18) | copy-start | bytes 196612
  61.5 14.7 %collective-permute-start.3 = (bf16[2064,128]{1,0:T(8,128)(2,1)S(1)}, bf16[2064,128]{1,0:T(8,128)(2,1)S(1)}, u32[]{:S(2)}, u32[]{:S(2)}) collective-permute-start(bf16[2064,128]{1,0:T(8,128)(2,1)S(1)} %pad_maximum_fusion.2), channel_id=1, source_target_pairs={{0,8},{4,12},{8,16},{12,20},{16,24},{20,28},{1,9},{5,13},{9,17},{1... | collective-permute-start | bytes 1585160 | tf_op jit(solution)/shard_map/ppermute | solution.py:20
  77.3 25.7 %collective-permute-start.4 = (bf16[2,16,64,128]{3,2,1,0:T(8,128)(2,1)}, bf16[2,16,64,128]{3,2,1,0:T(8,128)(2,1)S(1)}, u32[]{:S(2)}, u32[]{:S(2)}) collective-permute-start(bf16[2,16,64,128]{3,2,1,0:T(8,128)(2,1)} %fusion.34), channel_id=1, source_target_pairs={{0,16},{4,20},{8,24},{12,28},{1,17},{5,21},{9,25},{13,29},{2,18},{... | collective-permute-start | bytes 1572872 | tf_op jit(solution)/shard_map/ppermute | solution.py:20
  78.8 12.0 %copy-start.12 = (f32[2,16]{1,0:T(2,128)S(1)}, f32[2,16]{1,0:T(2,128)}, u32[]{:S(2)}) copy-start(f32[2,16]{1,0:T(2,128)} %get-tuple-element.11) | copy-start | bytes 388
  103.0 4.4 %copy-start.2 = (bf16[512,2048]{0,1:T(8,128)(2,1)S(1)}, bf16[512,2048]{0,1:T(8,128)(2,1)}, u32[]{:S(2)}) copy-start(bf16[512,2048]{0,1:T(8,128)(2,1)} %copy-done) | copy-start | bytes 6291460
  103.0 4.4 %copy-start.3 = (bf16[512,2048]{0,1:T(8,128)(2,1)S(1)}, bf16[512,2048]{0,1:T(8,128)(2,1)}, u32[]{:S(2)}) copy-start(bf16[512,2048]{0,1:T(8,128)(2,1)} %copy.69) | copy-start | bytes 6291460
  107.4 2.1 %copy-start.10 = (f32[2048]{0:T(1024)S(1)}, f32[2048]{0:T(1024)}, u32[]{:S(2)}) copy-start(f32[2048]{0:T(1024)} %convert_element_type.216) | copy-start | bytes 24580
  123.5 8.9 %collective-permute-start.6 = (bf16[128,4096]{1,0:T(8,128)(2,1)}, bf16[128,4096]{1,0:T(8,128)(2,1)S(1)}, u32[]{:S(2)}, u32[]{:S(2)}) collective-permute-start(bf16[128,4096]{1,0:T(8,128)(2,1)} %convolution_convert_fusion), channel_id=1, source_target_pairs={{0,1},{1,0},{2,3},{3,2},{4,5},{5,4},{6,7},{7,6},{8,9},{9,8},{10,11... | collective-permute-start | bytes 3145736 | tf_op jit(solution)/shard_map/ppermute | solution.py:189
  123.5 17.8 %slice-start = ((s8[16777216]{0:T(1024)(128)(4,1)}), s8[4194304]{0:T(1024)(128)(4,1)S(1)}, s32[]{:S(2)}) async-start(s8[16777216]{0:T(1024)(128)(4,1)} %bitcast.117), calls=%async_computation | async-start | bytes 8388608
  123.5 17.8 %slice-start.1 = ((s8[16777216]{0:T(1024)(128)(4,1)}), s8[4194304]{0:T(1024)(128)(4,1)S(1)}, s32[]{:S(2)}) async-start(s8[16777216]{0:T(1024)(128)(4,1)} %bitcast.117), calls=%async_computation.1 | async-start | bytes 8388608
  131.8 9.6 %slice-start.2 = ((s8[16777216]{0:T(1024)(128)(4,1)}), s8[4194304]{0:T(1024)(128)(4,1)S(1)}, s32[]{:S(2)}) async-start(s8[16777216]{0:T(1024)(128)(4,1)} %bitcast.117), calls=%async_computation.2 | async-start | bytes 8388608
  131.8 9.6 %slice-start.3 = ((s8[16777216]{0:T(1024)(128)(4,1)}), s8[4194304]{0:T(1024)(128)(4,1)S(1)}, s32[]{:S(2)}) async-start(s8[16777216]{0:T(1024)(128)(4,1)} %bitcast.117), calls=%async_computation.3 | async-start | bytes 8388608
  131.8 12.0 %collective-permute-start.5 = (bf16[128,4096]{1,0:T(8,128)(2,1)S(1)}, bf16[128,4096]{1,0:T(8,128)(2,1)S(1)}, u32[]{:S(2)}, u32[]{:S(2)}) collective-permute-start(bf16[128,4096]{1,0:T(8,128)(2,1)S(1)} %convolution_convert_fusion.2), channel_id=1, source_target_pairs={{0,1},{1,0},{2,3},{3,2},{4,5},{5,4},{6,7},{7,6},{8,9},{9,8},{10,11... | collective-permute-start | bytes 3145736 | tf_op jit(solution)/shard_map/ppermute | solution.py:189
  140.8 25.0 %collective-permute-start.7 = (bf16[128,4096]{1,0:T(8,128)(2,1)S(1)}, bf16[128,4096]{1,0:T(8,128)(2,1)S(1)}, u32[]{:S(2)}, u32[]{:S(2)}) collective-permute-start(bf16[128,4096]{1,0:T(8,128)(2,1)S(1)} %add_convert_fusion.1), channel_id=1, source_target_pairs={{0,2},{2,0},{1,3},{3,1},{4,6},{6,4},{5,7},{7,5},{8,10},{10,8},{9,1... | collective-permute-start | bytes 3145736 | tf_op jit(solution)/shard_map/ppermute | solution.py:218

commit v4 on v2

--- a/solution.py
+++ b/solution.py
@@ -182,14 +182,52 @@
     normed = (normed.reshape(tokens, width_here) * norm_gain.astype(jnp.float32)).astype(
         jnp.bfloat16
     )
-    projected = jnp.dot(normed, out_weight, preferred_element_type=jnp.float32).astype(jnp.bfloat16)
+    return reduce_rows(normed, out_weight)
+
+
+def swap(value, axis):
+    return lax.ppermute(value, axis, [(0, 1), (1, 0)])
+
+
+def reduce_rows(normed, out_weight):
+    tokens = normed.shape[0]
     outer = lax.axis_size("ty")
     inner = lax.axis_size("tc")
     piece = tokens // (outer * inner)
-    projected = projected.reshape(outer, inner, piece, -1).transpose(1, 0, 2, 3)
-    projected = lax.psum_scatter(projected, "tc", scatter_dimension=0, tiled=True)
-    projected = lax.psum_scatter(projected[0], "ty", scatter_dimension=0, tiled=True)
-    return projected.reshape(piece, -1)
+    ty = lax.axis_index("ty")
+    tc = lax.axis_index("tc")
+
+    def project(block):
+        partial = jnp.dot(block, out_weight, preferred_element_type=jnp.float32)
+        return partial.astype(jnp.bfloat16)
+
+    if inner != 2:
+        projected = project(normed).reshape(outer * inner, piece, -1)
+        return lax.psum_scatter(projected, ("ty", "tc"), scatter_dimension=0, tiled=True)[0]
+    other = 1 - tc
+    width = out_weight.shape[1]
+    chunks = 4 if width % (4 * 128) == 0 else 1
+    step = width // chunks
+    done = []
+    for c in range(chunks):
+        partial = jnp.dot(
+            normed, out_weight[:, c * step : (c + 1) * step], preferred_element_type=jnp.float32
+        ).astype(jnp.bfloat16)
+        partial = partial.reshape(outer, inner, piece, step)
+        sent = swap(lax.dynamic_index_in_dim(partial, other, 1, keepdims=False), "tc")
+        half = lax.dynamic_index_in_dim(partial, tc, 1, keepdims=False).astype(jnp.float32)
+        half = half + sent.astype(jnp.float32)
+        if outer == 2:
+            across = swap(
+                lax.dynamic_index_in_dim(half, 1 - ty, 0, keepdims=False).astype(jnp.bfloat16), "ty"
+            )
+            mine = lax.dynamic_index_in_dim(half, ty, 0, keepdims=False)
+            done.append((mine + across.astype(jnp.float32)).astype(jnp.bfloat16))
+        else:
+            done.append(
+                lax.psum_scatter(half.astype(jnp.bfloat16), "ty", scatter_dimension=0, tiled=True)[0]
+            )
+    return jnp.concatenate(done, axis=1)
 
 
 def solution(mesh):

time: 189 us -> 149 us (0.79)
  the two profiles are of different devices: /device:TPU:0 before, /device:TPU:30 now
where the time goes in v4:
time: 149 us; the launch traced here: 148 us
  waiting for transfers between devices  63.4 us (43%)
  matrix products  29.5 us (20%)
  other arithmetic  29 us (19%)
  local copies, waits for them, and re-layouts  13.6 us (9%)
  starting transfers between devices  12.3 us (8%)
    ppermute x5, waiting for transfers between devices, shifted(): return lax.ppermute(value, axis, pairs)  43.4 us
    ppermute x8, waiting for transfers between devices, swap(): return lax.ppermute(value, axis, [(0, 1), (1, 0)])  20 us
    dot_general x4, matrix products, reduce_rows(): jnp.dot(normed, out_weight[:, c * step:(c + 1) * step], preferred_element...  12 us
    convert_element_type x2, other arithmetic, conv_silu(): return lax.optimization_barrier(jax.nn.silu(summed).astype(jnp.bfloat16))  11.3 us
    dot_general x1, matrix products, block_parts(): jnp.einsum('ghij,jghp->ighp', mixing, inner_block, preferred_element_type...  10.5 us
    unnamed x43, local copies, waits for them, and re-layouts  9.42 us
    ppermute x5, starting transfers between devices, shifted(): return lax.ppermute(value, axis, pairs)  6.7 us
    ppermute x8, starting transfers between devices, swap(): return lax.ppermute(value, axis, [(0, 1), (1, 0)])  5.56 us
  transfers between devices with their start and end apart: 13, of which 8 were waited for; matrix products, arithmetic and copies ran while one was open for 24% of the time, Pallas kernels for 0%

profile of v4, /device:TPU:30, one launch (start us, length us, event | category | flops | bytes accessed | tf_op | source)
XLA Modules:
  0.0 148.5 jit_solution(6175669552825444903)
XLA Ops:
  1.6 1.3 collective-permute-start
  4.4 2.3 %reduce-window.6 = f32[16,2,4,128]{3,0,1,2:T(8,128)S(1)} reduce-window(f32[16,2,4,128]{3,0,1,2:T(8,128)S(1)} %bitcast.183, f32[]{:T(128)} %constant.62.clone.1), window={size=1x1x1x128 pad=0_0x0_0x0_0x127_0}, to_apply=%region_0.1 | reduce-window | flops 2080768 | bytes 131076 | tf_op jit(solution)/shard_map/reduce-window
  9.8 3.9 %copy.64 = bf16[512,2048]{0,1:T(8,128)(2,1)} copy(bf16[512,2048]{1,0:T(8,128)(2,1)} %param.12) | data formatting | bytes 4194304 | tf_op args[0]
  14.8 9.9 %multiply_convert_fusion.3 = bf16[512,2048]{0,1:T(8,128)(2,1)S(1)} fusion(bf16[512,2048]{0,1:T(8,128)(2,1)} %copy.64, bf16[3,2048]{0,1:T(8,128)(2,1)S(1)} %copy.63, f32[2048]{0:T(1024)S(1)} %bitcast.186, f32[2048]{0:T(1024)S(1)} %bitcast.187, f32[2048]{0:T(1024)S(1)} %bitcast.185, f32[2048]{0:T(1024)S(1)} %bitcast.184, f32[2048]{0:T(1024)S(1)} %convert_element_type.243), kind=kLoop, calls=%fused_computation.25 | loop fusion | flops 27262976 | bytes 4247552 | tf_op jit(solution)/shard_map/convert_element_type | solution.py:29
  25.0 1.3 multiply_convert_fusion.7
  27.9 1.3 collective-permute-start.1
  29.2 1.3 collective-permute-start.2
  31.3 4.0 %copy.77 = bf16[512,2048]{0,1:T(8,128)(2,1)} copy(bf16[512,2048]{1,0:T(8,128)(2,1)} %param.14) | data formatting | bytes 4194304 | tf_op args[2]
  36.0 1.8 %fusion.67 = f32[2,512,512]{2,1,0:T(8,128)} fusion(bf16[512,2,128]{0,2,1:T(8,128)(2,1)S(1)} %bitcast.166, bf16[512,2,128]{0,2,1:T(8,128)(2,1)S(1)} %bitcast.177), kind=kOutput, calls=%fused_computation.129 | convolution fusion | flops 134217728 | bytes 2621440 | tf_op jit(solution)/shard_map/ign,jgn->gij/dot_general | solution.py:40
  37.9 6.5 %collective-permute-done.1 = bf16[2064,128]{1,0:T(8,128)(2,1)S(1)} collective-permute-done((bf16[2064,128]{1,0:T(8,128)(2,1)}, bf16[2064,128]{1,0:T(8,128)(2,1)S(1)}, u32[]{:S(2)}, u32[]{:S(2)}) %collective-permute-start.1) | collective-permute-done | bytes 528416 | tf_op jit(solution)/shard_map/ppermute | solution.py:20
  44.5 12.5 %collective-permute-done.2 = bf16[2064,128]{1,0:T(8,128)(2,1)} collective-permute-done((bf16[2064,128]{1,0:T(8,128)(2,1)}, bf16[2064,128]{1,0:T(8,128)(2,1)}, u32[]{:S(2)}, u32[]{:S(2)}) %collective-permute-start.2) | collective-permute-done | bytes 528416 | tf_op jit(solution)/shard_map/ppermute | solution.py:20
  58.2 1.4 add_convert_fusion
  59.7 1.6 %collective-permute-start.3 = (bf16[2064,128]{1,0:T(8,128)(2,1)S(1)}, bf16[2064,128]{1,0:T(8,128)(2,1)S(1)}, u32[]{:S(2)}, u32[]{:S(2)}) collective-permute-start(bf16[2064,128]{1,0:T(8,128)(2,1)S(1)} %pad_maximum_fusion.3), channel_id=1, source_target_pairs={{0,8},{4,12},{8,16},{12,20},{16,24},{20,28},{1,9},{5,13},{9,17},{1... | collective-permute-start | bytes 1585160 | tf_op jit(solution)/shard_map/ppermute | solution.py:20
  61.2 1.1 slice_convert_fusion.1
  62.4 12.0 %collective-permute-done.3 = bf16[2064,128]{1,0:T(8,128)(2,1)S(1)} collective-permute-done((bf16[2064,128]{1,0:T(8,128)(2,1)S(1)}, bf16[2064,128]{1,0:T(8,128)(2,1)S(1)}, u32[]{:S(2)}, u32[]{:S(2)}) %collective-permute-start.3) | collective-permute-done | bytes 528416 | tf_op jit(solution)/shard_map/ppermute | solution.py:20
  74.4 1.1 fusion.50
  75.5 1.3 collective-permute-start.4
  76.8 10.5 %fusion = f32[2,16,64,512]{3,2,1,0:T(8,128)} fusion(bf16[512,2,16,64]{0,3,2,1:T(8,128)(2,1)S(1)} %bitcast.163, f32[2,16,512]{2,1,0:T(8,128)S(1)} %bitcast.182, f32[2,512,512]{2,1,0:T(8,128)S(1)} %copy-done.4, f32[2,16,512]{2,1,0:T(8,128)S(1)} %copy-done.7, pred[512,512]{1,0:T(8,128)(4,1)S(1)} %copy-done.6), kind=kOutput, calls=%fused_computation.1 | convolution fusion | flops 1115684864 | bytes 8781824 | tf_op jit(solution)/shard_map/ghij,jghp->ighp/dot_general | solution.py:44
  88.7 12.4 %collective-permute-done.4 = bf16[2,16,64,128]{3,2,1,0:T(8,128)(2,1)S(1)} collective-permute-done((bf16[2,16,64,128]{3,2,1,0:T(8,128)(2,1)}, bf16[2,16,64,128]{3,2,1,0:T(8,128)(2,1)S(1)}, u32[]{:S(2)}, u32[]{:S(2)}) %collective-permute-start.4) | collective-permute-done | bytes 524320 | tf_op jit(solution)/shard_map/ppermute | solution.py:20
  101.2 4.5 %fusion.6 = f32[1,512,2,16,64]{1,4,3,2,0:T(8,128)S(1)} fusion(f32[2,16,64,512]{3,2,1,0:T(8,128)} %fusion, bf16[512,2,128,1]{0,2,3,1:T(8,128)(2,1)S(1)} %bitcast.167, f32[512,2,16]{0,2,1:T(8,128)S(1)} %get-tuple-element.16, bf16[2,16,64,128]{3,2,1,0:T(8,128)(2,1)S(1)} %collective-permute-done.4, f32[2,16]{1,0:T(2,128)S(1)} %fusion.59, ...), kind=kOutput, calls=%fused_computation.10 | convolution fusion | flops 1614807040 | bytes 11862400 | tf_op jit(solution)/shard_map/vmap(ign,ghpn->ighp)/dot_general | solution.py:56
  105.7 2.3 %bitcast_reduce_fusion = (f32[512,2]{0,1:T(2,128)S(1)}, f32[512,2048]{0,1:T(8,128)S(1)}) fusion(bf16[512,2048]{0,1:T(8,128)(2,1)S(1)} %copy-done.3, bf16[512,2048]{0,1:T(8,128)(2,1)S(1)} %copy-done.2, f32[2048]{0:T(1024)S(1)} %mul.292, f32[1,512,2,16,64]{1,4,3,2,0:T(8,128)S(1)} %fusion.6), kind=kLoop, calls=%fused_computation.14 | loop fusion | flops 11533312 | bytes 12595200 | tf_op jit(solution)/shard_map/reduce_sum | solution.py:181
  108.5 4.9 %fusion.21 = bf16[512,1024]{1,0:T(8,128)(2,1)S(1)} fusion(bf16[512,2048]{0,1:T(8,128)(2,1)S(1)} %fusion.8, bf16[2048,4096]{1,0:T(8,128)(2,1)} %param.23), kind=kOutput, calls=%fused_computation.35 | convolution fusion | flops 2148007936 | bytes 7340032 | tf_op jit(solution)/shard_map/dot_general | solution.py:213
  113.5 2.3 %fusion.24 = bf16[512,1024]{1,0:T(8,128)(2,1)S(1)} fusion(bf16[512,2048]{0,1:T(8,128)(2,1)S(1)} %fusion.8, bf16[2048,4096]{1,0:T(8,128)(2,1)S(1)} %bitcast.191), kind=kOutput, calls=%fused_computation.36 | convolution fusion | flops 2148007936 | bytes 7340032 | tf_op jit(solution)/shard_map/dot_general | solution.py:213
  115.8 2.3 %fusion.27 = bf16[512,1024]{1,0:T(8,128)(2,1)S(1)} fusion(bf16[512,2048]{0,1:T(8,128)(2,1)S(1)} %fusion.8, bf16[2048,4096]{1,0:T(8,128)(2,1)S(1)} %bitcast.191), kind=kOutput, calls=%fused_computation.37 | convolution fusion | flops 2148007936 | bytes 7340032 | tf_op jit(solution)/shard_map/dot_general | solution.py:213
  118.3 2.3 %fusion.30 = bf16[512,1024]{1,0:T(8,128)(2,1)S(1)} fusion(bf16[512,2048]{0,1:T(8,128)(2,1)S(1)} %fusion.8, bf16[2048,4096]{1,0:T(8,128)(2,1)S(1)} %bitcast.191), kind=kOutput, calls=%fused_computation.38 | convolution fusion | flops 2148007936 | bytes 7340032 | tf_op jit(solution)/shard_map/dot_general | solution.py:213
  123.0 1.6 %collective-permute-start.8 = (bf16[128,1024]{1,0:T(8,128)(2,1)S(1)}, bf16[128,1024]{1,0:T(8,128)(2,1)S(1)}, u32[]{:S(2)}, u32[]{:S(2)}) collective-permute-start(bf16[128,1024]{1,0:T(8,128)(2,1)S(1)} %fusion.46), channel_id=1, source_target_pairs={{0,2},{2,0},{1,3},{3,1},{4,6},{6,4},{5,7},{7,5},{8,10},{10,8},{9,1... | collective-permute-start | bytes 786440 | tf_op jit(solution)/shard_map/ppermute | solution.py:189
  125.7 1.6 %collective-permute-start.12 = (bf16[128,1024]{1,0:T(8,128)(2,1)S(1)}, bf16[128,1024]{1,0:T(8,128)(2,1)S(1)}, u32[]{:S(2)}, u32[]{:S(2)}) collective-permute-start(bf16[128,1024]{1,0:T(8,128)(2,1)S(1)} %fusion.48), channel_id=1, source_target_pairs={{0,2},{2,0},{1,3},{3,1},{4,6},{6,4},{5,7},{7,5},{8,10},{10,8},{9,1... | collective-permute-start | bytes 786440 | tf_op jit(solution)/shard_map/ppermute | solution.py:189
  127.2 4.2 %collective-permute-done.6 = bf16[128,1024]{1,0:T(8,128)(2,1)S(1)} collective-permute-done((bf16[128,1024]{1,0:T(8,128)(2,1)S(1)}, bf16[128,1024]{1,0:T(8,128)(2,1)S(1)}, u32[]{:S(2)}, u32[]{:S(2)}) %collective-permute-start.6) | collective-permute-done | bytes 262176 | tf_op jit(solution)/shard_map/ppermute | solution.py:189
  131.5 5.5 %collective-permute-done.8 = bf16[128,1024]{1,0:T(8,128)(2,1)S(1)} collective-permute-done((bf16[128,1024]{1,0:T(8,128)(2,1)S(1)}, bf16[128,1024]{1,0:T(8,128)(2,1)S(1)}, u32[]{:S(2)}, u32[]{:S(2)}) %collective-permute-start.8) | collective-permute-done | bytes 262176 | tf_op jit(solution)/shard_map/ppermute | solution.py:189
  137.1 5.6 %collective-permute-done.10 = bf16[128,1024]{1,0:T(8,128)(2,1)S(1)} collective-permute-done((bf16[128,1024]{1,0:T(8,128)(2,1)S(1)}, bf16[128,1024]{1,0:T(8,128)(2,1)S(1)}, u32[]{:S(2)}, u32[]{:S(2)}) %collective-permute-start.10) | collective-permute-done | bytes 262176 | tf_op jit(solution)/shard_map/ppermute | solution.py:189
  142.7 4.6 %collective-permute-done.12 = bf16[128,1024]{1,0:T(8,128)(2,1)S(1)} collective-permute-done((bf16[128,1024]{1,0:T(8,128)(2,1)S(1)}, bf16[128,1024]{1,0:T(8,128)(2,1)S(1)}, u32[]{:S(2)}, u32[]{:S(2)}) %collective-permute-start.12) | collective-permute-done | bytes 262176 | tf_op jit(solution)/shard_map/ppermute | solution.py:189
  147.4 1.0 pad_maximum_fusion.1
  (118 shorter events, 17.5 us)
Async XLA Ops:
  0.0 13.7 %copy-start.5 = (bf16[512,2,256]{2,1,0:T(2,128)(2,1)S(1)}, bf16[512,2,256]{2,1,0:T(2,128)(2,1)}, u32[]{:S(2)}) copy-start(bf16[512,2,256]{2,1,0:T(2,128)(2,1)} %param.13) | copy-start | bytes 1572868
  0.0 14.5 %copy-start.11 = (bf16[2048]{0:T(1024)(128)(2,1)S(1)}, bf16[2048]{0:T(1024)(128)(2,1)}, u32[]{:S(2)}) copy-start(bf16[2048]{0:T(1024)(128)(2,1)} %param.18) | copy-start | bytes 12292
  0.0 14.5 %copy-start.13 = (bf16[2,256]{1,0:T(2,128)(2,1)S(1)}, bf16[2,256]{1,0:T(2,128)(2,1)}, u32[]{:S(2)}) copy-start(bf16[2,256]{1,0:T(2,128)(2,1)} %param.19) | copy-start | bytes 3076
  1.6 12.9 %collective-permute-start = (bf16[3,2560]{1,0:T(4,128)(2,1)S(1)}, bf16[3,2560]{1,0:T(4,128)(2,1)S(1)}, u32[]{:S(2)}, u32[]{:S(2)}) collective-permute-start(bf16[3,2560]{1,0:T(4,128)(2,1)S(1)} %pad_maximum_fusion.5), channel_id=1, source_target_pairs={{0,4},{4,8},{8,12},{12,16},{16,20},{20,24},{24,28},{1,5},{5,9},{9,... | collective-permute-start | bytes 46088 | tf_op jit(solution)/shard_map/ppermute | solution.py:20
  24.8 10.5 %copy-start = (bf16[512,2048]{0,1:T(8,128)(2,1)}, bf16[512,2048]{0,1:T(8,128)(2,1)S(1)}, u32[]{:S(2)}) copy-start(bf16[512,2048]{0,1:T(8,128)(2,1)S(1)} %multiply_convert_fusion.3) | copy-start | bytes 6291460
  26.4 8.9 %copy-start.14 = (f32[32]{0:T(128)S(1)}, f32[32]{0:T(128)}, u32[]{:S(2)}) copy-start(f32[32]{0:T(128)} %param.21) | copy-start | bytes 388
  26.4 9.1 %copy-start.12 = (bf16[2048]{0:T(1024)(128)(2,1)S(1)}, bf16[2048]{0:T(1024)(128)(2,1)}, u32[]{:S(2)}) copy-start(bf16[2048]{0:T(1024)(128)(2,1)} %param.22) | copy-start | bytes 12292
  27.9 16.5 %collective-permute-start.1 = (bf16[2064,128]{1,0:T(8,128)(2,1)}, bf16[2064,128]{1,0:T(8,128)(2,1)S(1)}, u32[]{:S(2)}, u32[]{:S(2)}) collective-permute-start(bf16[2064,128]{1,0:T(8,128)(2,1)} %pad_maximum_fusion.2), channel_id=1, source_target_pairs={{0,4},{4,8},{8,12},{12,16},{16,20},{20,24},{24,28},{1,5},{5,9},{9,... | collective-permute-start | bytes 1585160 | tf_op jit(solution)/shard_map/ppermute | solution.py:20
  29.2 27.8 %collective-permute-start.2 = (bf16[2064,128]{1,0:T(8,128)(2,1)}, bf16[2064,128]{1,0:T(8,128)(2,1)}, u32[]{:S(2)}, u32[]{:S(2)}) collective-permute-start(bf16[2064,128]{1,0:T(8,128)(2,1)} %pad_maximum_fusion.2), channel_id=1, source_target_pairs={{0,8},{4,12},{8,16},{12,20},{16,24},{20,28},{1,9},{5,13},{9,17},{1... | collective-permute-start | bytes 1585160 | tf_op jit(solution)/shard_map/ppermute | solution.py:20
  57.8 16.6 %copy-start.9 = (f32[2,16]{1,0:T(2,128)}, f32[2,16]{1,0:T(2,128)S(1)}, u32[]{:S(2)}) copy-start(f32[2,16]{1,0:T(2,128)S(1)} %get-tuple-element.11) | copy-start | bytes 388
  59.6 17.2 %copy-start.1 = (bf16[512,2048]{0,1:T(8,128)(2,1)S(1)}, bf16[512,2048]{0,1:T(8,128)(2,1)}, u32[]{:S(2)}) copy-start(bf16[512,2048]{0,1:T(8,128)(2,1)} %copy-done) | copy-start | bytes 6291460
  59.6 17.2 %copy-start.4 = (f32[2,512,512]{2,1,0:T(8,128)S(1)}, f32[2,512,512]{2,1,0:T(8,128)}, u32[]{:S(2)}) copy-start(f32[2,512,512]{2,1,0:T(8,128)} %fusion.67) | copy-start | bytes 6291460
  59.6 17.2 %copy-start.6 = (pred[512,512]{1,0:T(8,128)(4,1)S(1)}, pred[512,512]{1,0:T(8,128)(4,1)}, u32[]{:S(2)}) copy-start(pred[512,512]{1,0:T(8,128)(4,1)} %iota_compare_fusion) | copy-start | bytes 786436
  59.6 17.2 %copy-start.7 = (f32[2,16,512]{2,1,0:T(8,128)S(1)}, f32[2,16,512]{2,1,0:T(8,128)}, u32[]{:S(2)}) copy-start(f32[2,16,512]{2,1,0:T(8,128)} %get-tuple-element.18) | copy-start | bytes 196612
  59.7 14.7 %collective-permute-start.3 = (bf16[2064,128]{1,0:T(8,128)(2,1)S(1)}, bf16[2064,128]{1,0:T(8,128)(2,1)S(1)}, u32[]{:S(2)}, u32[]{:S(2)}) collective-permute-start(bf16[2064,128]{1,0:T(8,128)(2,1)S(1)} %pad_maximum_fusion.3), channel_id=1, source_target_pairs={{0,8},{4,12},{8,16},{12,20},{16,24},{20,28},{1,9},{5,13},{9,17},{1... | collective-permute-start | bytes 1585160 | tf_op jit(solution)/shard_map/ppermute | solution.py:20
  75.5 25.7 %collective-permute-start.4 = (bf16[2,16,64,128]{3,2,1,0:T(8,128)(2,1)}, bf16[2,16,64,128]{3,2,1,0:T(8,128)(2,1)S(1)}, u32[]{:S(2)}, u32[]{:S(2)}) collective-permute-start(bf16[2,16,64,128]{3,2,1,0:T(8,128)(2,1)} %fusion.50), channel_id=1, source_target_pairs={{0,16},{4,20},{8,24},{12,28},{1,17},{5,21},{9,25},{13,29},{2,18},{... | collective-permute-start | bytes 1572872 | tf_op jit(solution)/shard_map/ppermute | solution.py:20
  76.8 11.9 %copy-start.10 = (f32[2,16]{1,0:T(2,128)S(1)}, f32[2,16]{1,0:T(2,128)}, u32[]{:S(2)}) copy-start(f32[2,16]{1,0:T(2,128)} %copy-done.9) | copy-start | bytes 388
  101.2 4.5 %copy-start.2 = (bf16[512,2048]{0,1:T(8,128)(2,1)S(1)}, bf16[512,2048]{0,1:T(8,128)(2,1)}, u32[]{:S(2)}) copy-start(bf16[512,2048]{0,1:T(8,128)(2,1)} %copy-done) | copy-start | bytes 6291460
  101.2 4.5 %copy-start.3 = (bf16[512,2048]{0,1:T(8,128)(2,1)S(1)}, bf16[512,2048]{0,1:T(8,128)(2,1)}, u32[]{:S(2)}) copy-start(bf16[512,2048]{0,1:T(8,128)(2,1)} %copy.77) | copy-start | bytes 6291460
  105.7 2.3 %copy-start.8 = (f32[2048]{0:T(1024)S(1)}, f32[2048]{0:T(1024)}, u32[]{:S(2)}) copy-start(f32[2048]{0:T(1024)} %convert_element_type.279) | copy-start | bytes 24580
  105.7 7.7 %slice-start = ((s8[16777216]{0:T(1024)(128)(4,1)}), s8[4194304]{0:T(1024)(128)(4,1)S(1)}, s32[]{:S(2)}) async-start(s8[16777216]{0:T(1024)(128)(4,1)} %bitcast.190), calls=%async_computation | async-start | bytes 8388608
  105.7 7.7 %slice-start.1 = ((s8[16777216]{0:T(1024)(128)(4,1)}), s8[4194304]{0:T(1024)(128)(4,1)S(1)}, s32[]{:S(2)}) async-start(s8[16777216]{0:T(1024)(128)(4,1)} %bitcast.190), calls=%async_computation.1 | async-start | bytes 8388608
  108.0 5.4 %slice-start.2 = ((s8[16777216]{0:T(1024)(128)(4,1)}), s8[4194304]{0:T(1024)(128)(4,1)S(1)}, s32[]{:S(2)}) async-start(s8[16777216]{0:T(1024)(128)(4,1)} %bitcast.190), calls=%async_computation.2 | async-start | bytes 8388608
  108.5 5.0 %slice-start.3 = ((s8[16777216]{0:T(1024)(128)(4,1)}), s8[4194304]{0:T(1024)(128)(4,1)S(1)}, s32[]{:S(2)}) async-start(s8[16777216]{0:T(1024)(128)(4,1)} %bitcast.190), calls=%async_computation.3 | async-start | bytes 8388608
  118.2 3.8 %collective-permute-start.5 = (bf16[2,128,1024]{2,1,0:T(8,128)(2,1)S(1)}, bf16[2,128,1024]{2,1,0:T(8,128)(2,1)S(1)}, u32[]{:S(2)}, u32[]{:S(2)}) collective-permute-start(bf16[2,128,1024]{2,1,0:T(8,128)(2,1)S(1)} %dynamic-slice_bitcast_fusion.3), channel_id=1, source_target_pairs={{0,1},{1,0},{2,3},{3,2},{4,5},{5,4},{6,7},{7,6},{8,9},{9,8},{10,11... | collective-permute-start | bytes 1572872 | tf_op jit(solution)/shard_map/ppermute | solution.py:189
  120.7 2.1 %collective-permute-start.7 = (bf16[2,128,1024]{2,1,0:T(8,128)(2,1)S(1)}, bf16[2,128,1024]{2,1,0:T(8,128)(2,1)S(1)}, u32[]{:S(2)}, u32[]{:S(2)}) collective-permute-start(bf16[2,128,1024]{2,1,0:T(8,128)(2,1)S(1)} %dynamic-slice_bitcast_fusion.2), channel_id=1, source_target_pairs={{0,1},{1,0},{2,3},{3,2},{4,5},{5,4},{6,7},{7,6},{8,9},{9,8},{10,11... | collective-permute-start | bytes 1572872 | tf_op jit(solution)/shard_map/ppermute | solution.py:189
  121.3 3.3 %collective-permute-start.9 = (bf16[2,128,1024]{2,1,0:T(8,128)(2,1)S(1)}, bf16[2,128,1024]{2,1,0:T(8,128)(2,1)S(1)}, u32[]{:S(2)}, u32[]{:S(2)}) collective-permute-start(bf16[2,128,1024]{2,1,0:T(8,128)(2,1)S(1)} %dynamic-slice_bitcast_fusion.1), channel_id=1, source_target_pairs={{0,1},{1,0},{2,3},{3,2},{4,5},{5,4},{6,7},{7,6},{8,9},{9,8},{10,11... | collective-permute-start | bytes 1572872 | tf_op jit(solution)/shard_map/ppermute | solution.py:189
  121.4 4.0 %collective-permute-start.11 = (bf16[2,128,1024]{2,1,0:T(8,128)(2,1)S(1)}, bf16[2,128,1024]{2,1,0:T(8,128)(2,1)S(1)}, u32[]{:S(2)}, u32[]{:S(2)}) collective-permute-start(bf16[2,128,1024]{2,1,0:T(8,128)(2,1)S(1)} %dynamic-slice_bitcast_fusion), channel_id=1, source_target_pairs={{0,1},{1,0},{2,3},{3,2},{4,5},{5,4},{6,7},{7,6},{8,9},{9,8},{10,11... | collective-permute-start | bytes 1572872 | tf_op jit(solution)/shard_map/ppermute | solution.py:189
  122.2 9.2 %collective-permute-start.6 = (bf16[128,1024]{1,0:T(8,128)(2,1)S(1)}, bf16[128,1024]{1,0:T(8,128)(2,1)S(1)}, u32[]{:S(2)}, u32[]{:S(2)}) collective-permute-start(bf16[128,1024]{1,0:T(8,128)(2,1)S(1)} %fusion.45), channel_id=1, source_target_pairs={{0,2},{2,0},{1,3},{3,1},{4,6},{6,4},{5,7},{7,5},{8,10},{10,8},{9,1... | collective-permute-start | bytes 786440 | tf_op jit(solution)/shard_map/ppermute | solution.py:189
  123.0 14.0 %collective-permute-start.8 = (bf16[128,1024]{1,0:T(8,128)(2,1)S(1)}, bf16[128,1024]{1,0:T(8,128)(2,1)S(1)}, u32[]{:S(2)}, u32[]{:S(2)}) collective-permute-start(bf16[128,1024]{1,0:T(8,128)(2,1)S(1)} %fusion.46), channel_id=1, source_target_pairs={{0,2},{2,0},{1,3},{3,1},{4,6},{6,4},{5,7},{7,5},{8,10},{10,8},{9,1... | collective-permute-start | bytes 786440 | tf_op jit(solution)/shard_map/ppermute | solution.py:189
  124.8 17.9 %collective-permute-start.10 = (bf16[128,1024]{1,0:T(8,128)(2,1)S(1)}, bf16[128,1024]{1,0:T(8,128)(2,1)S(1)}, u32[]{:S(2)}, u32[]{:S(2)}) collective-permute-start(bf16[128,1024]{1,0:T(8,128)(2,1)S(1)} %fusion.47), channel_id=1, source_target_pairs={{0,2},{2,0},{1,3},{3,1},{4,6},{6,4},{5,7},{7,5},{8,10},{10,8},{9,1... | collective-permute-start | bytes 786440 | tf_op jit(solution)/shard_map/ppermute | solution.py:189
  125.7 21.7 %collective-permute-start.12 = (bf16[128,1024]{1,0:T(8,128)(2,1)S(1)}, bf16[128,1024]{1,0:T(8,128)(2,1)S(1)}, u32[]{:S(2)}, u32[]{:S(2)}) collective-permute-start(bf16[128,1024]{1,0:T(8,128)(2,1)S(1)} %fusion.48), channel_id=1, source_target_pairs={{0,2},{2,0},{1,3},{3,1},{4,6},{6,4},{5,7},{7,5},{8,10},{10,8},{9,1... | collective-permute-start | bytes 786440 | tf_op jit(solution)/shard_map/ppermute | solution.py:189

commit v5 on v4

--- a/solution.py
+++ b/solution.py
@@ -209,24 +209,35 @@
     chunks = 4 if width % (4 * 128) == 0 else 1
     step = width // chunks
     done = []
+    payloads = []
     for c in range(chunks):
+        source = normed
+        if c >= 2 and payloads[c - 2] is not None:
+            payloads[c - 2], source = lax.optimization_barrier((payloads[c - 2], normed))
         partial = jnp.dot(
-            normed, out_weight[:, c * step : (c + 1) * step], preferred_element_type=jnp.float32
+            source, out_weight[:, c * step : (c + 1) * step], preferred_element_type=jnp.float32
         ).astype(jnp.bfloat16)
         partial = partial.reshape(outer, inner, piece, step)
         sent = swap(lax.dynamic_index_in_dim(partial, other, 1, keepdims=False), "tc")
         half = lax.dynamic_index_in_dim(partial, tc, 1, keepdims=False).astype(jnp.float32)
         half = half + sent.astype(jnp.float32)
         if outer == 2:
-            across = swap(
-                lax.dynamic_index_in_dim(half, 1 - ty, 0, keepdims=False).astype(jnp.bfloat16), "ty"
+            payloads.append(
+                lax.dynamic_index_in_dim(half, 1 - ty, 0, keepdims=False).astype(jnp.bfloat16)
             )
+        else:
+            payloads.append(None)
+        done.append(half)
+    for c in range(chunks):
+        half = done[c]
+        if outer == 2:
+            across = swap(payloads[c], "ty")
             mine = lax.dynamic_index_in_dim(half, ty, 0, keepdims=False)
-            done.append((mine + across.astype(jnp.float32)).astype(jnp.bfloat16))
+            done[c] = (mine + across.astype(jnp.float32)).astype(jnp.bfloat16)
         else:
-            done.append(
-                lax.psum_scatter(half.astype(jnp.bfloat16), "ty", scatter_dimension=0, tiled=True)[0]
-            )
+            done[c] = lax.psum_scatter(
+                half.astype(jnp.bfloat16), "ty", scatter_dimension=0, tiled=True
+            )[0]
     return jnp.concatenate(done, axis=1)
 
 

time: 149 us -> 152 us (1.020)
  waiting for transfers between devices: 63.4 us -> 55.4 us
  matrix products: 29.5 us -> 36.4 us
  other arithmetic: 29 us -> 31.7 us
  local copies, waits for them, and re-layouts: 13.6 us -> 15.4 us
    ppermute x8, waiting for transfers between devices: 20 us -> 12.1 us  [swap(): return lax.ppermute(value, axis, [(0, 1), (1, 0)])]
    dot_general x4, matrix products: 12 us -> 18.1 us  [reduce_rows(): jnp.dot(source, out_weight[:, c * step:(c + 1) * step], preferred_element...]
    add x4, other arithmetic: 0.69 us -> 2.93 us  [reduce_rows(): half = half + sent.astype(jnp.float32)]
    squeeze x4, local copies, waits for them, and re-layouts: 0.16 us -> 1.84 us  [reduce_rows(): lax.dynamic_index_in_dim(partial, other, 1, keepdims=False)]
    unnamed x43 -> x37, local copies, waits for them, and re-layouts: 9.42 us -> 9.39 us
  transfers between devices with their start and end apart: 13 -> 13, of which waited for: 8 -> 7; matrix products, arithmetic and copies ran while one was open for 24% -> 33% of each run, Pallas kernels for 0% -> 0%
where the time goes in v5:
time: 152 us; the launch traced here: 151 us
  waiting for transfers between devices  55.4 us (36%)
  matrix products  36.4 us (24%)
  other arithmetic  31.7 us (21%)
  local copies, waits for them, and re-layouts  15.4 us (10%)
  starting transfers between devices  11.5 us (8%)
    ppermute x5, waiting for transfers between devices, shifted(): return lax.ppermute(value, axis, pairs)  43.4 us
    dot_general x4, matrix products, reduce_rows(): jnp.dot(source, out_weight[:, c * step:(c + 1) * step], preferred_element...  18.1 us
    ppermute x8, waiting for transfers between devices, swap(): return lax.ppermute(value, axis, [(0, 1), (1, 0)])  12.1 us
    convert_element_type x2, other arithmetic, conv_silu(): return lax.optimization_barrier(jax.nn.silu(summed).astype(jnp.bfloat16))  11.1 us
    dot_general x1, matrix products, block_parts(): jnp.einsum('ghij,jghp->ighp', mixing, inner_block, preferred_element_type...  10.6 us
    unnamed x37, local copies, waits for them, and re-layouts  9.39 us
    ppermute x5, starting transfers between devices, shifted(): return lax.ppermute(value, axis, pairs)  6.7 us
    ppermute x8, starting transfers between devices, swap(): return lax.ppermute(value, axis, [(0, 1), (1, 0)])  4.78 us
  transfers between devices with their start and end apart: 13, of which 7 were waited for; matrix products, arithmetic and copies ran while one was open for 33% of the time, Pallas kernels for 0%

profile of v5, /device:TPU:30, one launch (start us, length us, event | category | flops | bytes accessed | tf_op | source)
XLA Modules:
  0.0 151.0 jit_solution(9666083925861719935)
XLA Ops:
  1.6 1.3 collective-permute-start
  4.4 2.3 %reduce-window.6 = f32[16,2,4,128]{3,0,1,2:T(8,128)S(1)} reduce-window(f32[16,2,4,128]{3,0,1,2:T(8,128)S(1)} %bitcast.183, f32[]{:T(128)} %constant.62.clone.1), window={size=1x1x1x128 pad=0_0x0_0x0_0x127_0}, to_apply=%region_0.1 | reduce-window | flops 2080768 | bytes 131076 | tf_op jit(solution)/shard_map/reduce-window
  10.4 3.9 %copy.64 = bf16[512,2048]{0,1:T(8,128)(2,1)} copy(bf16[512,2048]{1,0:T(8,128)(2,1)} %param.12) | data formatting | bytes 4194304 | tf_op args[0]
  15.5 9.8 %multiply_convert_fusion.3 = bf16[512,2048]{0,1:T(8,128)(2,1)S(1)} fusion(bf16[512,2048]{0,1:T(8,128)(2,1)} %copy.64, bf16[3,2048]{0,1:T(8,128)(2,1)S(1)} %copy.63, f32[2048]{0:T(1024)S(1)} %bitcast.186, f32[2048]{0:T(1024)S(1)} %bitcast.187, f32[2048]{0:T(1024)S(1)} %bitcast.185, f32[2048]{0:T(1024)S(1)} %bitcast.184, f32[2048]{0:T(1024)S(1)} %convert_element_type.243), kind=kLoop, calls=%fused_computation.25 | loop fusion | flops 27262976 | bytes 4247552 | tf_op jit(solution)/shard_map/convert_element_type | solution.py:29
  25.5 1.3 multiply_convert_fusion.7
  26.9 1.6 %fusion.33 = bf16[2,16,64,128]{3,2,1,0:T(8,128)(2,1)S(1)} fusion(bf16[512,2,128,1]{0,2,3,1:T(8,128)(2,1)S(1)} %bitcast.176, bf16[512,2,16,64]{0,3,2,1:T(8,128)(2,1)S(1)} %bitcast.162, f32[512,2,16]{0,2,1:T(8,128)} %get-tuple-element.23), kind=kOutput, calls=%fused_computation.39 | convolution fusion | flops 271843328 | bytes 2949120 | tf_op jit(solution)/shard_map/jghp,jgn->ghpn/dot_general | solution.py:49
  29.3 1.3 collective-permute-start.1
  30.6 1.3 collective-permute-start.2
  32.7 4.0 %copy.77 = bf16[512,2048]{0,1:T(8,128)(2,1)} copy(bf16[512,2048]{1,0:T(8,128)(2,1)} %param.14) | data formatting | bytes 4194304 | tf_op args[2]
  37.4 1.8 %fusion.67 = f32[2,512,512]{2,1,0:T(8,128)} fusion(bf16[512,2,128]{0,2,1:T(8,128)(2,1)S(1)} %bitcast.166, bf16[512,2,128]{0,2,1:T(8,128)(2,1)S(1)} %bitcast.177), kind=kOutput, calls=%fused_computation.129 | convolution fusion | flops 134217728 | bytes 2621440 | tf_op jit(solution)/shard_map/ign,jgn->gij/dot_general | solution.py:40
  39.2 6.5 %collective-permute-done.1 = bf16[2064,128]{1,0:T(8,128)(2,1)S(1)} collective-permute-done((bf16[2064,128]{1,0:T(8,128)(2,1)}, bf16[2064,128]{1,0:T(8,128)(2,1)S(1)}, u32[]{:S(2)}, u32[]{:S(2)}) %collective-permute-start.1) | collective-permute-done | bytes 528416 | tf_op jit(solution)/shard_map/ppermute | solution.py:20
  45.8 12.5 %collective-permute-done.2 = bf16[2064,128]{1,0:T(8,128)(2,1)} collective-permute-done((bf16[2064,128]{1,0:T(8,128)(2,1)}, bf16[2064,128]{1,0:T(8,128)(2,1)}, u32[]{:S(2)}, u32[]{:S(2)}) %collective-permute-start.2) | collective-permute-done | bytes 528416 | tf_op jit(solution)/shard_map/ppermute | solution.py:20
  59.5 1.4 add_convert_fusion
  61.0 1.6 %collective-permute-start.3 = (bf16[2064,128]{1,0:T(8,128)(2,1)S(1)}, bf16[2064,128]{1,0:T(8,128)(2,1)S(1)}, u32[]{:S(2)}, u32[]{:S(2)}) collective-permute-start(bf16[2064,128]{1,0:T(8,128)(2,1)S(1)} %pad_maximum_fusion.3), channel_id=1, source_target_pairs={{0,8},{4,12},{8,16},{12,20},{16,24},{20,28},{1,9},{5,13},{9,17},{1... | collective-permute-start | bytes 1585160 | tf_op jit(solution)/shard_map/ppermute | solution.py:20
  62.6 1.1 slice_convert_fusion.1
  63.8 12.0 %collective-permute-done.3 = bf16[2064,128]{1,0:T(8,128)(2,1)S(1)} collective-permute-done((bf16[2064,128]{1,0:T(8,128)(2,1)S(1)}, bf16[2064,128]{1,0:T(8,128)(2,1)S(1)}, u32[]{:S(2)}, u32[]{:S(2)}) %collective-permute-start.3) | collective-permute-done | bytes 528416 | tf_op jit(solution)/shard_map/ppermute | solution.py:20
  75.8 1.1 fusion.50
  76.9 1.3 collective-permute-start.4
  78.2 10.6 %fusion = f32[2,16,64,512]{3,2,1,0:T(8,128)} fusion(bf16[512,2,16,64]{0,3,2,1:T(8,128)(2,1)S(1)} %bitcast.163, f32[2,16,512]{2,1,0:T(8,128)S(1)} %bitcast.182, f32[2,512,512]{2,1,0:T(8,128)S(1)} %copy-done.4, f32[2,16,512]{2,1,0:T(8,128)S(1)} %copy-done.8, pred[512,512]{1,0:T(8,128)(4,1)S(1)} %copy-done.7), kind=kOutput, calls=%fused_computation.1 | convolution fusion | flops 1115684864 | bytes 8781824 | tf_op jit(solution)/shard_map/ghij,jghp->ighp/dot_general | solution.py:44
  90.2 12.4 %collective-permute-done.4 = bf16[2,16,64,128]{3,2,1,0:T(8,128)(2,1)S(1)} collective-permute-done((bf16[2,16,64,128]{3,2,1,0:T(8,128)(2,1)}, bf16[2,16,64,128]{3,2,1,0:T(8,128)(2,1)S(1)}, u32[]{:S(2)}, u32[]{:S(2)}) %collective-permute-start.4) | collective-permute-done | bytes 524320 | tf_op jit(solution)/shard_map/ppermute | solution.py:20
  102.5 4.4 %fusion.6 = f32[1,512,2,16,64]{1,4,3,2,0:T(8,128)S(1)} fusion(f32[2,16,64,512]{3,2,1,0:T(8,128)} %fusion, bf16[512,2,128,1]{0,2,3,1:T(8,128)(2,1)S(1)} %bitcast.167, f32[512,2,16]{0,2,1:T(8,128)S(1)} %get-tuple-element.24, bf16[2,16,64,128]{3,2,1,0:T(8,128)(2,1)S(1)} %collective-permute-done.4, f32[2,16]{1,0:T(2,128)S(1)} %fusion.59, ...), kind=kOutput, calls=%fused_computation.10 | convolution fusion | flops 1614807040 | bytes 11862400 | tf_op jit(solution)/shard_map/vmap(ign,ghpn->ighp)/dot_general | solution.py:56
  106.9 2.2 %bitcast_reduce_fusion = (f32[512,2]{0,1:T(2,128)S(1)}, f32[512,2048]{0,1:T(8,128)S(1)}) fusion(bf16[512,2048]{0,1:T(8,128)(2,1)S(1)} %copy-done.3, bf16[512,2048]{0,1:T(8,128)(2,1)S(1)} %copy-done.2, f32[2048]{0:T(1024)S(1)} %mul.292, f32[1,512,2,16,64]{1,4,3,2,0:T(8,128)S(1)} %fusion.6), kind=kLoop, calls=%fused_computation.14 | loop fusion | flops 11533312 | bytes 12595200 | tf_op jit(solution)/shard_map/reduce_sum | solution.py:181
  109.6 4.5 %fusion.21 = bf16[512,1024]{1,0:T(8,128)(2,1)S(1)} fusion(bf16[512,2048]{0,1:T(8,128)(2,1)S(1)} %fusion.8, bf16[2048,4096]{1,0:T(8,128)(2,1)} %param.23), kind=kOutput, calls=%fused_computation.35 | convolution fusion | flops 2148007936 | bytes 7340032 | tf_op jit(solution)/shard_map/dot_general | solution.py:217
  115.1 4.5 %fusion.24 = bf16[512,1024]{1,0:T(8,128)(2,1)S(1)} fusion(bf16[512,2048]{0,1:T(8,128)(2,1)S(1)} %fusion.8, bf16[2048,4096]{1,0:T(8,128)(2,1)} %param.23), kind=kOutput, calls=%fused_computation.36 | convolution fusion | flops 2148007936 | bytes 7340032 | tf_op jit(solution)/shard_map/dot_general | solution.py:217
  121.0 1.4 convert_add_fusion.3
  123.0 1.2 convert_add_fusion.2
  124.2 1.6 %collective-permute-start.8 = (bf16[128,1024]{1,0:T(8,128)(2,1)S(1)}, bf16[128,1024]{1,0:T(8,128)(2,1)S(1)}, u32[]{:S(2)}, u32[]{:S(2)}) collective-permute-start(bf16[128,1024]{1,0:T(8,128)(2,1)S(1)} %fusion.46), channel_id=1, source_target_pairs={{0,2},{2,0},{1,3},{3,1},{4,6},{6,4},{5,7},{7,5},{8,10},{10,8},{9,1... | collective-permute-start | bytes 786440 | tf_op jit(solution)/shard_map/ppermute | solution.py:189
  125.9 4.5 %fusion.27 = bf16[512,1024]{1,0:T(8,128)(2,1)S(1)} fusion(bf16[512,2048]{0,1:T(8,128)(2,1)S(1)} %fusion.8, bf16[2048,4096]{1,0:T(8,128)(2,1)} %param.23), kind=kOutput, calls=%fused_computation.37 | convolution fusion | flops 2148007936 | bytes 7340032 | tf_op jit(solution)/shard_map/dot_general | solution.py:217
  130.5 4.5 %fusion.30 = bf16[512,1024]{1,0:T(8,128)(2,1)S(1)} fusion(bf16[512,2048]{0,1:T(8,128)(2,1)S(1)} %fusion.8, bf16[2048,4096]{1,0:T(8,128)(2,1)} %param.23), kind=kOutput, calls=%fused_computation.38 | convolution fusion | flops 2148007936 | bytes 7340032 | tf_op jit(solution)/shard_map/dot_general | solution.py:217
  138.4 6.8 %collective-permute-done.10 = bf16[128,1024]{1,0:T(8,128)(2,1)S(1)} collective-permute-done((bf16[128,1024]{1,0:T(8,128)(2,1)S(1)}, bf16[128,1024]{1,0:T(8,128)(2,1)S(1)}, u32[]{:S(2)}, u32[]{:S(2)}) %collective-permute-start.10) | collective-permute-done | bytes 262176 | tf_op jit(solution)/shard_map/ppermute | solution.py:189
  145.3 4.6 %collective-permute-done.12 = bf16[128,1024]{1,0:T(8,128)(2,1)S(1)} collective-permute-done((bf16[128,1024]{1,0:T(8,128)(2,1)S(1)}, bf16[128,1024]{1,0:T(8,128)(2,1)S(1)}, u32[]{:S(2)}, u32[]{:S(2)}) %collective-permute-start.12) | collective-permute-done | bytes 262176 | tf_op jit(solution)/shard_map/ppermute | solution.py:189
  150.0 1.0 pad_maximum_fusion.1
  (111 shorter events, 20.2 us)
Async XLA Ops:
  0.0 14.3 %copy-start.6 = (bf16[512,2,256]{2,1,0:T(2,128)(2,1)S(1)}, bf16[512,2,256]{2,1,0:T(2,128)(2,1)}, u32[]{:S(2)}) copy-start(bf16[512,2,256]{2,1,0:T(2,128)(2,1)} %param.13) | copy-start | bytes 1572868
  0.0 15.1 %copy-start.12 = (bf16[2048]{0:T(1024)(128)(2,1)S(1)}, bf16[2048]{0:T(1024)(128)(2,1)}, u32[]{:S(2)}) copy-start(bf16[2048]{0:T(1024)(128)(2,1)} %param.18) | copy-start | bytes 12292
  0.0 15.1 %copy-start.14 = (bf16[2,256]{1,0:T(2,128)(2,1)S(1)}, bf16[2,256]{1,0:T(2,128)(2,1)}, u32[]{:S(2)}) copy-start(bf16[2,256]{1,0:T(2,128)(2,1)} %param.19) | copy-start | bytes 3076
  1.6 13.6 %collective-permute-start = (bf16[3,2560]{1,0:T(4,128)(2,1)S(1)}, bf16[3,2560]{1,0:T(4,128)(2,1)S(1)}, u32[]{:S(2)}, u32[]{:S(2)}) collective-permute-start(bf16[3,2560]{1,0:T(4,128)(2,1)S(1)} %pad_maximum_fusion.5), channel_id=1, source_target_pairs={{0,4},{4,8},{8,12},{12,16},{16,20},{20,24},{24,28},{1,5},{5,9},{9,... | collective-permute-start | bytes 46088 | tf_op jit(solution)/shard_map/ppermute | solution.py:20
  25.3 11.4 %copy-start = (bf16[512,2048]{0,1:T(8,128)(2,1)}, bf16[512,2048]{0,1:T(8,128)(2,1)S(1)}, u32[]{:S(2)}) copy-start(bf16[512,2048]{0,1:T(8,128)(2,1)S(1)} %multiply_convert_fusion.3) | copy-start | bytes 6291460
  26.9 9.8 %copy-start.15 = (f32[32]{0:T(128)S(1)}, f32[32]{0:T(128)}, u32[]{:S(2)}) copy-start(f32[32]{0:T(128)} %param.21) | copy-start | bytes 388
  26.9 9.9 %copy-start.13 = (bf16[2048]{0:T(1024)(128)(2,1)S(1)}, bf16[2048]{0:T(1024)(128)(2,1)}, u32[]{:S(2)}) copy-start(bf16[2048]{0:T(1024)(128)(2,1)} %param.22) | copy-start | bytes 12292
  29.3 16.5 %collective-permute-start.1 = (bf16[2064,128]{1,0:T(8,128)(2,1)}, bf16[2064,128]{1,0:T(8,128)(2,1)S(1)}, u32[]{:S(2)}, u32[]{:S(2)}) collective-permute-start(bf16[2064,128]{1,0:T(8,128)(2,1)} %pad_maximum_fusion.2), channel_id=1, source_target_pairs={{0,4},{4,8},{8,12},{12,16},{16,20},{20,24},{24,28},{1,5},{5,9},{9,... | collective-permute-start | bytes 1585160 | tf_op jit(solution)/shard_map/ppermute | solution.py:20
  30.6 27.8 %collective-permute-start.2 = (bf16[2064,128]{1,0:T(8,128)(2,1)}, bf16[2064,128]{1,0:T(8,128)(2,1)}, u32[]{:S(2)}, u32[]{:S(2)}) collective-permute-start(bf16[2064,128]{1,0:T(8,128)(2,1)} %pad_maximum_fusion.2), channel_id=1, source_target_pairs={{0,8},{4,12},{8,16},{12,20},{16,24},{20,28},{1,9},{5,13},{9,17},{1... | collective-permute-start | bytes 1585160 | tf_op jit(solution)/shard_map/ppermute | solution.py:20
  59.1 16.6 %copy-start.10 = (f32[2,16]{1,0:T(2,128)}, f32[2,16]{1,0:T(2,128)S(1)}, u32[]{:S(2)}) copy-start(f32[2,16]{1,0:T(2,128)S(1)} %get-tuple-element.19) | copy-start | bytes 388
  60.9 17.2 %copy-start.1 = (bf16[512,2048]{0,1:T(8,128)(2,1)S(1)}, bf16[512,2048]{0,1:T(8,128)(2,1)}, u32[]{:S(2)}) copy-start(bf16[512,2048]{0,1:T(8,128)(2,1)} %copy-done) | copy-start | bytes 6291460
  60.9 17.2 %copy-start.4 = (f32[2,512,512]{2,1,0:T(8,128)S(1)}, f32[2,512,512]{2,1,0:T(8,128)}, u32[]{:S(2)}) copy-start(f32[2,512,512]{2,1,0:T(8,128)} %fusion.67) | copy-start | bytes 6291460
  61.0 17.2 %copy-start.7 = (pred[512,512]{1,0:T(8,128)(4,1)S(1)}, pred[512,512]{1,0:T(8,128)(4,1)}, u32[]{:S(2)}) copy-start(pred[512,512]{1,0:T(8,128)(4,1)} %iota_compare_fusion) | copy-start | bytes 786436
  61.0 17.2 %copy-start.8 = (f32[2,16,512]{2,1,0:T(8,128)S(1)}, f32[2,16,512]{2,1,0:T(8,128)}, u32[]{:S(2)}) copy-start(f32[2,16,512]{2,1,0:T(8,128)} %get-tuple-element.26) | copy-start | bytes 196612
  61.0 14.7 %collective-permute-start.3 = (bf16[2064,128]{1,0:T(8,128)(2,1)S(1)}, bf16[2064,128]{1,0:T(8,128)(2,1)S(1)}, u32[]{:S(2)}, u32[]{:S(2)}) collective-permute-start(bf16[2064,128]{1,0:T(8,128)(2,1)S(1)} %pad_maximum_fusion.3), channel_id=1, source_target_pairs={{0,8},{4,12},{8,16},{12,20},{16,24},{20,28},{1,9},{5,13},{9,17},{1... | collective-permute-start | bytes 1585160 | tf_op jit(solution)/shard_map/ppermute | solution.py:20
  76.9 25.7 %collective-permute-start.4 = (bf16[2,16,64,128]{3,2,1,0:T(8,128)(2,1)}, bf16[2,16,64,128]{3,2,1,0:T(8,128)(2,1)S(1)}, u32[]{:S(2)}, u32[]{:S(2)}) collective-permute-start(bf16[2,16,64,128]{3,2,1,0:T(8,128)(2,1)} %fusion.50), channel_id=1, source_target_pairs={{0,16},{4,20},{8,24},{12,28},{1,17},{5,21},{9,25},{13,29},{2,18},{... | collective-permute-start | bytes 1572872 | tf_op jit(solution)/shard_map/ppermute | solution.py:20
  78.2 12.0 %copy-start.11 = (f32[2,16]{1,0:T(2,128)S(1)}, f32[2,16]{1,0:T(2,128)}, u32[]{:S(2)}) copy-start(f32[2,16]{1,0:T(2,128)} %copy-done.10) | copy-start | bytes 388
  102.5 4.4 %copy-start.2 = (bf16[512,2048]{0,1:T(8,128)(2,1)S(1)}, bf16[512,2048]{0,1:T(8,128)(2,1)}, u32[]{:S(2)}) copy-start(bf16[512,2048]{0,1:T(8,128)(2,1)} %copy-done) | copy-start | bytes 6291460
  102.5 4.4 %copy-start.3 = (bf16[512,2048]{0,1:T(8,128)(2,1)S(1)}, bf16[512,2048]{0,1:T(8,128)(2,1)}, u32[]{:S(2)}) copy-start(bf16[512,2048]{0,1:T(8,128)(2,1)} %copy.77) | copy-start | bytes 6291460
  106.9 2.3 %copy-start.9 = (f32[2048]{0:T(1024)S(1)}, f32[2048]{0:T(1024)}, u32[]{:S(2)}) copy-start(f32[2048]{0:T(1024)} %convert_element_type.279) | copy-start | bytes 24580
  114.2 5.5 %copy-start.5 = (bf16[512,1024]{1,0:T(8,128)(2,1)}, bf16[512,1024]{1,0:T(8,128)(2,1)S(1)}, u32[]{:S(2)}) copy-start(bf16[512,1024]{1,0:T(8,128)(2,1)S(1)} %fusion.21) | copy-start | bytes 3145732
  115.1 5.9 %collective-permute-start.5 = (bf16[2,128,1024]{2,1,0:T(8,128)(2,1)}, bf16[2,128,1024]{2,1,0:T(8,128)(2,1)}, u32[]{:S(2)}, u32[]{:S(2)}) collective-permute-start(bf16[2,128,1024]{2,1,0:T(8,128)(2,1)} %dynamic-slice_bitcast_fusion.3), channel_id=1, source_target_pairs={{0,1},{1,0},{2,3},{3,2},{4,5},{5,4},{6,7},{7,6},{8,9},{9,8},{10,11... | collective-permute-start | bytes 1572872 | tf_op jit(solution)/shard_map/ppermute | solution.py:189
  120.5 2.5 %collective-permute-start.7 = (bf16[2,128,1024]{2,1,0:T(8,128)(2,1)}, bf16[2,128,1024]{2,1,0:T(8,128)(2,1)}, u32[]{:S(2)}, u32[]{:S(2)}) collective-permute-start(bf16[2,128,1024]{2,1,0:T(8,128)(2,1)} %dynamic-slice_bitcast_fusion.2), channel_id=1, source_target_pairs={{0,1},{1,0},{2,3},{3,2},{4,5},{5,4},{6,7},{7,6},{8,9},{9,8},{10,11... | collective-permute-start | bytes 1572872 | tf_op jit(solution)/shard_map/ppermute | solution.py:189
  122.4 13.2 %collective-permute-start.6 = (bf16[128,1024]{1,0:T(8,128)(2,1)S(1)}, bf16[128,1024]{1,0:T(8,128)(2,1)S(1)}, u32[]{:S(2)}, u32[]{:S(2)}) collective-permute-start(bf16[128,1024]{1,0:T(8,128)(2,1)S(1)} %fusion.45), channel_id=1, source_target_pairs={{0,2},{2,0},{1,3},{3,1},{4,6},{6,4},{5,7},{7,5},{8,10},{10,8},{9,1... | collective-permute-start | bytes 786440 | tf_op jit(solution)/shard_map/ppermute | solution.py:189
  124.2 14.1 %collective-permute-start.8 = (bf16[128,1024]{1,0:T(8,128)(2,1)S(1)}, bf16[128,1024]{1,0:T(8,128)(2,1)S(1)}, u32[]{:S(2)}, u32[]{:S(2)}) collective-permute-start(bf16[128,1024]{1,0:T(8,128)(2,1)S(1)} %fusion.46), channel_id=1, source_target_pairs={{0,2},{2,0},{1,3},{3,1},{4,6},{6,4},{5,7},{7,5},{8,10},{10,8},{9,1... | collective-permute-start | bytes 786440 | tf_op jit(solution)/shard_map/ppermute | solution.py:189
  130.4 5.3 %collective-permute-start.9 = (bf16[2,128,1024]{2,1,0:T(8,128)(2,1)S(1)}, bf16[2,128,1024]{2,1,0:T(8,128)(2,1)S(1)}, u32[]{:S(2)}, u32[]{:S(2)}) collective-permute-start(bf16[2,128,1024]{2,1,0:T(8,128)(2,1)S(1)} %dynamic-slice_bitcast_fusion.1), channel_id=1, source_target_pairs={{0,1},{1,0},{2,3},{3,2},{4,5},{5,4},{6,7},{7,6},{8,9},{9,8},{10,11... | collective-permute-start | bytes 1572872 | tf_op jit(solution)/shard_map/ppermute | solution.py:189
  135.1 2.1 %collective-permute-start.11 = (bf16[2,128,1024]{2,1,0:T(8,128)(2,1)S(1)}, bf16[2,128,1024]{2,1,0:T(8,128)(2,1)S(1)}, u32[]{:S(2)}, u32[]{:S(2)}) collective-permute-start(bf16[2,128,1024]{2,1,0:T(8,128)(2,1)S(1)} %dynamic-slice_bitcast_fusion), channel_id=1, source_target_pairs={{0,1},{1,0},{2,3},{3,2},{4,5},{5,4},{6,7},{7,6},{8,9},{9,8},{10,11... | collective-permute-start | bytes 1572872 | tf_op jit(solution)/shard_map/ppermute | solution.py:189
  136.0 9.2 %collective-permute-start.10 = (bf16[128,1024]{1,0:T(8,128)(2,1)S(1)}, bf16[128,1024]{1,0:T(8,128)(2,1)S(1)}, u32[]{:S(2)}, u32[]{:S(2)}) collective-permute-start(bf16[128,1024]{1,0:T(8,128)(2,1)S(1)} %fusion.47), channel_id=1, source_target_pairs={{0,2},{2,0},{1,3},{3,1},{4,6},{6,4},{5,7},{7,5},{8,10},{10,8},{9,1... | collective-permute-start | bytes 786440 | tf_op jit(solution)/shard_map/ppermute | solution.py:189
  137.4 12.5 %collective-permute-start.12 = (bf16[128,1024]{1,0:T(8,128)(2,1)S(1)}, bf16[128,1024]{1,0:T(8,128)(2,1)S(1)}, u32[]{:S(2)}, u32[]{:S(2)}) collective-permute-start(bf16[128,1024]{1,0:T(8,128)(2,1)S(1)} %fusion.48), channel_id=1, source_target_pairs={{0,2},{2,0},{1,3},{3,1},{4,6},{6,4},{5,7},{7,5},{8,10},{10,8},{9,1... | collective-permute-start | bytes 786440 | tf_op jit(solution)/shard_map/ppermute | solution.py:189

commit v6 on v4

--- a/solution.py
+++ b/solution.py
@@ -53,9 +53,15 @@
 
 
 def apply_state(c_block, state, cumulative):
-    return jnp.exp(cumulative)[..., None] * jnp.einsum(
-        "ign,ghpn->ighp", c_block.astype(jnp.float32), state, precision=lax.Precision.HIGHEST
-    )
+    high = state.astype(jnp.bfloat16)
+    rest = state - high.astype(jnp.float32)
+    middle = rest.astype(jnp.bfloat16)
+    low = (rest - middle.astype(jnp.float32)).astype(jnp.bfloat16)
+    applied = sum(
+        jnp.einsum("ign,ghpn->ighp", c_block, part, preferred_element_type=jnp.float32)
+        for part in (low, middle, high)
+    )
+    return jnp.exp(cumulative)[..., None] * applied
 
 
 def block_local(carried_in, inputs_block):

time: 149 us -> 153 us (1.027)
  the two profiles are of different devices: /device:TPU:30 before, /device:TPU:24 now
where the time goes in v6:
time: 153 us; the launch traced here: 152 us
  waiting for transfers between devices  61.3 us (40%)
  matrix products  31 us (20%)
  other arithmetic  30 us (20%)
  starting transfers between devices  14.9 us (10%)
  local copies, waits for them, and re-layouts  14 us (9%)
    ppermute x5, waiting for transfers between devices, shifted(): return lax.ppermute(value, axis, pairs)  41.3 us
    ppermute x8, waiting for transfers between devices, swap(): return lax.ppermute(value, axis, [(0, 1), (1, 0)])  19.9 us
    dot_general x4, matrix products, reduce_rows(): jnp.dot(normed, out_weight[:, c * step:(c + 1) * step], preferred_element...  11.9 us
    convert_element_type x2, other arithmetic, conv_silu(): return lax.optimization_barrier(jax.nn.silu(summed).astype(jnp.bfloat16))  11.1 us
    dot_general x1, matrix products, block_parts(): jnp.einsum('ghij,jghp->ighp', mixing, inner_block, preferred_element_type...  10.5 us
    unnamed x37, local copies, waits for them, and re-layouts  9.82 us
    ppermute x5, starting transfers between devices, shifted(): return lax.ppermute(value, axis, pairs)  9.31 us
    dot_general x3, matrix products, apply_state(): jnp.einsum('ign,ghpn->ighp', c_block, part, preferred_element_type=jnp.fl...  6.02 us
  transfers between devices with their start and end apart: 13, of which 8 were waited for; matrix products, arithmetic and copies ran while one was open for 23% of the time, Pallas kernels for 0%

profile of v6, /device:TPU:24, one launch (start us, length us, event | category | flops | bytes accessed | tf_op | source)
XLA Modules:
  0.0 151.7 jit_solution(11467571942926721717)
XLA Ops:
  1.6 3.4 %collective-permute-start = (bf16[3,2560]{1,0:T(4,128)(2,1)S(1)}, bf16[3,2560]{1,0:T(4,128)(2,1)S(1)}, u32[]{:S(2)}, u32[]{:S(2)}) collective-permute-start(bf16[3,2560]{1,0:T(4,128)(2,1)S(1)} %pad_maximum_fusion.5), channel_id=1, source_target_pairs={{0,4},{4,8},{8,12},{12,16},{16,20},{20,24},{24,28},{1,5},{5,9},{9,... | collective-permute-start | bytes 46088 | tf_op jit(solution)/shard_map/ppermute | solution.py:20
  8.2 2.3 %reduce-window.6 = f32[16,2,4,128]{3,0,1,2:T(8,128)S(1)} reduce-window(f32[16,2,4,128]{3,0,1,2:T(8,128)S(1)} %bitcast.186, f32[]{:T(128)} %constant.62.clone.1), window={size=1x1x1x128 pad=0_0x0_0x0_0x127_0}, to_apply=%region_0.1 | reduce-window | flops 2080768 | bytes 131076 | tf_op jit(solution)/shard_map/reduce-window
  11.9 3.9 %copy.68 = bf16[512,2048]{0,1:T(8,128)(2,1)} copy(bf16[512,2048]{1,0:T(8,128)(2,1)} %param.12) | data formatting | bytes 4194304 | tf_op args[0]
  16.9 9.7 %multiply_convert_fusion.3 = bf16[512,2048]{0,1:T(8,128)(2,1)S(1)} fusion(bf16[512,2048]{0,1:T(8,128)(2,1)} %copy.68, bf16[3,2048]{0,1:T(8,128)(2,1)S(1)} %copy.67, f32[2048]{0:T(1024)S(1)} %bitcast.189, f32[2048]{0:T(1024)S(1)} %bitcast.190, f32[2048]{0:T(1024)S(1)} %bitcast.188, f32[2048]{0:T(1024)S(1)} %bitcast.187, f32[2048]{0:T(1024)S(1)} %convert_element_type.257), kind=kLoop, calls=%fused_computation.25 | loop fusion | flops 27262976 | bytes 4247552 | tf_op jit(solution)/shard_map/convert_element_type | solution.py:29
  26.9 1.3 multiply_convert_fusion.7
  29.8 1.3 collective-permute-start.2
  31.1 1.9 %collective-permute-start.1 = (bf16[2064,128]{1,0:T(8,128)(2,1)}, bf16[2064,128]{1,0:T(8,128)(2,1)}, u32[]{:S(2)}, u32[]{:S(2)}) collective-permute-start(bf16[2064,128]{1,0:T(8,128)(2,1)} %pad_maximum_fusion.2), channel_id=1, source_target_pairs={{0,4},{4,8},{8,12},{12,16},{16,20},{20,24},{24,28},{1,5},{5,9},{9,... | collective-permute-start | bytes 1585160 | tf_op jit(solution)/shard_map/ppermute | solution.py:20
  33.9 3.9 %copy.83 = bf16[512,2048]{0,1:T(8,128)(2,1)} copy(bf16[512,2048]{1,0:T(8,128)(2,1)} %param.14) | data formatting | bytes 4194304 | tf_op args[2]
  37.9 1.8 %fusion.68 = f32[2,512,512]{2,1,0:T(8,128)} fusion(bf16[512,2,128]{0,2,1:T(8,128)(2,1)S(1)} %bitcast.164, bf16[512,2,128]{0,2,1:T(8,128)(2,1)S(1)} %bitcast.180), kind=kOutput, calls=%fused_computation.132 | convolution fusion | flops 134217728 | bytes 2621440 | tf_op jit(solution)/shard_map/ign,jgn->gij/dot_general | solution.py:40
  39.8 5.6 %collective-permute-done.2 = bf16[2064,128]{1,0:T(8,128)(2,1)S(1)} collective-permute-done((bf16[2064,128]{1,0:T(8,128)(2,1)}, bf16[2064,128]{1,0:T(8,128)(2,1)S(1)}, u32[]{:S(2)}, u32[]{:S(2)}) %collective-permute-start.2) | collective-permute-done | bytes 528416 | tf_op jit(solution)/shard_map/ppermute | solution.py:20
  45.5 11.0 %collective-permute-done.1 = bf16[2064,128]{1,0:T(8,128)(2,1)} collective-permute-done((bf16[2064,128]{1,0:T(8,128)(2,1)}, bf16[2064,128]{1,0:T(8,128)(2,1)}, u32[]{:S(2)}, u32[]{:S(2)}) %collective-permute-start.1) | collective-permute-done | bytes 528416 | tf_op jit(solution)/shard_map/ppermute | solution.py:20
  58.2 1.4 add_convert_fusion
  59.7 1.4 collective-permute-start.3
  62.3 12.3 %collective-permute-done.3 = bf16[2064,128]{1,0:T(8,128)(2,1)S(1)} collective-permute-done((bf16[2064,128]{1,0:T(8,128)(2,1)S(1)}, bf16[2064,128]{1,0:T(8,128)(2,1)S(1)}, u32[]{:S(2)}, u32[]{:S(2)}) %collective-permute-start.3) | collective-permute-done | bytes 528416 | tf_op jit(solution)/shard_map/ppermute | solution.py:20
  74.7 1.7 %fusion.63 = (bf16[2,16,64,128]{3,2,1,0:T(8,128)(2,1)}, f32[2,16,64,128]{3,2,1,0:T(8,128)S(1)}) fusion(f32[2,16,64,128]{3,2,1,0:T(8,128)S(1)} %bitcast.168, f32[2,16,64,128]{3,2,1,0:T(8,128)S(1)} %bitcast.169, f32[2,16]{1,0:T(2,128)} %copy-done.6, bf16[2,16,64,128]{3,2,1,0:T(8,128)(2,1)S(1)} %bitcast.170, f32[2,16]{1,0:T(2,128)S(1)} %copy-done.7), kind=kLoop, calls=%fused_computation.129 | loop fusion | flops 1572864 | bytes 4194560 | tf_op jit(solution)/shard_map/convert_element_type | solution.py:121
  76.4 1.3 collective-permute-start.4
  77.7 10.5 %fusion = f32[2,16,64,512]{3,2,1,0:T(8,128)} fusion(bf16[512,2,16,64]{0,3,2,1:T(8,128)(2,1)S(1)} %bitcast.163, f32[2,16,512]{2,1,0:T(8,128)S(1)} %bitcast.185, f32[2,512,512]{2,1,0:T(8,128)S(1)} %copy-done.2, f32[2,16,512]{2,1,0:T(8,128)S(1)} %copy-done.5, pred[512,512]{1,0:T(8,128)(4,1)S(1)} %copy-done.4), kind=kOutput, calls=%fused_computation.1 | convolution fusion | flops 1115684864 | bytes 8781824 | tf_op jit(solution)/shard_map/ghij,jghp->ighp/dot_general | solution.py:44
  90.2 12.4 %collective-permute-done.4 = bf16[2,16,64,128]{3,2,1,0:T(8,128)(2,1)} collective-permute-done((bf16[2,16,64,128]{3,2,1,0:T(8,128)(2,1)}, bf16[2,16,64,128]{3,2,1,0:T(8,128)(2,1)}, u32[]{:S(2)}, u32[]{:S(2)}) %collective-permute-start.4) | collective-permute-done | bytes 524320 | tf_op jit(solution)/shard_map/ppermute | solution.py:20
  102.6 1.8 %fusion.41 = f32[2,16,64,512]{3,2,1,0:T(8,128)S(1)} fusion(bf16[512,2,128,1]{0,2,3,1:T(8,128)(2,1)S(1)} %bitcast.165, f32[2,16,64,128]{3,2,1,0:T(8,128)S(1)} %get-tuple-element.10, bf16[2,16,64,128]{3,2,1,0:T(8,128)(2,1)} %collective-permute-done.4, f32[2,16]{1,0:T(2,128)S(1)} %fusion.58), kind=kOutput, calls=%fused_computation.64 | convolution fusion | flops 271056896 | bytes 6029440 | tf_op jit(solution)/shard_map/vmap(ign,ghpn->ighp)/dot_general | solution.py:61
  104.4 1.9 %fusion.37 = f32[2,16,64,512]{3,2,1,0:T(8,128)S(1)} fusion(bf16[512,2,128,1]{0,2,3,1:T(8,128)(2,1)S(1)} %bitcast.166, f32[2,16,64,128]{3,2,1,0:T(8,128)S(1)} %get-tuple-element.10, bf16[2,16,64,128]{3,2,1,0:T(8,128)(2,1)} %collective-permute-done.4, f32[2,16]{1,0:T(2,128)S(1)} %fusion.58), kind=kOutput, calls=%fused_computation.57 | convolution fusion | flops 270270464 | bytes 6029440 | tf_op jit(solution)/shard_map/vmap(ign,ghpn->ighp)/dot_general | solution.py:61
  106.7 2.3 %fusion.6 = f32[1,512,2,16,64]{1,4,3,2,0:T(8,128)S(1)} fusion(f32[2,16,64,512]{3,2,1,0:T(8,128)S(1)} %copy-done.1, f32[2,16,64,512]{3,2,1,0:T(8,128)S(1)} %fusion.41, f32[2,16,64,512]{3,2,1,0:T(8,128)S(1)} %fusion.37, bf16[512,2,128,1]{0,2,3,1:T(8,128)(2,1)S(1)} %bitcast.167, f32[512,2,16]{0,2,1:T(8,128)S(1)} %get-tuple-element.17, ...), kind=kOutput, calls=%fused_computation.10 | convolution fusion | flops 273678336 | bytes 18677888 | tf_op jit(solution)/shard_map/vmap(ign,ghpn->ighp)/dot_general | solution.py:61
  109.1 2.3 %bitcast_reduce_fusion = (f32[512,2]{0,1:T(2,128)S(1)}, f32[512,2048]{0,1:T(8,128)S(1)}) fusion(bf16[512,2048]{0,1:T(8,128)(2,1)S(1)} %copy-done, bf16[512,2048]{0,1:T(8,128)(2,1)S(1)} %multiply_convert_fusion.3, f32[2048]{0:T(1024)S(1)} %mul.292, f32[1,512,2,16,64]{1,4,3,2,0:T(8,128)S(1)} %fusion.6), kind=kLoop, calls=%fused_computation.14 | loop fusion | flops 11533312 | bytes 12595200 | tf_op jit(solution)/shard_map/reduce_sum | solution.py:187
  111.8 4.9 %fusion.30 = bf16[512,1024]{1,0:T(8,128)(2,1)S(1)} fusion(bf16[512,2048]{0,1:T(8,128)(2,1)S(1)} %fusion.8, bf16[2048,4096]{1,0:T(8,128)(2,1)} %param.23), kind=kOutput, calls=%fused_computation.38 | convolution fusion | flops 2148007936 | bytes 7340032 | tf_op jit(solution)/shard_map/dot_general | solution.py:219
  116.7 2.3 %fusion.27 = bf16[512,1024]{1,0:T(8,128)(2,1)S(1)} fusion(bf16[512,2048]{0,1:T(8,128)(2,1)S(1)} %fusion.8, bf16[2048,4096]{1,0:T(8,128)(2,1)S(1)} %bitcast.194), kind=kOutput, calls=%fused_computation.37 | convolution fusion | flops 2148007936 | bytes 7340032 | tf_op jit(solution)/shard_map/dot_general | solution.py:219
  119.1 2.3 %fusion.24 = bf16[512,1024]{1,0:T(8,128)(2,1)S(1)} fusion(bf16[512,2048]{0,1:T(8,128)(2,1)S(1)} %fusion.8, bf16[2048,4096]{1,0:T(8,128)(2,1)S(1)} %bitcast.194), kind=kOutput, calls=%fused_computation.36 | convolution fusion | flops 2148007936 | bytes 7340032 | tf_op jit(solution)/shard_map/dot_general | solution.py:219
  121.6 2.3 %fusion.21 = bf16[512,1024]{1,0:T(8,128)(2,1)S(1)} fusion(bf16[512,2048]{0,1:T(8,128)(2,1)S(1)} %fusion.8, bf16[2048,4096]{1,0:T(8,128)(2,1)S(1)} %bitcast.194), kind=kOutput, calls=%fused_computation.35 | convolution fusion | flops 2148007936 | bytes 7340032 | tf_op jit(solution)/shard_map/dot_general | solution.py:219
  125.5 1.6 %collective-permute-start.12 = (bf16[128,1024]{1,0:T(8,128)(2,1)S(1)}, bf16[128,1024]{1,0:T(8,128)(2,1)S(1)}, u32[]{:S(2)}, u32[]{:S(2)}) collective-permute-start(bf16[128,1024]{1,0:T(8,128)(2,1)S(1)} %fusion.49), channel_id=1, source_target_pairs={{0,2},{2,0},{1,3},{3,1},{4,6},{6,4},{5,7},{7,5},{8,10},{10,8},{9,1... | collective-permute-start | bytes 786440 | tf_op jit(solution)/shard_map/ppermute | solution.py:195
  128.1 1.6 %collective-permute-start.8 = (bf16[128,1024]{1,0:T(8,128)(2,1)S(1)}, bf16[128,1024]{1,0:T(8,128)(2,1)S(1)}, u32[]{:S(2)}, u32[]{:S(2)}) collective-permute-start(bf16[128,1024]{1,0:T(8,128)(2,1)S(1)} %fusion.47), channel_id=1, source_target_pairs={{0,2},{2,0},{1,3},{3,1},{4,6},{6,4},{5,7},{7,5},{8,10},{10,8},{9,1... | collective-permute-start | bytes 786440 | tf_op jit(solution)/shard_map/ppermute | solution.py:195
  130.5 4.2 %collective-permute-done.12 = bf16[128,1024]{1,0:T(8,128)(2,1)S(1)} collective-permute-done((bf16[128,1024]{1,0:T(8,128)(2,1)S(1)}, bf16[128,1024]{1,0:T(8,128)(2,1)S(1)}, u32[]{:S(2)}, u32[]{:S(2)}) %collective-permute-start.12) | collective-permute-done | bytes 262176 | tf_op jit(solution)/shard_map/ppermute | solution.py:195
  134.8 5.5 %collective-permute-done.10 = bf16[128,1024]{1,0:T(8,128)(2,1)S(1)} collective-permute-done((bf16[128,1024]{1,0:T(8,128)(2,1)S(1)}, bf16[128,1024]{1,0:T(8,128)(2,1)S(1)}, u32[]{:S(2)}, u32[]{:S(2)}) %collective-permute-start.10) | collective-permute-done | bytes 262176 | tf_op jit(solution)/shard_map/ppermute | solution.py:195
  140.4 5.5 %collective-permute-done.8 = bf16[128,1024]{1,0:T(8,128)(2,1)S(1)} collective-permute-done((bf16[128,1024]{1,0:T(8,128)(2,1)S(1)}, bf16[128,1024]{1,0:T(8,128)(2,1)S(1)}, u32[]{:S(2)}, u32[]{:S(2)}) %collective-permute-start.8) | collective-permute-done | bytes 262176 | tf_op jit(solution)/shard_map/ppermute | solution.py:195
  146.0 4.6 %collective-permute-done.6 = bf16[128,1024]{1,0:T(8,128)(2,1)S(1)} collective-permute-done((bf16[128,1024]{1,0:T(8,128)(2,1)S(1)}, bf16[128,1024]{1,0:T(8,128)(2,1)S(1)}, u32[]{:S(2)}, u32[]{:S(2)}) %collective-permute-start.6) | collective-permute-done | bytes 262176 | tf_op jit(solution)/shard_map/ppermute | solution.py:195
  (114 shorter events, 20.6 us)
Async XLA Ops:
  0.0 15.8 %copy-start.3 = (bf16[512,2,256]{2,1,0:T(2,128)(2,1)S(1)}, bf16[512,2,256]{2,1,0:T(2,128)(2,1)}, u32[]{:S(2)}) copy-start(bf16[512,2,256]{2,1,0:T(2,128)(2,1)} %param.13) | copy-start | bytes 1572868
  0.0 16.6 %copy-start.8 = (bf16[2048]{0:T(1024)(128)(2,1)S(1)}, bf16[2048]{0:T(1024)(128)(2,1)}, u32[]{:S(2)}) copy-start(bf16[2048]{0:T(1024)(128)(2,1)} %param.18) | copy-start | bytes 12292
  0.0 16.6 %copy-start.10 = (bf16[2,256]{1,0:T(2,128)(2,1)S(1)}, bf16[2,256]{1,0:T(2,128)(2,1)}, u32[]{:S(2)}) copy-start(bf16[2,256]{1,0:T(2,128)(2,1)} %param.19) | copy-start | bytes 3076
  1.6 15.0 %collective-permute-start = (bf16[3,2560]{1,0:T(4,128)(2,1)S(1)}, bf16[3,2560]{1,0:T(4,128)(2,1)S(1)}, u32[]{:S(2)}, u32[]{:S(2)}) collective-permute-start(bf16[3,2560]{1,0:T(4,128)(2,1)S(1)} %pad_maximum_fusion.5), channel_id=1, source_target_pairs={{0,4},{4,8},{8,12},{12,16},{16,20},{20,24},{24,28},{1,5},{5,9},{9,... | collective-permute-start | bytes 46088 | tf_op jit(solution)/shard_map/ppermute | solution.py:20
  28.3 9.5 %copy-start.11 = (f32[32]{0:T(128)S(1)}, f32[32]{0:T(128)}, u32[]{:S(2)}) copy-start(f32[32]{0:T(128)} %param.21) | copy-start | bytes 388
  28.3 9.7 %copy-start.9 = (bf16[2048]{0:T(1024)(128)(2,1)S(1)}, bf16[2048]{0:T(1024)(128)(2,1)}, u32[]{:S(2)}) copy-start(bf16[2048]{0:T(1024)(128)(2,1)} %param.22) | copy-start | bytes 12292
  29.8 15.6 %collective-permute-start.2 = (bf16[2064,128]{1,0:T(8,128)(2,1)}, bf16[2064,128]{1,0:T(8,128)(2,1)S(1)}, u32[]{:S(2)}, u32[]{:S(2)}) collective-permute-start(bf16[2064,128]{1,0:T(8,128)(2,1)} %pad_maximum_fusion.2), channel_id=1, source_target_pairs={{0,8},{4,12},{8,16},{12,20},{16,24},{20,28},{1,9},{5,13},{9,17},{1... | collective-permute-start | bytes 1585160 | tf_op jit(solution)/shard_map/ppermute | solution.py:20
  31.1 25.4 %collective-permute-start.1 = (bf16[2064,128]{1,0:T(8,128)(2,1)}, bf16[2064,128]{1,0:T(8,128)(2,1)}, u32[]{:S(2)}, u32[]{:S(2)}) collective-permute-start(bf16[2064,128]{1,0:T(8,128)(2,1)} %pad_maximum_fusion.2), channel_id=1, source_target_pairs={{0,4},{4,8},{8,12},{12,16},{16,20},{20,24},{24,28},{1,5},{5,9},{9,... | collective-permute-start | bytes 1585160 | tf_op jit(solution)/shard_map/ppermute | solution.py:20
  57.8 16.8 %copy-start.6 = (f32[2,16]{1,0:T(2,128)}, f32[2,16]{1,0:T(2,128)S(1)}, u32[]{:S(2)}) copy-start(f32[2,16]{1,0:T(2,128)S(1)} %get-tuple-element.14) | copy-start | bytes 388
  58.2 16.5 %copy-start.7 = (f32[2,16]{1,0:T(2,128)S(1)}, f32[2,16]{1,0:T(2,128)}, u32[]{:S(2)}) copy-start(f32[2,16]{1,0:T(2,128)} %get-tuple-element.13) | copy-start | bytes 388
  59.7 18.0 %copy-start.2 = (f32[2,512,512]{2,1,0:T(8,128)S(1)}, f32[2,512,512]{2,1,0:T(8,128)}, u32[]{:S(2)}) copy-start(f32[2,512,512]{2,1,0:T(8,128)} %fusion.68) | copy-start | bytes 6291460
  59.7 18.0 %copy-start.4 = (pred[512,512]{1,0:T(8,128)(4,1)S(1)}, pred[512,512]{1,0:T(8,128)(4,1)}, u32[]{:S(2)}) copy-start(pred[512,512]{1,0:T(8,128)(4,1)} %iota_compare_fusion) | copy-start | bytes 786436
  59.7 18.0 %copy-start.5 = (f32[2,16,512]{2,1,0:T(8,128)S(1)}, f32[2,16,512]{2,1,0:T(8,128)}, u32[]{:S(2)}) copy-start(f32[2,16,512]{2,1,0:T(8,128)} %get-tuple-element.20) | copy-start | bytes 196612
  59.7 14.9 %collective-permute-start.3 = (bf16[2064,128]{1,0:T(8,128)(2,1)S(1)}, bf16[2064,128]{1,0:T(8,128)(2,1)S(1)}, u32[]{:S(2)}, u32[]{:S(2)}) collective-permute-start(bf16[2064,128]{1,0:T(8,128)(2,1)S(1)} %pad_maximum_fusion.3), channel_id=1, source_target_pairs={{0,8},{4,12},{8,16},{12,20},{16,24},{20,28},{1,9},{5,13},{9,17},{1... | collective-permute-start | bytes 1585160 | tf_op jit(solution)/shard_map/ppermute | solution.py:20
  76.4 26.2 %collective-permute-start.4 = (bf16[2,16,64,128]{3,2,1,0:T(8,128)(2,1)}, bf16[2,16,64,128]{3,2,1,0:T(8,128)(2,1)}, u32[]{:S(2)}, u32[]{:S(2)}) collective-permute-start(bf16[2,16,64,128]{3,2,1,0:T(8,128)(2,1)} %get-tuple-element.9), channel_id=1, source_target_pairs={{0,16},{4,20},{8,24},{12,28},{1,17},{5,21},{9,25},{13,29},{2,18},{... | collective-permute-start | bytes 1572872 | tf_op jit(solution)/shard_map/ppermute | solution.py:20
  104.4 2.3 %copy-start.1 = (f32[2,16,64,512]{3,2,1,0:T(8,128)S(1)}, f32[2,16,64,512]{3,2,1,0:T(8,128)}, u32[]{:S(2)}) copy-start(f32[2,16,64,512]{3,2,1,0:T(8,128)} %fusion) | copy-start | bytes 12582916
  106.7 2.3 %copy-start = (bf16[512,2048]{0,1:T(8,128)(2,1)S(1)}, bf16[512,2048]{0,1:T(8,128)(2,1)}, u32[]{:S(2)}) copy-start(bf16[512,2048]{0,1:T(8,128)(2,1)} %copy.83) | copy-start | bytes 6291460
  109.0 7.6 %slice-start = ((s8[16777216]{0:T(1024)(128)(4,1)}), s8[4194304]{0:T(1024)(128)(4,1)S(1)}, s32[]{:S(2)}) async-start(s8[16777216]{0:T(1024)(128)(4,1)} %bitcast.193), calls=%async_computation | async-start | bytes 8388608
  109.1 7.6 %slice-start.1 = ((s8[16777216]{0:T(1024)(128)(4,1)}), s8[4194304]{0:T(1024)(128)(4,1)S(1)}, s32[]{:S(2)}) async-start(s8[16777216]{0:T(1024)(128)(4,1)} %bitcast.193), calls=%async_computation.1 | async-start | bytes 8388608
  111.3 5.4 %slice-start.2 = ((s8[16777216]{0:T(1024)(128)(4,1)}), s8[4194304]{0:T(1024)(128)(4,1)S(1)}, s32[]{:S(2)}) async-start(s8[16777216]{0:T(1024)(128)(4,1)} %bitcast.193), calls=%async_computation.2 | async-start | bytes 8388608
  111.8 4.9 %slice-start.3 = ((s8[16777216]{0:T(1024)(128)(4,1)}), s8[4194304]{0:T(1024)(128)(4,1)S(1)}, s32[]{:S(2)}) async-start(s8[16777216]{0:T(1024)(128)(4,1)} %bitcast.193), calls=%async_computation.3 | async-start | bytes 8388608
  121.5 3.8 %collective-permute-start.11 = (bf16[2,128,1024]{2,1,0:T(8,128)(2,1)S(1)}, bf16[2,128,1024]{2,1,0:T(8,128)(2,1)S(1)}, u32[]{:S(2)}, u32[]{:S(2)}) collective-permute-start(bf16[2,128,1024]{2,1,0:T(8,128)(2,1)S(1)} %dynamic-slice_bitcast_fusion), channel_id=1, source_target_pairs={{0,1},{1,0},{2,3},{3,2},{4,5},{5,4},{6,7},{7,6},{8,9},{9,8},{10,11... | collective-permute-start | bytes 1572872 | tf_op jit(solution)/shard_map/ppermute | solution.py:195
  124.0 3.1 %collective-permute-start.9 = (bf16[2,128,1024]{2,1,0:T(8,128)(2,1)S(1)}, bf16[2,128,1024]{2,1,0:T(8,128)(2,1)S(1)}, u32[]{:S(2)}, u32[]{:S(2)}) collective-permute-start(bf16[2,128,1024]{2,1,0:T(8,128)(2,1)S(1)} %dynamic-slice_bitcast_fusion.1), channel_id=1, source_target_pairs={{0,1},{1,0},{2,3},{3,2},{4,5},{5,4},{6,7},{7,6},{8,9},{9,8},{10,11... | collective-permute-start | bytes 1572872 | tf_op jit(solution)/shard_map/ppermute | solution.py:195
  124.6 3.3 %collective-permute-start.7 = (bf16[2,128,1024]{2,1,0:T(8,128)(2,1)S(1)}, bf16[2,128,1024]{2,1,0:T(8,128)(2,1)S(1)}, u32[]{:S(2)}, u32[]{:S(2)}) collective-permute-start(bf16[2,128,1024]{2,1,0:T(8,128)(2,1)S(1)} %dynamic-slice_bitcast_fusion.2), channel_id=1, source_target_pairs={{0,1},{1,0},{2,3},{3,2},{4,5},{5,4},{6,7},{7,6},{8,9},{9,8},{10,11... | collective-permute-start | bytes 1572872 | tf_op jit(solution)/shard_map/ppermute | solution.py:195
  124.7 5.0 %collective-permute-start.5 = (bf16[2,128,1024]{2,1,0:T(8,128)(2,1)S(1)}, bf16[2,128,1024]{2,1,0:T(8,128)(2,1)S(1)}, u32[]{:S(2)}, u32[]{:S(2)}) collective-permute-start(bf16[2,128,1024]{2,1,0:T(8,128)(2,1)S(1)} %dynamic-slice_bitcast_fusion.3), channel_id=1, source_target_pairs={{0,1},{1,0},{2,3},{3,2},{4,5},{5,4},{6,7},{7,6},{8,9},{9,8},{10,11... | collective-permute-start | bytes 1572872 | tf_op jit(solution)/shard_map/ppermute | solution.py:195
  125.5 9.2 %collective-permute-start.12 = (bf16[128,1024]{1,0:T(8,128)(2,1)S(1)}, bf16[128,1024]{1,0:T(8,128)(2,1)S(1)}, u32[]{:S(2)}, u32[]{:S(2)}) collective-permute-start(bf16[128,1024]{1,0:T(8,128)(2,1)S(1)} %fusion.49), channel_id=1, source_target_pairs={{0,2},{2,0},{1,3},{3,1},{4,6},{6,4},{5,7},{7,5},{8,10},{10,8},{9,1... | collective-permute-start | bytes 786440 | tf_op jit(solution)/shard_map/ppermute | solution.py:195
  127.3 13.0 %collective-permute-start.10 = (bf16[128,1024]{1,0:T(8,128)(2,1)S(1)}, bf16[128,1024]{1,0:T(8,128)(2,1)S(1)}, u32[]{:S(2)}, u32[]{:S(2)}) collective-permute-start(bf16[128,1024]{1,0:T(8,128)(2,1)S(1)} %fusion.48), channel_id=1, source_target_pairs={{0,2},{2,0},{1,3},{3,1},{4,6},{6,4},{5,7},{7,5},{8,10},{10,8},{9,1... | collective-permute-start | bytes 786440 | tf_op jit(solution)/shard_map/ppermute | solution.py:195
  128.1 17.8 %collective-permute-start.8 = (bf16[128,1024]{1,0:T(8,128)(2,1)S(1)}, bf16[128,1024]{1,0:T(8,128)(2,1)S(1)}, u32[]{:S(2)}, u32[]{:S(2)}) collective-permute-start(bf16[128,1024]{1,0:T(8,128)(2,1)S(1)} %fusion.47), channel_id=1, source_target_pairs={{0,2},{2,0},{1,3},{3,1},{4,6},{6,4},{5,7},{7,5},{8,10},{10,8},{9,1... | collective-permute-start | bytes 786440 | tf_op jit(solution)/shard_map/ppermute | solution.py:195
  129.9 20.7 %collective-permute-start.6 = (bf16[128,1024]{1,0:T(8,128)(2,1)S(1)}, bf16[128,1024]{1,0:T(8,128)(2,1)S(1)}, u32[]{:S(2)}, u32[]{:S(2)}) collective-permute-start(bf16[128,1024]{1,0:T(8,128)(2,1)S(1)} %fusion.46), channel_id=1, source_target_pairs={{0,2},{2,0},{1,3},{3,1},{4,6},{6,4},{5,7},{7,5},{8,10},{10,8},{9,1... | collective-permute-start | bytes 786440 | tf_op jit(solution)/shard_map/ppermute | solution.py:195

commit v7 on v4

--- a/solution.py
+++ b/solution.py
@@ -1,6 +1,8 @@
 import jax
 import jax.numpy as jnp
 from jax import lax
+from jax.experimental import pallas as pl
+from jax.experimental.pallas import tpu as pltpu
 from jax.sharding import Mesh, PartitionSpec as P
 
 SSM_HEAD_COUNT = 128
@@ -28,6 +30,33 @@
         )
     return lax.optimization_barrier(jax.nn.silu(summed).astype(jnp.bfloat16))
 
+
+def conv_kernel(halo_ref, x_ref, w_ref, b_ref, o_ref, pad_ref):
+    rows = x_ref.shape[0]
+    pad_ref[0:8, :] = halo_ref[...].astype(jnp.float32)
+    pad_ref[8 : 8 + rows, :] = x_ref[...].astype(jnp.float32)
+    summed = b_ref[...].astype(jnp.float32)
+    for k in range(CONV):
+        summed = summed + w_ref[k : k + 1, :].astype(jnp.float32) * pad_ref[8 - (CONV - 1) + k : 8 - (CONV - 1) + k + rows, :]
+    o_ref[...] = jax.nn.silu(summed).astype(o_ref.dtype)
+
+def conv_silu_kernel(halo, x, weight, bias):
+    rows, width = x.shape
+    block = 512 if width % 512 == 0 else width
+    halo8 = jnp.concatenate([jnp.zeros((8 - halo.shape[0], width), halo.dtype), halo], axis=0)
+    return pl.pallas_call(
+        conv_kernel,
+        grid=(width // block,),
+        in_specs=[
+            pl.BlockSpec((8, block), lambda j: (0, j)),
+            pl.BlockSpec((rows, block), lambda j: (0, j)),
+            pl.BlockSpec((CONV, block), lambda j: (0, j)),
+            pl.BlockSpec((1, block), lambda j: (0, j)),
+        ],
+        out_specs=pl.BlockSpec((rows, block), lambda j: (0, j)),
+        out_shape=jax.ShapeDtypeStruct((rows, width), jnp.bfloat16),
+        scratch_shapes=[pltpu.VMEM((rows + 8, block), jnp.float32)],
+    )(halo8, x, weight, bias.reshape(1, width))
 
 def block_parts(inner_block, b_block, c_block, step_sizes, log_rates):
     length = inner_block.shape[0]
@@ -137,9 +166,7 @@
         [inner_input[tokens - margin :], state_input[tokens - margin :].reshape(margin, -1)], axis=1
     )
     halo = shifted(halo, "ctx", 1)
-    inner_conv = conv_silu(
-        jnp.concatenate([halo[:, :inner_width], inner_input], axis=0), conv_inner, bias_inner, tokens
-    )
+    inner_conv = conv_silu_kernel(halo[:, :inner_width], inner_input, conv_inner, bias_inner)
     state_conv = conv_silu(
         jnp.concatenate([halo[:, inner_width:].reshape((margin,) + state_input.shape[1:]), state_input], axis=0),
         conv_states,

time: 149 us -> 173 us (1.16)
  local copies, waits for them, and re-layouts: 13.6 us -> 26.8 us
  Pallas kernels: 0 us -> 6.98 us
  waiting for transfers between devices: 63.4 us -> 68 us
  other arithmetic: 29 us -> 25.5 us
  matrix products: 29.5 us -> 31.5 us
    convert_element_type x2 -> x1, other arithmetic: 11.3 us -> 1.34 us  [conv_silu(): return lax.optimization_barrier(jax.nn.silu(summed).astype(jnp.bfloat16))]
    mul x0 -> x2, local copies, waits for them, and re-layouts: none -> 7.72 us  [the longest x1 6.58 us: body(): grouped * grouped]
    reshape x1 -> x4, local copies, waits for them, and re-layouts: 0.01 us -> 6.99 us  [the longest x1 5.52 us: body(): (partial_heads + correction).reshape(tokens, width_here)]
    pallas_call x0 -> x1, Pallas kernels: none -> 6.98 us  [conv_silu_kernel(): pl.pallas_call(conv_kernel, grid=(width // block,), in_specs=[pl.BlockSpe...]
    mul x0 -> x1, other arithmetic: none -> 6.35 us  [body(): grouped * grouped]
    ppermute x5, waiting for transfers between devices: 43.4 us -> 48.1 us  [shifted(): return lax.ppermute(value, axis, pairs)]
    unnamed x43 -> x38, local copies, waits for them, and re-layouts: 9.42 us -> 4.9 us
    pallas_call x0 -> x1, local copies, waits for them, and re-layouts: none -> 2.88 us  [conv_silu_kernel(): pl.pallas_call(conv_kernel, grid=(width // block,), in_specs=[pl.BlockSpe...]
  transfers between devices with their start and end apart: 13 -> 13, of which waited for: 8 -> 8; matrix products, arithmetic and copies ran while one was open for 24% -> 16% of each run, Pallas kernels for 0% -> 0%
where the time goes in v7:
time: 173 us; the launch traced here: 172 us
  waiting for transfers between devices  68 us (39%)
  matrix products  31.5 us (18%)
  local copies, waits for them, and re-layouts  26.8 us (15%)
  other arithmetic  25.5 us (15%)
  starting transfers between devices  12.4 us (7%)
  Pallas kernels  6.98 us (4%)
    ppermute x5, waiting for transfers between devices, shifted(): return lax.ppermute(value, axis, pairs)  48.1 us
    ppermute x8, waiting for transfers between devices, swap(): return lax.ppermute(value, axis, [(0, 1), (1, 0)])  20 us
    dot_general x4, matrix products, reduce_rows(): jnp.dot(normed, out_weight[:, c * step:(c + 1) * step], preferred_element...  12.2 us
    dot_general x1, matrix products, block_parts(): jnp.einsum('ghij,jghp->ighp', mixing, inner_block, preferred_element_type...  10.7 us
    pallas_call x1, Pallas kernels, conv_silu_kernel(): pl.pallas_call(conv_kernel, grid=(width // block,), in_specs=[pl.BlockSpe...  6.98 us
    ppermute x5, starting transfers between devices, shifted(): return lax.ppermute(value, axis, pairs)  6.88 us
    mul x1, local copies, waits for them, and re-layouts, body(): grouped * grouped  6.58 us
    mul x1, other arithmetic, body(): grouped * grouped  6.35 us
  transfers between devices with their start and end apart: 13, of which 8 were waited for; matrix products, arithmetic and copies ran while one was open for 16% of the time, Pallas kernels for 0%

profile of v7, /device:TPU:30, one launch (start us, length us, event | category | flops | bytes accessed | tf_op | source)
XLA Modules:
  0.0 171.9 jit_solution(6300254944083892147)
XLA Ops:
  1.5 1.3 collective-permute-start
  4.4 2.3 %reduce-window.6 = f32[16,2,4,128]{3,0,1,2:T(8,128)S(1)} reduce-window(f32[16,2,4,128]{3,0,1,2:T(8,128)S(1)} %bitcast.172, f32[]{:T(128)} %constant.62.clone.1), window={size=1x1x1x128 pad=0_0x0_0x0_0x127_0}, to_apply=%region_0.1 | reduce-window | flops 2080768 | bytes 131076 | tf_op jit(solution)/shard_map/reduce-window
  8.8 1.3 copy.83
  12.3 1.3 multiply_convert_fusion.7
  14.3 7.0 %shard_map.118 = bf16[512,2048]{1,0:T(8,128)(2,1)} custom-call(bf16[8,2048]{1,0:T(8,128)(2,1)} %concatenate.25.halo_ref, bf16[512,2048]{1,0:T(8,128)(2,1)} %x_ref.1, bf16[4,2048]{1,0:T(4,128)(2,1)} %w_ref.1, bf16[1,2048]{1,0:T(2,128)(2,1)} %reshape.159.b_ref), custom_call_target="tpu_custom_call" | custom-call | tf_op jit(solution)/shard_map/pallas_call | solution.py:47
  21.3 2.9 %copy.77 = bf16[512,2048]{0,1:T(8,128)(2,1)S(1)} copy(bf16[512,2048]{1,0:T(8,128)(2,1)} %shard_map.118) | data formatting | bytes 4194304 | tf_op jit(solution)/shard_map/pallas_call | solution.py:47
  27.0 1.3 collective-permute-start.2
  29.9 1.8 %fusion.63 = f32[2,512,512]{2,1,0:T(8,128)} fusion(bf16[512,2,128]{0,2,1:T(8,128)(2,1)S(1)} %bitcast.153, bf16[512,2,128]{0,2,1:T(8,128)(2,1)S(1)} %bitcast.166), kind=kOutput, calls=%fused_computation.114 | convolution fusion | flops 134217728 | bytes 2621440 | tf_op jit(solution)/shard_map/ign,jgn->gij/dot_general | solution.py:69
  31.7 10.6 %collective-permute-done.1 = bf16[2064,128]{1,0:T(8,128)(2,1)S(1)} collective-permute-done((bf16[2064,128]{1,0:T(8,128)(2,1)}, bf16[2064,128]{1,0:T(8,128)(2,1)S(1)}, u32[]{:S(2)}, u32[]{:S(2)}) %collective-permute-start.1) | collective-permute-done | bytes 528416 | tf_op jit(solution)/shard_map/ppermute | solution.py:22
  42.3 12.4 %collective-permute-done.2 = bf16[2064,128]{1,0:T(8,128)(2,1)S(1)} collective-permute-done((bf16[2064,128]{1,0:T(8,128)(2,1)}, bf16[2064,128]{1,0:T(8,128)(2,1)S(1)}, u32[]{:S(2)}, u32[]{:S(2)}) %collective-permute-start.2) | collective-permute-done | bytes 528416 | tf_op jit(solution)/shard_map/ppermute | solution.py:22
  56.1 1.6 collective-permute-start.3
  57.8 13.0 %collective-permute-done.3 = bf16[2064,128]{1,0:T(8,128)(2,1)S(1)} collective-permute-done((bf16[2064,128]{1,0:T(8,128)(2,1)S(1)}, bf16[2064,128]{1,0:T(8,128)(2,1)S(1)}, u32[]{:S(2)}, u32[]{:S(2)}) %collective-permute-start.3) | collective-permute-done | bytes 528416 | tf_op jit(solution)/shard_map/ppermute | solution.py:22
  72.0 1.5 collective-permute-start.4
  73.5 10.7 %fusion = f32[2,16,64,512]{3,2,1,0:T(8,128)} fusion(bf16[512,2,16,64]{0,3,2,1:T(8,128)(2,1)S(1)} %bitcast.156, f32[2,16,512]{2,1,0:T(8,128)S(1)} %bitcast.171, f32[2,512,512]{2,1,0:T(8,128)S(1)} %copy-done.3, f32[2,16,512]{2,1,0:T(8,128)S(1)} %copy-done.7, pred[512,512]{1,0:T(8,128)(4,1)S(1)} %copy-done.6), kind=kOutput, calls=%fused_computation.1 | convolution fusion | flops 1115684864 | bytes 8781824 | tf_op jit(solution)/shard_map/ghij,jghp->ighp/dot_general | solution.py:73
  85.6 12.1 %collective-permute-done.4 = bf16[2,16,64,128]{3,2,1,0:T(8,128)(2,1)S(1)} collective-permute-done((bf16[2,16,64,128]{3,2,1,0:T(8,128)(2,1)}, bf16[2,16,64,128]{3,2,1,0:T(8,128)(2,1)S(1)}, u32[]{:S(2)}, u32[]{:S(2)}) %collective-permute-start.4) | collective-permute-done | bytes 524320 | tf_op jit(solution)/shard_map/ppermute | solution.py:22
  97.6 6.2 %fusion.6 = f32[1,512,2,16,64]{1,4,3,2,0:T(8,128)} fusion(f32[2,16,64,512]{3,2,1,0:T(8,128)} %fusion, bf16[512,2,128,1]{0,2,3,1:T(8,128)(2,1)S(1)} %bitcast.154, f32[512,2,16]{0,2,1:T(8,128)S(1)} %get-tuple-element.14, bf16[2,16,64,128]{3,2,1,0:T(8,128)(2,1)S(1)} %collective-permute-done.4, f32[2,16]{1,0:T(2,128)S(1)} %fusion.55, ...), kind=kOutput, calls=%fused_computation.10 | convolution fusion | flops 1614807040 | bytes 11862400 | tf_op jit(solution)/shard_map/vmap(ign,ghpn->ighp)/dot_general | solution.py:85
  103.9 5.5 %copy.89 = f32[512,2048]{1,0:T(8,128)} copy(f32[512,2048]{0,1:T(8,128)} %bitcast.144) | data formatting | bytes 8388608 | tf_op jit(solution)/shard_map/reshape | solution.py:203
  109.4 6.3 %fusion.59 = f32[512,2048]{1,0:T(8,128)} fusion(bf16[512,2048]{1,0:T(8,128)(2,1)} %param.14, f32[512,2048]{1,0:T(8,128)} %copy.89, bf16[512,2048]{1,0:T(8,128)(2,1)S(1)} %copy-done.1, f32[2048]{0:T(1024)S(1)} %mul.220), kind=kLoop, calls=%fused_computation.111 | loop fusion | flops 10485760 | bytes 12591104 | tf_op jit(solution)/shard_map/mul | solution.py:208
  115.7 6.6 %mul.226 = f32[512,2,1024]{2,1,0:T(2,128)} reshape(f32[512,2048]{1,0:T(8,128)} %fusion.59) | data formatting | bytes 8388608 | tf_op jit(solution)/shard_map/mul | solution.py:208
  122.3 3.4 %reduce_sum.9 = f32[512,2]{1,0:T(8,128)S(1)} reduce(f32[512,2,1024]{2,1,0:T(2,128)} %mul.226, f32[]{:T(128)} %constant.62.clone.1), dimensions={2}, to_apply=%region_2.3 | reduce | flops 1047552 | bytes 4198404 | tf_op jit(solution)/shard_map/reduce_sum | solution.py:208
  126.9 2.0 %copy.112 = f32[64,8,2,1024]{3,1,2,0:T(8,128)S(1)} copy(f32[64,8,2,1024]{3,2,1,0:T(2,128)S(1)} %bitcast.145) | data formatting | bytes 8388608
  129.7 1.9 %multiply_convert_fusion.2 = bf16[512,2048]{1,0:T(8,128)(2,1)S(1)} fusion(f32[512,2048]{1,0:T(8,128)S(1)} %bitcast.146, f32[2048]{0:T(1024)S(1)} %copy-done.8, bf16[512,2048]{1,0:T(8,128)(2,1)S(1)} %copy-done.2, f32[512,2048]{1,0:T(8,128)S(1)} %copy-done, bf16[512,2048]{1,0:T(8,128)(2,1)S(1)} %copy-done.1, f32[2048]{0:T(1024)S(1)} %mul.220), kind=kLoop, calls=%fused_computation.19 | loop fusion | flops 12582912 | bytes 14696448 | tf_op jit(solution)/shard_map/convert_element_type | solution.py:209
  131.7 5.2 %fusion.17 = bf16[512,1024]{1,0:T(8,128)(2,1)S(1)} fusion(bf16[512,2048]{1,0:T(8,128)(2,1)S(1)} %multiply_convert_fusion.2, bf16[2048,4096]{1,0:T(8,128)(2,1)} %param.23), kind=kOutput, calls=%fused_computation.23 | convolution fusion | flops 2148007936 | bytes 7340032 | tf_op jit(solution)/shard_map/dot_general | solution.py:240
  136.9 2.3 %fusion.20 = bf16[512,1024]{1,0:T(8,128)(2,1)S(1)} fusion(bf16[512,2048]{1,0:T(8,128)(2,1)S(1)} %multiply_convert_fusion.2, bf16[2048,4096]{1,0:T(8,128)(2,1)S(1)} %bitcast.176), kind=kOutput, calls=%fused_computation.24 | convolution fusion | flops 2148007936 | bytes 7340032 | tf_op jit(solution)/shard_map/dot_general | solution.py:240
  139.3 2.3 %fusion.23 = bf16[512,1024]{1,0:T(8,128)(2,1)S(1)} fusion(bf16[512,2048]{1,0:T(8,128)(2,1)S(1)} %multiply_convert_fusion.2, bf16[2048,4096]{1,0:T(8,128)(2,1)S(1)} %bitcast.176), kind=kOutput, calls=%fused_computation.25 | convolution fusion | flops 2148007936 | bytes 7340032 | tf_op jit(solution)/shard_map/dot_general | solution.py:240
  141.7 2.3 %fusion.26 = bf16[512,1024]{1,0:T(8,128)(2,1)S(1)} fusion(bf16[512,2048]{1,0:T(8,128)(2,1)S(1)} %multiply_convert_fusion.2, bf16[2048,4096]{1,0:T(8,128)(2,1)S(1)} %bitcast.176), kind=kOutput, calls=%fused_computation.26 | convolution fusion | flops 2148007936 | bytes 7340032 | tf_op jit(solution)/shard_map/dot_general | solution.py:240
  146.4 1.6 collective-permute-start.8
  149.1 1.6 collective-permute-start.12
  150.6 4.2 %collective-permute-done.6 = bf16[128,1024]{1,0:T(8,128)(2,1)S(1)} collective-permute-done((bf16[128,1024]{1,0:T(8,128)(2,1)S(1)}, bf16[128,1024]{1,0:T(8,128)(2,1)S(1)}, u32[]{:S(2)}, u32[]{:S(2)}) %collective-permute-start.6) | collective-permute-done | bytes 262176 | tf_op jit(solution)/shard_map/ppermute | solution.py:216
  154.9 5.5 %collective-permute-done.8 = bf16[128,1024]{1,0:T(8,128)(2,1)S(1)} collective-permute-done((bf16[128,1024]{1,0:T(8,128)(2,1)S(1)}, bf16[128,1024]{1,0:T(8,128)(2,1)S(1)}, u32[]{:S(2)}, u32[]{:S(2)}) %collective-permute-start.8) | collective-permute-done | bytes 262176 | tf_op jit(solution)/shard_map/ppermute | solution.py:216
  160.5 5.5 %collective-permute-done.10 = bf16[128,1024]{1,0:T(8,128)(2,1)S(1)} collective-permute-done((bf16[128,1024]{1,0:T(8,128)(2,1)S(1)}, bf16[128,1024]{1,0:T(8,128)(2,1)S(1)}, u32[]{:S(2)}, u32[]{:S(2)}) %collective-permute-start.10) | collective-permute-done | bytes 262176 | tf_op jit(solution)/shard_map/ppermute | solution.py:216
  166.2 4.6 %collective-permute-done.12 = bf16[128,1024]{1,0:T(8,128)(2,1)S(1)} collective-permute-done((bf16[128,1024]{1,0:T(8,128)(2,1)S(1)}, bf16[128,1024]{1,0:T(8,128)(2,1)S(1)}, u32[]{:S(2)}, u32[]{:S(2)}) %collective-permute-start.12) | collective-permute-done | bytes 262176 | tf_op jit(solution)/shard_map/ppermute | solution.py:216
  (117 shorter events, 23.2 us)
Async XLA Ops:
  1.5 10.6 %collective-permute-start = (bf16[3,2560]{1,0:T(4,128)(2,1)S(1)}, bf16[3,2560]{1,0:T(4,128)(2,1)S(1)}, u32[]{:S(2)}, u32[]{:S(2)}) collective-permute-start(bf16[3,2560]{1,0:T(4,128)(2,1)S(1)} %pad_maximum_fusion.4), channel_id=1, source_target_pairs={{0,4},{4,8},{8,12},{12,16},{16,20},{20,24},{24,28},{1,5},{5,9},{9,... | collective-permute-start | bytes 46088 | tf_op jit(solution)/shard_map/ppermute | solution.py:22
  21.3 7.8 %copy-start.12 = (f32[32]{0:T(128)S(1)}, f32[32]{0:T(128)}, u32[]{:S(2)}) copy-start(f32[32]{0:T(128)} %param.21) | copy-start | bytes 388
  21.3 8.0 %copy-start.11 = (bf16[2048]{0:T(1024)(128)(2,1)S(1)}, bf16[2048]{0:T(1024)(128)(2,1)}, u32[]{:S(2)}) copy-start(bf16[2048]{0:T(1024)(128)(2,1)} %param.22) | copy-start | bytes 12292
  24.2 1.6 copy-start.4
  25.8 16.5 %collective-permute-start.1 = (bf16[2064,128]{1,0:T(8,128)(2,1)}, bf16[2064,128]{1,0:T(8,128)(2,1)S(1)}, u32[]{:S(2)}, u32[]{:S(2)}) collective-permute-start(bf16[2064,128]{1,0:T(8,128)(2,1)} %pad_maximum_fusion.1), channel_id=1, source_target_pairs={{0,4},{4,8},{8,12},{12,16},{16,20},{20,24},{24,28},{1,5},{5,9},{9,... | collective-permute-start | bytes 1585160 | tf_op jit(solution)/shard_map/ppermute | solution.py:22
  27.0 27.7 %collective-permute-start.2 = (bf16[2064,128]{1,0:T(8,128)(2,1)}, bf16[2064,128]{1,0:T(8,128)(2,1)S(1)}, u32[]{:S(2)}, u32[]{:S(2)}) collective-permute-start(bf16[2064,128]{1,0:T(8,128)(2,1)} %pad_maximum_fusion.1), channel_id=1, source_target_pairs={{0,8},{4,12},{8,16},{12,20},{16,24},{20,28},{1,9},{5,13},{9,17},{1... | collective-permute-start | bytes 1585160 | tf_op jit(solution)/shard_map/ppermute | solution.py:22
  55.6 15.3 %copy-start.9 = (f32[2,16]{1,0:T(2,128)S(1)}, f32[2,16]{1,0:T(2,128)}, u32[]{:S(2)}) copy-start(f32[2,16]{1,0:T(2,128)} %get-tuple-element.9) | copy-start | bytes 388
  56.0 17.4 %copy-start.3 = (f32[2,512,512]{2,1,0:T(8,128)S(1)}, f32[2,512,512]{2,1,0:T(8,128)}, u32[]{:S(2)}) copy-start(f32[2,512,512]{2,1,0:T(8,128)} %fusion.63) | copy-start | bytes 6291460
  56.1 17.4 %copy-start.5 = (bf16[512,2048]{0,1:T(8,128)(2,1)S(1)}, bf16[512,2048]{0,1:T(8,128)(2,1)}, u32[]{:S(2)}) copy-start(bf16[512,2048]{0,1:T(8,128)(2,1)} %copy-done.4) | copy-start | bytes 6291460
  56.1 17.4 %copy-start.6 = (pred[512,512]{1,0:T(8,128)(4,1)S(1)}, pred[512,512]{1,0:T(8,128)(4,1)}, u32[]{:S(2)}) copy-start(pred[512,512]{1,0:T(8,128)(4,1)} %iota_compare_fusion) | copy-start | bytes 786436
  56.1 17.4 %copy-start.7 = (f32[2,16,512]{2,1,0:T(8,128)S(1)}, f32[2,16,512]{2,1,0:T(8,128)}, u32[]{:S(2)}) copy-start(f32[2,16,512]{2,1,0:T(8,128)} %get-tuple-element.16) | copy-start | bytes 196612
  56.1 14.7 %collective-permute-start.3 = (bf16[2064,128]{1,0:T(8,128)(2,1)S(1)}, bf16[2064,128]{1,0:T(8,128)(2,1)S(1)}, u32[]{:S(2)}, u32[]{:S(2)}) collective-permute-start(bf16[2064,128]{1,0:T(8,128)(2,1)S(1)} %pad_maximum_fusion.2), channel_id=1, source_target_pairs={{0,8},{4,12},{8,16},{12,20},{16,24},{20,28},{1,9},{5,13},{9,17},{1... | collective-permute-start | bytes 1585160 | tf_op jit(solution)/shard_map/ppermute | solution.py:22
  72.0 25.7 %collective-permute-start.4 = (bf16[2,16,64,128]{3,2,1,0:T(8,128)(2,1)}, bf16[2,16,64,128]{3,2,1,0:T(8,128)(2,1)S(1)}, u32[]{:S(2)}, u32[]{:S(2)}) collective-permute-start(bf16[2,16,64,128]{3,2,1,0:T(8,128)(2,1)} %fusion.46), channel_id=1, source_target_pairs={{0,16},{4,20},{8,24},{12,28},{1,17},{5,21},{9,25},{13,29},{2,18},{... | collective-permute-start | bytes 1572872 | tf_op jit(solution)/shard_map/ppermute | solution.py:22
  73.5 12.1 %copy-start.10 = (f32[2,16]{1,0:T(2,128)S(1)}, f32[2,16]{1,0:T(2,128)}, u32[]{:S(2)}) copy-start(f32[2,16]{1,0:T(2,128)} %get-tuple-element.9) | copy-start | bytes 388
  103.8 5.5 %copy-start.1 = (bf16[512,2048]{1,0:T(8,128)(2,1)S(1)}, bf16[512,2048]{1,0:T(8,128)(2,1)}, u32[]{:S(2)}) copy-start(bf16[512,2048]{1,0:T(8,128)(2,1)} %shard_map.118) | copy-start | bytes 6291460
  126.9 2.2 %copy-start = (f32[512,2048]{1,0:T(8,128)S(1)}, f32[512,2048]{1,0:T(8,128)}, u32[]{:S(2)}) copy-start(f32[512,2048]{1,0:T(8,128)} %copy.89) | copy-start | bytes 12582916
  126.9 2.9 %copy-start.2 = (bf16[512,2048]{1,0:T(8,128)(2,1)S(1)}, bf16[512,2048]{1,0:T(8,128)(2,1)}, u32[]{:S(2)}) copy-start(bf16[512,2048]{1,0:T(8,128)(2,1)} %param.14) | copy-start | bytes 6291460
  126.9 2.9 %copy-start.8 = (f32[2048]{0:T(1024)S(1)}, f32[2048]{0:T(1024)}, u32[]{:S(2)}) copy-start(f32[2048]{0:T(1024)} %convert_element_type.247) | copy-start | bytes 24580
  126.9 10.0 %slice-start = ((s8[16777216]{0:T(1024)(128)(4,1)}), s8[4194304]{0:T(1024)(128)(4,1)S(1)}, s32[]{:S(2)}) async-start(s8[16777216]{0:T(1024)(128)(4,1)} %bitcast.175), calls=%async_computation | async-start | bytes 8388608
  129.7 7.1 %slice-start.1 = ((s8[16777216]{0:T(1024)(128)(4,1)}), s8[4194304]{0:T(1024)(128)(4,1)S(1)}, s32[]{:S(2)}) async-start(s8[16777216]{0:T(1024)(128)(4,1)} %bitcast.175), calls=%async_computation.1 | async-start | bytes 8388608
  129.7 7.1 %slice-start.2 = ((s8[16777216]{0:T(1024)(128)(4,1)}), s8[4194304]{0:T(1024)(128)(4,1)S(1)}, s32[]{:S(2)}) async-start(s8[16777216]{0:T(1024)(128)(4,1)} %bitcast.175), calls=%async_computation.2 | async-start | bytes 8388608
  131.7 5.2 %slice-start.3 = ((s8[16777216]{0:T(1024)(128)(4,1)}), s8[4194304]{0:T(1024)(128)(4,1)S(1)}, s32[]{:S(2)}) async-start(s8[16777216]{0:T(1024)(128)(4,1)} %bitcast.175), calls=%async_computation.3 | async-start | bytes 8388608
  141.6 3.7 %collective-permute-start.5 = (bf16[2,128,1024]{2,1,0:T(8,128)(2,1)S(1)}, bf16[2,128,1024]{2,1,0:T(8,128)(2,1)S(1)}, u32[]{:S(2)}, u32[]{:S(2)}) collective-permute-start(bf16[2,128,1024]{2,1,0:T(8,128)(2,1)S(1)} %dynamic-slice_bitcast_fusion.3), channel_id=1, source_target_pairs={{0,1},{1,0},{2,3},{3,2},{4,5},{5,4},{6,7},{7,6},{8,9},{9,8},{10,11... | collective-permute-start | bytes 1572872 | tf_op jit(solution)/shard_map/ppermute | solution.py:216
  144.1 2.1 %collective-permute-start.7 = (bf16[2,128,1024]{2,1,0:T(8,128)(2,1)S(1)}, bf16[2,128,1024]{2,1,0:T(8,128)(2,1)S(1)}, u32[]{:S(2)}, u32[]{:S(2)}) collective-permute-start(bf16[2,128,1024]{2,1,0:T(8,128)(2,1)S(1)} %dynamic-slice_bitcast_fusion.2), channel_id=1, source_target_pairs={{0,1},{1,0},{2,3},{3,2},{4,5},{5,4},{6,7},{7,6},{8,9},{9,8},{10,11... | collective-permute-start | bytes 1572872 | tf_op jit(solution)/shard_map/ppermute | solution.py:216
  144.7 3.3 %collective-permute-start.9 = (bf16[2,128,1024]{2,1,0:T(8,128)(2,1)S(1)}, bf16[2,128,1024]{2,1,0:T(8,128)(2,1)S(1)}, u32[]{:S(2)}, u32[]{:S(2)}) collective-permute-start(bf16[2,128,1024]{2,1,0:T(8,128)(2,1)S(1)} %dynamic-slice_bitcast_fusion.1), channel_id=1, source_target_pairs={{0,1},{1,0},{2,3},{3,2},{4,5},{5,4},{6,7},{7,6},{8,9},{9,8},{10,11... | collective-permute-start | bytes 1572872 | tf_op jit(solution)/shard_map/ppermute | solution.py:216
  144.8 4.0 %collective-permute-start.11 = (bf16[2,128,1024]{2,1,0:T(8,128)(2,1)S(1)}, bf16[2,128,1024]{2,1,0:T(8,128)(2,1)S(1)}, u32[]{:S(2)}, u32[]{:S(2)}) collective-permute-start(bf16[2,128,1024]{2,1,0:T(8,128)(2,1)S(1)} %dynamic-slice_bitcast_fusion), channel_id=1, source_target_pairs={{0,1},{1,0},{2,3},{3,2},{4,5},{5,4},{6,7},{7,6},{8,9},{9,8},{10,11... | collective-permute-start | bytes 1572872 | tf_op jit(solution)/shard_map/ppermute | solution.py:216
  145.6 9.2 %collective-permute-start.6 = (bf16[128,1024]{1,0:T(8,128)(2,1)S(1)}, bf16[128,1024]{1,0:T(8,128)(2,1)S(1)}, u32[]{:S(2)}, u32[]{:S(2)}) collective-permute-start(bf16[128,1024]{1,0:T(8,128)(2,1)S(1)} %fusion.41), channel_id=1, source_target_pairs={{0,2},{2,0},{1,3},{3,1},{4,6},{6,4},{5,7},{7,5},{8,10},{10,8},{9,1... | collective-permute-start | bytes 786440 | tf_op jit(solution)/shard_map/ppermute | solution.py:216
  146.4 14.0 %collective-permute-start.8 = (bf16[128,1024]{1,0:T(8,128)(2,1)S(1)}, bf16[128,1024]{1,0:T(8,128)(2,1)S(1)}, u32[]{:S(2)}, u32[]{:S(2)}) collective-permute-start(bf16[128,1024]{1,0:T(8,128)(2,1)S(1)} %fusion.42), channel_id=1, source_target_pairs={{0,2},{2,0},{1,3},{3,1},{4,6},{6,4},{5,7},{7,5},{8,10},{10,8},{9,1... | collective-permute-start | bytes 786440 | tf_op jit(solution)/shard_map/ppermute | solution.py:216
  148.2 17.9 %collective-permute-start.10 = (bf16[128,1024]{1,0:T(8,128)(2,1)S(1)}, bf16[128,1024]{1,0:T(8,128)(2,1)S(1)}, u32[]{:S(2)}, u32[]{:S(2)}) collective-permute-start(bf16[128,1024]{1,0:T(8,128)(2,1)S(1)} %fusion.43), channel_id=1, source_target_pairs={{0,2},{2,0},{1,3},{3,1},{4,6},{6,4},{5,7},{7,5},{8,10},{10,8},{9,1... | collective-permute-start | bytes 786440 | tf_op jit(solution)/shard_map/ppermute | solution.py:216
  149.1 21.7 %collective-permute-start.12 = (bf16[128,1024]{1,0:T(8,128)(2,1)S(1)}, bf16[128,1024]{1,0:T(8,128)(2,1)S(1)}, u32[]{:S(2)}, u32[]{:S(2)}) collective-permute-start(bf16[128,1024]{1,0:T(8,128)(2,1)S(1)} %fusion.44), channel_id=1, source_target_pairs={{0,2},{2,0},{1,3},{3,1},{4,6},{6,4},{5,7},{7,5},{8,10},{10,8},{9,1... | collective-permute-start | bytes 786440 | tf_op jit(solution)/shard_map/ppermute | solution.py:216

commit v8 on v4

--- a/solution.py
+++ b/solution.py
@@ -15,7 +15,10 @@
 
 
 def shifted(value, axis, by):
-    count = lax.axis_size(axis)
+    names = axis if isinstance(axis, tuple) else (axis,)
+    count = 1
+    for name in names:
+        count *= lax.axis_size(name)
     pairs = [(i, i + by) for i in range(count) if 0 <= i + by < count]
     return lax.ppermute(value, axis, pairs)
 
@@ -94,9 +97,8 @@
     return weight, state
 
 
-def entering_state(total, state, axis):
+def entering_state(weight, state, axis):
     count = lax.axis_size(axis)
-    weight = jnp.exp(total)
     if count == 1:
         return jnp.zeros_like(state)
     own = pack(weight, state)
@@ -114,6 +116,34 @@
         span *= 2
     far = shifted(state.astype(jnp.bfloat16), axis, span).astype(jnp.float32)
     return weight[..., None, None] * far + state
+
+
+def entering_pairs(total, state, lo, hi):
+    shape = state.shape
+    heads = total.size
+    half = heads // 2
+    weight = jnp.exp(total).reshape(heads)
+    state = state.reshape((heads,) + shape[-2:])
+    first = lax.axis_index(lo) == 0
+    mine_w = jnp.where(first, weight[:half], weight[half:])
+    mine_s = jnp.where(first, state[:half], state[half:])
+    other_w = jnp.where(first, weight[half:], weight[:half])
+    other_s = jnp.where(first, state[half:], state[:half])
+    got_w, got_s = unpack(swap(pack(other_w, other_s), lo), (half,), (half,) + shape[-2:])
+    w_first = jnp.where(first, mine_w, got_w)
+    s_first = jnp.where(first, mine_s, got_s)
+    w_second = jnp.where(first, got_w, mine_w)
+    s_second = jnp.where(first, got_s, mine_s)
+    pair_w = w_first * w_second
+    pair_s = w_second[:, None, None] * s_first + s_second
+    at_first = entering_state(pair_w, pair_s, hi)
+    at_second = w_first[:, None, None] * at_first + s_first
+    keep = jnp.where(first, at_first, at_second)
+    give = jnp.where(first, at_second, at_first)
+    got = swap(give.astype(jnp.bfloat16), lo).astype(jnp.float32)
+    lower = jnp.where(first, keep, got)
+    upper = jnp.where(first, got, keep)
+    return jnp.concatenate([lower, upper], axis=0).reshape(shape)
 
 
 def body(
@@ -136,7 +166,7 @@
     halo = jnp.concatenate(
         [inner_input[tokens - margin :], state_input[tokens - margin :].reshape(margin, -1)], axis=1
     )
-    halo = shifted(halo, "ctx", 1)
+    halo = shifted(halo, ("chi", "clo"), 1)
     inner_conv = conv_silu(
         jnp.concatenate([halo[:, :inner_width], inner_input], axis=0), conv_inner, bias_inner, tokens
     )
@@ -170,7 +200,7 @@
         (local_state, device_total), (partial_heads, factors) = lax.scan(
             block_local, (start_state, start_total), inputs_all
         )
-    state_in = entering_state(device_total, local_state, "ctx")
+    state_in = entering_pairs(device_total, local_state, "clo", "chi")
     correction = jax.vmap(apply_state, in_axes=(0, None, 0))(c_all, state_in, factors)
     width_here = groups_here * per_group * HEAD_DIM
     mixed_heads = (partial_heads + correction).reshape(tokens, width_here) + jnp.repeat(
@@ -233,15 +263,16 @@
 def solution(mesh):
     cores = 2
     split = Mesh(
-        mesh.devices.reshape(mesh.shape["ctx"], mesh.shape["tp"] // cores, cores),
-        ("ctx", "ty", "tc"),
+        mesh.devices.reshape(mesh.shape["ctx"] // 2, 2, mesh.shape["tp"] // cores, cores),
+        ("chi", "clo", "ty", "tc"),
     )
     tp = ("ty", "tc")
+    ctx = ("chi", "clo")
     placed = (
-        P("ctx", tp),
-        P("ctx", None, tp),
-        P("ctx", tp),
-        P("ctx", tp),
+        P(ctx, tp),
+        P(ctx, None, tp),
+        P(ctx, tp),
+        P(ctx, tp),
         P(None, tp),
         P(None, None, tp),
         P(tp),
@@ -252,5 +283,5 @@
         P(tp, None),
     )
     return jax.shard_map(
-        body, mesh=split, in_specs=placed, out_specs=P(("ctx",) + tp, None), check_vma=False
-    )
+        body, mesh=split, in_specs=placed, out_specs=P(ctx + tp, None), check_vma=False
+    )

time: 149 us -> 137 us (0.919)
  the two profiles are of different devices: /device:TPU:30 before, /device:TPU:0 now
where the time goes in v8:
time: 137 us; the launch traced here: 135 us
  other arithmetic  31.3 us (23%)
  starting transfers between devices  30.8 us (22%)
  waiting for transfers between devices  29.5 us (22%)
  matrix products  23.8 us (17%)
  local copies, waits for them, and re-layouts  18.8 us (14%)
    ppermute x10, waiting for transfers between devices, swap(): return lax.ppermute(value, axis, [(0, 1), (1, 0)])  25.4 us
    ppermute x4, starting transfers between devices, shifted(): return lax.ppermute(value, axis, pairs)  23.5 us
    unnamed x39, local copies, waits for them, and re-layouts  12.6 us
    convert_element_type x2, other arithmetic, conv_silu(): return lax.optimization_barrier(jax.nn.silu(summed).astype(jnp.bfloat16))  11.2 us
    dot_general x1, matrix products, block_parts(): jnp.einsum('ghij,jghp->ighp', mixing, inner_block, preferred_element_type...  9.45 us
    dot_general x4, matrix products, reduce_rows(): jnp.dot(normed, out_weight[:, c * step:(c + 1) * step], preferred_element...  9.37 us
    ppermute x10, starting transfers between devices, swap(): return lax.ppermute(value, axis, [(0, 1), (1, 0)])  7.29 us
    ppermute x4, waiting for transfers between devices, shifted(): return lax.ppermute(value, axis, pairs)  4.09 us
  transfers between devices with their start and end apart: 14, of which 6 were waited for; matrix products, arithmetic and copies ran while one was open for 26% of the time, Pallas kernels for 0%

profile of v8, /device:TPU:0, one launch (start us, length us, event | category | flops | bytes accessed | tf_op | source)
XLA Modules:
  0.0 134.8 jit_solution(9905049717288498911)
XLA Ops:
  1.6 4.8 %collective-permute-start = (bf16[3,2560]{1,0:T(4,128)(2,1)S(1)}, bf16[3,2560]{1,0:T(4,128)(2,1)S(1)}, u32[]{:S(2)}, u32[]{:S(2)}) collective-permute-start(bf16[3,2560]{1,0:T(4,128)(2,1)S(1)} %pad_maximum_fusion.6), channel_id=1, source_target_pairs={{0,4},{4,8},{8,12},{12,16},{16,20},{20,24},{24,28},{1,5},{5,9},{9,... | collective-permute-start | bytes 46088 | tf_op jit(solution)/shard_map/ppermute | solution.py:23
  8.0 2.3 %reduce-window.6 = f32[16,2,4,128]{3,0,1,2:T(8,128)S(1)} reduce-window(f32[16,2,4,128]{3,0,1,2:T(8,128)S(1)} %bitcast.238, f32[]{:T(128)} %constant.65.clone.1), window={size=1x1x1x128 pad=0_0x0_0x0_0x127_0}, to_apply=%region_0.1 | reduce-window | flops 2080768 | bytes 131076 | tf_op jit(solution)/shard_map/reduce-window
  13.9 3.9 %copy.64 = bf16[512,2048]{0,1:T(8,128)(2,1)} copy(bf16[512,2048]{1,0:T(8,128)(2,1)} %param.12) | data formatting | bytes 4194304 | tf_op args[0]
  18.9 9.8 %multiply_convert_fusion.3 = bf16[512,2048]{0,1:T(8,128)(2,1)S(1)} fusion(bf16[512,2048]{0,1:T(8,128)(2,1)} %copy.64, bf16[3,2048]{0,1:T(8,128)(2,1)S(1)} %copy.63, f32[2048]{0:T(1024)S(1)} %bitcast.241, f32[2048]{0:T(1024)S(1)} %bitcast.242, f32[2048]{0:T(1024)S(1)} %bitcast.240, f32[2048]{0:T(1024)S(1)} %bitcast.239, f32[2048]{0:T(1024)S(1)} %convert_element_type.235), kind=kLoop, calls=%fused_computation.25 | loop fusion | flops 27262976 | bytes 4247552 | tf_op jit(solution)/shard_map/convert_element_type | solution.py:32
  29.0 1.3 multiply_convert_fusion.5
  31.1 1.6 %fusion.19 = f32[2,16,64,128]{3,2,1,0:T(8,128)S(1)} fusion(bf16[512,2,128,1]{0,2,3,1:T(8,128)(2,1)S(1)} %bitcast.223, bf16[512,2,16,64]{0,3,2,1:T(8,128)(2,1)S(1)} %bitcast.210, f32[512,2,16]{0,2,1:T(8,128)} %get-tuple-element.17), kind=kOutput, calls=%fused_computation.32 | convolution fusion | flops 271581184 | bytes 3473408 | tf_op jit(solution)/shard_map/jghp,jgn->ghpn/dot_general | solution.py:52
  32.7 1.6 %collective-permute-start.1 = (bf16[1040,128]{1,0:T(8,128)(2,1)S(1)}, bf16[1040,128]{1,0:T(8,128)(2,1)S(1)}, u32[]{:S(2)}, u32[]{:S(2)}) collective-permute-start(bf16[1040,128]{1,0:T(8,128)(2,1)S(1)} %pad_maximum_fusion.4), channel_id=1, source_target_pairs={{0,4},{4,0},{1,5},{5,1},{2,6},{6,2},{3,7},{7,3},{8,12},{12,8},{9,1... | collective-permute-start | bytes 798728 | tf_op jit(solution)/shard_map/ppermute | solution.py:219
  35.2 5.4 %collective-permute-done.1 = bf16[1040,128]{1,0:T(8,128)(2,1)S(1)} collective-permute-done((bf16[1040,128]{1,0:T(8,128)(2,1)S(1)}, bf16[1040,128]{1,0:T(8,128)(2,1)S(1)}, u32[]{:S(2)}, u32[]{:S(2)}) %collective-permute-start.1) | collective-permute-done | bytes 266272 | tf_op jit(solution)/shard_map/ppermute | solution.py:219
  44.1 1.3 fusion.42
  46.1 5.2 %collective-permute-start.3 = (bf16[1040,128]{1,0:T(8,128)(2,1)}, bf16[1040,128]{1,0:T(8,128)(2,1)}, u32[]{:S(2)}, u32[]{:S(2)}) collective-permute-start(bf16[1040,128]{1,0:T(8,128)(2,1)} %pad_maximum_fusion.5), channel_id=1, source_target_pairs={{0,16},{8,24},{1,17},{9,25},{2,18},{10,26},{3,19},{11,27},{4,20},{... | collective-permute-start | bytes 798728 | tf_op jit(solution)/shard_map/ppermute | solution.py:23
  51.3 4.2 %collective-permute-start.2 = (bf16[1040,128]{1,0:T(8,128)(2,1)}, bf16[1040,128]{1,0:T(8,128)(2,1)}, u32[]{:S(2)}, u32[]{:S(2)}) collective-permute-start(bf16[1040,128]{1,0:T(8,128)(2,1)} %pad_maximum_fusion.5), channel_id=1, source_target_pairs={{0,8},{8,16},{16,24},{1,9},{9,17},{17,25},{2,10},{10,18},{18,26},{... | collective-permute-start | bytes 798728 | tf_op jit(solution)/shard_map/ppermute | solution.py:23
  56.3 3.9 %copy.77 = bf16[512,2048]{0,1:T(8,128)(2,1)} copy(bf16[512,2048]{1,0:T(8,128)(2,1)} %param.14) | data formatting | bytes 4194304 | tf_op args[2]
  63.8 1.0 slice.208
  64.8 1.0 slice.209
  65.9 9.3 %collective-permute-start.4 = (bf16[16,64,128]{2,1,0:T(8,128)(2,1)S(1)}, bf16[16,64,128]{2,1,0:T(8,128)(2,1)S(1)}, u32[]{:S(2)}, u32[]{:S(2)}) collective-permute-start(bf16[16,64,128]{2,1,0:T(8,128)(2,1)S(1)} %fusion.43), channel_id=1, source_target_pairs={{0,16},{8,24},{1,17},{9,25},{2,18},{10,26},{3,19},{11,27},{4,20},{... | collective-permute-start | bytes 786440 | tf_op jit(solution)/shard_map/ppermute | solution.py:23
  75.2 1.4 %fusion.69 = f32[2,512,512]{2,1,0:T(8,128)S(1)} fusion(bf16[512,2,128]{0,2,1:T(8,128)(2,1)S(1)} %bitcast.221, bf16[512,2,128]{0,2,1:T(8,128)(2,1)} %bitcast.224), kind=kOutput, calls=%fused_computation.145 | convolution fusion | flops 134217728 | bytes 2621440 | tf_op jit(solution)/shard_map/ign,jgn->gij/dot_general | solution.py:43
  76.7 4.1 %collective-permute-done.4 = bf16[16,64,128]{2,1,0:T(8,128)(2,1)S(1)} collective-permute-done((bf16[16,64,128]{2,1,0:T(8,128)(2,1)S(1)}, bf16[16,64,128]{2,1,0:T(8,128)(2,1)S(1)}, u32[]{:S(2)}, u32[]{:S(2)}) %collective-permute-start.4) | collective-permute-done | bytes 262176 | tf_op jit(solution)/shard_map/ppermute | solution.py:23
  81.3 9.5 %fusion = f32[2,16,64,512]{3,2,1,0:T(8,128)S(1)} fusion(bf16[512,2,16,64]{0,3,2,1:T(8,128)(2,1)S(1)} %bitcast.211, f32[2,16,512]{2,1,0:T(8,128)S(1)} %bitcast.237, f32[2,512,512]{2,1,0:T(8,128)S(1)} %fusion.69, f32[2,16,512]{2,1,0:T(8,128)S(1)} %copy-done.6, pred[512,512]{1,0:T(8,128)(4,1)S(1)} %copy-done.5), kind=kOutput, calls=%fused_computation.1 | convolution fusion | flops 1115684864 | bytes 8781824 | tf_op jit(solution)/shard_map/ghij,jghp->ighp/dot_general | solution.py:47
  91.3 2.0 %fusion.6 = f32[1,512,2,16,64]{1,4,3,2,0:T(8,128)S(1)} fusion(f32[2,16,64,512]{3,2,1,0:T(8,128)S(1)} %fusion, f32[2,16,64,128]{3,2,1,0:T(8,128)S(1)} %bitcast.214, bf16[512,2,128,1]{0,2,3,1:T(8,128)(2,1)S(1)} %bitcast.222, f32[512,2,16]{0,2,1:T(8,128)S(1)} %get-tuple-element.16), kind=kOutput, calls=%fused_computation.10 | convolution fusion | flops 1612709888 | bytes 9764864 | tf_op jit(solution)/shard_map/vmap(ign,ghpn->ighp)/dot_general | solution.py:59
  93.4 2.3 %bitcast_reduce_fusion = (f32[512,2]{0,1:T(2,128)S(1)}, f32[512,2048]{0,1:T(8,128)S(1)}) fusion(bf16[512,2048]{0,1:T(8,128)(2,1)S(1)} %copy-done, bf16[512,2048]{0,1:T(8,128)(2,1)S(1)} %multiply_convert_fusion.3, f32[2048]{0:T(1024)S(1)} %copy-done.7, f32[1,512,2,16,64]{1,4,3,2,0:T(8,128)S(1)} %fusion.6), kind=kLoop, calls=%fused_computation.14 | loop fusion | flops 11533312 | bytes 12595200 | tf_op jit(solution)/shard_map/reduce_sum | solution.py:211
  96.3 1.2 slice-done.3
  97.5 2.3 %fusion.21 = bf16[512,1024]{1,0:T(8,128)(2,1)S(1)} fusion(bf16[512,2048]{0,1:T(8,128)(2,1)S(1)} %fusion.8, bf16[2048,4096]{1,0:T(8,128)(2,1)S(1)} %bitcast.246), kind=kOutput, calls=%fused_computation.35 | convolution fusion | flops 2148007936 | bytes 7340032 | tf_op jit(solution)/shard_map/dot_general | solution.py:243
  99.8 2.3 %fusion.24 = bf16[512,1024]{1,0:T(8,128)(2,1)S(1)} fusion(bf16[512,2048]{0,1:T(8,128)(2,1)S(1)} %fusion.8, bf16[2048,4096]{1,0:T(8,128)(2,1)S(1)} %bitcast.246), kind=kOutput, calls=%fused_computation.36 | convolution fusion | flops 2148007936 | bytes 7340032 | tf_op jit(solution)/shard_map/dot_general | solution.py:243
  102.2 2.3 %fusion.27 = bf16[512,1024]{1,0:T(8,128)(2,1)S(1)} fusion(bf16[512,2048]{0,1:T(8,128)(2,1)S(1)} %fusion.8, bf16[2048,4096]{1,0:T(8,128)(2,1)S(1)} %bitcast.246), kind=kOutput, calls=%fused_computation.37 | convolution fusion | flops 2148007936 | bytes 7340032 | tf_op jit(solution)/shard_map/dot_general | solution.py:243
  104.6 2.3 %fusion.30 = bf16[512,1024]{1,0:T(8,128)(2,1)S(1)} fusion(bf16[512,2048]{0,1:T(8,128)(2,1)S(1)} %fusion.8, bf16[2048,4096]{1,0:T(8,128)(2,1)S(1)} %bitcast.246), kind=kOutput, calls=%fused_computation.38 | convolution fusion | flops 2148007936 | bytes 7340032 | tf_op jit(solution)/shard_map/dot_general | solution.py:243
  108.5 1.6 %collective-permute-start.7 = (bf16[128,1024]{1,0:T(8,128)(2,1)S(1)}, bf16[128,1024]{1,0:T(8,128)(2,1)S(1)}, u32[]{:S(2)}, u32[]{:S(2)}) collective-permute-start(bf16[128,1024]{1,0:T(8,128)(2,1)S(1)} %fusion.45), channel_id=1, source_target_pairs={{0,2},{2,0},{1,3},{3,1},{4,6},{6,4},{5,7},{7,5},{8,10},{10,8},{9,1... | collective-permute-start | bytes 786440 | tf_op jit(solution)/shard_map/ppermute | solution.py:219
  111.2 1.5 %collective-permute-start.11 = (bf16[128,1024]{1,0:T(8,128)(2,1)S(1)}, bf16[128,1024]{1,0:T(8,128)(2,1)S(1)}, u32[]{:S(2)}, u32[]{:S(2)}) collective-permute-start(bf16[128,1024]{1,0:T(8,128)(2,1)S(1)} %fusion.47), channel_id=1, source_target_pairs={{0,2},{2,0},{1,3},{3,1},{4,6},{6,4},{5,7},{7,5},{8,10},{10,8},{9,1... | collective-permute-start | bytes 786440 | tf_op jit(solution)/shard_map/ppermute | solution.py:219
  113.6 4.2 %collective-permute-done.7 = bf16[128,1024]{1,0:T(8,128)(2,1)S(1)} collective-permute-done((bf16[128,1024]{1,0:T(8,128)(2,1)S(1)}, bf16[128,1024]{1,0:T(8,128)(2,1)S(1)}, u32[]{:S(2)}, u32[]{:S(2)}) %collective-permute-start.7) | collective-permute-done | bytes 262176 | tf_op jit(solution)/shard_map/ppermute | solution.py:219
  117.8 5.5 %collective-permute-done.9 = bf16[128,1024]{1,0:T(8,128)(2,1)S(1)} collective-permute-done((bf16[128,1024]{1,0:T(8,128)(2,1)S(1)}, bf16[128,1024]{1,0:T(8,128)(2,1)S(1)}, u32[]{:S(2)}, u32[]{:S(2)}) %collective-permute-start.9) | collective-permute-done | bytes 262176 | tf_op jit(solution)/shard_map/ppermute | solution.py:219
  123.5 5.5 %collective-permute-done.11 = bf16[128,1024]{1,0:T(8,128)(2,1)S(1)} collective-permute-done((bf16[128,1024]{1,0:T(8,128)(2,1)S(1)}, bf16[128,1024]{1,0:T(8,128)(2,1)S(1)}, u32[]{:S(2)}, u32[]{:S(2)}) %collective-permute-start.11) | collective-permute-done | bytes 262176 | tf_op jit(solution)/shard_map/ppermute | solution.py:219
  129.1 4.6 %collective-permute-done.13 = bf16[128,1024]{1,0:T(8,128)(2,1)S(1)} collective-permute-done((bf16[128,1024]{1,0:T(8,128)(2,1)S(1)}, bf16[128,1024]{1,0:T(8,128)(2,1)S(1)}, u32[]{:S(2)}, u32[]{:S(2)}) %collective-permute-start.13) | collective-permute-done | bytes 262176 | tf_op jit(solution)/shard_map/ppermute | solution.py:219
  133.8 1.0 pad_maximum_fusion.2
  (119 shorter events, 23.7 us)
Async XLA Ops:
  0.0 17.8 %copy-start.4 = (bf16[512,2,256]{2,1,0:T(2,128)(2,1)S(1)}, bf16[512,2,256]{2,1,0:T(2,128)(2,1)}, u32[]{:S(2)}) copy-start(bf16[512,2,256]{2,1,0:T(2,128)(2,1)} %param.13) | copy-start | bytes 1572868
  0.0 18.6 %copy-start.10 = (bf16[2048]{0:T(1024)(128)(2,1)S(1)}, bf16[2048]{0:T(1024)(128)(2,1)}, u32[]{:S(2)}) copy-start(bf16[2048]{0:T(1024)(128)(2,1)} %param.18) | copy-start | bytes 12292
  0.0 18.6 %copy-start.12 = (bf16[2,256]{1,0:T(2,128)(2,1)S(1)}, bf16[2,256]{1,0:T(2,128)(2,1)}, u32[]{:S(2)}) copy-start(bf16[2,256]{1,0:T(2,128)(2,1)} %param.19) | copy-start | bytes 3076
  1.6 17.0 %collective-permute-start = (bf16[3,2560]{1,0:T(4,128)(2,1)S(1)}, bf16[3,2560]{1,0:T(4,128)(2,1)S(1)}, u32[]{:S(2)}, u32[]{:S(2)}) collective-permute-start(bf16[3,2560]{1,0:T(4,128)(2,1)S(1)} %pad_maximum_fusion.6), channel_id=1, source_target_pairs={{0,4},{4,8},{8,12},{12,16},{16,20},{20,24},{24,28},{1,5},{5,9},{9,... | collective-permute-start | bytes 46088 | tf_op jit(solution)/shard_map/ppermute | solution.py:23
  30.4 0.7 copy-start.1
  32.7 7.9 %collective-permute-start.1 = (bf16[1040,128]{1,0:T(8,128)(2,1)S(1)}, bf16[1040,128]{1,0:T(8,128)(2,1)S(1)}, u32[]{:S(2)}, u32[]{:S(2)}) collective-permute-start(bf16[1040,128]{1,0:T(8,128)(2,1)S(1)} %pad_maximum_fusion.4), channel_id=1, source_target_pairs={{0,4},{4,0},{1,5},{5,1},{2,6},{6,2},{3,7},{7,3},{8,12},{12,8},{9,1... | collective-permute-start | bytes 798728 | tf_op jit(solution)/shard_map/ppermute | solution.py:219
  40.6 0.7 copy-start.2
  42.0 0.6 copy-start.11
  42.0 14.3 %copy-start.8 = (f32[16]{0:T(128)}, f32[16]{0:T(128)S(1)}, u32[]{:S(2)}) copy-start(f32[16]{0:T(128)S(1)} %get-tuple-element.13) | copy-start | bytes 196
  46.1 16.2 %collective-permute-start.3 = (bf16[1040,128]{1,0:T(8,128)(2,1)}, bf16[1040,128]{1,0:T(8,128)(2,1)}, u32[]{:S(2)}, u32[]{:S(2)}) collective-permute-start(bf16[1040,128]{1,0:T(8,128)(2,1)} %pad_maximum_fusion.5), channel_id=1, source_target_pairs={{0,16},{8,24},{1,17},{9,25},{2,18},{10,26},{3,19},{11,27},{4,20},{... | collective-permute-start | bytes 798728 | tf_op jit(solution)/shard_map/ppermute | solution.py:23
  51.3 11.7 %collective-permute-start.2 = (bf16[1040,128]{1,0:T(8,128)(2,1)}, bf16[1040,128]{1,0:T(8,128)(2,1)}, u32[]{:S(2)}, u32[]{:S(2)}) collective-permute-start(bf16[1040,128]{1,0:T(8,128)(2,1)} %pad_maximum_fusion.5), channel_id=1, source_target_pairs={{0,8},{8,16},{16,24},{1,9},{9,17},{17,25},{2,10},{10,18},{18,26},{... | collective-permute-start | bytes 798728 | tf_op jit(solution)/shard_map/ppermute | solution.py:23
  61.6 19.2 %copy-start.9 = (f32[16]{0:T(128)S(1)}, f32[16]{0:T(128)}, u32[]{:S(2)}) copy-start(f32[16]{0:T(128)} %copy-done.8) | copy-start | bytes 196
  62.3 14.3 %copy-start.3 = (bf16[1040,128]{1,0:T(8,128)(2,1)S(1)}, bf16[1040,128]{1,0:T(8,128)(2,1)}, u32[]{:S(2)}) copy-start(bf16[1040,128]{1,0:T(8,128)(2,1)} %copy-done.2) | copy-start | bytes 798724
  62.3 18.9 %copy-start.5 = (pred[512,512]{1,0:T(8,128)(4,1)S(1)}, pred[512,512]{1,0:T(8,128)(4,1)}, u32[]{:S(2)}) copy-start(pred[512,512]{1,0:T(8,128)(4,1)} %iota_compare_fusion) | copy-start | bytes 786436
  62.3 18.9 %copy-start.6 = (f32[2,16,512]{2,1,0:T(8,128)S(1)}, f32[2,16,512]{2,1,0:T(8,128)}, u32[]{:S(2)}) copy-start(f32[2,16,512]{2,1,0:T(8,128)} %get-tuple-element.19) | copy-start | bytes 196612
  65.9 14.9 %collective-permute-start.4 = (bf16[16,64,128]{2,1,0:T(8,128)(2,1)S(1)}, bf16[16,64,128]{2,1,0:T(8,128)(2,1)S(1)}, u32[]{:S(2)}, u32[]{:S(2)}) collective-permute-start(bf16[16,64,128]{2,1,0:T(8,128)(2,1)S(1)} %fusion.43), channel_id=1, source_target_pairs={{0,16},{8,24},{1,17},{9,25},{2,18},{10,26},{3,19},{11,27},{4,20},{... | collective-permute-start | bytes 786440 | tf_op jit(solution)/shard_map/ppermute | solution.py:23
  81.2 9.6 %collective-permute-start.5 = (bf16[16,64,128]{2,1,0:T(8,128)(2,1)S(1)}, bf16[16,64,128]{2,1,0:T(8,128)(2,1)S(1)}, u32[]{:S(2)}, u32[]{:S(2)}) collective-permute-start(bf16[16,64,128]{2,1,0:T(8,128)(2,1)S(1)} %select_convert_fusion), channel_id=1, source_target_pairs={{0,4},{4,0},{1,5},{5,1},{2,6},{6,2},{3,7},{7,3},{8,12},{12,8},{9,1... | collective-permute-start | bytes 786440 | tf_op jit(solution)/shard_map/ppermute | solution.py:219
  90.7 5.4 %slice-start = ((s8[16777216]{0:T(1024)(128)(4,1)}), s8[4194304]{0:T(1024)(128)(4,1)S(1)}, s32[]{:S(2)}) async-start(s8[16777216]{0:T(1024)(128)(4,1)} %bitcast.245), calls=%async_computation | async-start | bytes 8388608
  91.3 2.1 %copy-start = (bf16[512,2048]{0,1:T(8,128)(2,1)S(1)}, bf16[512,2048]{0,1:T(8,128)(2,1)}, u32[]{:S(2)}) copy-start(bf16[512,2048]{0,1:T(8,128)(2,1)} %copy.77) | copy-start | bytes 6291460
  91.3 2.1 %copy-start.7 = (f32[2048]{0:T(1024)S(1)}, f32[2048]{0:T(1024)}, u32[]{:S(2)}) copy-start(f32[2048]{0:T(1024)} %mul.296) | copy-start | bytes 24580
  91.3 4.8 %slice-start.1 = ((s8[16777216]{0:T(1024)(128)(4,1)}), s8[4194304]{0:T(1024)(128)(4,1)S(1)}, s32[]{:S(2)}) async-start(s8[16777216]{0:T(1024)(128)(4,1)} %bitcast.245), calls=%async_computation.1 | async-start | bytes 8388608
  93.4 2.9 %slice-start.2 = ((s8[16777216]{0:T(1024)(128)(4,1)}), s8[4194304]{0:T(1024)(128)(4,1)S(1)}, s32[]{:S(2)}) async-start(s8[16777216]{0:T(1024)(128)(4,1)} %bitcast.245), calls=%async_computation.2 | async-start | bytes 8388608
  93.4 4.0 %slice-start.3 = ((s8[16777216]{0:T(1024)(128)(4,1)}), s8[4194304]{0:T(1024)(128)(4,1)S(1)}, s32[]{:S(2)}) async-start(s8[16777216]{0:T(1024)(128)(4,1)} %bitcast.245), calls=%async_computation.3 | async-start | bytes 8388608
  104.6 3.8 %collective-permute-start.6 = (bf16[2,128,1024]{2,1,0:T(8,128)(2,1)S(1)}, bf16[2,128,1024]{2,1,0:T(8,128)(2,1)S(1)}, u32[]{:S(2)}, u32[]{:S(2)}) collective-permute-start(bf16[2,128,1024]{2,1,0:T(8,128)(2,1)S(1)} %dynamic-slice_bitcast_fusion.3), channel_id=1, source_target_pairs={{0,1},{1,0},{2,3},{3,2},{4,5},{5,4},{6,7},{7,6},{8,9},{9,8},{10,11... | collective-permute-start | bytes 1572872 | tf_op jit(solution)/shard_map/ppermute | solution.py:219
  107.0 3.1 %collective-permute-start.8 = (bf16[2,128,1024]{2,1,0:T(8,128)(2,1)S(1)}, bf16[2,128,1024]{2,1,0:T(8,128)(2,1)S(1)}, u32[]{:S(2)}, u32[]{:S(2)}) collective-permute-start(bf16[2,128,1024]{2,1,0:T(8,128)(2,1)S(1)} %dynamic-slice_bitcast_fusion.2), channel_id=1, source_target_pairs={{0,1},{1,0},{2,3},{3,2},{4,5},{5,4},{6,7},{7,6},{8,9},{9,8},{10,11... | collective-permute-start | bytes 1572872 | tf_op jit(solution)/shard_map/ppermute | solution.py:219
  107.6 3.3 %collective-permute-start.10 = (bf16[2,128,1024]{2,1,0:T(8,128)(2,1)S(1)}, bf16[2,128,1024]{2,1,0:T(8,128)(2,1)S(1)}, u32[]{:S(2)}, u32[]{:S(2)}) collective-permute-start(bf16[2,128,1024]{2,1,0:T(8,128)(2,1)S(1)} %dynamic-slice_bitcast_fusion.1), channel_id=1, source_target_pairs={{0,1},{1,0},{2,3},{3,2},{4,5},{5,4},{6,7},{7,6},{8,9},{9,8},{10,11... | collective-permute-start | bytes 1572872 | tf_op jit(solution)/shard_map/ppermute | solution.py:219
  107.8 5.0 %collective-permute-start.12 = (bf16[2,128,1024]{2,1,0:T(8,128)(2,1)S(1)}, bf16[2,128,1024]{2,1,0:T(8,128)(2,1)S(1)}, u32[]{:S(2)}, u32[]{:S(2)}) collective-permute-start(bf16[2,128,1024]{2,1,0:T(8,128)(2,1)S(1)} %dynamic-slice_bitcast_fusion), channel_id=1, source_target_pairs={{0,1},{1,0},{2,3},{3,2},{4,5},{5,4},{6,7},{7,6},{8,9},{9,8},{10,11... | collective-permute-start | bytes 1572872 | tf_op jit(solution)/shard_map/ppermute | solution.py:219
  108.5 9.2 %collective-permute-start.7 = (bf16[128,1024]{1,0:T(8,128)(2,1)S(1)}, bf16[128,1024]{1,0:T(8,128)(2,1)S(1)}, u32[]{:S(2)}, u32[]{:S(2)}) collective-permute-start(bf16[128,1024]{1,0:T(8,128)(2,1)S(1)} %fusion.45), channel_id=1, source_target_pairs={{0,2},{2,0},{1,3},{3,1},{4,6},{6,4},{5,7},{7,5},{8,10},{10,8},{9,1... | collective-permute-start | bytes 786440 | tf_op jit(solution)/shard_map/ppermute | solution.py:219
  110.3 13.1 %collective-permute-start.9 = (bf16[128,1024]{1,0:T(8,128)(2,1)S(1)}, bf16[128,1024]{1,0:T(8,128)(2,1)S(1)}, u32[]{:S(2)}, u32[]{:S(2)}) collective-permute-start(bf16[128,1024]{1,0:T(8,128)(2,1)S(1)} %fusion.46), channel_id=1, source_target_pairs={{0,2},{2,0},{1,3},{3,1},{4,6},{6,4},{5,7},{7,5},{8,10},{10,8},{9,1... | collective-permute-start | bytes 786440 | tf_op jit(solution)/shard_map/ppermute | solution.py:219
  111.2 17.8 %collective-permute-start.11 = (bf16[128,1024]{1,0:T(8,128)(2,1)S(1)}, bf16[128,1024]{1,0:T(8,128)(2,1)S(1)}, u32[]{:S(2)}, u32[]{:S(2)}) collective-permute-start(bf16[128,1024]{1,0:T(8,128)(2,1)S(1)} %fusion.47), channel_id=1, source_target_pairs={{0,2},{2,0},{1,3},{3,1},{4,6},{6,4},{5,7},{7,5},{8,10},{10,8},{9,1... | collective-permute-start | bytes 786440 | tf_op jit(solution)/shard_map/ppermute | solution.py:219
  112.9 20.8 %collective-permute-start.13 = (bf16[128,1024]{1,0:T(8,128)(2,1)S(1)}, bf16[128,1024]{1,0:T(8,128)(2,1)S(1)}, u32[]{:S(2)}, u32[]{:S(2)}) collective-permute-start(bf16[128,1024]{1,0:T(8,128)(2,1)S(1)} %fusion.48), channel_id=1, source_target_pairs={{0,2},{2,0},{1,3},{3,1},{4,6},{6,4},{5,7},{7,5},{8,10},{10,8},{9,1... | collective-permute-start | bytes 786440 | tf_op jit(solution)/shard_map/ppermute | solution.py:219

commit v9 on v8

--- a/solution.py
+++ b/solution.py
@@ -32,9 +32,8 @@
     return lax.optimization_barrier(jax.nn.silu(summed).astype(jnp.bfloat16))
 
 
-def block_parts(inner_block, b_block, c_block, step_sizes, log_rates):
+def diagonal_of(inner_block, b_block, c_block, step_sizes, cumulative):
     length = inner_block.shape[0]
-    cumulative = jnp.cumsum(log_rates, axis=0)
     along = jnp.transpose(cumulative, (1, 2, 0))
     causal = lax.broadcasted_iota(jnp.int32, (length, length), 0) >= lax.broadcasted_iota(
         jnp.int32, (length, length), 1
@@ -44,14 +43,19 @@
     mixing = (
         decays * scores[:, None] * jnp.transpose(step_sizes, (1, 2, 0))[:, :, None, :]
     ).astype(jnp.bfloat16)
-    diagonal = jnp.einsum(
-        "ghij,jghp->ighp", mixing, inner_block, preferred_element_type=jnp.float32
-    )
+    return jnp.einsum("ghij,jghp->ighp", mixing, inner_block, preferred_element_type=jnp.float32)
+
+
+def state_of(inner_block, b_block, step_sizes, cumulative):
     tail_weight = jnp.exp(cumulative[-1][None] - cumulative) * step_sizes
     weighted = (inner_block * tail_weight[..., None]).astype(jnp.bfloat16)
-    block_state = jnp.einsum(
-        "jghp,jgn->ghpn", weighted, b_block, preferred_element_type=jnp.float32
-    )
+    return jnp.einsum("jghp,jgn->ghpn", weighted, b_block, preferred_element_type=jnp.float32)
+
+
+def block_parts(inner_block, b_block, c_block, step_sizes, log_rates):
+    cumulative = jnp.cumsum(log_rates, axis=0)
+    diagonal = diagonal_of(inner_block, b_block, c_block, step_sizes, cumulative)
+    block_state = state_of(inner_block, b_block, step_sizes, cumulative)
     return diagonal, cumulative, block_state
 
 
@@ -97,14 +101,14 @@
     return weight, state
 
 
-def entering_state(weight, state, axis):
+def entering_state(weight, state, axis, work=None, work_inputs=()):
     count = lax.axis_size(axis)
     if count == 1:
-        return jnp.zeros_like(state)
+        return jnp.zeros_like(state), run(work, work_inputs)
     own = pack(weight, state)
+    if count == 2:
+        return unpack(shifted(own, axis, 1), weight.shape, state.shape)[1], run(work, work_inputs)
     near_w, near_s = unpack(shifted(own, axis, 1), weight.shape, state.shape)
-    if count == 2:
-        return near_s
     far_w, far_s = unpack(shifted(own, axis, 2), weight.shape, state.shape)
     state = near_w[..., None, None] * far_s + near_s
     weight = near_w * far_w
@@ -114,11 +118,21 @@
         state = weight[..., None, None] * far_s + state
         weight = weight * far_w
         span *= 2
-    far = shifted(state.astype(jnp.bfloat16), axis, span).astype(jnp.float32)
-    return weight[..., None, None] * far + state
-
-
-def entering_pairs(total, state, lo, hi):
+    payload = state.astype(jnp.bfloat16)
+    if work is not None:
+        payload, work_inputs = lax.optimization_barrier((payload, work_inputs))
+    far = shifted(payload, axis, span)
+    done = run(work, work_inputs)
+    if work is not None:
+        far, done = lax.optimization_barrier((far, done))
+    return weight[..., None, None] * far.astype(jnp.float32) + state, done
+
+
+def run(work, work_inputs):
+    return None if work is None else work(*work_inputs)
+
+
+def entering_pairs(total, state, lo, hi, work=None, work_inputs=()):
     shape = state.shape
     heads = total.size
     half = heads // 2
@@ -136,14 +150,14 @@
     s_second = jnp.where(first, got_s, mine_s)
     pair_w = w_first * w_second
     pair_s = w_second[:, None, None] * s_first + s_second
-    at_first = entering_state(pair_w, pair_s, hi)
+    at_first, done = entering_state(pair_w, pair_s, hi, work, work_inputs)
     at_second = w_first[:, None, None] * at_first + s_first
     keep = jnp.where(first, at_first, at_second)
     give = jnp.where(first, at_second, at_first)
     got = swap(give.astype(jnp.bfloat16), lo).astype(jnp.float32)
     lower = jnp.where(first, keep, got)
     upper = jnp.where(first, got, keep)
-    return jnp.concatenate([lower, upper], axis=0).reshape(shape)
+    return jnp.concatenate([lower, upper], axis=0).reshape(shape), done
 
 
 def body(
@@ -190,17 +204,26 @@
         log_rates.reshape(blocks, BLK, groups_here, per_group),
     )
     if blocks == 1:
-        diagonal, cumulative, local_state = block_parts(*(x[0] for x in inputs_all))
+        inner_block, b_block, c_block, step_block, rate_block = (x[0] for x in inputs_all)
+        cumulative = jnp.cumsum(rate_block, axis=0)
+        local_state = state_of(inner_block, b_block, step_block, cumulative)
+        state_in, diagonal = entering_pairs(
+            cumulative[-1],
+            local_state,
+            "clo",
+            "chi",
+            lambda x, b, c: diagonal_of(x, b, c, step_block, cumulative),
+            (inner_block, b_block, c_block),
+        )
         partial_heads = diagonal[None]
         factors = cumulative[None]
-        device_total = cumulative[-1]
     else:
         start_state = jnp.zeros((groups_here, per_group, HEAD_DIM, STATE), jnp.float32)
         start_total = jnp.zeros((groups_here, per_group), jnp.float32)
         (local_state, device_total), (partial_heads, factors) = lax.scan(
             block_local, (start_state, start_total), inputs_all
         )
-    state_in = entering_pairs(device_total, local_state, "clo", "chi")
+        state_in = entering_pairs(device_total, local_state, "clo", "chi")[0]
     correction = jax.vmap(apply_state, in_axes=(0, None, 0))(c_all, state_in, factors)
     width_here = groups_here * per_group * HEAD_DIM
     mixed_heads = (partial_heads + correction).reshape(tokens, width_here) + jnp.repeat(

time: 137 us -> 141 us (1.029)
  waiting for transfers between devices: 29.5 us -> 35.4 us
  local copies, waits for them, and re-layouts: 18.8 us -> 14.3 us
  matrix products: 23.8 us -> 26.6 us
    ppermute x10, waiting for transfers between devices: 25.4 us -> 28.9 us  [swap(): return lax.ppermute(value, axis, [(0, 1), (1, 0)])]
    dot_general x4, matrix products: 9.37 us -> 11.9 us  [reduce_rows(): jnp.dot(normed, out_weight[:, c * step:(c + 1) * step], preferred_element...]
    ppermute x4, waiting for transfers between devices: 4.09 us -> 6.52 us  [shifted(): return lax.ppermute(value, axis, pairs)]
    unnamed x39 -> x45, local copies, waits for them, and re-layouts: 12.6 us -> 10.6 us
    slice x2, local copies, waits for them, and re-layouts: 1.94 us -> 0.04 us  [unpack(): state = packed[:count].astype(jnp.float32).reshape(state_shape)]
    convert_element_type x3, other arithmetic: 1.43 us -> 0.01 us  [unpack(): flat = packed[count:].reshape(-1).astype(jnp.float32)]
    another operation x3 -> x2, other arithmetic: 3.04 us -> 2.32 us
  transfers between devices with their start and end apart: 14 -> 14, of which waited for: 6 -> 8; matrix products, arithmetic and copies ran while one was open for 26% -> 23% of each run, Pallas kernels for 0% -> 0%
where the time goes in v9:
time: 141 us; the launch traced here: 140 us
  waiting for transfers between devices  35.4 us (25%)
  starting transfers between devices  31.9 us (23%)
  other arithmetic  31.1 us (22%)
  matrix products  26.6 us (19%)
  local copies, waits for them, and re-layouts  14.3 us (10%)
    ppermute x10, waiting for transfers between devices, swap(): return lax.ppermute(value, axis, [(0, 1), (1, 0)])  28.9 us
    ppermute x4, starting transfers between devices, shifted(): return lax.ppermute(value, axis, pairs)  24 us
    dot_general x4, matrix products, reduce_rows(): jnp.dot(normed, out_weight[:, c * step:(c + 1) * step], preferred_element...  11.9 us
    convert_element_type x2, other arithmetic, conv_silu(): return lax.optimization_barrier(jax.nn.silu(summed).astype(jnp.bfloat16))  11.8 us
    unnamed x45, local copies, waits for them, and re-layouts  10.6 us
    dot_general x1, matrix products, diagonal_of(): jnp.einsum('ghij,jghp->ighp', mixing, inner_block, preferred_element_type...  10.5 us
    ppermute x10, starting transfers between devices, swap(): return lax.ppermute(value, axis, [(0, 1), (1, 0)])  7.89 us
    ppermute x4, waiting for transfers between devices, shifted(): return lax.ppermute(value, axis, pairs)  6.52 us
  transfers between devices with their start and end apart: 14, of which 8 were waited for; matrix products, arithmetic and copies ran while one was open for 23% of the time, Pallas kernels for 0%

profile of v9, /device:TPU:0, one launch (start us, length us, event | category | flops | bytes accessed | tf_op | source)
XLA Modules:
  0.0 140.0 jit_solution(13387097757369749738)
XLA Ops:
  1.6 4.8 %collective-permute-start = (bf16[3,2560]{1,0:T(4,128)(2,1)S(1)}, bf16[3,2560]{1,0:T(4,128)(2,1)S(1)}, u32[]{:S(2)}, u32[]{:S(2)}) collective-permute-start(bf16[3,2560]{1,0:T(4,128)(2,1)S(1)} %pad_maximum_fusion.6), channel_id=1, source_target_pairs={{0,4},{4,8},{8,12},{12,16},{16,20},{20,24},{24,28},{1,5},{5,9},{9,... | collective-permute-start | bytes 46088 | tf_op jit(solution)/shard_map/ppermute | solution.py:23
  8.0 2.3 %reduce-window.6 = f32[16,2,4,128]{3,0,1,2:T(8,128)S(1)} reduce-window(f32[16,2,4,128]{3,0,1,2:T(8,128)S(1)} %bitcast.238, f32[]{:T(128)} %constant.68.clone.1), window={size=1x1x1x128 pad=0_0x0_0x0_0x127_0}, to_apply=%region_0.1 | reduce-window | flops 2080768 | bytes 131076 | tf_op jit(solution)/shard_map/reduce-window
  12.5 1.3 bitcast_convert_fusion.3
  13.9 3.9 %copy.64 = bf16[512,2048]{0,1:T(8,128)(2,1)} copy(bf16[512,2048]{1,0:T(8,128)(2,1)} %param.12) | data formatting | bytes 4194304 | tf_op args[0]
  18.9 9.7 %multiply_convert_fusion.3 = bf16[512,2048]{0,1:T(8,128)(2,1)S(1)} fusion(bf16[512,2048]{0,1:T(8,128)(2,1)} %copy.64, bf16[3,2048]{0,1:T(8,128)(2,1)S(1)} %copy.63, f32[2048]{0:T(1024)S(1)} %bitcast.241, f32[2048]{0:T(1024)S(1)} %bitcast.242, f32[2048]{0:T(1024)S(1)} %bitcast.240, f32[2048]{0:T(1024)S(1)} %bitcast.239, f32[2048]{0:T(1024)S(1)} %convert_element_type.235), kind=kLoop, calls=%fused_computation.25 | loop fusion | flops 27262976 | bytes 4247552 | tf_op jit(solution)/shard_map/convert_element_type | solution.py:32
  28.9 2.0 %multiply_convert_fusion.7 = bf16[512,2,256]{0,2,1:T(8,128)(2,1)S(1)} fusion(bf16[512,2,256]{0,2,1:T(8,128)(2,1)S(1)} %copy.71, bf16[3,2,256]{0,2,1:T(8,128)(2,1)S(1)} %bitcast.234, f32[2,256]{1,0:T(2,128)} %get-tuple-element.40, f32[2,256]{1,0:T(2,128)} %get-tuple-element.41, f32[2,256]{1,0:T(2,128)S(1)} %get-tuple-element.39, ...), kind=kLoop, calls=%fused_computation.47 | loop fusion | flops 6815744 | bytes 1061888 | tf_op jit(solution)/shard_map/convert_element_type | solution.py:32
  33.1 1.6 %collective-permute-start.1 = (bf16[1040,128]{1,0:T(8,128)(2,1)S(1)}, bf16[1040,128]{1,0:T(8,128)(2,1)S(1)}, u32[]{:S(2)}, u32[]{:S(2)}) collective-permute-start(bf16[1040,128]{1,0:T(8,128)(2,1)S(1)} %pad_maximum_fusion.4), channel_id=1, source_target_pairs={{0,4},{4,0},{1,5},{5,1},{2,6},{6,2},{3,7},{7,3},{8,12},{12,8},{9,1... | collective-permute-start | bytes 798728 | tf_op jit(solution)/shard_map/ppermute | solution.py:242
  35.6 5.5 %collective-permute-done.1 = bf16[1040,128]{1,0:T(8,128)(2,1)S(1)} collective-permute-done((bf16[1040,128]{1,0:T(8,128)(2,1)S(1)}, bf16[1040,128]{1,0:T(8,128)(2,1)S(1)}, u32[]{:S(2)}, u32[]{:S(2)}) %collective-permute-start.1) | collective-permute-done | bytes 266272 | tf_op jit(solution)/shard_map/ppermute | solution.py:242
  43.8 1.2 fusion.43
  45.0 4.5 %collective-permute-start.3 = (bf16[1040,128]{1,0:T(8,128)(2,1)S(1)}, bf16[1040,128]{1,0:T(8,128)(2,1)S(1)}, u32[]{:S(2)}, u32[]{:S(2)}) collective-permute-start(bf16[1040,128]{1,0:T(8,128)(2,1)S(1)} %pad_maximum_fusion.5), channel_id=1, source_target_pairs={{0,16},{8,24},{1,17},{9,25},{2,18},{10,26},{3,19},{11,27},{4,20},{... | collective-permute-start | bytes 798728 | tf_op jit(solution)/shard_map/ppermute | solution.py:23
  49.6 3.5 %collective-permute-start.2 = (bf16[1040,128]{1,0:T(8,128)(2,1)S(1)}, bf16[1040,128]{1,0:T(8,128)(2,1)S(1)}, u32[]{:S(2)}, u32[]{:S(2)}) collective-permute-start(bf16[1040,128]{1,0:T(8,128)(2,1)S(1)} %pad_maximum_fusion.5), channel_id=1, source_target_pairs={{0,8},{8,16},{16,24},{1,9},{9,17},{17,25},{2,10},{10,18},{18,26},{... | collective-permute-start | bytes 798728 | tf_op jit(solution)/shard_map/ppermute | solution.py:23
  53.2 3.2 %collective-permute-done.3 = bf16[1040,128]{1,0:T(8,128)(2,1)S(1)} collective-permute-done((bf16[1040,128]{1,0:T(8,128)(2,1)S(1)}, bf16[1040,128]{1,0:T(8,128)(2,1)S(1)}, u32[]{:S(2)}, u32[]{:S(2)}) %collective-permute-start.3) | collective-permute-done | bytes 266272 | tf_op jit(solution)/shard_map/ppermute | solution.py:23
  56.4 3.4 %collective-permute-done.2 = bf16[1040,128]{1,0:T(8,128)(2,1)S(1)} collective-permute-done((bf16[1040,128]{1,0:T(8,128)(2,1)S(1)}, bf16[1040,128]{1,0:T(8,128)(2,1)S(1)}, u32[]{:S(2)}, u32[]{:S(2)}) %collective-permute-start.2) | collective-permute-done | bytes 266272 | tf_op jit(solution)/shard_map/ppermute | solution.py:23
  60.0 11.2 %collective-permute-start.4 = (bf16[16,64,128]{2,1,0:T(8,128)(2,1)S(1)}, bf16[16,64,128]{2,1,0:T(8,128)(2,1)S(1)}, u32[]{:S(2)}, u32[]{:S(2)}) collective-permute-start(bf16[16,64,128]{2,1,0:T(8,128)(2,1)S(1)} %fusion.44), channel_id=1, source_target_pairs={{0,16},{8,24},{1,17},{9,25},{2,18},{10,26},{3,19},{11,27},{4,20},{... | collective-permute-start | bytes 786440 | tf_op jit(solution)/shard_map/ppermute | solution.py:23
  71.2 1.4 %fusion.70 = f32[2,512,512]{2,1,0:T(8,128)S(1)} fusion(bf16[512,2,128]{0,2,1:T(8,128)(2,1)} %bitcast.221, bf16[512,2,128]{0,2,1:T(8,128)(2,1)S(1)} %bitcast.224), kind=kOutput, calls=%fused_computation.146 | convolution fusion | flops 134217728 | bytes 2621440 | tf_op jit(solution)/shard_map/ign,jgn->gij/dot_general | solution.py:42
  72.7 10.5 %fusion.17 = f32[512,2,16,64]{0,3,2,1:T(8,128)} fusion(bf16[512,2,16,64]{0,3,2,1:T(8,128)(2,1)S(1)} %bitcast.211, f32[2,16,512]{2,1,0:T(8,128)S(1)} %bitcast.237, f32[2,512,512]{2,1,0:T(8,128)S(1)} %fusion.70, f32[2,16,512]{2,1,0:T(8,128)S(1)} %copy-done.9, pred[512,512]{1,0:T(8,128)(4,1)S(1)} %iota_compare_fusion), kind=kOutput, calls=%fused_computation.30 | convolution fusion | flops 1115684864 | bytes 8781824 | tf_op jit(solution)/shard_map/ghij,jghp->ighp/dot_general | solution.py:46
  83.3 1.1 select_convert_fusion
  85.0 3.9 %copy.77 = bf16[512,2048]{0,1:T(8,128)(2,1)} copy(bf16[512,2048]{1,0:T(8,128)(2,1)} %param.14) | data formatting | bytes 4194304 | tf_op args[2]
  89.1 3.5 %collective-permute-done.5 = bf16[16,64,128]{2,1,0:T(8,128)(2,1)} collective-permute-done((bf16[16,64,128]{2,1,0:T(8,128)(2,1)}, bf16[16,64,128]{2,1,0:T(8,128)(2,1)}, u32[]{:S(2)}, u32[]{:S(2)}) %collective-permute-start.5) | collective-permute-done | bytes 262176 | tf_op jit(solution)/shard_map/ppermute | solution.py:242
  92.6 1.5 %convert_select_fusion.1 = (f32[16,64,128]{2,1,0:T(8,128)S(1)}, f32[16,64,128]{2,1,0:T(8,128)S(1)}) fusion(bf16[16,64,128]{2,1,0:T(8,128)(2,1)} %collective-permute-done.5, pred[]{:T(512)S(6)} %eq.3, f32[16,64,128]{2,1,0:T(8,128)} %bitcast.213, f32[16]{0:T(128)S(1)} %copy-done.10, bf16[16,64,128]{2,1,0:T(8,128)(2,1)} %bitcast.220, ...), kind=kLoop, calls=%fused_computation.51 | loop fusion | flops 1835008 | bytes 3671232 | tf_op jit(solution)/shard_map/jit(_where)/select_n | solution.py:158
  95.3 2.1 %fusion.6 = f32[1,512,2,16,64]{1,4,3,2,0:T(8,128)S(1)} fusion(f32[512,2,16,64]{0,3,2,1:T(8,128)S(1)} %copy-done.2, f32[512,2,16]{0,2,1:T(8,128)S(1)} %get-tuple-element.28, f32[2,16,64,128]{3,2,1,0:T(8,128)S(1)} %bitcast.214, bf16[512,2,128,1]{0,2,3,1:T(8,128)(2,1)S(1)} %bitcast.222), kind=kOutput, calls=%fused_computation.10 | convolution fusion | flops 1612709888 | bytes 9764864 | tf_op jit(solution)/shard_map/vmap(ign,ghpn->ighp)/dot_general | solution.py:63
  97.4 2.3 %bitcast_reduce_fusion = (f32[512,2]{0,1:T(2,128)S(1)}, f32[512,2048]{0,1:T(8,128)S(1)}) fusion(bf16[512,2048]{0,1:T(8,128)(2,1)S(1)} %copy-done, bf16[512,2048]{0,1:T(8,128)(2,1)S(1)} %multiply_convert_fusion.3, f32[2048]{0:T(1024)S(1)} %mul.296, f32[1,512,2,16,64]{1,4,3,2,0:T(8,128)S(1)} %fusion.6), kind=kLoop, calls=%fused_computation.14 | loop fusion | flops 11533312 | bytes 12595200 | tf_op jit(solution)/shard_map/reduce_sum | solution.py:234
  100.1 4.8 %fusion.22 = bf16[512,1024]{1,0:T(8,128)(2,1)S(1)} fusion(bf16[512,2048]{0,1:T(8,128)(2,1)S(1)} %fusion.8, bf16[2048,4096]{1,0:T(8,128)(2,1)} %param.23), kind=kOutput, calls=%fused_computation.36 | convolution fusion | flops 2148007936 | bytes 7340032 | tf_op jit(solution)/shard_map/dot_general | solution.py:266
  105.0 2.3 %fusion.25 = bf16[512,1024]{1,0:T(8,128)(2,1)S(1)} fusion(bf16[512,2048]{0,1:T(8,128)(2,1)S(1)} %fusion.8, bf16[2048,4096]{1,0:T(8,128)(2,1)S(1)} %bitcast.246), kind=kOutput, calls=%fused_computation.37 | convolution fusion | flops 2148007936 | bytes 7340032 | tf_op jit(solution)/shard_map/dot_general | solution.py:266
  107.4 2.3 %fusion.28 = bf16[512,1024]{1,0:T(8,128)(2,1)S(1)} fusion(bf16[512,2048]{0,1:T(8,128)(2,1)S(1)} %fusion.8, bf16[2048,4096]{1,0:T(8,128)(2,1)S(1)} %bitcast.246), kind=kOutput, calls=%fused_computation.38 | convolution fusion | flops 2148007936 | bytes 7340032 | tf_op jit(solution)/shard_map/dot_general | solution.py:266
  109.9 2.3 %fusion.31 = bf16[512,1024]{1,0:T(8,128)(2,1)S(1)} fusion(bf16[512,2048]{0,1:T(8,128)(2,1)S(1)} %fusion.8, bf16[2048,4096]{1,0:T(8,128)(2,1)S(1)} %bitcast.246), kind=kOutput, calls=%fused_computation.39 | convolution fusion | flops 2148007936 | bytes 7340032 | tf_op jit(solution)/shard_map/dot_general | solution.py:266
  113.8 1.6 %collective-permute-start.7 = (bf16[128,1024]{1,0:T(8,128)(2,1)S(1)}, bf16[128,1024]{1,0:T(8,128)(2,1)S(1)}, u32[]{:S(2)}, u32[]{:S(2)}) collective-permute-start(bf16[128,1024]{1,0:T(8,128)(2,1)S(1)} %fusion.46), channel_id=1, source_target_pairs={{0,2},{2,0},{1,3},{3,1},{4,6},{6,4},{5,7},{7,5},{8,10},{10,8},{9,1... | collective-permute-start | bytes 786440 | tf_op jit(solution)/shard_map/ppermute | solution.py:242
  116.4 1.6 %collective-permute-start.11 = (bf16[128,1024]{1,0:T(8,128)(2,1)S(1)}, bf16[128,1024]{1,0:T(8,128)(2,1)S(1)}, u32[]{:S(2)}, u32[]{:S(2)}) collective-permute-start(bf16[128,1024]{1,0:T(8,128)(2,1)S(1)} %fusion.48), channel_id=1, source_target_pairs={{0,2},{2,0},{1,3},{3,1},{4,6},{6,4},{5,7},{7,5},{8,10},{10,8},{9,1... | collective-permute-start | bytes 786440 | tf_op jit(solution)/shard_map/ppermute | solution.py:242
  118.8 4.2 %collective-permute-done.7 = bf16[128,1024]{1,0:T(8,128)(2,1)S(1)} collective-permute-done((bf16[128,1024]{1,0:T(8,128)(2,1)S(1)}, bf16[128,1024]{1,0:T(8,128)(2,1)S(1)}, u32[]{:S(2)}, u32[]{:S(2)}) %collective-permute-start.7) | collective-permute-done | bytes 262176 | tf_op jit(solution)/shard_map/ppermute | solution.py:242
  123.1 5.5 %collective-permute-done.9 = bf16[128,1024]{1,0:T(8,128)(2,1)S(1)} collective-permute-done((bf16[128,1024]{1,0:T(8,128)(2,1)S(1)}, bf16[128,1024]{1,0:T(8,128)(2,1)S(1)}, u32[]{:S(2)}, u32[]{:S(2)}) %collective-permute-start.9) | collective-permute-done | bytes 262176 | tf_op jit(solution)/shard_map/ppermute | solution.py:242
  128.7 5.5 %collective-permute-done.11 = bf16[128,1024]{1,0:T(8,128)(2,1)S(1)} collective-permute-done((bf16[128,1024]{1,0:T(8,128)(2,1)S(1)}, bf16[128,1024]{1,0:T(8,128)(2,1)S(1)}, u32[]{:S(2)}, u32[]{:S(2)}) %collective-permute-start.11) | collective-permute-done | bytes 262176 | tf_op jit(solution)/shard_map/ppermute | solution.py:242
  134.3 4.6 %collective-permute-done.13 = bf16[128,1024]{1,0:T(8,128)(2,1)S(1)} collective-permute-done((bf16[128,1024]{1,0:T(8,128)(2,1)S(1)}, bf16[128,1024]{1,0:T(8,128)(2,1)S(1)}, u32[]{:S(2)}, u32[]{:S(2)}) %collective-permute-start.13) | collective-permute-done | bytes 262176 | tf_op jit(solution)/shard_map/ppermute | solution.py:242
  (125 shorter events, 20.0 us)
Async XLA Ops:
  0.0 17.8 %copy-start.8 = (bf16[512,2,256]{2,1,0:T(2,128)(2,1)S(1)}, bf16[512,2,256]{2,1,0:T(2,128)(2,1)}, u32[]{:S(2)}) copy-start(bf16[512,2,256]{2,1,0:T(2,128)(2,1)} %param.13) | copy-start | bytes 1572868
  0.0 18.5 %copy-start.11 = (bf16[2048]{0:T(1024)(128)(2,1)S(1)}, bf16[2048]{0:T(1024)(128)(2,1)}, u32[]{:S(2)}) copy-start(bf16[2048]{0:T(1024)(128)(2,1)} %param.18) | copy-start | bytes 12292
  0.0 18.5 %copy-start.14 = (bf16[2,256]{1,0:T(2,128)(2,1)S(1)}, bf16[2,256]{1,0:T(2,128)(2,1)}, u32[]{:S(2)}) copy-start(bf16[2,256]{1,0:T(2,128)(2,1)} %param.19) | copy-start | bytes 3076
  1.6 17.0 %collective-permute-start = (bf16[3,2560]{1,0:T(4,128)(2,1)S(1)}, bf16[3,2560]{1,0:T(4,128)(2,1)S(1)}, u32[]{:S(2)}, u32[]{:S(2)}) collective-permute-start(bf16[3,2560]{1,0:T(4,128)(2,1)S(1)} %pad_maximum_fusion.6), channel_id=1, source_target_pairs={{0,4},{4,8},{8,12},{12,16},{16,20},{20,24},{24,28},{1,5},{5,9},{9,... | collective-permute-start | bytes 46088 | tf_op jit(solution)/shard_map/ppermute | solution.py:23
  33.1 7.9 %collective-permute-start.1 = (bf16[1040,128]{1,0:T(8,128)(2,1)S(1)}, bf16[1040,128]{1,0:T(8,128)(2,1)S(1)}, u32[]{:S(2)}, u32[]{:S(2)}) collective-permute-start(bf16[1040,128]{1,0:T(8,128)(2,1)S(1)} %pad_maximum_fusion.4), channel_id=1, source_target_pairs={{0,4},{4,0},{1,5},{5,1},{2,6},{6,2},{3,7},{7,3},{8,12},{12,8},{9,1... | collective-permute-start | bytes 798728 | tf_op jit(solution)/shard_map/ppermute | solution.py:242
  42.4 28.9 %copy-start.6 = (bf16[512,1,256]{0,2,1:T(8,128)(2,1)S(1)}, bf16[512,1,256]{0,2,1:T(8,128)(2,1)}, u32[]{:S(2)}) copy-start(bf16[512,1,256]{0,2,1:T(8,128)(2,1)} %copy-done.5) | copy-start | bytes 786436
  42.4 30.3 %copy-start.9 = (f32[2,16,512]{2,1,0:T(8,128)S(1)}, f32[2,16,512]{2,1,0:T(8,128)}, u32[]{:S(2)}) copy-start(f32[2,16,512]{2,1,0:T(8,128)} %get-tuple-element.30) | copy-start | bytes 196612
  45.0 11.3 %collective-permute-start.3 = (bf16[1040,128]{1,0:T(8,128)(2,1)S(1)}, bf16[1040,128]{1,0:T(8,128)(2,1)S(1)}, u32[]{:S(2)}, u32[]{:S(2)}) collective-permute-start(bf16[1040,128]{1,0:T(8,128)(2,1)S(1)} %pad_maximum_fusion.5), channel_id=1, source_target_pairs={{0,16},{8,24},{1,17},{9,25},{2,18},{10,26},{3,19},{11,27},{4,20},{... | collective-permute-start | bytes 798728 | tf_op jit(solution)/shard_map/ppermute | solution.py:23
  49.6 10.1 %collective-permute-start.2 = (bf16[1040,128]{1,0:T(8,128)(2,1)S(1)}, bf16[1040,128]{1,0:T(8,128)(2,1)S(1)}, u32[]{:S(2)}, u32[]{:S(2)}) collective-permute-start(bf16[1040,128]{1,0:T(8,128)(2,1)S(1)} %pad_maximum_fusion.5), channel_id=1, source_target_pairs={{0,8},{8,16},{16,24},{1,9},{9,17},{17,25},{2,10},{10,18},{18,26},{... | collective-permute-start | bytes 798728 | tf_op jit(solution)/shard_map/ppermute | solution.py:23
  53.2 30.0 %copy-start.1 = (f32[1024,128]{1,0:T(8,128)}, f32[1024,128]{1,0:T(8,128)S(1)}, u32[]{:S(2)}) copy-start(f32[1024,128]{1,0:T(8,128)S(1)} %slice_convert_fusion) | copy-start | bytes 1572868
  59.9 23.4 %copy-start.3 = (bf16[1024,128]{1,0:T(8,128)(2,1)}, bf16[1024,128]{1,0:T(8,128)(2,1)S(1)}, u32[]{:S(2)}) copy-start(bf16[1024,128]{1,0:T(8,128)(2,1)S(1)} %slice.205) | copy-start | bytes 786436
  60.0 23.2 %collective-permute-start.4 = (bf16[16,64,128]{2,1,0:T(8,128)(2,1)S(1)}, bf16[16,64,128]{2,1,0:T(8,128)(2,1)S(1)}, u32[]{:S(2)}, u32[]{:S(2)}) collective-permute-start(bf16[16,64,128]{2,1,0:T(8,128)(2,1)S(1)} %fusion.44), channel_id=1, source_target_pairs={{0,16},{8,24},{1,17},{9,25},{2,18},{10,26},{3,19},{11,27},{4,20},{... | collective-permute-start | bytes 786440 | tf_op jit(solution)/shard_map/ppermute | solution.py:23
  72.7 10.6 %copy-start.10 = (f32[16]{0:T(128)S(1)}, f32[16]{0:T(128)}, u32[]{:S(2)}) copy-start(f32[16]{0:T(128)} %get-tuple-element.25) | copy-start | bytes 196
  83.2 5.7 %copy-start.15 = (f32[32]{0:T(128)S(1)}, f32[32]{0:T(128)}, u32[]{:S(2)}) copy-start(f32[32]{0:T(128)} %param.21) | copy-start | bytes 388
  83.2 5.9 %copy-start.12 = (bf16[2048]{0:T(1024)(128)(2,1)S(1)}, bf16[2048]{0:T(1024)(128)(2,1)}, u32[]{:S(2)}) copy-start(bf16[2048]{0:T(1024)(128)(2,1)} %param.22) | copy-start | bytes 12292
  83.2 1.1 copy-start.7
  84.4 8.3 %collective-permute-start.5 = (bf16[16,64,128]{2,1,0:T(8,128)(2,1)}, bf16[16,64,128]{2,1,0:T(8,128)(2,1)}, u32[]{:S(2)}, u32[]{:S(2)}) collective-permute-start(bf16[16,64,128]{2,1,0:T(8,128)(2,1)} %select_convert_fusion), channel_id=1, source_target_pairs={{0,4},{4,0},{1,5},{5,1},{2,6},{6,2},{3,7},{7,3},{8,12},{12,8},{9,1... | collective-permute-start | bytes 786440 | tf_op jit(solution)/shard_map/ppermute | solution.py:242
  89.1 6.1 %copy-start.2 = (f32[512,2,16,64]{0,3,2,1:T(8,128)S(1)}, f32[512,2,16,64]{0,3,2,1:T(8,128)}, u32[]{:S(2)}) copy-start(f32[512,2,16,64]{0,3,2,1:T(8,128)} %fusion.17) | copy-start | bytes 12582916
  89.1 6.1 %copy-start.4 = (bf16[512,1,256]{0,2,1:T(8,128)(2,1)S(1)}, bf16[512,1,256]{0,2,1:T(8,128)(2,1)}, u32[]{:S(2)}) copy-start(bf16[512,1,256]{0,2,1:T(8,128)(2,1)} %get-tuple-element.26) | copy-start | bytes 786436
  95.2 2.1 %copy-start = (bf16[512,2048]{0,1:T(8,128)(2,1)S(1)}, bf16[512,2048]{0,1:T(8,128)(2,1)}, u32[]{:S(2)}) copy-start(bf16[512,2048]{0,1:T(8,128)(2,1)} %copy.77) | copy-start | bytes 6291460
  97.3 7.6 %slice-start = ((s8[16777216]{0:T(1024)(128)(4,1)}), s8[4194304]{0:T(1024)(128)(4,1)S(1)}, s32[]{:S(2)}) async-start(s8[16777216]{0:T(1024)(128)(4,1)} %bitcast.245), calls=%async_computation | async-start | bytes 8388608
  97.4 7.6 %slice-start.1 = ((s8[16777216]{0:T(1024)(128)(4,1)}), s8[4194304]{0:T(1024)(128)(4,1)S(1)}, s32[]{:S(2)}) async-start(s8[16777216]{0:T(1024)(128)(4,1)} %bitcast.245), calls=%async_computation.1 | async-start | bytes 8388608
  99.7 5.3 %slice-start.2 = ((s8[16777216]{0:T(1024)(128)(4,1)}), s8[4194304]{0:T(1024)(128)(4,1)S(1)}, s32[]{:S(2)}) async-start(s8[16777216]{0:T(1024)(128)(4,1)} %bitcast.245), calls=%async_computation.2 | async-start | bytes 8388608
  100.1 4.9 %slice-start.3 = ((s8[16777216]{0:T(1024)(128)(4,1)}), s8[4194304]{0:T(1024)(128)(4,1)S(1)}, s32[]{:S(2)}) async-start(s8[16777216]{0:T(1024)(128)(4,1)} %bitcast.245), calls=%async_computation.3 | async-start | bytes 8388608
  109.8 3.8 %collective-permute-start.6 = (bf16[2,128,1024]{2,1,0:T(8,128)(2,1)S(1)}, bf16[2,128,1024]{2,1,0:T(8,128)(2,1)S(1)}, u32[]{:S(2)}, u32[]{:S(2)}) collective-permute-start(bf16[2,128,1024]{2,1,0:T(8,128)(2,1)S(1)} %dynamic-slice_bitcast_fusion.3), channel_id=1, source_target_pairs={{0,1},{1,0},{2,3},{3,2},{4,5},{5,4},{6,7},{7,6},{8,9},{9,8},{10,11... | collective-permute-start | bytes 1572872 | tf_op jit(solution)/shard_map/ppermute | solution.py:242
  112.3 3.1 %collective-permute-start.8 = (bf16[2,128,1024]{2,1,0:T(8,128)(2,1)S(1)}, bf16[2,128,1024]{2,1,0:T(8,128)(2,1)S(1)}, u32[]{:S(2)}, u32[]{:S(2)}) collective-permute-start(bf16[2,128,1024]{2,1,0:T(8,128)(2,1)S(1)} %dynamic-slice_bitcast_fusion.2), channel_id=1, source_target_pairs={{0,1},{1,0},{2,3},{3,2},{4,5},{5,4},{6,7},{7,6},{8,9},{9,8},{10,11... | collective-permute-start | bytes 1572872 | tf_op jit(solution)/shard_map/ppermute | solution.py:242
  112.9 3.3 %collective-permute-start.10 = (bf16[2,128,1024]{2,1,0:T(8,128)(2,1)S(1)}, bf16[2,128,1024]{2,1,0:T(8,128)(2,1)S(1)}, u32[]{:S(2)}, u32[]{:S(2)}) collective-permute-start(bf16[2,128,1024]{2,1,0:T(8,128)(2,1)S(1)} %dynamic-slice_bitcast_fusion.1), channel_id=1, source_target_pairs={{0,1},{1,0},{2,3},{3,2},{4,5},{5,4},{6,7},{7,6},{8,9},{9,8},{10,11... | collective-permute-start | bytes 1572872 | tf_op jit(solution)/shard_map/ppermute | solution.py:242
  113.0 5.0 %collective-permute-start.12 = (bf16[2,128,1024]{2,1,0:T(8,128)(2,1)S(1)}, bf16[2,128,1024]{2,1,0:T(8,128)(2,1)S(1)}, u32[]{:S(2)}, u32[]{:S(2)}) collective-permute-start(bf16[2,128,1024]{2,1,0:T(8,128)(2,1)S(1)} %dynamic-slice_bitcast_fusion), channel_id=1, source_target_pairs={{0,1},{1,0},{2,3},{3,2},{4,5},{5,4},{6,7},{7,6},{8,9},{9,8},{10,11... | collective-permute-start | bytes 1572872 | tf_op jit(solution)/shard_map/ppermute | solution.py:242
  113.8 9.2 %collective-permute-start.7 = (bf16[128,1024]{1,0:T(8,128)(2,1)S(1)}, bf16[128,1024]{1,0:T(8,128)(2,1)S(1)}, u32[]{:S(2)}, u32[]{:S(2)}) collective-permute-start(bf16[128,1024]{1,0:T(8,128)(2,1)S(1)} %fusion.46), channel_id=1, source_target_pairs={{0,2},{2,0},{1,3},{3,1},{4,6},{6,4},{5,7},{7,5},{8,10},{10,8},{9,1... | collective-permute-start | bytes 786440 | tf_op jit(solution)/shard_map/ppermute | solution.py:242
  115.6 13.0 %collective-permute-start.9 = (bf16[128,1024]{1,0:T(8,128)(2,1)S(1)}, bf16[128,1024]{1,0:T(8,128)(2,1)S(1)}, u32[]{:S(2)}, u32[]{:S(2)}) collective-permute-start(bf16[128,1024]{1,0:T(8,128)(2,1)S(1)} %fusion.47), channel_id=1, source_target_pairs={{0,2},{2,0},{1,3},{3,1},{4,6},{6,4},{5,7},{7,5},{8,10},{10,8},{9,1... | collective-permute-start | bytes 786440 | tf_op jit(solution)/shard_map/ppermute | solution.py:242
  116.4 17.8 %collective-permute-start.11 = (bf16[128,1024]{1,0:T(8,128)(2,1)S(1)}, bf16[128,1024]{1,0:T(8,128)(2,1)S(1)}, u32[]{:S(2)}, u32[]{:S(2)}) collective-permute-start(bf16[128,1024]{1,0:T(8,128)(2,1)S(1)} %fusion.48), channel_id=1, source_target_pairs={{0,2},{2,0},{1,3},{3,1},{4,6},{6,4},{5,7},{7,5},{8,10},{10,8},{9,1... | collective-permute-start | bytes 786440 | tf_op jit(solution)/shard_map/ppermute | solution.py:242
  118.2 20.7 %collective-permute-start.13 = (bf16[128,1024]{1,0:T(8,128)(2,1)S(1)}, bf16[128,1024]{1,0:T(8,128)(2,1)S(1)}, u32[]{:S(2)}, u32[]{:S(2)}) collective-permute-start(bf16[128,1024]{1,0:T(8,128)(2,1)S(1)} %fusion.49), channel_id=1, source_target_pairs={{0,2},{2,0},{1,3},{3,1},{4,6},{6,4},{5,7},{7,5},{8,10},{10,8},{9,1... | collective-permute-start | bytes 786440 | tf_op jit(solution)/shard_map/ppermute | solution.py:242
  (2 other events, 1.2 us)

commit v10 on v8

--- a/solution.py
+++ b/solution.py
@@ -1,6 +1,8 @@
 import jax
 import jax.numpy as jnp
 from jax import lax
+from jax.experimental import pallas as pl
+from jax.experimental.pallas import tpu as pltpu
 from jax.sharding import Mesh, PartitionSpec as P
 
 SSM_HEAD_COUNT = 128
@@ -31,6 +33,33 @@
         )
     return lax.optimization_barrier(jax.nn.silu(summed).astype(jnp.bfloat16))
 
+
+def conv_kernel(halo_ref, x_ref, w_ref, b_ref, o_ref, pad_ref):
+    rows = x_ref.shape[0]
+    pad_ref[0:8, :] = halo_ref[...].astype(jnp.float32)
+    pad_ref[8 : 8 + rows, :] = x_ref[...].astype(jnp.float32)
+    summed = b_ref[...].astype(jnp.float32)
+    for k in range(CONV):
+        summed = summed + w_ref[k : k + 1, :].astype(jnp.float32) * pad_ref[8 - (CONV - 1) + k : 8 - (CONV - 1) + k + rows, :]
+    o_ref[...] = jnp.transpose(jax.nn.silu(summed)).astype(o_ref.dtype)
+
+def conv_silu_kernel(halo, x, weight, bias):
+    rows, width = x.shape
+    block = 512 if width % 512 == 0 else width
+    halo8 = jnp.concatenate([jnp.zeros((8 - halo.shape[0], width), halo.dtype), halo], axis=0)
+    return pl.pallas_call(
+        conv_kernel,
+        grid=(width // block,),
+        in_specs=[
+            pl.BlockSpec((8, block), lambda j: (0, j)),
+            pl.BlockSpec((rows, block), lambda j: (0, j)),
+            pl.BlockSpec((CONV, block), lambda j: (0, j)),
+            pl.BlockSpec((1, block), lambda j: (0, j)),
+        ],
+        out_specs=pl.BlockSpec((block, rows), lambda j: (j, 0)),
+        out_shape=jax.ShapeDtypeStruct((width, rows), jnp.bfloat16),
+        scratch_shapes=[pltpu.VMEM((rows + 8, block), jnp.float32)],
+    )(halo8, x, weight, bias.reshape(1, width))
 
 def block_parts(inner_block, b_block, c_block, step_sizes, log_rates):
     length = inner_block.shape[0]
@@ -167,8 +196,8 @@
         [inner_input[tokens - margin :], state_input[tokens - margin :].reshape(margin, -1)], axis=1
     )
     halo = shifted(halo, ("chi", "clo"), 1)
-    inner_conv = conv_silu(
-        jnp.concatenate([halo[:, :inner_width], inner_input], axis=0), conv_inner, bias_inner, tokens
+    inner_conv = jnp.transpose(
+        conv_silu_kernel(halo[:, :inner_width], inner_input, conv_inner, bias_inner)
     )
     state_conv = conv_silu(
         jnp.concatenate([halo[:, inner_width:].reshape((margin,) + state_input.shape[1:]), state_input], axis=0),

time: 137 us -> 135 us (0.985); the launches traced: 135 us -> 135 us
  other arithmetic: 31.3 us -> 19.1 us
  waiting for transfers between devices: 29.5 us -> 38.6 us
  local copies, waits for them, and re-layouts: 18.8 us -> 12.3 us
  Pallas kernels: 0 us -> 6.01 us
  matrix products: 23.8 us -> 25.7 us
  starting transfers between devices: 30.8 us -> 32.5 us
    convert_element_type x2 -> x1, other arithmetic: 11.2 us -> 1.34 us  [conv_silu(): return lax.optimization_barrier(jax.nn.silu(summed).astype(jnp.bfloat16))]
    unnamed x39 -> x40, local copies, waits for them, and re-layouts: 12.6 us -> 5.64 us
    ppermute x10, waiting for transfers between devices: 25.4 us -> 31.9 us  [swap(): return lax.ppermute(value, axis, [(0, 1), (1, 0)])]
    pallas_call x0 -> x1, Pallas kernels: none -> 6.01 us  [conv_silu_kernel(): pl.pallas_call(conv_kernel, grid=(width // block,), in_specs=[pl.BlockSpe...]
    ppermute x4, waiting for transfers between devices: 4.09 us -> 6.67 us  [shifted(): return lax.ppermute(value, axis, pairs)]
    slice x2, local copies, waits for them, and re-layouts: 1.94 us -> 0.04 us  [unpack(): state = packed[:count].astype(jnp.float32).reshape(state_shape)]
    reshape x1 -> x3, local copies, waits for them, and re-layouts: 0.01 us -> 1.48 us  [the longest x1 1.29 us: conv_silu_kernel(): bias.reshape(1, width)]
    convert_element_type x3, other arithmetic: 1.43 us -> 0.01 us  [unpack(): flat = packed[count:].reshape(-1).astype(jnp.float32)]
  transfers between devices with their start and end apart: 14 -> 14, of which waited for: 6 -> 8; matrix products, arithmetic and copies ran while one was open for 26% -> 16% of each run, Pallas kernels for 0% -> 0%
where the time goes in v10:
time: 135 us
  waiting for transfers between devices  38.6 us (29%)
  starting transfers between devices  32.5 us (24%)
  matrix products  25.7 us (19%)
  other arithmetic  19.1 us (14%)
  local copies, waits for them, and re-layouts  12.3 us (9%)
  Pallas kernels  6.01 us (4%)
    ppermute x10, waiting for transfers between devices, swap(): return lax.ppermute(value, axis, [(0, 1), (1, 0)])  31.9 us
    ppermute x4, starting transfers between devices, shifted(): return lax.ppermute(value, axis, pairs)  24.5 us
    dot_general x1, matrix products, block_parts(): jnp.einsum('ghij,jghp->ighp', mixing, inner_block, preferred_element_type...  10.5 us
    dot_general x4, matrix products, reduce_rows(): jnp.dot(normed, out_weight[:, c * step:(c + 1) * step], preferred_element...  9.57 us
    ppermute x10, starting transfers between devices, swap(): return lax.ppermute(value, axis, [(0, 1), (1, 0)])  7.95 us
    ppermute x4, waiting for transfers between devices, shifted(): return lax.ppermute(value, axis, pairs)  6.67 us
    pallas_call x1, Pallas kernels, conv_silu_kernel(): pl.pallas_call(conv_kernel, grid=(width // block,), in_specs=[pl.BlockSpe...  6.01 us
    unnamed x40, local copies, waits for them, and re-layouts  5.64 us
  transfers between devices with their start and end apart: 14, of which 8 were waited for; matrix products, arithmetic and copies ran while one was open for 16% of the time, Pallas kernels for 0%

profile of v10, /device:TPU:0, one launch (start us, length us, event | category | flops | bytes accessed | tf_op | source)
XLA Modules:
  0.0 134.8 jit_solution(4203324661052045773)
XLA Ops:
  1.5 4.8 %collective-permute-start = (bf16[3,2560]{1,0:T(4,128)(2,1)S(1)}, bf16[3,2560]{1,0:T(4,128)(2,1)S(1)}, u32[]{:S(2)}, u32[]{:S(2)}) collective-permute-start(bf16[3,2560]{1,0:T(4,128)(2,1)S(1)} %pad_maximum_fusion.5), channel_id=1, source_target_pairs={{0,4},{4,8},{8,12},{12,16},{16,20},{20,24},{24,28},{1,5},{5,9},{9,... | collective-permute-start | bytes 46088 | tf_op jit(solution)/shard_map/ppermute | solution.py:25
  7.9 2.3 %reduce-window.6 = f32[16,2,4,128]{3,0,1,2:T(8,128)S(1)} reduce-window(f32[16,2,4,128]{3,0,1,2:T(8,128)S(1)} %bitcast.238, f32[]{:T(128)} %constant.65.clone.1), window={size=1x1x1x128 pad=0_0x0_0x0_0x127_0}, to_apply=%region_0.1 | reduce-window | flops 2080768 | bytes 131076 | tf_op jit(solution)/shard_map/reduce-window
  12.3 1.3 copy.44
  14.3 1.3 reshape.137.b_ref
  15.8 1.3 multiply_convert_fusion.6
  18.6 6.0 %shard_map.118 = bf16[2048,512]{1,0:T(8,128)(2,1)} custom-call(bf16[8,2048]{1,0:T(8,128)(2,1)} %concatenate.28.halo_ref, bf16[512,2048]{1,0:T(8,128)(2,1)} %x_ref.1, bf16[4,2048]{1,0:T(4,128)(2,1)} %w_ref.1, bf16[1,2048]{1,0:T(2,128)(2,1)} %reshape.137.b_ref), custom_call_target="tpu_custom_call" | custom-call | tf_op jit(solution)/shard_map/pallas_call | solution.py:50
  24.6 2.3 %fusion.17 = f32[2,16,64,128]{3,2,1,0:T(8,128)S(1)} fusion(bf16[512,2,128,1]{0,2,3,1:T(8,128)(2,1)S(1)} %bitcast.221, bf16[512,2,16,64]{0,3,2,1:T(8,128)(2,1)} %bitcast.210, f32[512,2,16]{0,2,1:T(8,128)S(1)} %get-tuple-element.17), kind=kOutput, calls=%fused_computation.25 | convolution fusion | flops 271581184 | bytes 3473408 | tf_op jit(solution)/shard_map/jghp,jgn->ghpn/dot_general | solution.py:81
  27.0 1.6 %collective-permute-start.1 = (bf16[1040,128]{1,0:T(8,128)(2,1)S(1)}, bf16[1040,128]{1,0:T(8,128)(2,1)S(1)}, u32[]{:S(2)}, u32[]{:S(2)}) collective-permute-start(bf16[1040,128]{1,0:T(8,128)(2,1)S(1)} %pad_maximum_fusion.3), channel_id=1, source_target_pairs={{0,4},{4,0},{1,5},{5,1},{2,6},{6,2},{3,7},{7,3},{8,12},{12,8},{9,1... | collective-permute-start | bytes 798728 | tf_op jit(solution)/shard_map/ppermute | solution.py:248
  28.7 6.2 %collective-permute-done.1 = bf16[1040,128]{1,0:T(8,128)(2,1)S(1)} collective-permute-done((bf16[1040,128]{1,0:T(8,128)(2,1)S(1)}, bf16[1040,128]{1,0:T(8,128)(2,1)S(1)}, u32[]{:S(2)}, u32[]{:S(2)}) %collective-permute-start.1) | collective-permute-done | bytes 266272 | tf_op jit(solution)/shard_map/ppermute | solution.py:248
  35.5 4.5 %collective-permute-start.3 = (bf16[1040,128]{1,0:T(8,128)(2,1)S(1)}, bf16[1040,128]{1,0:T(8,128)(2,1)S(1)}, u32[]{:S(2)}, u32[]{:S(2)}) collective-permute-start(bf16[1040,128]{1,0:T(8,128)(2,1)S(1)} %pad_maximum_fusion.4), channel_id=1, source_target_pairs={{0,16},{8,24},{1,17},{9,25},{2,18},{10,26},{3,19},{11,27},{4,20},{... | collective-permute-start | bytes 798728 | tf_op jit(solution)/shard_map/ppermute | solution.py:25
  40.0 3.5 %collective-permute-start.2 = (bf16[1040,128]{1,0:T(8,128)(2,1)S(1)}, bf16[1040,128]{1,0:T(8,128)(2,1)S(1)}, u32[]{:S(2)}, u32[]{:S(2)}) collective-permute-start(bf16[1040,128]{1,0:T(8,128)(2,1)S(1)} %pad_maximum_fusion.4), channel_id=1, source_target_pairs={{0,8},{8,16},{16,24},{1,9},{9,17},{17,25},{2,10},{10,18},{18,26},{... | collective-permute-start | bytes 798728 | tf_op jit(solution)/shard_map/ppermute | solution.py:25
  43.5 3.3 %collective-permute-done.3 = bf16[1040,128]{1,0:T(8,128)(2,1)S(1)} collective-permute-done((bf16[1040,128]{1,0:T(8,128)(2,1)S(1)}, bf16[1040,128]{1,0:T(8,128)(2,1)S(1)}, u32[]{:S(2)}, u32[]{:S(2)}) %collective-permute-start.3) | collective-permute-done | bytes 266272 | tf_op jit(solution)/shard_map/ppermute | solution.py:25
  46.8 3.4 %collective-permute-done.2 = bf16[1040,128]{1,0:T(8,128)(2,1)S(1)} collective-permute-done((bf16[1040,128]{1,0:T(8,128)(2,1)S(1)}, bf16[1040,128]{1,0:T(8,128)(2,1)S(1)}, u32[]{:S(2)}, u32[]{:S(2)}) %collective-permute-start.2) | collective-permute-done | bytes 266272 | tf_op jit(solution)/shard_map/ppermute | solution.py:25
  52.4 11.7 %collective-permute-start.4 = (bf16[16,64,128]{2,1,0:T(8,128)(2,1)}, bf16[16,64,128]{2,1,0:T(8,128)(2,1)}, u32[]{:S(2)}, u32[]{:S(2)}) collective-permute-start(bf16[16,64,128]{2,1,0:T(8,128)(2,1)} %fusion.41), channel_id=1, source_target_pairs={{0,16},{8,24},{1,17},{9,25},{2,18},{10,26},{3,19},{11,27},{4,20},{... | collective-permute-start | bytes 786440 | tf_op jit(solution)/shard_map/ppermute | solution.py:25
  64.8 2.9 %copy.50 = bf16[512,2048]{0,1:T(8,128)(2,1)S(1)} copy(bf16[512,2048]{1,0:T(8,128)(2,1)} %param.14) | data formatting | bytes 4194304 | tf_op args[2]
  70.9 1.4 %select_convert_fusion = bf16[16,64,128]{2,1,0:T(8,128)(2,1)S(1)} fusion(f32[16,64,128]{2,1,0:T(8,128)S(1)} %bitcast.212, bf16[16,64,128]{2,1,0:T(8,128)(2,1)} %bitcast.218, bf16[16,64,128]{2,1,0:T(8,128)(2,1)S(1)} %bitcast.215, bf16[16,64,128]{2,1,0:T(8,128)(2,1)} %collective-permute-done.4, f32[16]{0:T(128)} %copy-done.11, f32[16]{0:T(128)} %copy-done.9, ...), kind=kLoop, calls=%fused_computation.73 | loop fusion | flops 1703936 | bytes 2622656 | tf_op jit(solution)/shard_map/convert_element_type | solution.py:172
  73.0 1.5 %fusion.67 = f32[2,512,512]{2,1,0:T(8,128)S(1)} fusion(bf16[512,2,128]{0,2,1:T(8,128)(2,1)} %bitcast.223, bf16[512,2,128]{0,2,1:T(8,128)(2,1)} %bitcast.222), kind=kOutput, calls=%fused_computation.133 | convolution fusion | flops 134217728 | bytes 2621440 | tf_op jit(solution)/shard_map/ign,jgn->gij/dot_general | solution.py:72
  74.6 5.8 %collective-permute-done.5 = bf16[16,64,128]{2,1,0:T(8,128)(2,1)S(1)} collective-permute-done((bf16[16,64,128]{2,1,0:T(8,128)(2,1)S(1)}, bf16[16,64,128]{2,1,0:T(8,128)(2,1)S(1)}, u32[]{:S(2)}, u32[]{:S(2)}) %collective-permute-start.5) | collective-permute-done | bytes 262176 | tf_op jit(solution)/shard_map/ppermute | solution.py:248
  80.3 1.4 %convert_select_fusion.1 = (f32[16,64,128]{2,1,0:T(8,128)S(1)}, f32[16,64,128]{2,1,0:T(8,128)S(1)}) fusion(bf16[16,64,128]{2,1,0:T(8,128)(2,1)S(1)} %collective-permute-done.5, pred[]{:T(512)S(6)} %eq.3, f32[16,64,128]{2,1,0:T(8,128)S(1)} %bitcast.213, f32[16]{0:T(128)S(1)} %copy-done.12, bf16[16,64,128]{2,1,0:T(8,128)(2,1)S(1)} %bitcast.219, ...), kind=kLoop, calls=%fused_computation.42 | loop fusion | flops 1835008 | bytes 3671232 | tf_op jit(solution)/shard_map/jit(_where)/select_n | solution.py:173
  81.9 1.9 %fusion.68 = f32[2,16,64,512]{3,2,1,0:T(8,128)S(1)} fusion(f32[2,16,64,128]{3,2,1,0:T(8,128)S(1)} %bitcast.220, bf16[512,2,128,1]{0,2,3,1:T(8,128)(2,1)S(1)} %bitcast.224), kind=kOutput, calls=%fused_computation.134 | convolution fusion | flops 1610612736 | bytes 5505024 | tf_op jit(solution)/shard_map/vmap(ign,ghpn->ighp)/dot_general | solution.py:88
  83.9 10.5 %fusion.6 = f32[1,512,2,16,64]{1,4,3,2,0:T(8,128)S(1)} fusion(f32[2,16,64,512]{3,2,1,0:T(8,128)S(1)} %fusion.68, bf16[512,2,16,64]{0,3,2,1:T(8,128)(2,1)S(1)} %bitcast.211, f32[2,16,512]{2,1,0:T(8,128)S(1)} %bitcast.237, f32[2,512,512]{2,1,0:T(8,128)S(1)} %fusion.67, f32[2,16,512]{2,1,0:T(8,128)S(1)} %get-tuple-element.18, ...), kind=kOutput, calls=%fused_computation.10 | convolution fusion | flops 1117782016 | bytes 13041664 | tf_op jit(solution)/shard_map/ghij,jghp->ighp/dot_general | solution.py:76
  94.4 2.3 %bitcast_reduce_fusion = (f32[512,2]{0,1:T(2,128)S(1)}, f32[512,2048]{0,1:T(8,128)S(1)}) fusion(bf16[512,2048]{0,1:T(8,128)(2,1)S(1)} %copy.50, bf16[2048,512]{1,0:T(8,128)(2,1)S(1)} %copy-done, f32[2048]{0:T(1024)S(1)} %copy-done.8, f32[1,512,2,16,64]{1,4,3,2,0:T(8,128)S(1)} %fusion.6), kind=kLoop, calls=%fused_computation.14 | loop fusion | flops 11533312 | bytes 12595200 | tf_op jit(solution)/shard_map/reduce_sum | solution.py:240
  97.2 2.4 %fusion.19 = bf16[512,1024]{1,0:T(8,128)(2,1)S(1)} fusion(bf16[512,2048]{0,1:T(8,128)(2,1)S(1)} %fusion.8, bf16[2048,4096]{1,0:T(8,128)(2,1)S(1)} %bitcast.242), kind=kOutput, calls=%fused_computation.27 | convolution fusion | flops 2148007936 | bytes 7340032 | tf_op jit(solution)/shard_map/dot_general | solution.py:272
  99.6 2.4 %fusion.22 = bf16[512,1024]{1,0:T(8,128)(2,1)S(1)} fusion(bf16[512,2048]{0,1:T(8,128)(2,1)S(1)} %fusion.8, bf16[2048,4096]{1,0:T(8,128)(2,1)S(1)} %bitcast.242), kind=kOutput, calls=%fused_computation.28 | convolution fusion | flops 2148007936 | bytes 7340032 | tf_op jit(solution)/shard_map/dot_general | solution.py:272
  102.0 2.4 %fusion.25 = bf16[512,1024]{1,0:T(8,128)(2,1)S(1)} fusion(bf16[512,2048]{0,1:T(8,128)(2,1)S(1)} %fusion.8, bf16[2048,4096]{1,0:T(8,128)(2,1)S(1)} %bitcast.242), kind=kOutput, calls=%fused_computation.29 | convolution fusion | flops 2148007936 | bytes 7340032 | tf_op jit(solution)/shard_map/dot_general | solution.py:272
  104.5 2.4 %fusion.28 = bf16[512,1024]{1,0:T(8,128)(2,1)S(1)} fusion(bf16[512,2048]{0,1:T(8,128)(2,1)S(1)} %fusion.8, bf16[2048,4096]{1,0:T(8,128)(2,1)S(1)} %bitcast.242), kind=kOutput, calls=%fused_computation.30 | convolution fusion | flops 2148007936 | bytes 7340032 | tf_op jit(solution)/shard_map/dot_general | solution.py:272
  108.5 1.6 %collective-permute-start.7 = (bf16[128,1024]{1,0:T(8,128)(2,1)S(1)}, bf16[128,1024]{1,0:T(8,128)(2,1)S(1)}, u32[]{:S(2)}, u32[]{:S(2)}) collective-permute-start(bf16[128,1024]{1,0:T(8,128)(2,1)S(1)} %fusion.43), channel_id=1, source_target_pairs={{0,2},{2,0},{1,3},{3,1},{4,6},{6,4},{5,7},{7,5},{8,10},{10,8},{9,1... | collective-permute-start | bytes 786440 | tf_op jit(solution)/shard_map/ppermute | solution.py:248
  111.1 1.6 %collective-permute-start.11 = (bf16[128,1024]{1,0:T(8,128)(2,1)S(1)}, bf16[128,1024]{1,0:T(8,128)(2,1)S(1)}, u32[]{:S(2)}, u32[]{:S(2)}) collective-permute-start(bf16[128,1024]{1,0:T(8,128)(2,1)S(1)} %fusion.45), channel_id=1, source_target_pairs={{0,2},{2,0},{1,3},{3,1},{4,6},{6,4},{5,7},{7,5},{8,10},{10,8},{9,1... | collective-permute-start | bytes 786440 | tf_op jit(solution)/shard_map/ppermute | solution.py:248
  113.5 4.2 %collective-permute-done.7 = bf16[128,1024]{1,0:T(8,128)(2,1)S(1)} collective-permute-done((bf16[128,1024]{1,0:T(8,128)(2,1)S(1)}, bf16[128,1024]{1,0:T(8,128)(2,1)S(1)}, u32[]{:S(2)}, u32[]{:S(2)}) %collective-permute-start.7) | collective-permute-done | bytes 262176 | tf_op jit(solution)/shard_map/ppermute | solution.py:248
  117.8 5.5 %collective-permute-done.9 = bf16[128,1024]{1,0:T(8,128)(2,1)S(1)} collective-permute-done((bf16[128,1024]{1,0:T(8,128)(2,1)S(1)}, bf16[128,1024]{1,0:T(8,128)(2,1)S(1)}, u32[]{:S(2)}, u32[]{:S(2)}) %collective-permute-start.9) | collective-permute-done | bytes 262176 | tf_op jit(solution)/shard_map/ppermute | solution.py:248
  123.4 5.5 %collective-permute-done.11 = bf16[128,1024]{1,0:T(8,128)(2,1)S(1)} collective-permute-done((bf16[128,1024]{1,0:T(8,128)(2,1)S(1)}, bf16[128,1024]{1,0:T(8,128)(2,1)S(1)}, u32[]{:S(2)}, u32[]{:S(2)}) %collective-permute-start.11) | collective-permute-done | bytes 262176 | tf_op jit(solution)/shard_map/ppermute | solution.py:248
  129.0 4.6 %collective-permute-done.13 = bf16[128,1024]{1,0:T(8,128)(2,1)S(1)} collective-permute-done((bf16[128,1024]{1,0:T(8,128)(2,1)S(1)}, bf16[128,1024]{1,0:T(8,128)(2,1)S(1)}, u32[]{:S(2)}, u32[]{:S(2)}) %collective-permute-start.13) | collective-permute-done | bytes 262176 | tf_op jit(solution)/shard_map/ppermute | solution.py:248
  (119 shorter events, 20.4 us)
Async XLA Ops:
  1.5 14.1 %collective-permute-start = (bf16[3,2560]{1,0:T(4,128)(2,1)S(1)}, bf16[3,2560]{1,0:T(4,128)(2,1)S(1)}, u32[]{:S(2)}, u32[]{:S(2)}) collective-permute-start(bf16[3,2560]{1,0:T(4,128)(2,1)S(1)} %pad_maximum_fusion.5), channel_id=1, source_target_pairs={{0,4},{4,8},{8,12},{12,16},{16,20},{20,24},{24,28},{1,5},{5,9},{9,... | collective-permute-start | bytes 46088 | tf_op jit(solution)/shard_map/ppermute | solution.py:25
  17.9 9.1 %copy-start.3 = (bf16[512,1,256]{0,2,1:T(8,128)(2,1)}, bf16[512,1,256]{0,2,1:T(8,128)(2,1)S(1)}, u32[]{:S(2)}) copy-start(bf16[512,1,256]{0,2,1:T(8,128)(2,1)S(1)} %get-tuple-element.15) | copy-start | bytes 786436
  27.0 7.9 %collective-permute-start.1 = (bf16[1040,128]{1,0:T(8,128)(2,1)S(1)}, bf16[1040,128]{1,0:T(8,128)(2,1)S(1)}, u32[]{:S(2)}, u32[]{:S(2)}) collective-permute-start(bf16[1040,128]{1,0:T(8,128)(2,1)S(1)} %pad_maximum_fusion.3), channel_id=1, source_target_pairs={{0,4},{4,0},{1,5},{5,1},{2,6},{6,2},{3,7},{7,3},{8,12},{12,8},{9,1... | collective-permute-start | bytes 798728 | tf_op jit(solution)/shard_map/ppermute | solution.py:248
  34.9 29.9 %copy-start.5 = (bf16[1040,128]{1,0:T(8,128)(2,1)}, bf16[1040,128]{1,0:T(8,128)(2,1)S(1)}, u32[]{:S(2)}) copy-start(bf16[1040,128]{1,0:T(8,128)(2,1)S(1)} %collective-permute-done.1) | copy-start | bytes 798724
  35.0 29.8 %copy-start.11 = (f32[16]{0:T(128)}, f32[16]{0:T(128)S(1)}, u32[]{:S(2)}) copy-start(f32[16]{0:T(128)S(1)} %get-tuple-element.13) | copy-start | bytes 196
  35.5 11.3 %collective-permute-start.3 = (bf16[1040,128]{1,0:T(8,128)(2,1)S(1)}, bf16[1040,128]{1,0:T(8,128)(2,1)S(1)}, u32[]{:S(2)}, u32[]{:S(2)}) collective-permute-start(bf16[1040,128]{1,0:T(8,128)(2,1)S(1)} %pad_maximum_fusion.4), channel_id=1, source_target_pairs={{0,16},{8,24},{1,17},{9,25},{2,18},{10,26},{3,19},{11,27},{4,20},{... | collective-permute-start | bytes 798728 | tf_op jit(solution)/shard_map/ppermute | solution.py:25
  40.0 10.2 %collective-permute-start.2 = (bf16[1040,128]{1,0:T(8,128)(2,1)S(1)}, bf16[1040,128]{1,0:T(8,128)(2,1)S(1)}, u32[]{:S(2)}, u32[]{:S(2)}) collective-permute-start(bf16[1040,128]{1,0:T(8,128)(2,1)S(1)} %pad_maximum_fusion.4), channel_id=1, source_target_pairs={{0,8},{8,16},{16,24},{1,9},{9,17},{17,25},{2,10},{10,18},{18,26},{... | collective-permute-start | bytes 798728 | tf_op jit(solution)/shard_map/ppermute | solution.py:25
  50.8 14.1 %copy-start.9 = (f32[16]{0:T(128)}, f32[16]{0:T(128)S(1)}, u32[]{:S(2)}) copy-start(f32[16]{0:T(128)S(1)} %get-tuple-element.10) | copy-start | bytes 196
  50.8 0.7 copy-start.1
  52.4 18.5 %collective-permute-start.4 = (bf16[16,64,128]{2,1,0:T(8,128)(2,1)}, bf16[16,64,128]{2,1,0:T(8,128)(2,1)}, u32[]{:S(2)}, u32[]{:S(2)}) collective-permute-start(bf16[16,64,128]{2,1,0:T(8,128)(2,1)} %fusion.41), channel_id=1, source_target_pairs={{0,16},{8,24},{1,17},{9,25},{2,18},{10,26},{3,19},{11,27},{4,20},{... | collective-permute-start | bytes 786440 | tf_op jit(solution)/shard_map/ppermute | solution.py:25
  69.1 11.2 %copy-start.10 = (f32[16]{0:T(128)S(1)}, f32[16]{0:T(128)}, u32[]{:S(2)}) copy-start(f32[16]{0:T(128)} %copy-done.9) | copy-start | bytes 196
  69.1 11.2 %copy-start.12 = (f32[16]{0:T(128)S(1)}, f32[16]{0:T(128)}, u32[]{:S(2)}) copy-start(f32[16]{0:T(128)} %copy-done.11) | copy-start | bytes 196
  69.8 10.5 %copy-start.2 = (bf16[1024,128]{1,0:T(8,128)(2,1)S(1)}, bf16[1024,128]{1,0:T(8,128)(2,1)}, u32[]{:S(2)}) copy-start(bf16[1024,128]{1,0:T(8,128)(2,1)} %copy-done.1) | copy-start | bytes 786436
  69.8 10.5 %copy-start.13 = (f32[16]{0:T(128)S(1)}, f32[16]{0:T(128)}, u32[]{:S(2)}) copy-start(f32[16]{0:T(128)} %get-tuple-element.9) | copy-start | bytes 196
  72.3 8.0 %collective-permute-start.5 = (bf16[16,64,128]{2,1,0:T(8,128)(2,1)S(1)}, bf16[16,64,128]{2,1,0:T(8,128)(2,1)S(1)}, u32[]{:S(2)}, u32[]{:S(2)}) collective-permute-start(bf16[16,64,128]{2,1,0:T(8,128)(2,1)S(1)} %select_convert_fusion), channel_id=1, source_target_pairs={{0,4},{4,0},{1,5},{5,1},{2,6},{6,2},{3,7},{7,3},{8,12},{12,8},{9,1... | collective-permute-start | bytes 786440 | tf_op jit(solution)/shard_map/ppermute | solution.py:248
  74.6 7.4 %copy-start.4 = (bf16[512,1,256]{0,2,1:T(8,128)(2,1)S(1)}, bf16[512,1,256]{0,2,1:T(8,128)(2,1)}, u32[]{:S(2)}) copy-start(bf16[512,1,256]{0,2,1:T(8,128)(2,1)} %get-tuple-element.14) | copy-start | bytes 786436
  81.7 2.1 %copy-start = (bf16[2048,512]{1,0:T(8,128)(2,1)S(1)}, bf16[2048,512]{1,0:T(8,128)(2,1)}, u32[]{:S(2)}) copy-start(bf16[2048,512]{1,0:T(8,128)(2,1)} %shard_map.118) | copy-start | bytes 6291460
  81.7 2.1 %copy-start.6 = (pred[512,512]{1,0:T(8,128)(4,1)S(1)}, pred[512,512]{1,0:T(8,128)(4,1)}, u32[]{:S(2)}) copy-start(pred[512,512]{1,0:T(8,128)(4,1)} %iota_compare_fusion) | copy-start | bytes 786436
  81.7 2.1 %copy-start.7 = (f32[512,2,16]{0,2,1:T(8,128)S(1)}, f32[512,2,16]{0,2,1:T(8,128)}, u32[]{:S(2)}) copy-start(f32[512,2,16]{0,2,1:T(8,128)} %get-tuple-element.16) | copy-start | bytes 196612
  83.8 13.3 %slice-start = ((s8[16777216]{0:T(1024)(128)(4,1)}), s8[4194304]{0:T(1024)(128)(4,1)S(1)}, s32[]{:S(2)}) async-start(s8[16777216]{0:T(1024)(128)(4,1)} %bitcast.241), calls=%async_computation | async-start | bytes 8388608
  83.9 10.5 %copy-start.8 = (f32[2048]{0:T(1024)S(1)}, f32[2048]{0:T(1024)}, u32[]{:S(2)}) copy-start(f32[2048]{0:T(1024)} %mul.224) | copy-start | bytes 24580
  83.9 13.3 %slice-start.1 = ((s8[16777216]{0:T(1024)(128)(4,1)}), s8[4194304]{0:T(1024)(128)(4,1)S(1)}, s32[]{:S(2)}) async-start(s8[16777216]{0:T(1024)(128)(4,1)} %bitcast.241), calls=%async_computation.1 | async-start | bytes 8388608
  83.9 13.3 %slice-start.2 = ((s8[16777216]{0:T(1024)(128)(4,1)}), s8[4194304]{0:T(1024)(128)(4,1)S(1)}, s32[]{:S(2)}) async-start(s8[16777216]{0:T(1024)(128)(4,1)} %bitcast.241), calls=%async_computation.2 | async-start | bytes 8388608
  83.9 13.3 %slice-start.3 = ((s8[16777216]{0:T(1024)(128)(4,1)}), s8[4194304]{0:T(1024)(128)(4,1)S(1)}, s32[]{:S(2)}) async-start(s8[16777216]{0:T(1024)(128)(4,1)} %bitcast.241), calls=%async_computation.3 | async-start | bytes 8388608
  104.5 3.8 %collective-permute-start.6 = (bf16[2,128,1024]{2,1,0:T(8,128)(2,1)S(1)}, bf16[2,128,1024]{2,1,0:T(8,128)(2,1)S(1)}, u32[]{:S(2)}, u32[]{:S(2)}) collective-permute-start(bf16[2,128,1024]{2,1,0:T(8,128)(2,1)S(1)} %dynamic-slice_bitcast_fusion.3), channel_id=1, source_target_pairs={{0,1},{1,0},{2,3},{3,2},{4,5},{5,4},{6,7},{7,6},{8,9},{9,8},{10,11... | collective-permute-start | bytes 1572872 | tf_op jit(solution)/shard_map/ppermute | solution.py:248
  107.0 3.1 %collective-permute-start.8 = (bf16[2,128,1024]{2,1,0:T(8,128)(2,1)S(1)}, bf16[2,128,1024]{2,1,0:T(8,128)(2,1)S(1)}, u32[]{:S(2)}, u32[]{:S(2)}) collective-permute-start(bf16[2,128,1024]{2,1,0:T(8,128)(2,1)S(1)} %dynamic-slice_bitcast_fusion.2), channel_id=1, source_target_pairs={{0,1},{1,0},{2,3},{3,2},{4,5},{5,4},{6,7},{7,6},{8,9},{9,8},{10,11... | collective-permute-start | bytes 1572872 | tf_op jit(solution)/shard_map/ppermute | solution.py:248
  107.6 3.3 %collective-permute-start.10 = (bf16[2,128,1024]{2,1,0:T(8,128)(2,1)S(1)}, bf16[2,128,1024]{2,1,0:T(8,128)(2,1)S(1)}, u32[]{:S(2)}, u32[]{:S(2)}) collective-permute-start(bf16[2,128,1024]{2,1,0:T(8,128)(2,1)S(1)} %dynamic-slice_bitcast_fusion.1), channel_id=1, source_target_pairs={{0,1},{1,0},{2,3},{3,2},{4,5},{5,4},{6,7},{7,6},{8,9},{9,8},{10,11... | collective-permute-start | bytes 1572872 | tf_op jit(solution)/shard_map/ppermute | solution.py:248
  107.7 5.0 %collective-permute-start.12 = (bf16[2,128,1024]{2,1,0:T(8,128)(2,1)S(1)}, bf16[2,128,1024]{2,1,0:T(8,128)(2,1)S(1)}, u32[]{:S(2)}, u32[]{:S(2)}) collective-permute-start(bf16[2,128,1024]{2,1,0:T(8,128)(2,1)S(1)} %dynamic-slice_bitcast_fusion), channel_id=1, source_target_pairs={{0,1},{1,0},{2,3},{3,2},{4,5},{5,4},{6,7},{7,6},{8,9},{9,8},{10,11... | collective-permute-start | bytes 1572872 | tf_op jit(solution)/shard_map/ppermute | solution.py:248
  108.5 9.2 %collective-permute-start.7 = (bf16[128,1024]{1,0:T(8,128)(2,1)S(1)}, bf16[128,1024]{1,0:T(8,128)(2,1)S(1)}, u32[]{:S(2)}, u32[]{:S(2)}) collective-permute-start(bf16[128,1024]{1,0:T(8,128)(2,1)S(1)} %fusion.43), channel_id=1, source_target_pairs={{0,2},{2,0},{1,3},{3,1},{4,6},{6,4},{5,7},{7,5},{8,10},{10,8},{9,1... | collective-permute-start | bytes 786440 | tf_op jit(solution)/shard_map/ppermute | solution.py:248
  110.3 13.0 %collective-permute-start.9 = (bf16[128,1024]{1,0:T(8,128)(2,1)S(1)}, bf16[128,1024]{1,0:T(8,128)(2,1)S(1)}, u32[]{:S(2)}, u32[]{:S(2)}) collective-permute-start(bf16[128,1024]{1,0:T(8,128)(2,1)S(1)} %fusion.44), channel_id=1, source_target_pairs={{0,2},{2,0},{1,3},{3,1},{4,6},{6,4},{5,7},{7,5},{8,10},{10,8},{9,1... | collective-permute-start | bytes 786440 | tf_op jit(solution)/shard_map/ppermute | solution.py:248
  111.1 17.8 %collective-permute-start.11 = (bf16[128,1024]{1,0:T(8,128)(2,1)S(1)}, bf16[128,1024]{1,0:T(8,128)(2,1)S(1)}, u32[]{:S(2)}, u32[]{:S(2)}) collective-permute-start(bf16[128,1024]{1,0:T(8,128)(2,1)S(1)} %fusion.45), channel_id=1, source_target_pairs={{0,2},{2,0},{1,3},{3,1},{4,6},{6,4},{5,7},{7,5},{8,10},{10,8},{9,1... | collective-permute-start | bytes 786440 | tf_op jit(solution)/shard_map/ppermute | solution.py:248
  112.9 20.7 %collective-permute-start.13 = (bf16[128,1024]{1,0:T(8,128)(2,1)S(1)}, bf16[128,1024]{1,0:T(8,128)(2,1)S(1)}, u32[]{:S(2)}, u32[]{:S(2)}) collective-permute-start(bf16[128,1024]{1,0:T(8,128)(2,1)S(1)} %fusion.46), channel_id=1, source_target_pairs={{0,2},{2,0},{1,3},{3,1},{4,6},{6,4},{5,7},{7,5},{8,10},{10,8},{9,1... | collective-permute-start | bytes 786440 | tf_op jit(solution)/shard_map/ppermute | solution.py:248

commit v11 on v9

--- a/solution.py
+++ b/solution.py
@@ -1,6 +1,8 @@
 import jax
 import jax.numpy as jnp
 from jax import lax
+from jax.experimental import pallas as pl
+from jax.experimental.pallas import tpu as pltpu
 from jax.sharding import Mesh, PartitionSpec as P
 
 SSM_HEAD_COUNT = 128
@@ -31,6 +33,33 @@
         )
     return lax.optimization_barrier(jax.nn.silu(summed).astype(jnp.bfloat16))
 
+
+def conv_kernel(halo_ref, x_ref, w_ref, b_ref, o_ref, pad_ref):
+    rows = x_ref.shape[0]
+    pad_ref[0:8, :] = halo_ref[...].astype(jnp.float32)
+    pad_ref[8 : 8 + rows, :] = x_ref[...].astype(jnp.float32)
+    summed = b_ref[...].astype(jnp.float32)
+    for k in range(CONV):
+        summed = summed + w_ref[k : k + 1, :].astype(jnp.float32) * pad_ref[8 - (CONV - 1) + k : 8 - (CONV - 1) + k + rows, :]
+    o_ref[...] = jnp.transpose(jax.nn.silu(summed)).astype(o_ref.dtype)
+
+def conv_silu_kernel(halo, x, weight, bias):
+    rows, width = x.shape
+    block = 512 if width % 512 == 0 else width
+    halo8 = jnp.concatenate([jnp.zeros((8 - halo.shape[0], width), halo.dtype), halo], axis=0)
+    return pl.pallas_call(
+        conv_kernel,
+        grid=(width // block,),
+        in_specs=[
+            pl.BlockSpec((8, block), lambda j: (0, j)),
+            pl.BlockSpec((rows, block), lambda j: (0, j)),
+            pl.BlockSpec((CONV, block), lambda j: (0, j)),
+            pl.BlockSpec((1, block), lambda j: (0, j)),
+        ],
+        out_specs=pl.BlockSpec((block, rows), lambda j: (j, 0)),
+        out_shape=jax.ShapeDtypeStruct((width, rows), jnp.bfloat16),
+        scratch_shapes=[pltpu.VMEM((rows + 8, block), jnp.float32)],
+    )(halo8, x, weight, bias.reshape(1, width))
 
 def diagonal_of(inner_block, b_block, c_block, step_sizes, cumulative):
     length = inner_block.shape[0]
@@ -181,8 +210,8 @@
         [inner_input[tokens - margin :], state_input[tokens - margin :].reshape(margin, -1)], axis=1
     )
     halo = shifted(halo, ("chi", "clo"), 1)
-    inner_conv = conv_silu(
-        jnp.concatenate([halo[:, :inner_width], inner_input], axis=0), conv_inner, bias_inner, tokens
+    inner_conv = jnp.transpose(
+        conv_silu_kernel(halo[:, :inner_width], inner_input, conv_inner, bias_inner)
     )
     state_conv = conv_silu(
         jnp.concatenate([halo[:, inner_width:].reshape((margin,) + state_input.shape[1:]), state_input], axis=0),

time: 141 us -> 134 us (0.950)
  other arithmetic: 31.1 us -> 19.8 us
  Pallas kernels: 0 us -> 6.01 us
  local copies, waits for them, and re-layouts: 14.3 us -> 11.9 us
  matrix products: 26.6 us -> 28.3 us
    convert_element_type x2 -> x1, other arithmetic: 11.8 us -> 1.34 us  [conv_silu(): return lax.optimization_barrier(jax.nn.silu(summed).astype(jnp.bfloat16))]
    pallas_call x0 -> x1, Pallas kernels: none -> 6.01 us  [conv_silu_kernel(): pl.pallas_call(conv_kernel, grid=(width // block,), in_specs=[pl.BlockSpe...]
    unnamed x45 -> x40, local copies, waits for them, and re-layouts: 10.6 us -> 6.53 us
    dot_general x1, matrix products: 0.71 us -> 2.3 us  [state_of(): jnp.einsum('jghp,jgn->ghpn', weighted, b_block, preferred_element_type=jn...]
    mul x2 -> x1, other arithmetic: 2.22 us -> 0.74 us  [conv_silu(): weight[k].astype(jnp.float32) * padded[k:k + row_count].astype(jnp.float32)]
    reshape x1 -> x3, local copies, waits for them, and re-layouts: 0.01 us -> 1.47 us  [the longest x1 1.29 us: conv_silu_kernel(): bias.reshape(1, width)]
  transfers between devices with their start and end apart: 14 -> 14, of which waited for: 8 -> 8; matrix products, arithmetic and copies ran while one was open for 23% -> 22% of each run, Pallas kernels for 0% -> 0%
where the time goes in v11:
time: 134 us
  waiting for transfers between devices  35.4 us (26%)
  starting transfers between devices  31.8 us (24%)
  matrix products  28.3 us (21%)
  other arithmetic  19.8 us (15%)
  local copies, waits for them, and re-layouts  11.9 us (9%)
  Pallas kernels  6.01 us (4%)
    ppermute x10, waiting for transfers between devices, swap(): return lax.ppermute(value, axis, [(0, 1), (1, 0)])  28.9 us
    ppermute x4, starting transfers between devices, shifted(): return lax.ppermute(value, axis, pairs)  23.9 us
    dot_general x4, matrix products, reduce_rows(): jnp.dot(normed, out_weight[:, c * step:(c + 1) * step], preferred_element...  11.9 us
    dot_general x1, matrix products, diagonal_of(): jnp.einsum('ghij,jghp->ighp', mixing, inner_block, preferred_element_type...  10.5 us
    ppermute x10, starting transfers between devices, swap(): return lax.ppermute(value, axis, [(0, 1), (1, 0)])  7.91 us
    unnamed x40, local copies, waits for them, and re-layouts  6.53 us
    ppermute x4, waiting for transfers between devices, shifted(): return lax.ppermute(value, axis, pairs)  6.53 us
    pallas_call x1, Pallas kernels, conv_silu_kernel(): pl.pallas_call(conv_kernel, grid=(width // block,), in_specs=[pl.BlockSpe...  6.01 us
  transfers between devices with their start and end apart: 14, of which 8 were waited for; matrix products, arithmetic and copies ran while one was open for 22% of the time, Pallas kernels for 0%

profile of v11, /device:TPU:0, one launch (start us, length us, event | category | flops | bytes accessed | tf_op | source)
XLA Modules:
  0.0 133.7 jit_solution(17192155162073899233)
XLA Ops:
  1.5 4.8 %collective-permute-start = (bf16[3,2560]{1,0:T(4,128)(2,1)S(1)}, bf16[3,2560]{1,0:T(4,128)(2,1)S(1)}, u32[]{:S(2)}, u32[]{:S(2)}) collective-permute-start(bf16[3,2560]{1,0:T(4,128)(2,1)S(1)} %pad_maximum_fusion.5), channel_id=1, source_target_pairs={{0,4},{4,8},{8,12},{12,16},{16,20},{20,24},{24,28},{1,5},{5,9},{9,... | collective-permute-start | bytes 46088 | tf_op jit(solution)/shard_map/ppermute | solution.py:25
  7.9 2.3 %reduce-window.6 = f32[16,2,4,128]{3,0,1,2:T(8,128)S(1)} reduce-window(f32[16,2,4,128]{3,0,1,2:T(8,128)S(1)} %bitcast.238, f32[]{:T(128)} %constant.68.clone.1), window={size=1x1x1x128 pad=0_0x0_0x0_0x127_0}, to_apply=%region_0.1 | reduce-window | flops 2080768 | bytes 131076 | tf_op jit(solution)/shard_map/reduce-window
  12.3 1.3 copy.44
  14.3 1.3 reshape.137.b_ref
  15.8 1.3 %multiply_convert_fusion.6 = bf16[512,2,256]{0,2,1:T(8,128)(2,1)S(1)} fusion(bf16[512,2,256]{0,2,1:T(8,128)(2,1)S(1)} %copy.44, bf16[3,2,256]{0,2,1:T(8,128)(2,1)S(1)} %bitcast.234, f32[2,256]{1,0:T(2,128)S(1)} %get-tuple-element.36, f32[2,256]{1,0:T(2,128)S(1)} %get-tuple-element.37, f32[2,256]{1,0:T(2,128)S(1)} %get-tuple-element.35, ...), kind=kLoop, calls=%fused_computation.39 | loop fusion | flops 6815744 | bytes 1061888 | tf_op jit(solution)/shard_map/convert_element_type | solution.py:34
  18.6 6.0 %shard_map.118 = bf16[2048,512]{1,0:T(8,128)(2,1)} custom-call(bf16[8,2048]{1,0:T(8,128)(2,1)} %concatenate.28.halo_ref, bf16[512,2048]{1,0:T(8,128)(2,1)} %x_ref.1, bf16[4,2048]{1,0:T(4,128)(2,1)} %w_ref.1, bf16[1,2048]{1,0:T(2,128)(2,1)} %reshape.137.b_ref), custom_call_target="tpu_custom_call" | custom-call | tf_op jit(solution)/shard_map/pallas_call | solution.py:50
  24.6 2.3 %fusion.18 = f32[2,16,64,128]{3,2,1,0:T(8,128)S(1)} fusion(bf16[512,2,128,1]{0,2,3,1:T(8,128)(2,1)S(1)} %bitcast.223, bf16[512,2,16,64]{0,3,2,1:T(8,128)(2,1)} %bitcast.210, f32[512,2,16]{0,2,1:T(8,128)S(1)} %get-tuple-element.29), kind=kOutput, calls=%fused_computation.26 | convolution fusion | flops 271581184 | bytes 3473408 | tf_op jit(solution)/shard_map/jghp,jgn->ghpn/dot_general | solution.py:81
  27.0 1.6 %collective-permute-start.1 = (bf16[1040,128]{1,0:T(8,128)(2,1)S(1)}, bf16[1040,128]{1,0:T(8,128)(2,1)S(1)}, u32[]{:S(2)}, u32[]{:S(2)}) collective-permute-start(bf16[1040,128]{1,0:T(8,128)(2,1)S(1)} %pad_maximum_fusion.3), channel_id=1, source_target_pairs={{0,4},{4,0},{1,5},{5,1},{2,6},{6,2},{3,7},{7,3},{8,12},{12,8},{9,1... | collective-permute-start | bytes 798728 | tf_op jit(solution)/shard_map/ppermute | solution.py:271
  29.5 5.5 %collective-permute-done.1 = bf16[1040,128]{1,0:T(8,128)(2,1)S(1)} collective-permute-done((bf16[1040,128]{1,0:T(8,128)(2,1)S(1)}, bf16[1040,128]{1,0:T(8,128)(2,1)S(1)}, u32[]{:S(2)}, u32[]{:S(2)}) %collective-permute-start.1) | collective-permute-done | bytes 266272 | tf_op jit(solution)/shard_map/ppermute | solution.py:271
  37.6 1.2 fusion.41
  38.9 4.5 %collective-permute-start.3 = (bf16[1040,128]{1,0:T(8,128)(2,1)S(1)}, bf16[1040,128]{1,0:T(8,128)(2,1)S(1)}, u32[]{:S(2)}, u32[]{:S(2)}) collective-permute-start(bf16[1040,128]{1,0:T(8,128)(2,1)S(1)} %pad_maximum_fusion.4), channel_id=1, source_target_pairs={{0,16},{8,24},{1,17},{9,25},{2,18},{10,26},{3,19},{11,27},{4,20},{... | collective-permute-start | bytes 798728 | tf_op jit(solution)/shard_map/ppermute | solution.py:25
  43.5 3.5 %collective-permute-start.2 = (bf16[1040,128]{1,0:T(8,128)(2,1)S(1)}, bf16[1040,128]{1,0:T(8,128)(2,1)S(1)}, u32[]{:S(2)}, u32[]{:S(2)}) collective-permute-start(bf16[1040,128]{1,0:T(8,128)(2,1)S(1)} %pad_maximum_fusion.4), channel_id=1, source_target_pairs={{0,8},{8,16},{16,24},{1,9},{9,17},{17,25},{2,10},{10,18},{18,26},{... | collective-permute-start | bytes 798728 | tf_op jit(solution)/shard_map/ppermute | solution.py:25
  47.1 3.2 %collective-permute-done.3 = bf16[1040,128]{1,0:T(8,128)(2,1)S(1)} collective-permute-done((bf16[1040,128]{1,0:T(8,128)(2,1)S(1)}, bf16[1040,128]{1,0:T(8,128)(2,1)S(1)}, u32[]{:S(2)}, u32[]{:S(2)}) %collective-permute-start.3) | collective-permute-done | bytes 266272 | tf_op jit(solution)/shard_map/ppermute | solution.py:25
  50.2 3.4 %collective-permute-done.2 = bf16[1040,128]{1,0:T(8,128)(2,1)S(1)} collective-permute-done((bf16[1040,128]{1,0:T(8,128)(2,1)S(1)}, bf16[1040,128]{1,0:T(8,128)(2,1)S(1)}, u32[]{:S(2)}, u32[]{:S(2)}) %collective-permute-start.2) | collective-permute-done | bytes 266272 | tf_op jit(solution)/shard_map/ppermute | solution.py:25
  53.9 11.0 %collective-permute-start.4 = (bf16[16,64,128]{2,1,0:T(8,128)(2,1)S(1)}, bf16[16,64,128]{2,1,0:T(8,128)(2,1)S(1)}, u32[]{:S(2)}, u32[]{:S(2)}) collective-permute-start(bf16[16,64,128]{2,1,0:T(8,128)(2,1)S(1)} %fusion.42), channel_id=1, source_target_pairs={{0,16},{8,24},{1,17},{9,25},{2,18},{10,26},{3,19},{11,27},{4,20},{... | collective-permute-start | bytes 786440 | tf_op jit(solution)/shard_map/ppermute | solution.py:25
  64.9 1.4 %fusion.68 = f32[2,512,512]{2,1,0:T(8,128)S(1)} fusion(bf16[512,2,128]{0,2,1:T(8,128)(2,1)} %bitcast.221, bf16[512,2,128]{0,2,1:T(8,128)(2,1)S(1)} %bitcast.224), kind=kOutput, calls=%fused_computation.134 | convolution fusion | flops 134217728 | bytes 2621440 | tf_op jit(solution)/shard_map/ign,jgn->gij/dot_general | solution.py:71
  66.4 10.5 %fusion.17 = f32[512,2,16,64]{0,3,2,1:T(8,128)} fusion(bf16[512,2,16,64]{0,3,2,1:T(8,128)(2,1)S(1)} %bitcast.211, f32[2,16,512]{2,1,0:T(8,128)S(1)} %bitcast.237, f32[2,512,512]{2,1,0:T(8,128)S(1)} %fusion.68, f32[2,16,512]{2,1,0:T(8,128)S(1)} %copy-done.9, pred[512,512]{1,0:T(8,128)(4,1)S(1)} %iota_compare_fusion), kind=kOutput, calls=%fused_computation.25 | convolution fusion | flops 1115684864 | bytes 8781824 | tf_op jit(solution)/shard_map/ghij,jghp->ighp/dot_general | solution.py:75
  78.7 3.9 %copy.50 = bf16[512,2048]{0,1:T(8,128)(2,1)} copy(bf16[512,2048]{1,0:T(8,128)(2,1)} %param.14) | data formatting | bytes 4194304 | tf_op args[2]
  82.8 3.5 %collective-permute-done.5 = bf16[16,64,128]{2,1,0:T(8,128)(2,1)} collective-permute-done((bf16[16,64,128]{2,1,0:T(8,128)(2,1)}, bf16[16,64,128]{2,1,0:T(8,128)(2,1)}, u32[]{:S(2)}, u32[]{:S(2)}) %collective-permute-start.5) | collective-permute-done | bytes 262176 | tf_op jit(solution)/shard_map/ppermute | solution.py:271
  86.3 1.5 %convert_select_fusion.1 = (f32[16,64,128]{2,1,0:T(8,128)S(1)}, f32[16,64,128]{2,1,0:T(8,128)S(1)}) fusion(bf16[16,64,128]{2,1,0:T(8,128)(2,1)} %collective-permute-done.5, pred[]{:T(512)S(6)} %eq.3, f32[16,64,128]{2,1,0:T(8,128)} %bitcast.213, f32[16]{0:T(128)S(1)} %copy-done.10, bf16[16,64,128]{2,1,0:T(8,128)(2,1)} %bitcast.220, ...), kind=kLoop, calls=%fused_computation.43 | loop fusion | flops 1835008 | bytes 3671232 | tf_op jit(solution)/shard_map/jit(_where)/select_n | solution.py:187
  89.0 2.1 %fusion.6 = f32[1,512,2,16,64]{1,4,3,2,0:T(8,128)S(1)} fusion(f32[512,2,16,64]{0,3,2,1:T(8,128)S(1)} %copy-done.3, f32[512,2,16]{0,2,1:T(8,128)S(1)} %get-tuple-element.28, f32[2,16,64,128]{3,2,1,0:T(8,128)S(1)} %bitcast.214, bf16[512,2,128,1]{0,2,3,1:T(8,128)(2,1)S(1)} %bitcast.222), kind=kOutput, calls=%fused_computation.10 | convolution fusion | flops 1612709888 | bytes 9764864 | tf_op jit(solution)/shard_map/vmap(ign,ghpn->ighp)/dot_general | solution.py:92
  91.1 2.2 %bitcast_reduce_fusion = (f32[512,2]{0,1:T(2,128)S(1)}, f32[512,2048]{0,1:T(8,128)S(1)}) fusion(bf16[512,2048]{0,1:T(8,128)(2,1)S(1)} %copy-done.1, bf16[2048,512]{1,0:T(8,128)(2,1)S(1)} %copy-done, f32[2048]{0:T(1024)S(1)} %mul.224, f32[1,512,2,16,64]{1,4,3,2,0:T(8,128)S(1)} %fusion.6), kind=kLoop, calls=%fused_computation.14 | loop fusion | flops 11533312 | bytes 12595200 | tf_op jit(solution)/shard_map/reduce_sum | solution.py:263
  93.8 4.9 %fusion.20 = bf16[512,1024]{1,0:T(8,128)(2,1)S(1)} fusion(bf16[512,2048]{0,1:T(8,128)(2,1)S(1)} %fusion.8, bf16[2048,4096]{1,0:T(8,128)(2,1)} %param.23), kind=kOutput, calls=%fused_computation.28 | convolution fusion | flops 2148007936 | bytes 7340032 | tf_op jit(solution)/shard_map/dot_general | solution.py:295
  98.7 2.3 %fusion.23 = bf16[512,1024]{1,0:T(8,128)(2,1)S(1)} fusion(bf16[512,2048]{0,1:T(8,128)(2,1)S(1)} %fusion.8, bf16[2048,4096]{1,0:T(8,128)(2,1)S(1)} %bitcast.242), kind=kOutput, calls=%fused_computation.29 | convolution fusion | flops 2148007936 | bytes 7340032 | tf_op jit(solution)/shard_map/dot_general | solution.py:295
  101.1 2.3 %fusion.26 = bf16[512,1024]{1,0:T(8,128)(2,1)S(1)} fusion(bf16[512,2048]{0,1:T(8,128)(2,1)S(1)} %fusion.8, bf16[2048,4096]{1,0:T(8,128)(2,1)S(1)} %bitcast.242), kind=kOutput, calls=%fused_computation.30 | convolution fusion | flops 2148007936 | bytes 7340032 | tf_op jit(solution)/shard_map/dot_general | solution.py:295
  103.6 2.3 %fusion.29 = bf16[512,1024]{1,0:T(8,128)(2,1)S(1)} fusion(bf16[512,2048]{0,1:T(8,128)(2,1)S(1)} %fusion.8, bf16[2048,4096]{1,0:T(8,128)(2,1)S(1)} %bitcast.242), kind=kOutput, calls=%fused_computation.31 | convolution fusion | flops 2148007936 | bytes 7340032 | tf_op jit(solution)/shard_map/dot_general | solution.py:295
  107.5 1.6 %collective-permute-start.7 = (bf16[128,1024]{1,0:T(8,128)(2,1)S(1)}, bf16[128,1024]{1,0:T(8,128)(2,1)S(1)}, u32[]{:S(2)}, u32[]{:S(2)}) collective-permute-start(bf16[128,1024]{1,0:T(8,128)(2,1)S(1)} %fusion.44), channel_id=1, source_target_pairs={{0,2},{2,0},{1,3},{3,1},{4,6},{6,4},{5,7},{7,5},{8,10},{10,8},{9,1... | collective-permute-start | bytes 786440 | tf_op jit(solution)/shard_map/ppermute | solution.py:271
  110.1 1.6 %collective-permute-start.11 = (bf16[128,1024]{1,0:T(8,128)(2,1)S(1)}, bf16[128,1024]{1,0:T(8,128)(2,1)S(1)}, u32[]{:S(2)}, u32[]{:S(2)}) collective-permute-start(bf16[128,1024]{1,0:T(8,128)(2,1)S(1)} %fusion.46), channel_id=1, source_target_pairs={{0,2},{2,0},{1,3},{3,1},{4,6},{6,4},{5,7},{7,5},{8,10},{10,8},{9,1... | collective-permute-start | bytes 786440 | tf_op jit(solution)/shard_map/ppermute | solution.py:271
  112.5 4.2 %collective-permute-done.7 = bf16[128,1024]{1,0:T(8,128)(2,1)S(1)} collective-permute-done((bf16[128,1024]{1,0:T(8,128)(2,1)S(1)}, bf16[128,1024]{1,0:T(8,128)(2,1)S(1)}, u32[]{:S(2)}, u32[]{:S(2)}) %collective-permute-start.7) | collective-permute-done | bytes 262176 | tf_op jit(solution)/shard_map/ppermute | solution.py:271
  116.8 5.5 %collective-permute-done.9 = bf16[128,1024]{1,0:T(8,128)(2,1)S(1)} collective-permute-done((bf16[128,1024]{1,0:T(8,128)(2,1)S(1)}, bf16[128,1024]{1,0:T(8,128)(2,1)S(1)}, u32[]{:S(2)}, u32[]{:S(2)}) %collective-permute-start.9) | collective-permute-done | bytes 262176 | tf_op jit(solution)/shard_map/ppermute | solution.py:271
  122.4 5.5 %collective-permute-done.11 = bf16[128,1024]{1,0:T(8,128)(2,1)S(1)} collective-permute-done((bf16[128,1024]{1,0:T(8,128)(2,1)S(1)}, bf16[128,1024]{1,0:T(8,128)(2,1)S(1)}, u32[]{:S(2)}, u32[]{:S(2)}) %collective-permute-start.11) | collective-permute-done | bytes 262176 | tf_op jit(solution)/shard_map/ppermute | solution.py:271
  128.0 4.6 %collective-permute-done.13 = bf16[128,1024]{1,0:T(8,128)(2,1)S(1)} collective-permute-done((bf16[128,1024]{1,0:T(8,128)(2,1)S(1)}, bf16[128,1024]{1,0:T(8,128)(2,1)S(1)}, u32[]{:S(2)}, u32[]{:S(2)}) %collective-permute-start.13) | collective-permute-done | bytes 262176 | tf_op jit(solution)/shard_map/ppermute | solution.py:271
  (119 shorter events, 19.7 us)
Async XLA Ops:
  1.5 14.1 %collective-permute-start = (bf16[3,2560]{1,0:T(4,128)(2,1)S(1)}, bf16[3,2560]{1,0:T(4,128)(2,1)S(1)}, u32[]{:S(2)}, u32[]{:S(2)}) collective-permute-start(bf16[3,2560]{1,0:T(4,128)(2,1)S(1)} %pad_maximum_fusion.5), channel_id=1, source_target_pairs={{0,4},{4,8},{8,12},{12,16},{16,20},{20,24},{24,28},{1,5},{5,9},{9,... | collective-permute-start | bytes 46088 | tf_op jit(solution)/shard_map/ppermute | solution.py:25
  17.9 9.1 %copy-start.6 = (bf16[512,1,256]{0,2,1:T(8,128)(2,1)}, bf16[512,1,256]{0,2,1:T(8,128)(2,1)S(1)}, u32[]{:S(2)}) copy-start(bf16[512,1,256]{0,2,1:T(8,128)(2,1)S(1)} %get-tuple-element.27) | copy-start | bytes 786436
  27.0 39.4 %copy-start = (bf16[2048,512]{1,0:T(8,128)(2,1)S(1)}, bf16[2048,512]{1,0:T(8,128)(2,1)}, u32[]{:S(2)}) copy-start(bf16[2048,512]{1,0:T(8,128)(2,1)} %shard_map.118) | copy-start | bytes 6291460
  27.0 7.9 %collective-permute-start.1 = (bf16[1040,128]{1,0:T(8,128)(2,1)S(1)}, bf16[1040,128]{1,0:T(8,128)(2,1)S(1)}, u32[]{:S(2)}, u32[]{:S(2)}) collective-permute-start(bf16[1040,128]{1,0:T(8,128)(2,1)S(1)} %pad_maximum_fusion.3), channel_id=1, source_target_pairs={{0,4},{4,0},{1,5},{5,1},{2,6},{6,2},{3,7},{7,3},{8,12},{12,8},{9,1... | collective-permute-start | bytes 798728 | tf_op jit(solution)/shard_map/ppermute | solution.py:271
  35.6 0.5 copy-start.12
  36.3 28.7 %copy-start.7 = (bf16[512,1,256]{0,2,1:T(8,128)(2,1)S(1)}, bf16[512,1,256]{0,2,1:T(8,128)(2,1)}, u32[]{:S(2)}) copy-start(bf16[512,1,256]{0,2,1:T(8,128)(2,1)} %copy-done.6) | copy-start | bytes 786436
  36.3 30.1 %copy-start.9 = (f32[2,16,512]{2,1,0:T(8,128)S(1)}, f32[2,16,512]{2,1,0:T(8,128)}, u32[]{:S(2)}) copy-start(f32[2,16,512]{2,1,0:T(8,128)} %get-tuple-element.30) | copy-start | bytes 196612
  38.9 11.3 %collective-permute-start.3 = (bf16[1040,128]{1,0:T(8,128)(2,1)S(1)}, bf16[1040,128]{1,0:T(8,128)(2,1)S(1)}, u32[]{:S(2)}, u32[]{:S(2)}) collective-permute-start(bf16[1040,128]{1,0:T(8,128)(2,1)S(1)} %pad_maximum_fusion.4), channel_id=1, source_target_pairs={{0,16},{8,24},{1,17},{9,25},{2,18},{10,26},{3,19},{11,27},{4,20},{... | collective-permute-start | bytes 798728 | tf_op jit(solution)/shard_map/ppermute | solution.py:25
  43.5 10.1 %collective-permute-start.2 = (bf16[1040,128]{1,0:T(8,128)(2,1)S(1)}, bf16[1040,128]{1,0:T(8,128)(2,1)S(1)}, u32[]{:S(2)}, u32[]{:S(2)}) collective-permute-start(bf16[1040,128]{1,0:T(8,128)(2,1)S(1)} %pad_maximum_fusion.4), channel_id=1, source_target_pairs={{0,8},{8,16},{16,24},{1,9},{9,17},{17,25},{2,10},{10,18},{18,26},{... | collective-permute-start | bytes 798728 | tf_op jit(solution)/shard_map/ppermute | solution.py:25
  47.1 29.9 %copy-start.2 = (f32[1024,128]{1,0:T(8,128)}, f32[1024,128]{1,0:T(8,128)S(1)}, u32[]{:S(2)}) copy-start(f32[1024,128]{1,0:T(8,128)S(1)} %slice_convert_fusion) | copy-start | bytes 1572868
  53.7 23.2 %copy-start.4 = (bf16[1024,128]{1,0:T(8,128)(2,1)}, bf16[1024,128]{1,0:T(8,128)(2,1)S(1)}, u32[]{:S(2)}) copy-start(bf16[1024,128]{1,0:T(8,128)(2,1)S(1)} %slice.173) | copy-start | bytes 786436
  53.9 23.0 %collective-permute-start.4 = (bf16[16,64,128]{2,1,0:T(8,128)(2,1)S(1)}, bf16[16,64,128]{2,1,0:T(8,128)(2,1)S(1)}, u32[]{:S(2)}, u32[]{:S(2)}) collective-permute-start(bf16[16,64,128]{2,1,0:T(8,128)(2,1)S(1)} %fusion.42), channel_id=1, source_target_pairs={{0,16},{8,24},{1,17},{9,25},{2,18},{10,26},{3,19},{11,27},{4,20},{... | collective-permute-start | bytes 786440 | tf_op jit(solution)/shard_map/ppermute | solution.py:25
  66.4 10.6 %copy-start.10 = (f32[16]{0:T(128)S(1)}, f32[16]{0:T(128)}, u32[]{:S(2)}) copy-start(f32[16]{0:T(128)} %get-tuple-element.25) | copy-start | bytes 196
  76.9 5.7 %copy-start.13 = (f32[32]{0:T(128)S(1)}, f32[32]{0:T(128)}, u32[]{:S(2)}) copy-start(f32[32]{0:T(128)} %param.21) | copy-start | bytes 388
  76.9 5.9 %copy-start.11 = (bf16[2048]{0:T(1024)(128)(2,1)S(1)}, bf16[2048]{0:T(1024)(128)(2,1)}, u32[]{:S(2)}) copy-start(bf16[2048]{0:T(1024)(128)(2,1)} %param.22) | copy-start | bytes 12292
  76.9 1.1 copy-start.8
  78.0 8.3 %collective-permute-start.5 = (bf16[16,64,128]{2,1,0:T(8,128)(2,1)}, bf16[16,64,128]{2,1,0:T(8,128)(2,1)}, u32[]{:S(2)}, u32[]{:S(2)}) collective-permute-start(bf16[16,64,128]{2,1,0:T(8,128)(2,1)} %select_convert_fusion), channel_id=1, source_target_pairs={{0,4},{4,0},{1,5},{5,1},{2,6},{6,2},{3,7},{7,3},{8,12},{12,8},{9,1... | collective-permute-start | bytes 786440 | tf_op jit(solution)/shard_map/ppermute | solution.py:271
  82.8 6.1 %copy-start.3 = (f32[512,2,16,64]{0,3,2,1:T(8,128)S(1)}, f32[512,2,16,64]{0,3,2,1:T(8,128)}, u32[]{:S(2)}) copy-start(f32[512,2,16,64]{0,3,2,1:T(8,128)} %fusion.17) | copy-start | bytes 12582916
  82.8 6.1 %copy-start.5 = (bf16[512,1,256]{0,2,1:T(8,128)(2,1)S(1)}, bf16[512,1,256]{0,2,1:T(8,128)(2,1)}, u32[]{:S(2)}) copy-start(bf16[512,1,256]{0,2,1:T(8,128)(2,1)} %get-tuple-element.26) | copy-start | bytes 786436
  88.9 2.1 %copy-start.1 = (bf16[512,2048]{0,1:T(8,128)(2,1)S(1)}, bf16[512,2048]{0,1:T(8,128)(2,1)}, u32[]{:S(2)}) copy-start(bf16[512,2048]{0,1:T(8,128)(2,1)} %copy.50) | copy-start | bytes 6291460
  91.1 7.6 %slice-start = ((s8[16777216]{0:T(1024)(128)(4,1)}), s8[4194304]{0:T(1024)(128)(4,1)S(1)}, s32[]{:S(2)}) async-start(s8[16777216]{0:T(1024)(128)(4,1)} %bitcast.241), calls=%async_computation | async-start | bytes 8388608
  91.1 7.6 %slice-start.1 = ((s8[16777216]{0:T(1024)(128)(4,1)}), s8[4194304]{0:T(1024)(128)(4,1)S(1)}, s32[]{:S(2)}) async-start(s8[16777216]{0:T(1024)(128)(4,1)} %bitcast.241), calls=%async_computation.1 | async-start | bytes 8388608
  93.3 5.4 %slice-start.2 = ((s8[16777216]{0:T(1024)(128)(4,1)}), s8[4194304]{0:T(1024)(128)(4,1)S(1)}, s32[]{:S(2)}) async-start(s8[16777216]{0:T(1024)(128)(4,1)} %bitcast.241), calls=%async_computation.2 | async-start | bytes 8388608
  93.8 4.9 %slice-start.3 = ((s8[16777216]{0:T(1024)(128)(4,1)}), s8[4194304]{0:T(1024)(128)(4,1)S(1)}, s32[]{:S(2)}) async-start(s8[16777216]{0:T(1024)(128)(4,1)} %bitcast.241), calls=%async_computation.3 | async-start | bytes 8388608
  103.5 3.8 %collective-permute-start.6 = (bf16[2,128,1024]{2,1,0:T(8,128)(2,1)S(1)}, bf16[2,128,1024]{2,1,0:T(8,128)(2,1)S(1)}, u32[]{:S(2)}, u32[]{:S(2)}) collective-permute-start(bf16[2,128,1024]{2,1,0:T(8,128)(2,1)S(1)} %dynamic-slice_bitcast_fusion.3), channel_id=1, source_target_pairs={{0,1},{1,0},{2,3},{3,2},{4,5},{5,4},{6,7},{7,6},{8,9},{9,8},{10,11... | collective-permute-start | bytes 1572872 | tf_op jit(solution)/shard_map/ppermute | solution.py:271
  106.0 3.1 %collective-permute-start.8 = (bf16[2,128,1024]{2,1,0:T(8,128)(2,1)S(1)}, bf16[2,128,1024]{2,1,0:T(8,128)(2,1)S(1)}, u32[]{:S(2)}, u32[]{:S(2)}) collective-permute-start(bf16[2,128,1024]{2,1,0:T(8,128)(2,1)S(1)} %dynamic-slice_bitcast_fusion.2), channel_id=1, source_target_pairs={{0,1},{1,0},{2,3},{3,2},{4,5},{5,4},{6,7},{7,6},{8,9},{9,8},{10,11... | collective-permute-start | bytes 1572872 | tf_op jit(solution)/shard_map/ppermute | solution.py:271
  106.6 3.3 %collective-permute-start.10 = (bf16[2,128,1024]{2,1,0:T(8,128)(2,1)S(1)}, bf16[2,128,1024]{2,1,0:T(8,128)(2,1)S(1)}, u32[]{:S(2)}, u32[]{:S(2)}) collective-permute-start(bf16[2,128,1024]{2,1,0:T(8,128)(2,1)S(1)} %dynamic-slice_bitcast_fusion.1), channel_id=1, source_target_pairs={{0,1},{1,0},{2,3},{3,2},{4,5},{5,4},{6,7},{7,6},{8,9},{9,8},{10,11... | collective-permute-start | bytes 1572872 | tf_op jit(solution)/shard_map/ppermute | solution.py:271
  106.7 5.0 %collective-permute-start.12 = (bf16[2,128,1024]{2,1,0:T(8,128)(2,1)S(1)}, bf16[2,128,1024]{2,1,0:T(8,128)(2,1)S(1)}, u32[]{:S(2)}, u32[]{:S(2)}) collective-permute-start(bf16[2,128,1024]{2,1,0:T(8,128)(2,1)S(1)} %dynamic-slice_bitcast_fusion), channel_id=1, source_target_pairs={{0,1},{1,0},{2,3},{3,2},{4,5},{5,4},{6,7},{7,6},{8,9},{9,8},{10,11... | collective-permute-start | bytes 1572872 | tf_op jit(solution)/shard_map/ppermute | solution.py:271
  107.5 9.2 %collective-permute-start.7 = (bf16[128,1024]{1,0:T(8,128)(2,1)S(1)}, bf16[128,1024]{1,0:T(8,128)(2,1)S(1)}, u32[]{:S(2)}, u32[]{:S(2)}) collective-permute-start(bf16[128,1024]{1,0:T(8,128)(2,1)S(1)} %fusion.44), channel_id=1, source_target_pairs={{0,2},{2,0},{1,3},{3,1},{4,6},{6,4},{5,7},{7,5},{8,10},{10,8},{9,1... | collective-permute-start | bytes 786440 | tf_op jit(solution)/shard_map/ppermute | solution.py:271
  109.3 13.0 %collective-permute-start.9 = (bf16[128,1024]{1,0:T(8,128)(2,1)S(1)}, bf16[128,1024]{1,0:T(8,128)(2,1)S(1)}, u32[]{:S(2)}, u32[]{:S(2)}) collective-permute-start(bf16[128,1024]{1,0:T(8,128)(2,1)S(1)} %fusion.45), channel_id=1, source_target_pairs={{0,2},{2,0},{1,3},{3,1},{4,6},{6,4},{5,7},{7,5},{8,10},{10,8},{9,1... | collective-permute-start | bytes 786440 | tf_op jit(solution)/shard_map/ppermute | solution.py:271
  110.1 17.8 %collective-permute-start.11 = (bf16[128,1024]{1,0:T(8,128)(2,1)S(1)}, bf16[128,1024]{1,0:T(8,128)(2,1)S(1)}, u32[]{:S(2)}, u32[]{:S(2)}) collective-permute-start(bf16[128,1024]{1,0:T(8,128)(2,1)S(1)} %fusion.46), channel_id=1, source_target_pairs={{0,2},{2,0},{1,3},{3,1},{4,6},{6,4},{5,7},{7,5},{8,10},{10,8},{9,1... | collective-permute-start | bytes 786440 | tf_op jit(solution)/shard_map/ppermute | solution.py:271
  111.9 20.7 %collective-permute-start.13 = (bf16[128,1024]{1,0:T(8,128)(2,1)S(1)}, bf16[128,1024]{1,0:T(8,128)(2,1)S(1)}, u32[]{:S(2)}, u32[]{:S(2)}) collective-permute-start(bf16[128,1024]{1,0:T(8,128)(2,1)S(1)} %fusion.47), channel_id=1, source_target_pairs={{0,2},{2,0},{1,3},{3,1},{4,6},{6,4},{5,7},{7,5},{8,10},{10,8},{9,1... | collective-permute-start | bytes 786440 | tf_op jit(solution)/shard_map/ppermute | solution.py:271

commit v12 on v11

--- a/solution.py
+++ b/solution.py
@@ -291,24 +291,35 @@
     chunks = 4 if width % (4 * 128) == 0 else 1
     step = width // chunks
     done = []
+    payloads = []
     for c in range(chunks):
+        source = normed
+        if c == chunks - 1 and c > 0 and payloads[0] is not None:
+            payloads[0], source = lax.optimization_barrier((payloads[0], normed))
         partial = jnp.dot(
-            normed, out_weight[:, c * step : (c + 1) * step], preferred_element_type=jnp.float32
+            source, out_weight[:, c * step : (c + 1) * step], preferred_element_type=jnp.float32
         ).astype(jnp.bfloat16)
         partial = partial.reshape(outer, inner, piece, step)
         sent = swap(lax.dynamic_index_in_dim(partial, other, 1, keepdims=False), "tc")
         half = lax.dynamic_index_in_dim(partial, tc, 1, keepdims=False).astype(jnp.float32)
         half = half + sent.astype(jnp.float32)
         if outer == 2:
-            across = swap(
-                lax.dynamic_index_in_dim(half, 1 - ty, 0, keepdims=False).astype(jnp.bfloat16), "ty"
+            payloads.append(
+                lax.dynamic_index_in_dim(half, 1 - ty, 0, keepdims=False).astype(jnp.bfloat16)
             )
+        else:
+            payloads.append(None)
+        done.append(half)
+    for c in range(chunks):
+        half = done[c]
+        if outer == 2:
+            across = swap(payloads[c], "ty")
             mine = lax.dynamic_index_in_dim(half, ty, 0, keepdims=False)
-            done.append((mine + across.astype(jnp.float32)).astype(jnp.bfloat16))
+            done[c] = (mine + across.astype(jnp.float32)).astype(jnp.bfloat16)
         else:
-            done.append(
-                lax.psum_scatter(half.astype(jnp.bfloat16), "ty", scatter_dimension=0, tiled=True)[0]
-            )
+            done[c] = lax.psum_scatter(
+                half.astype(jnp.bfloat16), "ty", scatter_dimension=0, tiled=True
+            )[0]
     return jnp.concatenate(done, axis=1)
 
 

time: 134 us -> 132 us (0.985)
  waiting for transfers between devices: 35.4 us -> 32.4 us
    ppermute x10, waiting for transfers between devices: 28.9 us -> 25.8 us  [swap(): return lax.ppermute(value, axis, [(0, 1), (1, 0)])]
  transfers between devices with their start and end apart: 14 -> 14, of which waited for: 8 -> 8; matrix products, arithmetic and copies ran while one was open for 22% -> 24% of each run, Pallas kernels for 0% -> 0%
where the time goes in v12:
time: 132 us; the launch traced here: 131 us
  waiting for transfers between devices  32.4 us (25%)
  starting transfers between devices  32.3 us (24%)
  matrix products  28.3 us (21%)
  other arithmetic  19.8 us (15%)
  local copies, waits for them, and re-layouts  11.9 us (9%)
  Pallas kernels  6.01 us (5%)
    ppermute x10, waiting for transfers between devices, swap(): return lax.ppermute(value, axis, [(0, 1), (1, 0)])  25.8 us
    ppermute x4, starting transfers between devices, shifted(): return lax.ppermute(value, axis, pairs)  23.9 us
    dot_general x4, matrix products, reduce_rows(): jnp.dot(source, out_weight[:, c * step:(c + 1) * step], preferred_element...  11.9 us
    dot_general x1, matrix products, diagonal_of(): jnp.einsum('ghij,jghp->ighp', mixing, inner_block, preferred_element_type...  10.5 us
    ppermute x10, starting transfers between devices, swap(): return lax.ppermute(value, axis, [(0, 1), (1, 0)])  8.42 us
    unnamed x40, local copies, waits for them, and re-layouts  6.53 us
    ppermute x4, waiting for transfers between devices, shifted(): return lax.ppermute(value, axis, pairs)  6.53 us
    pallas_call x1, Pallas kernels, conv_silu_kernel(): pl.pallas_call(conv_kernel, grid=(width // block,), in_specs=[pl.BlockSpe...  6.01 us
  transfers between devices with their start and end apart: 14, of which 8 were waited for; matrix products, arithmetic and copies ran while one was open for 24% of the time, Pallas kernels for 0%

profile of v12, /device:TPU:0, one launch (start us, length us, event | category | flops | bytes accessed | tf_op | source)
XLA Modules:
  0.0 131.3 jit_solution(17889914812044434705)
XLA Ops:
  1.5 4.8 %collective-permute-start = (bf16[3,2560]{1,0:T(4,128)(2,1)S(1)}, bf16[3,2560]{1,0:T(4,128)(2,1)S(1)}, u32[]{:S(2)}, u32[]{:S(2)}) collective-permute-start(bf16[3,2560]{1,0:T(4,128)(2,1)S(1)} %pad_maximum_fusion.5), channel_id=1, source_target_pairs={{0,4},{4,8},{8,12},{12,16},{16,20},{20,24},{24,28},{1,5},{5,9},{9,... | collective-permute-start | bytes 46088 | tf_op jit(solution)/shard_map/ppermute | solution.py:25
  7.9 2.3 %reduce-window.6 = f32[16,2,4,128]{3,0,1,2:T(8,128)S(1)} reduce-window(f32[16,2,4,128]{3,0,1,2:T(8,128)S(1)} %bitcast.238, f32[]{:T(128)} %constant.68.clone.1), window={size=1x1x1x128 pad=0_0x0_0x0_0x127_0}, to_apply=%region_0.1 | reduce-window | flops 2080768 | bytes 131076 | tf_op jit(solution)/shard_map/reduce-window
  12.3 1.3 copy.44
  14.3 1.3 reshape.137.b_ref
  15.8 1.3 %multiply_convert_fusion.6 = bf16[512,2,256]{0,2,1:T(8,128)(2,1)S(1)} fusion(bf16[512,2,256]{0,2,1:T(8,128)(2,1)S(1)} %copy.44, bf16[3,2,256]{0,2,1:T(8,128)(2,1)S(1)} %bitcast.234, f32[2,256]{1,0:T(2,128)S(1)} %get-tuple-element.40, f32[2,256]{1,0:T(2,128)S(1)} %get-tuple-element.41, f32[2,256]{1,0:T(2,128)S(1)} %get-tuple-element.39, ...), kind=kLoop, calls=%fused_computation.39 | loop fusion | flops 6815744 | bytes 1061888 | tf_op jit(solution)/shard_map/convert_element_type | solution.py:34
  18.6 6.0 %shard_map.118 = bf16[2048,512]{1,0:T(8,128)(2,1)} custom-call(bf16[8,2048]{1,0:T(8,128)(2,1)} %concatenate.28.halo_ref, bf16[512,2048]{1,0:T(8,128)(2,1)} %x_ref.1, bf16[4,2048]{1,0:T(4,128)(2,1)} %w_ref.1, bf16[1,2048]{1,0:T(2,128)(2,1)} %reshape.137.b_ref), custom_call_target="tpu_custom_call" | custom-call | tf_op jit(solution)/shard_map/pallas_call | solution.py:50
  24.6 2.3 %fusion.18 = f32[2,16,64,128]{3,2,1,0:T(8,128)S(1)} fusion(bf16[512,2,128,1]{0,2,3,1:T(8,128)(2,1)S(1)} %bitcast.223, bf16[512,2,16,64]{0,3,2,1:T(8,128)(2,1)} %bitcast.210, f32[512,2,16]{0,2,1:T(8,128)S(1)} %get-tuple-element.33), kind=kOutput, calls=%fused_computation.26 | convolution fusion | flops 271581184 | bytes 3473408 | tf_op jit(solution)/shard_map/jghp,jgn->ghpn/dot_general | solution.py:81
  27.0 1.6 %collective-permute-start.1 = (bf16[1040,128]{1,0:T(8,128)(2,1)S(1)}, bf16[1040,128]{1,0:T(8,128)(2,1)S(1)}, u32[]{:S(2)}, u32[]{:S(2)}) collective-permute-start(bf16[1040,128]{1,0:T(8,128)(2,1)S(1)} %pad_maximum_fusion.3), channel_id=1, source_target_pairs={{0,4},{4,0},{1,5},{5,1},{2,6},{6,2},{3,7},{7,3},{8,12},{12,8},{9,1... | collective-permute-start | bytes 798728 | tf_op jit(solution)/shard_map/ppermute | solution.py:271
  29.5 5.5 %collective-permute-done.1 = bf16[1040,128]{1,0:T(8,128)(2,1)S(1)} collective-permute-done((bf16[1040,128]{1,0:T(8,128)(2,1)S(1)}, bf16[1040,128]{1,0:T(8,128)(2,1)S(1)}, u32[]{:S(2)}, u32[]{:S(2)}) %collective-permute-start.1) | collective-permute-done | bytes 266272 | tf_op jit(solution)/shard_map/ppermute | solution.py:271
  38.9 4.5 %collective-permute-start.3 = (bf16[1040,128]{1,0:T(8,128)(2,1)S(1)}, bf16[1040,128]{1,0:T(8,128)(2,1)S(1)}, u32[]{:S(2)}, u32[]{:S(2)}) collective-permute-start(bf16[1040,128]{1,0:T(8,128)(2,1)S(1)} %pad_maximum_fusion.4), channel_id=1, source_target_pairs={{0,16},{8,24},{1,17},{9,25},{2,18},{10,26},{3,19},{11,27},{4,20},{... | collective-permute-start | bytes 798728 | tf_op jit(solution)/shard_map/ppermute | solution.py:25
  43.5 3.5 %collective-permute-start.2 = (bf16[1040,128]{1,0:T(8,128)(2,1)S(1)}, bf16[1040,128]{1,0:T(8,128)(2,1)S(1)}, u32[]{:S(2)}, u32[]{:S(2)}) collective-permute-start(bf16[1040,128]{1,0:T(8,128)(2,1)S(1)} %pad_maximum_fusion.4), channel_id=1, source_target_pairs={{0,8},{8,16},{16,24},{1,9},{9,17},{17,25},{2,10},{10,18},{18,26},{... | collective-permute-start | bytes 798728 | tf_op jit(solution)/shard_map/ppermute | solution.py:25
  47.1 3.2 %collective-permute-done.3 = bf16[1040,128]{1,0:T(8,128)(2,1)S(1)} collective-permute-done((bf16[1040,128]{1,0:T(8,128)(2,1)S(1)}, bf16[1040,128]{1,0:T(8,128)(2,1)S(1)}, u32[]{:S(2)}, u32[]{:S(2)}) %collective-permute-start.3) | collective-permute-done | bytes 266272 | tf_op jit(solution)/shard_map/ppermute | solution.py:25
  50.2 3.4 %collective-permute-done.2 = bf16[1040,128]{1,0:T(8,128)(2,1)S(1)} collective-permute-done((bf16[1040,128]{1,0:T(8,128)(2,1)S(1)}, bf16[1040,128]{1,0:T(8,128)(2,1)S(1)}, u32[]{:S(2)}, u32[]{:S(2)}) %collective-permute-start.2) | collective-permute-done | bytes 266272 | tf_op jit(solution)/shard_map/ppermute | solution.py:25
  53.9 11.0 %collective-permute-start.4 = (bf16[16,64,128]{2,1,0:T(8,128)(2,1)S(1)}, bf16[16,64,128]{2,1,0:T(8,128)(2,1)S(1)}, u32[]{:S(2)}, u32[]{:S(2)}) collective-permute-start(bf16[16,64,128]{2,1,0:T(8,128)(2,1)S(1)} %fusion.42), channel_id=1, source_target_pairs={{0,16},{8,24},{1,17},{9,25},{2,18},{10,26},{3,19},{11,27},{4,20},{... | collective-permute-start | bytes 786440 | tf_op jit(solution)/shard_map/ppermute | solution.py:25
  64.9 1.4 %fusion.68 = f32[2,512,512]{2,1,0:T(8,128)S(1)} fusion(bf16[512,2,128]{0,2,1:T(8,128)(2,1)} %bitcast.221, bf16[512,2,128]{0,2,1:T(8,128)(2,1)S(1)} %bitcast.224), kind=kOutput, calls=%fused_computation.134 | convolution fusion | flops 134217728 | bytes 2621440 | tf_op jit(solution)/shard_map/ign,jgn->gij/dot_general | solution.py:71
  66.4 10.5 %fusion.17 = f32[512,2,16,64]{0,3,2,1:T(8,128)} fusion(bf16[512,2,16,64]{0,3,2,1:T(8,128)(2,1)S(1)} %bitcast.211, f32[2,16,512]{2,1,0:T(8,128)S(1)} %bitcast.237, f32[2,512,512]{2,1,0:T(8,128)S(1)} %fusion.68, f32[2,16,512]{2,1,0:T(8,128)S(1)} %copy-done.9, pred[512,512]{1,0:T(8,128)(4,1)S(1)} %iota_compare_fusion), kind=kOutput, calls=%fused_computation.25 | convolution fusion | flops 1115684864 | bytes 8781824 | tf_op jit(solution)/shard_map/ghij,jghp->ighp/dot_general | solution.py:75
  78.7 3.9 %copy.50 = bf16[512,2048]{0,1:T(8,128)(2,1)} copy(bf16[512,2048]{1,0:T(8,128)(2,1)} %param.14) | data formatting | bytes 4194304 | tf_op args[2]
  82.8 3.5 %collective-permute-done.5 = bf16[16,64,128]{2,1,0:T(8,128)(2,1)} collective-permute-done((bf16[16,64,128]{2,1,0:T(8,128)(2,1)}, bf16[16,64,128]{2,1,0:T(8,128)(2,1)}, u32[]{:S(2)}, u32[]{:S(2)}) %collective-permute-start.5) | collective-permute-done | bytes 262176 | tf_op jit(solution)/shard_map/ppermute | solution.py:271
  86.3 1.5 %convert_select_fusion.1 = (f32[16,64,128]{2,1,0:T(8,128)S(1)}, f32[16,64,128]{2,1,0:T(8,128)S(1)}) fusion(bf16[16,64,128]{2,1,0:T(8,128)(2,1)} %collective-permute-done.5, pred[]{:T(512)S(6)} %eq.3, f32[16,64,128]{2,1,0:T(8,128)} %bitcast.213, f32[16]{0:T(128)S(1)} %copy-done.10, bf16[16,64,128]{2,1,0:T(8,128)(2,1)} %bitcast.220, ...), kind=kLoop, calls=%fused_computation.43 | loop fusion | flops 1835008 | bytes 3671232 | tf_op jit(solution)/shard_map/jit(_where)/select_n | solution.py:187
  89.0 2.1 %fusion.6 = f32[1,512,2,16,64]{1,4,3,2,0:T(8,128)S(1)} fusion(f32[512,2,16,64]{0,3,2,1:T(8,128)S(1)} %copy-done.3, f32[512,2,16]{0,2,1:T(8,128)S(1)} %get-tuple-element.32, f32[2,16,64,128]{3,2,1,0:T(8,128)S(1)} %bitcast.214, bf16[512,2,128,1]{0,2,3,1:T(8,128)(2,1)S(1)} %bitcast.222), kind=kOutput, calls=%fused_computation.10 | convolution fusion | flops 1612709888 | bytes 9764864 | tf_op jit(solution)/shard_map/vmap(ign,ghpn->ighp)/dot_general | solution.py:92
  91.1 2.2 %bitcast_reduce_fusion = (f32[512,2]{0,1:T(2,128)S(1)}, f32[512,2048]{0,1:T(8,128)S(1)}) fusion(bf16[512,2048]{0,1:T(8,128)(2,1)S(1)} %copy-done.1, bf16[2048,512]{1,0:T(8,128)(2,1)S(1)} %copy-done, f32[2048]{0:T(1024)S(1)} %mul.224, f32[1,512,2,16,64]{1,4,3,2,0:T(8,128)S(1)} %fusion.6), kind=kLoop, calls=%fused_computation.14 | loop fusion | flops 11533312 | bytes 12595200 | tf_op jit(solution)/shard_map/reduce_sum | solution.py:263
  93.8 4.9 %fusion.20 = bf16[512,1024]{1,0:T(8,128)(2,1)S(1)} fusion(bf16[512,2048]{0,1:T(8,128)(2,1)S(1)} %fusion.8, bf16[2048,4096]{1,0:T(8,128)(2,1)} %param.23), kind=kOutput, calls=%fused_computation.28 | convolution fusion | flops 2148007936 | bytes 7340032 | tf_op jit(solution)/shard_map/dot_general | solution.py:299
  98.7 2.3 %fusion.23 = bf16[512,1024]{1,0:T(8,128)(2,1)S(1)} fusion(bf16[512,2048]{0,1:T(8,128)(2,1)S(1)} %fusion.8, bf16[2048,4096]{1,0:T(8,128)(2,1)S(1)} %bitcast.242), kind=kOutput, calls=%fused_computation.29 | convolution fusion | flops 2148007936 | bytes 7340032 | tf_op jit(solution)/shard_map/dot_general | solution.py:299
  101.8 2.3 %fusion.26 = bf16[512,1024]{1,0:T(8,128)(2,1)S(1)} fusion(bf16[512,2048]{0,1:T(8,128)(2,1)S(1)} %fusion.8, bf16[2048,4096]{1,0:T(8,128)(2,1)S(1)} %bitcast.242), kind=kOutput, calls=%fused_computation.30 | convolution fusion | flops 2148007936 | bytes 7340032 | tf_op jit(solution)/shard_map/dot_general | solution.py:299
  104.5 1.6 %collective-permute-start.7 = (bf16[128,1024]{1,0:T(8,128)(2,1)S(1)}, bf16[128,1024]{1,0:T(8,128)(2,1)S(1)}, u32[]{:S(2)}, u32[]{:S(2)}) collective-permute-start(bf16[128,1024]{1,0:T(8,128)(2,1)S(1)} %fusion.44), channel_id=1, source_target_pairs={{0,2},{2,0},{1,3},{3,1},{4,6},{6,4},{5,7},{7,5},{8,10},{10,8},{9,1... | collective-permute-start | bytes 786440 | tf_op jit(solution)/shard_map/ppermute | solution.py:271
  106.9 2.3 %fusion.29 = bf16[512,1024]{1,0:T(8,128)(2,1)S(1)} fusion(bf16[512,2048]{0,1:T(8,128)(2,1)S(1)} %fusion.8, bf16[2048,4096]{1,0:T(8,128)(2,1)S(1)} %bitcast.242), kind=kOutput, calls=%fused_computation.31 | convolution fusion | flops 2148007936 | bytes 7340032 | tf_op jit(solution)/shard_map/dot_general | solution.py:299
  109.7 1.6 %collective-permute-start.11 = (bf16[128,1024]{1,0:T(8,128)(2,1)S(1)}, bf16[128,1024]{1,0:T(8,128)(2,1)S(1)}, u32[]{:S(2)}, u32[]{:S(2)}) collective-permute-start(bf16[128,1024]{1,0:T(8,128)(2,1)S(1)} %fusion.46), channel_id=1, source_target_pairs={{0,2},{2,0},{1,3},{3,1},{4,6},{6,4},{5,7},{7,5},{8,10},{10,8},{9,1... | collective-permute-start | bytes 786440 | tf_op jit(solution)/shard_map/ppermute | solution.py:271
  111.2 2.5 %collective-permute-done.7 = bf16[128,1024]{1,0:T(8,128)(2,1)S(1)} collective-permute-done((bf16[128,1024]{1,0:T(8,128)(2,1)S(1)}, bf16[128,1024]{1,0:T(8,128)(2,1)S(1)}, u32[]{:S(2)}, u32[]{:S(2)}) %collective-permute-start.7) | collective-permute-done | bytes 262176 | tf_op jit(solution)/shard_map/ppermute | solution.py:271
  114.0 1.6 %collective-permute-start.13 = (bf16[128,1024]{1,0:T(8,128)(2,1)S(1)}, bf16[128,1024]{1,0:T(8,128)(2,1)S(1)}, u32[]{:S(2)}, u32[]{:S(2)}) collective-permute-start(bf16[128,1024]{1,0:T(8,128)(2,1)S(1)} %fusion.47), channel_id=1, source_target_pairs={{0,2},{2,0},{1,3},{3,1},{4,6},{6,4},{5,7},{7,5},{8,10},{10,8},{9,1... | collective-permute-start | bytes 786440 | tf_op jit(solution)/shard_map/ppermute | solution.py:271
  115.6 3.7 %collective-permute-done.9 = bf16[128,1024]{1,0:T(8,128)(2,1)S(1)} collective-permute-done((bf16[128,1024]{1,0:T(8,128)(2,1)S(1)}, bf16[128,1024]{1,0:T(8,128)(2,1)S(1)}, u32[]{:S(2)}, u32[]{:S(2)}) %collective-permute-start.9) | collective-permute-done | bytes 262176 | tf_op jit(solution)/shard_map/ppermute | solution.py:271
  119.4 5.6 %collective-permute-done.11 = bf16[128,1024]{1,0:T(8,128)(2,1)S(1)} collective-permute-done((bf16[128,1024]{1,0:T(8,128)(2,1)S(1)}, bf16[128,1024]{1,0:T(8,128)(2,1)S(1)}, u32[]{:S(2)}, u32[]{:S(2)}) %collective-permute-start.11) | collective-permute-done | bytes 262176 | tf_op jit(solution)/shard_map/ppermute | solution.py:271
  125.0 5.1 %collective-permute-done.13 = bf16[128,1024]{1,0:T(8,128)(2,1)S(1)} collective-permute-done((bf16[128,1024]{1,0:T(8,128)(2,1)S(1)}, bf16[128,1024]{1,0:T(8,128)(2,1)S(1)}, u32[]{:S(2)}, u32[]{:S(2)}) %collective-permute-start.13) | collective-permute-done | bytes 262176 | tf_op jit(solution)/shard_map/ppermute | solution.py:271
  (119 shorter events, 19.9 us)
Async XLA Ops:
  1.5 14.1 %collective-permute-start = (bf16[3,2560]{1,0:T(4,128)(2,1)S(1)}, bf16[3,2560]{1,0:T(4,128)(2,1)S(1)}, u32[]{:S(2)}, u32[]{:S(2)}) collective-permute-start(bf16[3,2560]{1,0:T(4,128)(2,1)S(1)} %pad_maximum_fusion.5), channel_id=1, source_target_pairs={{0,4},{4,8},{8,12},{12,16},{16,20},{20,24},{24,28},{1,5},{5,9},{9,... | collective-permute-start | bytes 46088 | tf_op jit(solution)/shard_map/ppermute | solution.py:25
  17.9 9.1 %copy-start.6 = (bf16[512,1,256]{0,2,1:T(8,128)(2,1)}, bf16[512,1,256]{0,2,1:T(8,128)(2,1)S(1)}, u32[]{:S(2)}) copy-start(bf16[512,1,256]{0,2,1:T(8,128)(2,1)S(1)} %get-tuple-element.31) | copy-start | bytes 786436
  27.0 39.4 %copy-start = (bf16[2048,512]{1,0:T(8,128)(2,1)S(1)}, bf16[2048,512]{1,0:T(8,128)(2,1)}, u32[]{:S(2)}) copy-start(bf16[2048,512]{1,0:T(8,128)(2,1)} %shard_map.118) | copy-start | bytes 6291460
  27.0 7.9 %collective-permute-start.1 = (bf16[1040,128]{1,0:T(8,128)(2,1)S(1)}, bf16[1040,128]{1,0:T(8,128)(2,1)S(1)}, u32[]{:S(2)}, u32[]{:S(2)}) collective-permute-start(bf16[1040,128]{1,0:T(8,128)(2,1)S(1)} %pad_maximum_fusion.3), channel_id=1, source_target_pairs={{0,4},{4,0},{1,5},{5,1},{2,6},{6,2},{3,7},{7,3},{8,12},{12,8},{9,1... | collective-permute-start | bytes 798728 | tf_op jit(solution)/shard_map/ppermute | solution.py:271
  35.6 0.5 copy-start.12
  36.3 28.7 %copy-start.7 = (bf16[512,1,256]{0,2,1:T(8,128)(2,1)S(1)}, bf16[512,1,256]{0,2,1:T(8,128)(2,1)}, u32[]{:S(2)}) copy-start(bf16[512,1,256]{0,2,1:T(8,128)(2,1)} %copy-done.6) | copy-start | bytes 786436
  36.3 30.1 %copy-start.9 = (f32[2,16,512]{2,1,0:T(8,128)S(1)}, f32[2,16,512]{2,1,0:T(8,128)}, u32[]{:S(2)}) copy-start(f32[2,16,512]{2,1,0:T(8,128)} %get-tuple-element.34) | copy-start | bytes 196612
  38.9 11.3 %collective-permute-start.3 = (bf16[1040,128]{1,0:T(8,128)(2,1)S(1)}, bf16[1040,128]{1,0:T(8,128)(2,1)S(1)}, u32[]{:S(2)}, u32[]{:S(2)}) collective-permute-start(bf16[1040,128]{1,0:T(8,128)(2,1)S(1)} %pad_maximum_fusion.4), channel_id=1, source_target_pairs={{0,16},{8,24},{1,17},{9,25},{2,18},{10,26},{3,19},{11,27},{4,20},{... | collective-permute-start | bytes 798728 | tf_op jit(solution)/shard_map/ppermute | solution.py:25
  43.5 10.1 %collective-permute-start.2 = (bf16[1040,128]{1,0:T(8,128)(2,1)S(1)}, bf16[1040,128]{1,0:T(8,128)(2,1)S(1)}, u32[]{:S(2)}, u32[]{:S(2)}) collective-permute-start(bf16[1040,128]{1,0:T(8,128)(2,1)S(1)} %pad_maximum_fusion.4), channel_id=1, source_target_pairs={{0,8},{8,16},{16,24},{1,9},{9,17},{17,25},{2,10},{10,18},{18,26},{... | collective-permute-start | bytes 798728 | tf_op jit(solution)/shard_map/ppermute | solution.py:25
  47.1 29.9 %copy-start.2 = (f32[1024,128]{1,0:T(8,128)}, f32[1024,128]{1,0:T(8,128)S(1)}, u32[]{:S(2)}) copy-start(f32[1024,128]{1,0:T(8,128)S(1)} %slice_convert_fusion) | copy-start | bytes 1572868
  53.7 23.2 %copy-start.4 = (bf16[1024,128]{1,0:T(8,128)(2,1)}, bf16[1024,128]{1,0:T(8,128)(2,1)S(1)}, u32[]{:S(2)}) copy-start(bf16[1024,128]{1,0:T(8,128)(2,1)S(1)} %slice.173) | copy-start | bytes 786436
  53.9 23.0 %collective-permute-start.4 = (bf16[16,64,128]{2,1,0:T(8,128)(2,1)S(1)}, bf16[16,64,128]{2,1,0:T(8,128)(2,1)S(1)}, u32[]{:S(2)}, u32[]{:S(2)}) collective-permute-start(bf16[16,64,128]{2,1,0:T(8,128)(2,1)S(1)} %fusion.42), channel_id=1, source_target_pairs={{0,16},{8,24},{1,17},{9,25},{2,18},{10,26},{3,19},{11,27},{4,20},{... | collective-permute-start | bytes 786440 | tf_op jit(solution)/shard_map/ppermute | solution.py:25
  66.4 10.6 %copy-start.10 = (f32[16]{0:T(128)S(1)}, f32[16]{0:T(128)}, u32[]{:S(2)}) copy-start(f32[16]{0:T(128)} %get-tuple-element.29) | copy-start | bytes 196
  76.9 5.7 %copy-start.13 = (f32[32]{0:T(128)S(1)}, f32[32]{0:T(128)}, u32[]{:S(2)}) copy-start(f32[32]{0:T(128)} %param.21) | copy-start | bytes 388
  76.9 5.9 %copy-start.11 = (bf16[2048]{0:T(1024)(128)(2,1)S(1)}, bf16[2048]{0:T(1024)(128)(2,1)}, u32[]{:S(2)}) copy-start(bf16[2048]{0:T(1024)(128)(2,1)} %param.22) | copy-start | bytes 12292
  76.9 1.1 copy-start.8
  78.0 8.3 %collective-permute-start.5 = (bf16[16,64,128]{2,1,0:T(8,128)(2,1)}, bf16[16,64,128]{2,1,0:T(8,128)(2,1)}, u32[]{:S(2)}, u32[]{:S(2)}) collective-permute-start(bf16[16,64,128]{2,1,0:T(8,128)(2,1)} %select_convert_fusion), channel_id=1, source_target_pairs={{0,4},{4,0},{1,5},{5,1},{2,6},{6,2},{3,7},{7,3},{8,12},{12,8},{9,1... | collective-permute-start | bytes 786440 | tf_op jit(solution)/shard_map/ppermute | solution.py:271
  82.8 6.1 %copy-start.3 = (f32[512,2,16,64]{0,3,2,1:T(8,128)S(1)}, f32[512,2,16,64]{0,3,2,1:T(8,128)}, u32[]{:S(2)}) copy-start(f32[512,2,16,64]{0,3,2,1:T(8,128)} %fusion.17) | copy-start | bytes 12582916
  82.8 6.1 %copy-start.5 = (bf16[512,1,256]{0,2,1:T(8,128)(2,1)S(1)}, bf16[512,1,256]{0,2,1:T(8,128)(2,1)}, u32[]{:S(2)}) copy-start(bf16[512,1,256]{0,2,1:T(8,128)(2,1)} %get-tuple-element.30) | copy-start | bytes 786436
  88.9 2.1 %copy-start.1 = (bf16[512,2048]{0,1:T(8,128)(2,1)S(1)}, bf16[512,2048]{0,1:T(8,128)(2,1)}, u32[]{:S(2)}) copy-start(bf16[512,2048]{0,1:T(8,128)(2,1)} %copy.50) | copy-start | bytes 6291460
  91.1 7.6 %slice-start = ((s8[16777216]{0:T(1024)(128)(4,1)}), s8[4194304]{0:T(1024)(128)(4,1)S(1)}, s32[]{:S(2)}) async-start(s8[16777216]{0:T(1024)(128)(4,1)} %bitcast.241), calls=%async_computation | async-start | bytes 8388608
  91.1 7.6 %slice-start.1 = ((s8[16777216]{0:T(1024)(128)(4,1)}), s8[4194304]{0:T(1024)(128)(4,1)S(1)}, s32[]{:S(2)}) async-start(s8[16777216]{0:T(1024)(128)(4,1)} %bitcast.241), calls=%async_computation.1 | async-start | bytes 8388608
  93.3 5.4 %slice-start.2 = ((s8[16777216]{0:T(1024)(128)(4,1)}), s8[4194304]{0:T(1024)(128)(4,1)S(1)}, s32[]{:S(2)}) async-start(s8[16777216]{0:T(1024)(128)(4,1)} %bitcast.241), calls=%async_computation.2 | async-start | bytes 8388608
  93.8 4.9 %slice-start.3 = ((s8[16777216]{0:T(1024)(128)(4,1)}), s8[4194304]{0:T(1024)(128)(4,1)S(1)}, s32[]{:S(2)}) async-start(s8[16777216]{0:T(1024)(128)(4,1)} %bitcast.241), calls=%async_computation.3 | async-start | bytes 8388608
  101.1 3.2 %collective-permute-start.6 = (bf16[2,128,1024]{2,1,0:T(8,128)(2,1)S(1)}, bf16[2,128,1024]{2,1,0:T(8,128)(2,1)S(1)}, u32[]{:S(2)}, u32[]{:S(2)}) collective-permute-start(bf16[2,128,1024]{2,1,0:T(8,128)(2,1)S(1)} %dynamic-slice_bitcast_fusion.3), channel_id=1, source_target_pairs={{0,1},{1,0},{2,3},{3,2},{4,5},{5,4},{6,7},{7,6},{8,9},{9,8},{10,11... | collective-permute-start | bytes 1572872 | tf_op jit(solution)/shard_map/ppermute | solution.py:271
  101.3 4.9 %collective-permute-start.8 = (bf16[2,128,1024]{2,1,0:T(8,128)(2,1)S(1)}, bf16[2,128,1024]{2,1,0:T(8,128)(2,1)S(1)}, u32[]{:S(2)}, u32[]{:S(2)}) collective-permute-start(bf16[2,128,1024]{2,1,0:T(8,128)(2,1)S(1)} %dynamic-slice_bitcast_fusion.2), channel_id=1, source_target_pairs={{0,1},{1,0},{2,3},{3,2},{4,5},{5,4},{6,7},{7,6},{8,9},{9,8},{10,11... | collective-permute-start | bytes 1572872 | tf_op jit(solution)/shard_map/ppermute | solution.py:271
  104.2 5.2 %collective-permute-start.10 = (bf16[2,128,1024]{2,1,0:T(8,128)(2,1)S(1)}, bf16[2,128,1024]{2,1,0:T(8,128)(2,1)S(1)}, u32[]{:S(2)}, u32[]{:S(2)}) collective-permute-start(bf16[2,128,1024]{2,1,0:T(8,128)(2,1)S(1)} %dynamic-slice_bitcast_fusion.1), channel_id=1, source_target_pairs={{0,1},{1,0},{2,3},{3,2},{4,5},{5,4},{6,7},{7,6},{8,9},{9,8},{10,11... | collective-permute-start | bytes 1572872 | tf_op jit(solution)/shard_map/ppermute | solution.py:271
  104.5 9.2 %collective-permute-start.7 = (bf16[128,1024]{1,0:T(8,128)(2,1)S(1)}, bf16[128,1024]{1,0:T(8,128)(2,1)S(1)}, u32[]{:S(2)}, u32[]{:S(2)}) collective-permute-start(bf16[128,1024]{1,0:T(8,128)(2,1)S(1)} %fusion.44), channel_id=1, source_target_pairs={{0,2},{2,0},{1,3},{3,1},{4,6},{6,4},{5,7},{7,5},{8,10},{10,8},{9,1... | collective-permute-start | bytes 786440 | tf_op jit(solution)/shard_map/ppermute | solution.py:271
  106.4 13.0 %collective-permute-start.9 = (bf16[128,1024]{1,0:T(8,128)(2,1)S(1)}, bf16[128,1024]{1,0:T(8,128)(2,1)S(1)}, u32[]{:S(2)}, u32[]{:S(2)}) collective-permute-start(bf16[128,1024]{1,0:T(8,128)(2,1)S(1)} %fusion.45), channel_id=1, source_target_pairs={{0,2},{2,0},{1,3},{3,1},{4,6},{6,4},{5,7},{7,5},{8,10},{10,8},{9,1... | collective-permute-start | bytes 786440 | tf_op jit(solution)/shard_map/ppermute | solution.py:271
  109.3 4.4 %collective-permute-start.12 = (bf16[2,128,1024]{2,1,0:T(8,128)(2,1)S(1)}, bf16[2,128,1024]{2,1,0:T(8,128)(2,1)S(1)}, u32[]{:S(2)}, u32[]{:S(2)}) collective-permute-start(bf16[2,128,1024]{2,1,0:T(8,128)(2,1)S(1)} %dynamic-slice_bitcast_fusion), channel_id=1, source_target_pairs={{0,1},{1,0},{2,3},{3,2},{4,5},{5,4},{6,7},{7,6},{8,9},{9,8},{10,11... | collective-permute-start | bytes 1572872 | tf_op jit(solution)/shard_map/ppermute | solution.py:271
  109.7 15.3 %collective-permute-start.11 = (bf16[128,1024]{1,0:T(8,128)(2,1)S(1)}, bf16[128,1024]{1,0:T(8,128)(2,1)S(1)}, u32[]{:S(2)}, u32[]{:S(2)}) collective-permute-start(bf16[128,1024]{1,0:T(8,128)(2,1)S(1)} %fusion.46), channel_id=1, source_target_pairs={{0,2},{2,0},{1,3},{3,1},{4,6},{6,4},{5,7},{7,5},{8,10},{10,8},{9,1... | collective-permute-start | bytes 786440 | tf_op jit(solution)/shard_map/ppermute | solution.py:271
  114.0 16.1 %collective-permute-start.13 = (bf16[128,1024]{1,0:T(8,128)(2,1)S(1)}, bf16[128,1024]{1,0:T(8,128)(2,1)S(1)}, u32[]{:S(2)}, u32[]{:S(2)}) collective-permute-start(bf16[128,1024]{1,0:T(8,128)(2,1)S(1)} %fusion.47), channel_id=1, source_target_pairs={{0,2},{2,0},{1,3},{3,1},{4,6},{6,4},{5,7},{7,5},{8,10},{10,8},{9,1... | collective-permute-start | bytes 786440 | tf_op jit(solution)/shard_map/ppermute | solution.py:271

commit v13 on v12

--- a/solution.py
+++ b/solution.py
@@ -213,12 +213,14 @@
     inner_conv = jnp.transpose(
         conv_silu_kernel(halo[:, :inner_width], inner_input, conv_inner, bias_inner)
     )
-    state_conv = conv_silu(
-        jnp.concatenate([halo[:, inner_width:].reshape((margin,) + state_input.shape[1:]), state_input], axis=0),
-        conv_states,
-        bias_states,
-        tokens,
-    )
+    state_conv = jnp.transpose(
+        conv_silu_kernel(
+            halo[:, inner_width:],
+            state_input.reshape(tokens, -1),
+            conv_states.reshape(CONV, -1),
+            bias_states.reshape(-1),
+        )
+    ).reshape(state_input.shape)
     groups_here = state_input.shape[2] // STATE
     per_group = SSM_HEAD_COUNT // GROUPS
     blocks = tokens // BLK

time: 132 us -> 137 us (1.038)
  local copies, waits for them, and re-layouts: 11.9 us -> 16.4 us
  Pallas kernels: 6.01 us -> 8.92 us
  other arithmetic: 19.8 us -> 17.1 us
    unnamed x40 -> x42, local copies, waits for them, and re-layouts: 6.53 us -> 9.63 us
    pallas_call x1 -> x2, Pallas kernels: 6.01 us -> 8.92 us  [conv_silu_kernel(): pl.pallas_call(conv_kernel, grid=(width // block,), in_specs=[pl.BlockSpe...]
    convert_element_type x2 -> x0, other arithmetic: 2.02 us -> none  [the longest x1 1.34 us: conv_silu(): return lax.optimization_barrier(jax.nn.silu(summed).astype(jnp.bfloat16))]
  transfers between devices with their start and end apart: 14 -> 14, of which waited for: 8 -> 8; matrix products, arithmetic and copies ran while one was open for 24% -> 25% of each run, Pallas kernels for 0% -> 0%
where the time goes in v13:
time: 137 us; the launch traced here: 136 us
  waiting for transfers between devices  32.4 us (24%)
  starting transfers between devices  32.3 us (24%)
  matrix products  28.3 us (21%)
  other arithmetic  17.1 us (12%)
  local copies, waits for them, and re-layouts  16.4 us (12%)
  Pallas kernels  8.92 us (7%)
    ppermute x10, waiting for transfers between devices, swap(): return lax.ppermute(value, axis, [(0, 1), (1, 0)])  25.8 us
    ppermute x4, starting transfers between devices, shifted(): return lax.ppermute(value, axis, pairs)  23.9 us
    dot_general x4, matrix products, reduce_rows(): jnp.dot(source, out_weight[:, c * step:(c + 1) * step], preferred_element...  11.9 us
    dot_general x1, matrix products, diagonal_of(): jnp.einsum('ghij,jghp->ighp', mixing, inner_block, preferred_element_type...  10.5 us
    unnamed x42, local copies, waits for them, and re-layouts  9.63 us
    pallas_call x2, Pallas kernels, conv_silu_kernel(): pl.pallas_call(conv_kernel, grid=(width // block,), in_specs=[pl.BlockSpe...  8.92 us
    ppermute x10, starting transfers between devices, swap(): return lax.ppermute(value, axis, [(0, 1), (1, 0)])  8.41 us
    ppermute x4, waiting for transfers between devices, shifted(): return lax.ppermute(value, axis, pairs)  6.52 us
  transfers between devices with their start and end apart: 14, of which 8 were waited for; matrix products, arithmetic and copies ran while one was open for 25% of the time, Pallas kernels for 0%

profile of v13, /device:TPU:0, one launch (start us, length us, event | category | flops | bytes accessed | tf_op | source)
XLA Modules:
  0.0 136.0 jit_solution(7553437744172163956)
XLA Ops:
  1.5 4.8 %collective-permute-start = (bf16[3,2560]{1,0:T(4,128)(2,1)S(1)}, bf16[3,2560]{1,0:T(4,128)(2,1)S(1)}, u32[]{:S(2)}, u32[]{:S(2)}) collective-permute-start(bf16[3,2560]{1,0:T(4,128)(2,1)S(1)} %pad_maximum_fusion.4), channel_id=1, source_target_pairs={{0,4},{4,8},{8,12},{12,16},{16,20},{20,24},{24,28},{1,5},{5,9},{9,... | collective-permute-start | bytes 46088 | tf_op jit(solution)/shard_map/ppermute | solution.py:25
  7.9 2.3 %reduce-window.6 = f32[16,2,4,128]{3,0,1,2:T(8,128)S(1)} reduce-window(f32[16,2,4,128]{3,0,1,2:T(8,128)S(1)} %bitcast.237, f32[]{:T(128)} %constant.67.clone.1), window={size=1x1x1x128 pad=0_0x0_0x0_0x127_0}, to_apply=%region_0.1 | reduce-window | flops 2080768 | bytes 131076 | tf_op jit(solution)/shard_map/reduce-window
  12.9 1.9 %copy.64 = bf16[64,8,2,256]{3,1,2,0:T(8,128)(2,1)} copy(bf16[64,8,2,256]{3,2,1,0:T(2,128)(2,1)} %bitcast.233) | data formatting | bytes 1048576
  18.6 2.8 %shard_map.119 = bf16[512,512]{1,0:T(8,128)(2,1)} custom-call(bf16[8,512]{1,0:T(8,128)(2,1)} %concatenate.29.halo_ref, bf16[512,512]{1,0:T(8,128)(2,1)} %bitcast.222, bf16[4,512]{1,0:T(4,128)(2,1)} %bitcast.238, bf16[1,512]{1,0:T(2,128)(2,1)} %bitcast.241), custom_call_target="tpu_custom_call" | custom-call | tf_op jit(solution)/shard_map/pallas_call | solution.py:50
  21.4 1.8 %fusion.65 = (bf16[512,1,256]{0,2,1:T(8,128)(2,1)}, bf16[512,1,256]{0,2,1:T(8,128)(2,1)S(1)}) fusion(bf16[512,2,256]{0,2,1:T(8,128)(2,1)} %bitcast.223), kind=kLoop, calls=%fused_computation.121 | loop fusion | bytes 1048576 | tf_op jit(solution)/shard_map/slice | solution.py:229
  23.2 6.1 %shard_map.118 = bf16[2048,512]{1,0:T(8,128)(2,1)} custom-call(bf16[8,2048]{1,0:T(8,128)(2,1)} %concatenate.28.halo_ref, bf16[512,2048]{1,0:T(8,128)(2,1)} %x_ref.1, bf16[4,2048]{1,0:T(4,128)(2,1)} %w_ref.1, bf16[1,2048]{1,0:T(2,128)(2,1)} %reshape.142.b_ref), custom_call_target="tpu_custom_call" | custom-call | tf_op jit(solution)/shard_map/pallas_call | solution.py:50
  29.3 2.3 %fusion.18 = f32[2,16,64,128]{3,2,1,0:T(8,128)S(1)} fusion(bf16[512,2,128,1]{0,2,3,1:T(8,128)(2,1)S(1)} %bitcast.220, bf16[512,2,16,64]{0,3,2,1:T(8,128)(2,1)} %bitcast.207, f32[512,2,16]{0,2,1:T(8,128)S(1)} %get-tuple-element.33), kind=kOutput, calls=%fused_computation.26 | convolution fusion | flops 271581184 | bytes 3473408 | tf_op jit(solution)/shard_map/jghp,jgn->ghpn/dot_general | solution.py:81
  31.7 1.6 %collective-permute-start.1 = (bf16[1040,128]{1,0:T(8,128)(2,1)S(1)}, bf16[1040,128]{1,0:T(8,128)(2,1)S(1)}, u32[]{:S(2)}, u32[]{:S(2)}) collective-permute-start(bf16[1040,128]{1,0:T(8,128)(2,1)S(1)} %pad_maximum_fusion.2), channel_id=1, source_target_pairs={{0,4},{4,0},{1,5},{5,1},{2,6},{6,2},{3,7},{7,3},{8,12},{12,8},{9,1... | collective-permute-start | bytes 798728 | tf_op jit(solution)/shard_map/ppermute | solution.py:273
  34.1 5.5 %collective-permute-done.1 = bf16[1040,128]{1,0:T(8,128)(2,1)S(1)} collective-permute-done((bf16[1040,128]{1,0:T(8,128)(2,1)S(1)}, bf16[1040,128]{1,0:T(8,128)(2,1)S(1)}, u32[]{:S(2)}, u32[]{:S(2)}) %collective-permute-start.1) | collective-permute-done | bytes 266272 | tf_op jit(solution)/shard_map/ppermute | solution.py:273
  43.6 4.5 %collective-permute-start.3 = (bf16[1040,128]{1,0:T(8,128)(2,1)S(1)}, bf16[1040,128]{1,0:T(8,128)(2,1)S(1)}, u32[]{:S(2)}, u32[]{:S(2)}) collective-permute-start(bf16[1040,128]{1,0:T(8,128)(2,1)S(1)} %pad_maximum_fusion.3), channel_id=1, source_target_pairs={{0,16},{8,24},{1,17},{9,25},{2,18},{10,26},{3,19},{11,27},{4,20},{... | collective-permute-start | bytes 798728 | tf_op jit(solution)/shard_map/ppermute | solution.py:25
  48.2 3.5 %collective-permute-start.2 = (bf16[1040,128]{1,0:T(8,128)(2,1)S(1)}, bf16[1040,128]{1,0:T(8,128)(2,1)S(1)}, u32[]{:S(2)}, u32[]{:S(2)}) collective-permute-start(bf16[1040,128]{1,0:T(8,128)(2,1)S(1)} %pad_maximum_fusion.3), channel_id=1, source_target_pairs={{0,8},{8,16},{16,24},{1,9},{9,17},{17,25},{2,10},{10,18},{18,26},{... | collective-permute-start | bytes 798728 | tf_op jit(solution)/shard_map/ppermute | solution.py:25
  51.8 3.2 %collective-permute-done.3 = bf16[1040,128]{1,0:T(8,128)(2,1)S(1)} collective-permute-done((bf16[1040,128]{1,0:T(8,128)(2,1)S(1)}, bf16[1040,128]{1,0:T(8,128)(2,1)S(1)}, u32[]{:S(2)}, u32[]{:S(2)}) %collective-permute-start.3) | collective-permute-done | bytes 266272 | tf_op jit(solution)/shard_map/ppermute | solution.py:25
  54.9 3.4 %collective-permute-done.2 = bf16[1040,128]{1,0:T(8,128)(2,1)S(1)} collective-permute-done((bf16[1040,128]{1,0:T(8,128)(2,1)S(1)}, bf16[1040,128]{1,0:T(8,128)(2,1)S(1)}, u32[]{:S(2)}, u32[]{:S(2)}) %collective-permute-start.2) | collective-permute-done | bytes 266272 | tf_op jit(solution)/shard_map/ppermute | solution.py:25
  58.6 11.0 %collective-permute-start.4 = (bf16[16,64,128]{2,1,0:T(8,128)(2,1)S(1)}, bf16[16,64,128]{2,1,0:T(8,128)(2,1)S(1)}, u32[]{:S(2)}, u32[]{:S(2)}) collective-permute-start(bf16[16,64,128]{2,1,0:T(8,128)(2,1)S(1)} %fusion.40), channel_id=1, source_target_pairs={{0,16},{8,24},{1,17},{9,25},{2,18},{10,26},{3,19},{11,27},{4,20},{... | collective-permute-start | bytes 786440 | tf_op jit(solution)/shard_map/ppermute | solution.py:25
  69.6 1.4 %fusion.66 = f32[2,512,512]{2,1,0:T(8,128)S(1)} fusion(bf16[512,2,128]{0,2,1:T(8,128)(2,1)} %bitcast.218, bf16[512,2,128]{0,2,1:T(8,128)(2,1)S(1)} %bitcast.221), kind=kOutput, calls=%fused_computation.122 | convolution fusion | flops 134217728 | bytes 2621440 | tf_op jit(solution)/shard_map/ign,jgn->gij/dot_general | solution.py:71
  71.1 10.5 %fusion.17 = f32[512,2,16,64]{0,3,2,1:T(8,128)} fusion(bf16[512,2,16,64]{0,3,2,1:T(8,128)(2,1)S(1)} %bitcast.208, f32[2,16,512]{2,1,0:T(8,128)S(1)} %bitcast.236, f32[2,512,512]{2,1,0:T(8,128)S(1)} %fusion.66, f32[2,16,512]{2,1,0:T(8,128)S(1)} %copy-done.9, pred[512,512]{1,0:T(8,128)(4,1)S(1)} %iota_compare_fusion), kind=kOutput, calls=%fused_computation.25 | convolution fusion | flops 1115684864 | bytes 8781824 | tf_op jit(solution)/shard_map/ghij,jghp->ighp/dot_general | solution.py:75
  83.4 3.9 %copy.44 = bf16[512,2048]{0,1:T(8,128)(2,1)} copy(bf16[512,2048]{1,0:T(8,128)(2,1)} %param.14) | data formatting | bytes 4194304 | tf_op args[2]
  87.5 3.5 %collective-permute-done.5 = bf16[16,64,128]{2,1,0:T(8,128)(2,1)} collective-permute-done((bf16[16,64,128]{2,1,0:T(8,128)(2,1)}, bf16[16,64,128]{2,1,0:T(8,128)(2,1)}, u32[]{:S(2)}, u32[]{:S(2)}) %collective-permute-start.5) | collective-permute-done | bytes 262176 | tf_op jit(solution)/shard_map/ppermute | solution.py:273
  91.0 1.5 %convert_select_fusion.1 = (f32[16,64,128]{2,1,0:T(8,128)S(1)}, f32[16,64,128]{2,1,0:T(8,128)S(1)}) fusion(bf16[16,64,128]{2,1,0:T(8,128)(2,1)} %collective-permute-done.5, pred[]{:T(512)S(6)} %eq.3, f32[16,64,128]{2,1,0:T(8,128)} %bitcast.210, f32[16]{0:T(128)S(1)} %copy-done.10, bf16[16,64,128]{2,1,0:T(8,128)(2,1)} %bitcast.217, ...), kind=kLoop, calls=%fused_computation.40 | loop fusion | flops 1835008 | bytes 3671232 | tf_op jit(solution)/shard_map/jit(_where)/select_n | solution.py:187
  93.7 2.1 %fusion.6 = f32[1,512,2,16,64]{1,4,3,2,0:T(8,128)S(1)} fusion(f32[512,2,16,64]{0,3,2,1:T(8,128)S(1)} %copy-done.3, f32[512,2,16]{0,2,1:T(8,128)S(1)} %get-tuple-element.32, f32[2,16,64,128]{3,2,1,0:T(8,128)S(1)} %bitcast.211, bf16[512,2,128,1]{0,2,3,1:T(8,128)(2,1)S(1)} %bitcast.219), kind=kOutput, calls=%fused_computation.10 | convolution fusion | flops 1612709888 | bytes 9764864 | tf_op jit(solution)/shard_map/vmap(ign,ghpn->ighp)/dot_general | solution.py:92
  95.8 2.2 %bitcast_reduce_fusion = (f32[512,2]{0,1:T(2,128)S(1)}, f32[512,2048]{0,1:T(8,128)S(1)}) fusion(bf16[512,2048]{0,1:T(8,128)(2,1)S(1)} %copy-done.1, bf16[2048,512]{1,0:T(8,128)(2,1)S(1)} %copy-done, f32[2048]{0:T(1024)S(1)} %mul.151, f32[1,512,2,16,64]{1,4,3,2,0:T(8,128)S(1)} %fusion.6), kind=kLoop, calls=%fused_computation.14 | loop fusion | flops 11533312 | bytes 12595200 | tf_op jit(solution)/shard_map/reduce_sum | solution.py:265
  98.5 4.9 %fusion.20 = bf16[512,1024]{1,0:T(8,128)(2,1)S(1)} fusion(bf16[512,2048]{0,1:T(8,128)(2,1)S(1)} %fusion.8, bf16[2048,4096]{1,0:T(8,128)(2,1)} %param.23), kind=kOutput, calls=%fused_computation.28 | convolution fusion | flops 2148007936 | bytes 7340032 | tf_op jit(solution)/shard_map/dot_general | solution.py:301
  103.4 2.3 %fusion.23 = bf16[512,1024]{1,0:T(8,128)(2,1)S(1)} fusion(bf16[512,2048]{0,1:T(8,128)(2,1)S(1)} %fusion.8, bf16[2048,4096]{1,0:T(8,128)(2,1)S(1)} %bitcast.245), kind=kOutput, calls=%fused_computation.29 | convolution fusion | flops 2148007936 | bytes 7340032 | tf_op jit(solution)/shard_map/dot_general | solution.py:301
  106.5 2.3 %fusion.26 = bf16[512,1024]{1,0:T(8,128)(2,1)S(1)} fusion(bf16[512,2048]{0,1:T(8,128)(2,1)S(1)} %fusion.8, bf16[2048,4096]{1,0:T(8,128)(2,1)S(1)} %bitcast.245), kind=kOutput, calls=%fused_computation.30 | convolution fusion | flops 2148007936 | bytes 7340032 | tf_op jit(solution)/shard_map/dot_general | solution.py:301
  109.2 1.6 %collective-permute-start.7 = (bf16[128,1024]{1,0:T(8,128)(2,1)S(1)}, bf16[128,1024]{1,0:T(8,128)(2,1)S(1)}, u32[]{:S(2)}, u32[]{:S(2)}) collective-permute-start(bf16[128,1024]{1,0:T(8,128)(2,1)S(1)} %fusion.42), channel_id=1, source_target_pairs={{0,2},{2,0},{1,3},{3,1},{4,6},{6,4},{5,7},{7,5},{8,10},{10,8},{9,1... | collective-permute-start | bytes 786440 | tf_op jit(solution)/shard_map/ppermute | solution.py:273
  111.6 2.3 %fusion.29 = bf16[512,1024]{1,0:T(8,128)(2,1)S(1)} fusion(bf16[512,2048]{0,1:T(8,128)(2,1)S(1)} %fusion.8, bf16[2048,4096]{1,0:T(8,128)(2,1)S(1)} %bitcast.245), kind=kOutput, calls=%fused_computation.31 | convolution fusion | flops 2148007936 | bytes 7340032 | tf_op jit(solution)/shard_map/dot_general | solution.py:301
  114.4 1.6 %collective-permute-start.11 = (bf16[128,1024]{1,0:T(8,128)(2,1)S(1)}, bf16[128,1024]{1,0:T(8,128)(2,1)S(1)}, u32[]{:S(2)}, u32[]{:S(2)}) collective-permute-start(bf16[128,1024]{1,0:T(8,128)(2,1)S(1)} %fusion.44), channel_id=1, source_target_pairs={{0,2},{2,0},{1,3},{3,1},{4,6},{6,4},{5,7},{7,5},{8,10},{10,8},{9,1... | collective-permute-start | bytes 786440 | tf_op jit(solution)/shard_map/ppermute | solution.py:273
  115.9 2.5 %collective-permute-done.7 = bf16[128,1024]{1,0:T(8,128)(2,1)S(1)} collective-permute-done((bf16[128,1024]{1,0:T(8,128)(2,1)S(1)}, bf16[128,1024]{1,0:T(8,128)(2,1)S(1)}, u32[]{:S(2)}, u32[]{:S(2)}) %collective-permute-start.7) | collective-permute-done | bytes 262176 | tf_op jit(solution)/shard_map/ppermute | solution.py:273
  118.7 1.6 %collective-permute-start.13 = (bf16[128,1024]{1,0:T(8,128)(2,1)S(1)}, bf16[128,1024]{1,0:T(8,128)(2,1)S(1)}, u32[]{:S(2)}, u32[]{:S(2)}) collective-permute-start(bf16[128,1024]{1,0:T(8,128)(2,1)S(1)} %fusion.45), channel_id=1, source_target_pairs={{0,2},{2,0},{1,3},{3,1},{4,6},{6,4},{5,7},{7,5},{8,10},{10,8},{9,1... | collective-permute-start | bytes 786440 | tf_op jit(solution)/shard_map/ppermute | solution.py:273
  120.3 3.7 %collective-permute-done.9 = bf16[128,1024]{1,0:T(8,128)(2,1)S(1)} collective-permute-done((bf16[128,1024]{1,0:T(8,128)(2,1)S(1)}, bf16[128,1024]{1,0:T(8,128)(2,1)S(1)}, u32[]{:S(2)}, u32[]{:S(2)}) %collective-permute-start.9) | collective-permute-done | bytes 262176 | tf_op jit(solution)/shard_map/ppermute | solution.py:273
  124.1 5.6 %collective-permute-done.11 = bf16[128,1024]{1,0:T(8,128)(2,1)S(1)} collective-permute-done((bf16[128,1024]{1,0:T(8,128)(2,1)S(1)}, bf16[128,1024]{1,0:T(8,128)(2,1)S(1)}, u32[]{:S(2)}, u32[]{:S(2)}) %collective-permute-start.11) | collective-permute-done | bytes 262176 | tf_op jit(solution)/shard_map/ppermute | solution.py:273
  129.7 5.1 %collective-permute-done.13 = bf16[128,1024]{1,0:T(8,128)(2,1)S(1)} collective-permute-done((bf16[128,1024]{1,0:T(8,128)(2,1)S(1)}, bf16[128,1024]{1,0:T(8,128)(2,1)S(1)}, u32[]{:S(2)}, u32[]{:S(2)}) %collective-permute-start.13) | collective-permute-done | bytes 262176 | tf_op jit(solution)/shard_map/ppermute | solution.py:273
  (119 shorter events, 21.9 us)
Async XLA Ops:
  1.5 15.8 %collective-permute-start = (bf16[3,2560]{1,0:T(4,128)(2,1)S(1)}, bf16[3,2560]{1,0:T(4,128)(2,1)S(1)}, u32[]{:S(2)}, u32[]{:S(2)}) collective-permute-start(bf16[3,2560]{1,0:T(4,128)(2,1)S(1)} %pad_maximum_fusion.4), channel_id=1, source_target_pairs={{0,4},{4,8},{8,12},{12,16},{16,20},{20,24},{24,28},{1,5},{5,9},{9,... | collective-permute-start | bytes 46088 | tf_op jit(solution)/shard_map/ppermute | solution.py:25
  23.2 8.5 %copy-start.6 = (bf16[512,1,256]{0,2,1:T(8,128)(2,1)}, bf16[512,1,256]{0,2,1:T(8,128)(2,1)S(1)}, u32[]{:S(2)}) copy-start(bf16[512,1,256]{0,2,1:T(8,128)(2,1)S(1)} %get-tuple-element.31) | copy-start | bytes 786436
  31.7 39.4 %copy-start = (bf16[2048,512]{1,0:T(8,128)(2,1)S(1)}, bf16[2048,512]{1,0:T(8,128)(2,1)}, u32[]{:S(2)}) copy-start(bf16[2048,512]{1,0:T(8,128)(2,1)} %shard_map.118) | copy-start | bytes 6291460
  31.7 7.9 %collective-permute-start.1 = (bf16[1040,128]{1,0:T(8,128)(2,1)S(1)}, bf16[1040,128]{1,0:T(8,128)(2,1)S(1)}, u32[]{:S(2)}, u32[]{:S(2)}) collective-permute-start(bf16[1040,128]{1,0:T(8,128)(2,1)S(1)} %pad_maximum_fusion.2), channel_id=1, source_target_pairs={{0,4},{4,0},{1,5},{5,1},{2,6},{6,2},{3,7},{7,3},{8,12},{12,8},{9,1... | collective-permute-start | bytes 798728 | tf_op jit(solution)/shard_map/ppermute | solution.py:273
  40.3 0.5 copy-start.12
  40.9 28.7 %copy-start.7 = (bf16[512,1,256]{0,2,1:T(8,128)(2,1)S(1)}, bf16[512,1,256]{0,2,1:T(8,128)(2,1)}, u32[]{:S(2)}) copy-start(bf16[512,1,256]{0,2,1:T(8,128)(2,1)} %copy-done.6) | copy-start | bytes 786436
  40.9 30.2 %copy-start.9 = (f32[2,16,512]{2,1,0:T(8,128)S(1)}, f32[2,16,512]{2,1,0:T(8,128)}, u32[]{:S(2)}) copy-start(f32[2,16,512]{2,1,0:T(8,128)} %get-tuple-element.34) | copy-start | bytes 196612
  43.6 11.3 %collective-permute-start.3 = (bf16[1040,128]{1,0:T(8,128)(2,1)S(1)}, bf16[1040,128]{1,0:T(8,128)(2,1)S(1)}, u32[]{:S(2)}, u32[]{:S(2)}) collective-permute-start(bf16[1040,128]{1,0:T(8,128)(2,1)S(1)} %pad_maximum_fusion.3), channel_id=1, source_target_pairs={{0,16},{8,24},{1,17},{9,25},{2,18},{10,26},{3,19},{11,27},{4,20},{... | collective-permute-start | bytes 798728 | tf_op jit(solution)/shard_map/ppermute | solution.py:25
  48.2 10.1 %collective-permute-start.2 = (bf16[1040,128]{1,0:T(8,128)(2,1)S(1)}, bf16[1040,128]{1,0:T(8,128)(2,1)S(1)}, u32[]{:S(2)}, u32[]{:S(2)}) collective-permute-start(bf16[1040,128]{1,0:T(8,128)(2,1)S(1)} %pad_maximum_fusion.3), channel_id=1, source_target_pairs={{0,8},{8,16},{16,24},{1,9},{9,17},{17,25},{2,10},{10,18},{18,26},{... | collective-permute-start | bytes 798728 | tf_op jit(solution)/shard_map/ppermute | solution.py:25
  51.7 29.9 %copy-start.2 = (f32[1024,128]{1,0:T(8,128)}, f32[1024,128]{1,0:T(8,128)S(1)}, u32[]{:S(2)}) copy-start(f32[1024,128]{1,0:T(8,128)S(1)} %slice_convert_fusion) | copy-start | bytes 1572868
  58.4 23.2 %copy-start.4 = (bf16[1024,128]{1,0:T(8,128)(2,1)}, bf16[1024,128]{1,0:T(8,128)(2,1)S(1)}, u32[]{:S(2)}) copy-start(bf16[1024,128]{1,0:T(8,128)(2,1)S(1)} %slice.141) | copy-start | bytes 786436
  58.6 23.0 %collective-permute-start.4 = (bf16[16,64,128]{2,1,0:T(8,128)(2,1)S(1)}, bf16[16,64,128]{2,1,0:T(8,128)(2,1)S(1)}, u32[]{:S(2)}, u32[]{:S(2)}) collective-permute-start(bf16[16,64,128]{2,1,0:T(8,128)(2,1)S(1)} %fusion.40), channel_id=1, source_target_pairs={{0,16},{8,24},{1,17},{9,25},{2,18},{10,26},{3,19},{11,27},{4,20},{... | collective-permute-start | bytes 786440 | tf_op jit(solution)/shard_map/ppermute | solution.py:25
  71.1 10.6 %copy-start.10 = (f32[16]{0:T(128)S(1)}, f32[16]{0:T(128)}, u32[]{:S(2)}) copy-start(f32[16]{0:T(128)} %get-tuple-element.29) | copy-start | bytes 196
  81.6 5.7 %copy-start.13 = (f32[32]{0:T(128)S(1)}, f32[32]{0:T(128)}, u32[]{:S(2)}) copy-start(f32[32]{0:T(128)} %param.21) | copy-start | bytes 388
  81.6 5.9 %copy-start.11 = (bf16[2048]{0:T(1024)(128)(2,1)S(1)}, bf16[2048]{0:T(1024)(128)(2,1)}, u32[]{:S(2)}) copy-start(bf16[2048]{0:T(1024)(128)(2,1)} %param.22) | copy-start | bytes 12292
  81.6 1.1 copy-start.8
  82.7 8.3 %collective-permute-start.5 = (bf16[16,64,128]{2,1,0:T(8,128)(2,1)}, bf16[16,64,128]{2,1,0:T(8,128)(2,1)}, u32[]{:S(2)}, u32[]{:S(2)}) collective-permute-start(bf16[16,64,128]{2,1,0:T(8,128)(2,1)} %select_convert_fusion), channel_id=1, source_target_pairs={{0,4},{4,0},{1,5},{5,1},{2,6},{6,2},{3,7},{7,3},{8,12},{12,8},{9,1... | collective-permute-start | bytes 786440 | tf_op jit(solution)/shard_map/ppermute | solution.py:273
  87.5 6.1 %copy-start.3 = (f32[512,2,16,64]{0,3,2,1:T(8,128)S(1)}, f32[512,2,16,64]{0,3,2,1:T(8,128)}, u32[]{:S(2)}) copy-start(f32[512,2,16,64]{0,3,2,1:T(8,128)} %fusion.17) | copy-start | bytes 12582916
  87.5 6.1 %copy-start.5 = (bf16[512,1,256]{0,2,1:T(8,128)(2,1)S(1)}, bf16[512,1,256]{0,2,1:T(8,128)(2,1)}, u32[]{:S(2)}) copy-start(bf16[512,1,256]{0,2,1:T(8,128)(2,1)} %get-tuple-element.30) | copy-start | bytes 786436
  93.6 2.1 %copy-start.1 = (bf16[512,2048]{0,1:T(8,128)(2,1)S(1)}, bf16[512,2048]{0,1:T(8,128)(2,1)}, u32[]{:S(2)}) copy-start(bf16[512,2048]{0,1:T(8,128)(2,1)} %copy.44) | copy-start | bytes 6291460
  95.8 7.6 %slice-start = ((s8[16777216]{0:T(1024)(128)(4,1)}), s8[4194304]{0:T(1024)(128)(4,1)S(1)}, s32[]{:S(2)}) async-start(s8[16777216]{0:T(1024)(128)(4,1)} %bitcast.244), calls=%async_computation | async-start | bytes 8388608
  95.8 7.6 %slice-start.1 = ((s8[16777216]{0:T(1024)(128)(4,1)}), s8[4194304]{0:T(1024)(128)(4,1)S(1)}, s32[]{:S(2)}) async-start(s8[16777216]{0:T(1024)(128)(4,1)} %bitcast.244), calls=%async_computation.1 | async-start | bytes 8388608
  98.0 5.4 %slice-start.2 = ((s8[16777216]{0:T(1024)(128)(4,1)}), s8[4194304]{0:T(1024)(128)(4,1)S(1)}, s32[]{:S(2)}) async-start(s8[16777216]{0:T(1024)(128)(4,1)} %bitcast.244), calls=%async_computation.2 | async-start | bytes 8388608
  98.5 4.9 %slice-start.3 = ((s8[16777216]{0:T(1024)(128)(4,1)}), s8[4194304]{0:T(1024)(128)(4,1)S(1)}, s32[]{:S(2)}) async-start(s8[16777216]{0:T(1024)(128)(4,1)} %bitcast.244), calls=%async_computation.3 | async-start | bytes 8388608
  105.8 3.2 %collective-permute-start.6 = (bf16[2,128,1024]{2,1,0:T(8,128)(2,1)S(1)}, bf16[2,128,1024]{2,1,0:T(8,128)(2,1)S(1)}, u32[]{:S(2)}, u32[]{:S(2)}) collective-permute-start(bf16[2,128,1024]{2,1,0:T(8,128)(2,1)S(1)} %dynamic-slice_bitcast_fusion.3), channel_id=1, source_target_pairs={{0,1},{1,0},{2,3},{3,2},{4,5},{5,4},{6,7},{7,6},{8,9},{9,8},{10,11... | collective-permute-start | bytes 1572872 | tf_op jit(solution)/shard_map/ppermute | solution.py:273
  106.0 4.9 %collective-permute-start.8 = (bf16[2,128,1024]{2,1,0:T(8,128)(2,1)S(1)}, bf16[2,128,1024]{2,1,0:T(8,128)(2,1)S(1)}, u32[]{:S(2)}, u32[]{:S(2)}) collective-permute-start(bf16[2,128,1024]{2,1,0:T(8,128)(2,1)S(1)} %dynamic-slice_bitcast_fusion.2), channel_id=1, source_target_pairs={{0,1},{1,0},{2,3},{3,2},{4,5},{5,4},{6,7},{7,6},{8,9},{9,8},{10,11... | collective-permute-start | bytes 1572872 | tf_op jit(solution)/shard_map/ppermute | solution.py:273
  108.9 5.2 %collective-permute-start.10 = (bf16[2,128,1024]{2,1,0:T(8,128)(2,1)S(1)}, bf16[2,128,1024]{2,1,0:T(8,128)(2,1)S(1)}, u32[]{:S(2)}, u32[]{:S(2)}) collective-permute-start(bf16[2,128,1024]{2,1,0:T(8,128)(2,1)S(1)} %dynamic-slice_bitcast_fusion.1), channel_id=1, source_target_pairs={{0,1},{1,0},{2,3},{3,2},{4,5},{5,4},{6,7},{7,6},{8,9},{9,8},{10,11... | collective-permute-start | bytes 1572872 | tf_op jit(solution)/shard_map/ppermute | solution.py:273
  109.2 9.2 %collective-permute-start.7 = (bf16[128,1024]{1,0:T(8,128)(2,1)S(1)}, bf16[128,1024]{1,0:T(8,128)(2,1)S(1)}, u32[]{:S(2)}, u32[]{:S(2)}) collective-permute-start(bf16[128,1024]{1,0:T(8,128)(2,1)S(1)} %fusion.42), channel_id=1, source_target_pairs={{0,2},{2,0},{1,3},{3,1},{4,6},{6,4},{5,7},{7,5},{8,10},{10,8},{9,1... | collective-permute-start | bytes 786440 | tf_op jit(solution)/shard_map/ppermute | solution.py:273
  111.1 13.0 %collective-permute-start.9 = (bf16[128,1024]{1,0:T(8,128)(2,1)S(1)}, bf16[128,1024]{1,0:T(8,128)(2,1)S(1)}, u32[]{:S(2)}, u32[]{:S(2)}) collective-permute-start(bf16[128,1024]{1,0:T(8,128)(2,1)S(1)} %fusion.43), channel_id=1, source_target_pairs={{0,2},{2,0},{1,3},{3,1},{4,6},{6,4},{5,7},{7,5},{8,10},{10,8},{9,1... | collective-permute-start | bytes 786440 | tf_op jit(solution)/shard_map/ppermute | solution.py:273
  114.0 4.4 %collective-permute-start.12 = (bf16[2,128,1024]{2,1,0:T(8,128)(2,1)S(1)}, bf16[2,128,1024]{2,1,0:T(8,128)(2,1)S(1)}, u32[]{:S(2)}, u32[]{:S(2)}) collective-permute-start(bf16[2,128,1024]{2,1,0:T(8,128)(2,1)S(1)} %dynamic-slice_bitcast_fusion), channel_id=1, source_target_pairs={{0,1},{1,0},{2,3},{3,2},{4,5},{5,4},{6,7},{7,6},{8,9},{9,8},{10,11... | collective-permute-start | bytes 1572872 | tf_op jit(solution)/shard_map/ppermute | solution.py:273
  114.4 15.3 %collective-permute-start.11 = (bf16[128,1024]{1,0:T(8,128)(2,1)S(1)}, bf16[128,1024]{1,0:T(8,128)(2,1)S(1)}, u32[]{:S(2)}, u32[]{:S(2)}) collective-permute-start(bf16[128,1024]{1,0:T(8,128)(2,1)S(1)} %fusion.44), channel_id=1, source_target_pairs={{0,2},{2,0},{1,3},{3,1},{4,6},{6,4},{5,7},{7,5},{8,10},{10,8},{9,1... | collective-permute-start | bytes 786440 | tf_op jit(solution)/shard_map/ppermute | solution.py:273
  118.7 16.1 %collective-permute-start.13 = (bf16[128,1024]{1,0:T(8,128)(2,1)S(1)}, bf16[128,1024]{1,0:T(8,128)(2,1)S(1)}, u32[]{:S(2)}, u32[]{:S(2)}) collective-permute-start(bf16[128,1024]{1,0:T(8,128)(2,1)S(1)} %fusion.45), channel_id=1, source_target_pairs={{0,2},{2,0},{1,3},{3,1},{4,6},{6,4},{5,7},{7,5},{8,10},{10,8},{9,1... | collective-permute-start | bytes 786440 | tf_op jit(solution)/shard_map/ppermute | solution.py:273

commit v14 on v12

--- a/solution.py
+++ b/solution.py
@@ -45,7 +45,7 @@
 
 def conv_silu_kernel(halo, x, weight, bias):
     rows, width = x.shape
-    block = 512 if width % 512 == 0 else width
+    block = 1024 if width % 1024 == 0 else width
     halo8 = jnp.concatenate([jnp.zeros((8 - halo.shape[0], width), halo.dtype), halo], axis=0)
     return pl.pallas_call(
         conv_kernel,

time: 132 us -> 132 us (level)
  no operation moved by 1% of the time
where the time goes in v14:
time: 132 us; the launch traced here: 131 us
  starting transfers between devices  32.4 us (25%)
  waiting for transfers between devices  32.4 us (25%)
  matrix products  28.2 us (21%)
  other arithmetic  19.9 us (15%)
  local copies, waits for them, and re-layouts  11.9 us (9%)
  Pallas kernels  5.9 us (4%)
    ppermute x10, waiting for transfers between devices, swap(): return lax.ppermute(value, axis, [(0, 1), (1, 0)])  25.9 us
    ppermute x4, starting transfers between devices, shifted(): return lax.ppermute(value, axis, pairs)  24 us
    dot_general x4, matrix products, reduce_rows(): jnp.dot(source, out_weight[:, c * step:(c + 1) * step], preferred_element...  11.9 us
    dot_general x1, matrix products, diagonal_of(): jnp.einsum('ghij,jghp->ighp', mixing, inner_block, preferred_element_type...  10.5 us
    ppermute x10, starting transfers between devices, swap(): return lax.ppermute(value, axis, [(0, 1), (1, 0)])  8.4 us
    unnamed x40, local copies, waits for them, and re-layouts  6.53 us
    ppermute x4, waiting for transfers between devices, shifted(): return lax.ppermute(value, axis, pairs)  6.53 us
    pallas_call x1, Pallas kernels, conv_silu_kernel(): pl.pallas_call(conv_kernel, grid=(width // block,), in_specs=[pl.BlockSpe...  5.9 us
  transfers between devices with their start and end apart: 14, of which 8 were waited for; matrix products, arithmetic and copies ran while one was open for 24% of the time, Pallas kernels for 0%

profile of v14, /device:TPU:0, one launch (start us, length us, event | category | flops | bytes accessed | tf_op | source)
XLA Modules:
  0.0 131.3 jit_solution(6794126827803481723)
XLA Ops:
  1.5 4.8 %collective-permute-start = (bf16[3,2560]{1,0:T(4,128)(2,1)S(1)}, bf16[3,2560]{1,0:T(4,128)(2,1)S(1)}, u32[]{:S(2)}, u32[]{:S(2)}) collective-permute-start(bf16[3,2560]{1,0:T(4,128)(2,1)S(1)} %pad_maximum_fusion.5), channel_id=1, source_target_pairs={{0,4},{4,8},{8,12},{12,16},{16,20},{20,24},{24,28},{1,5},{5,9},{9,... | collective-permute-start | bytes 46088 | tf_op jit(solution)/shard_map/ppermute | solution.py:25
  7.9 2.3 %reduce-window.6 = f32[16,2,4,128]{3,0,1,2:T(8,128)S(1)} reduce-window(f32[16,2,4,128]{3,0,1,2:T(8,128)S(1)} %bitcast.238, f32[]{:T(128)} %constant.68.clone.1), window={size=1x1x1x128 pad=0_0x0_0x0_0x127_0}, to_apply=%region_0.1 | reduce-window | flops 2080768 | bytes 131076 | tf_op jit(solution)/shard_map/reduce-window
  12.3 1.3 copy.44
  14.3 1.3 reshape.137.b_ref
  15.8 1.3 %multiply_convert_fusion.6 = bf16[512,2,256]{0,2,1:T(8,128)(2,1)S(1)} fusion(bf16[512,2,256]{0,2,1:T(8,128)(2,1)S(1)} %copy.44, bf16[3,2,256]{0,2,1:T(8,128)(2,1)S(1)} %bitcast.234, f32[2,256]{1,0:T(2,128)S(1)} %get-tuple-element.40, f32[2,256]{1,0:T(2,128)S(1)} %get-tuple-element.41, f32[2,256]{1,0:T(2,128)S(1)} %get-tuple-element.39, ...), kind=kLoop, calls=%fused_computation.39 | loop fusion | flops 6815744 | bytes 1061888 | tf_op jit(solution)/shard_map/convert_element_type | solution.py:34
  18.6 5.9 %shard_map.118 = bf16[2048,512]{1,0:T(8,128)(2,1)} custom-call(bf16[8,2048]{1,0:T(8,128)(2,1)} %concatenate.28.halo_ref, bf16[512,2048]{1,0:T(8,128)(2,1)} %x_ref.1, bf16[4,2048]{1,0:T(4,128)(2,1)} %w_ref.1, bf16[1,2048]{1,0:T(2,128)(2,1)} %reshape.137.b_ref), custom_call_target="tpu_custom_call" | custom-call | tf_op jit(solution)/shard_map/pallas_call | solution.py:50
  24.5 2.3 %fusion.18 = f32[2,16,64,128]{3,2,1,0:T(8,128)S(1)} fusion(bf16[512,2,128,1]{0,2,3,1:T(8,128)(2,1)S(1)} %bitcast.223, bf16[512,2,16,64]{0,3,2,1:T(8,128)(2,1)} %bitcast.210, f32[512,2,16]{0,2,1:T(8,128)S(1)} %get-tuple-element.33), kind=kOutput, calls=%fused_computation.26 | convolution fusion | flops 271581184 | bytes 3473408 | tf_op jit(solution)/shard_map/jghp,jgn->ghpn/dot_general | solution.py:81
  26.9 1.6 %collective-permute-start.1 = (bf16[1040,128]{1,0:T(8,128)(2,1)S(1)}, bf16[1040,128]{1,0:T(8,128)(2,1)S(1)}, u32[]{:S(2)}, u32[]{:S(2)}) collective-permute-start(bf16[1040,128]{1,0:T(8,128)(2,1)S(1)} %pad_maximum_fusion.3), channel_id=1, source_target_pairs={{0,4},{4,0},{1,5},{5,1},{2,6},{6,2},{3,7},{7,3},{8,12},{12,8},{9,1... | collective-permute-start | bytes 798728 | tf_op jit(solution)/shard_map/ppermute | solution.py:271
  29.4 5.5 %collective-permute-done.1 = bf16[1040,128]{1,0:T(8,128)(2,1)S(1)} collective-permute-done((bf16[1040,128]{1,0:T(8,128)(2,1)S(1)}, bf16[1040,128]{1,0:T(8,128)(2,1)S(1)}, u32[]{:S(2)}, u32[]{:S(2)}) %collective-permute-start.1) | collective-permute-done | bytes 266272 | tf_op jit(solution)/shard_map/ppermute | solution.py:271
  38.8 4.5 %collective-permute-start.3 = (bf16[1040,128]{1,0:T(8,128)(2,1)S(1)}, bf16[1040,128]{1,0:T(8,128)(2,1)S(1)}, u32[]{:S(2)}, u32[]{:S(2)}) collective-permute-start(bf16[1040,128]{1,0:T(8,128)(2,1)S(1)} %pad_maximum_fusion.4), channel_id=1, source_target_pairs={{0,16},{8,24},{1,17},{9,25},{2,18},{10,26},{3,19},{11,27},{4,20},{... | collective-permute-start | bytes 798728 | tf_op jit(solution)/shard_map/ppermute | solution.py:25
  43.4 3.5 %collective-permute-start.2 = (bf16[1040,128]{1,0:T(8,128)(2,1)S(1)}, bf16[1040,128]{1,0:T(8,128)(2,1)S(1)}, u32[]{:S(2)}, u32[]{:S(2)}) collective-permute-start(bf16[1040,128]{1,0:T(8,128)(2,1)S(1)} %pad_maximum_fusion.4), channel_id=1, source_target_pairs={{0,8},{8,16},{16,24},{1,9},{9,17},{17,25},{2,10},{10,18},{18,26},{... | collective-permute-start | bytes 798728 | tf_op jit(solution)/shard_map/ppermute | solution.py:25
  47.0 3.2 %collective-permute-done.3 = bf16[1040,128]{1,0:T(8,128)(2,1)S(1)} collective-permute-done((bf16[1040,128]{1,0:T(8,128)(2,1)S(1)}, bf16[1040,128]{1,0:T(8,128)(2,1)S(1)}, u32[]{:S(2)}, u32[]{:S(2)}) %collective-permute-start.3) | collective-permute-done | bytes 266272 | tf_op jit(solution)/shard_map/ppermute | solution.py:25
  50.1 3.4 %collective-permute-done.2 = bf16[1040,128]{1,0:T(8,128)(2,1)S(1)} collective-permute-done((bf16[1040,128]{1,0:T(8,128)(2,1)S(1)}, bf16[1040,128]{1,0:T(8,128)(2,1)S(1)}, u32[]{:S(2)}, u32[]{:S(2)}) %collective-permute-start.2) | collective-permute-done | bytes 266272 | tf_op jit(solution)/shard_map/ppermute | solution.py:25
  53.8 11.2 %collective-permute-start.4 = (bf16[16,64,128]{2,1,0:T(8,128)(2,1)S(1)}, bf16[16,64,128]{2,1,0:T(8,128)(2,1)S(1)}, u32[]{:S(2)}, u32[]{:S(2)}) collective-permute-start(bf16[16,64,128]{2,1,0:T(8,128)(2,1)S(1)} %fusion.42), channel_id=1, source_target_pairs={{0,16},{8,24},{1,17},{9,25},{2,18},{10,26},{3,19},{11,27},{4,20},{... | collective-permute-start | bytes 786440 | tf_op jit(solution)/shard_map/ppermute | solution.py:25
  65.0 1.4 %fusion.68 = f32[2,512,512]{2,1,0:T(8,128)S(1)} fusion(bf16[512,2,128]{0,2,1:T(8,128)(2,1)} %bitcast.221, bf16[512,2,128]{0,2,1:T(8,128)(2,1)S(1)} %bitcast.224), kind=kOutput, calls=%fused_computation.134 | convolution fusion | flops 134217728 | bytes 2621440 | tf_op jit(solution)/shard_map/ign,jgn->gij/dot_general | solution.py:71
  66.5 10.5 %fusion.17 = f32[512,2,16,64]{0,3,2,1:T(8,128)} fusion(bf16[512,2,16,64]{0,3,2,1:T(8,128)(2,1)S(1)} %bitcast.211, f32[2,16,512]{2,1,0:T(8,128)S(1)} %bitcast.237, f32[2,512,512]{2,1,0:T(8,128)S(1)} %fusion.68, f32[2,16,512]{2,1,0:T(8,128)S(1)} %copy-done.9, pred[512,512]{1,0:T(8,128)(4,1)S(1)} %iota_compare_fusion), kind=kOutput, calls=%fused_computation.25 | convolution fusion | flops 1115684864 | bytes 8781824 | tf_op jit(solution)/shard_map/ghij,jghp->ighp/dot_general | solution.py:75
  78.8 3.9 %copy.50 = bf16[512,2048]{0,1:T(8,128)(2,1)} copy(bf16[512,2048]{1,0:T(8,128)(2,1)} %param.14) | data formatting | bytes 4194304 | tf_op args[2]
  82.9 3.5 %collective-permute-done.5 = bf16[16,64,128]{2,1,0:T(8,128)(2,1)} collective-permute-done((bf16[16,64,128]{2,1,0:T(8,128)(2,1)}, bf16[16,64,128]{2,1,0:T(8,128)(2,1)}, u32[]{:S(2)}, u32[]{:S(2)}) %collective-permute-start.5) | collective-permute-done | bytes 262176 | tf_op jit(solution)/shard_map/ppermute | solution.py:271
  86.4 1.5 %convert_select_fusion.1 = (f32[16,64,128]{2,1,0:T(8,128)S(1)}, f32[16,64,128]{2,1,0:T(8,128)S(1)}) fusion(bf16[16,64,128]{2,1,0:T(8,128)(2,1)} %collective-permute-done.5, pred[]{:T(512)S(6)} %eq.3, f32[16,64,128]{2,1,0:T(8,128)} %bitcast.213, f32[16]{0:T(128)S(1)} %copy-done.10, bf16[16,64,128]{2,1,0:T(8,128)(2,1)} %bitcast.220, ...), kind=kLoop, calls=%fused_computation.43 | loop fusion | flops 1835008 | bytes 3671232 | tf_op jit(solution)/shard_map/jit(_where)/select_n | solution.py:187
  89.0 2.1 %fusion.6 = f32[1,512,2,16,64]{1,4,3,2,0:T(8,128)S(1)} fusion(f32[512,2,16,64]{0,3,2,1:T(8,128)S(1)} %copy-done.3, f32[512,2,16]{0,2,1:T(8,128)S(1)} %get-tuple-element.32, f32[2,16,64,128]{3,2,1,0:T(8,128)S(1)} %bitcast.214, bf16[512,2,128,1]{0,2,3,1:T(8,128)(2,1)S(1)} %bitcast.222), kind=kOutput, calls=%fused_computation.10 | convolution fusion | flops 1612709888 | bytes 9764864 | tf_op jit(solution)/shard_map/vmap(ign,ghpn->ighp)/dot_general | solution.py:92
  91.2 2.3 %bitcast_reduce_fusion = (f32[512,2]{0,1:T(2,128)S(1)}, f32[512,2048]{0,1:T(8,128)S(1)}) fusion(bf16[512,2048]{0,1:T(8,128)(2,1)S(1)} %copy-done.1, bf16[2048,512]{1,0:T(8,128)(2,1)S(1)} %copy-done, f32[2048]{0:T(1024)S(1)} %mul.224, f32[1,512,2,16,64]{1,4,3,2,0:T(8,128)S(1)} %fusion.6), kind=kLoop, calls=%fused_computation.14 | loop fusion | flops 11533312 | bytes 12595200 | tf_op jit(solution)/shard_map/reduce_sum | solution.py:263
  93.9 4.8 %fusion.20 = bf16[512,1024]{1,0:T(8,128)(2,1)S(1)} fusion(bf16[512,2048]{0,1:T(8,128)(2,1)S(1)} %fusion.8, bf16[2048,4096]{1,0:T(8,128)(2,1)} %param.23), kind=kOutput, calls=%fused_computation.28 | convolution fusion | flops 2148007936 | bytes 7340032 | tf_op jit(solution)/shard_map/dot_general | solution.py:299
  98.8 2.3 %fusion.23 = bf16[512,1024]{1,0:T(8,128)(2,1)S(1)} fusion(bf16[512,2048]{0,1:T(8,128)(2,1)S(1)} %fusion.8, bf16[2048,4096]{1,0:T(8,128)(2,1)S(1)} %bitcast.242), kind=kOutput, calls=%fused_computation.29 | convolution fusion | flops 2148007936 | bytes 7340032 | tf_op jit(solution)/shard_map/dot_general | solution.py:299
  101.9 2.3 %fusion.26 = bf16[512,1024]{1,0:T(8,128)(2,1)S(1)} fusion(bf16[512,2048]{0,1:T(8,128)(2,1)S(1)} %fusion.8, bf16[2048,4096]{1,0:T(8,128)(2,1)S(1)} %bitcast.242), kind=kOutput, calls=%fused_computation.30 | convolution fusion | flops 2148007936 | bytes 7340032 | tf_op jit(solution)/shard_map/dot_general | solution.py:299
  104.6 1.6 %collective-permute-start.7 = (bf16[128,1024]{1,0:T(8,128)(2,1)S(1)}, bf16[128,1024]{1,0:T(8,128)(2,1)S(1)}, u32[]{:S(2)}, u32[]{:S(2)}) collective-permute-start(bf16[128,1024]{1,0:T(8,128)(2,1)S(1)} %fusion.44), channel_id=1, source_target_pairs={{0,2},{2,0},{1,3},{3,1},{4,6},{6,4},{5,7},{7,5},{8,10},{10,8},{9,1... | collective-permute-start | bytes 786440 | tf_op jit(solution)/shard_map/ppermute | solution.py:271
  107.0 2.3 %fusion.29 = bf16[512,1024]{1,0:T(8,128)(2,1)S(1)} fusion(bf16[512,2048]{0,1:T(8,128)(2,1)S(1)} %fusion.8, bf16[2048,4096]{1,0:T(8,128)(2,1)S(1)} %bitcast.242), kind=kOutput, calls=%fused_computation.31 | convolution fusion | flops 2148007936 | bytes 7340032 | tf_op jit(solution)/shard_map/dot_general | solution.py:299
  109.7 1.6 %collective-permute-start.11 = (bf16[128,1024]{1,0:T(8,128)(2,1)S(1)}, bf16[128,1024]{1,0:T(8,128)(2,1)S(1)}, u32[]{:S(2)}, u32[]{:S(2)}) collective-permute-start(bf16[128,1024]{1,0:T(8,128)(2,1)S(1)} %fusion.46), channel_id=1, source_target_pairs={{0,2},{2,0},{1,3},{3,1},{4,6},{6,4},{5,7},{7,5},{8,10},{10,8},{9,1... | collective-permute-start | bytes 786440 | tf_op jit(solution)/shard_map/ppermute | solution.py:271
  111.3 2.5 %collective-permute-done.7 = bf16[128,1024]{1,0:T(8,128)(2,1)S(1)} collective-permute-done((bf16[128,1024]{1,0:T(8,128)(2,1)S(1)}, bf16[128,1024]{1,0:T(8,128)(2,1)S(1)}, u32[]{:S(2)}, u32[]{:S(2)}) %collective-permute-start.7) | collective-permute-done | bytes 262176 | tf_op jit(solution)/shard_map/ppermute | solution.py:271
  114.1 1.6 %collective-permute-start.13 = (bf16[128,1024]{1,0:T(8,128)(2,1)S(1)}, bf16[128,1024]{1,0:T(8,128)(2,1)S(1)}, u32[]{:S(2)}, u32[]{:S(2)}) collective-permute-start(bf16[128,1024]{1,0:T(8,128)(2,1)S(1)} %fusion.47), channel_id=1, source_target_pairs={{0,2},{2,0},{1,3},{3,1},{4,6},{6,4},{5,7},{7,5},{8,10},{10,8},{9,1... | collective-permute-start | bytes 786440 | tf_op jit(solution)/shard_map/ppermute | solution.py:271
  115.7 3.7 %collective-permute-done.9 = bf16[128,1024]{1,0:T(8,128)(2,1)S(1)} collective-permute-done((bf16[128,1024]{1,0:T(8,128)(2,1)S(1)}, bf16[128,1024]{1,0:T(8,128)(2,1)S(1)}, u32[]{:S(2)}, u32[]{:S(2)}) %collective-permute-start.9) | collective-permute-done | bytes 262176 | tf_op jit(solution)/shard_map/ppermute | solution.py:271
  119.5 5.6 %collective-permute-done.11 = bf16[128,1024]{1,0:T(8,128)(2,1)S(1)} collective-permute-done((bf16[128,1024]{1,0:T(8,128)(2,1)S(1)}, bf16[128,1024]{1,0:T(8,128)(2,1)S(1)}, u32[]{:S(2)}, u32[]{:S(2)}) %collective-permute-start.11) | collective-permute-done | bytes 262176 | tf_op jit(solution)/shard_map/ppermute | solution.py:271
  125.1 5.1 %collective-permute-done.13 = bf16[128,1024]{1,0:T(8,128)(2,1)S(1)} collective-permute-done((bf16[128,1024]{1,0:T(8,128)(2,1)S(1)}, bf16[128,1024]{1,0:T(8,128)(2,1)S(1)}, u32[]{:S(2)}, u32[]{:S(2)}) %collective-permute-start.13) | collective-permute-done | bytes 262176 | tf_op jit(solution)/shard_map/ppermute | solution.py:271
  (119 shorter events, 19.9 us)
Async XLA Ops:
  1.5 14.1 %collective-permute-start = (bf16[3,2560]{1,0:T(4,128)(2,1)S(1)}, bf16[3,2560]{1,0:T(4,128)(2,1)S(1)}, u32[]{:S(2)}, u32[]{:S(2)}) collective-permute-start(bf16[3,2560]{1,0:T(4,128)(2,1)S(1)} %pad_maximum_fusion.5), channel_id=1, source_target_pairs={{0,4},{4,8},{8,12},{12,16},{16,20},{20,24},{24,28},{1,5},{5,9},{9,... | collective-permute-start | bytes 46088 | tf_op jit(solution)/shard_map/ppermute | solution.py:25
  17.9 9.0 %copy-start.6 = (bf16[512,1,256]{0,2,1:T(8,128)(2,1)}, bf16[512,1,256]{0,2,1:T(8,128)(2,1)S(1)}, u32[]{:S(2)}) copy-start(bf16[512,1,256]{0,2,1:T(8,128)(2,1)S(1)} %get-tuple-element.31) | copy-start | bytes 786436
  26.9 39.5 %copy-start = (bf16[2048,512]{1,0:T(8,128)(2,1)S(1)}, bf16[2048,512]{1,0:T(8,128)(2,1)}, u32[]{:S(2)}) copy-start(bf16[2048,512]{1,0:T(8,128)(2,1)} %shard_map.118) | copy-start | bytes 6291460
  26.9 7.9 %collective-permute-start.1 = (bf16[1040,128]{1,0:T(8,128)(2,1)S(1)}, bf16[1040,128]{1,0:T(8,128)(2,1)S(1)}, u32[]{:S(2)}, u32[]{:S(2)}) collective-permute-start(bf16[1040,128]{1,0:T(8,128)(2,1)S(1)} %pad_maximum_fusion.3), channel_id=1, source_target_pairs={{0,4},{4,0},{1,5},{5,1},{2,6},{6,2},{3,7},{7,3},{8,12},{12,8},{9,1... | collective-permute-start | bytes 798728 | tf_op jit(solution)/shard_map/ppermute | solution.py:271
  35.5 0.5 copy-start.12
  36.1 28.8 %copy-start.7 = (bf16[512,1,256]{0,2,1:T(8,128)(2,1)S(1)}, bf16[512,1,256]{0,2,1:T(8,128)(2,1)}, u32[]{:S(2)}) copy-start(bf16[512,1,256]{0,2,1:T(8,128)(2,1)} %copy-done.6) | copy-start | bytes 786436
  36.1 30.3 %copy-start.9 = (f32[2,16,512]{2,1,0:T(8,128)S(1)}, f32[2,16,512]{2,1,0:T(8,128)}, u32[]{:S(2)}) copy-start(f32[2,16,512]{2,1,0:T(8,128)} %get-tuple-element.34) | copy-start | bytes 196612
  38.8 11.3 %collective-permute-start.3 = (bf16[1040,128]{1,0:T(8,128)(2,1)S(1)}, bf16[1040,128]{1,0:T(8,128)(2,1)S(1)}, u32[]{:S(2)}, u32[]{:S(2)}) collective-permute-start(bf16[1040,128]{1,0:T(8,128)(2,1)S(1)} %pad_maximum_fusion.4), channel_id=1, source_target_pairs={{0,16},{8,24},{1,17},{9,25},{2,18},{10,26},{3,19},{11,27},{4,20},{... | collective-permute-start | bytes 798728 | tf_op jit(solution)/shard_map/ppermute | solution.py:25
  43.4 10.1 %collective-permute-start.2 = (bf16[1040,128]{1,0:T(8,128)(2,1)S(1)}, bf16[1040,128]{1,0:T(8,128)(2,1)S(1)}, u32[]{:S(2)}, u32[]{:S(2)}) collective-permute-start(bf16[1040,128]{1,0:T(8,128)(2,1)S(1)} %pad_maximum_fusion.4), channel_id=1, source_target_pairs={{0,8},{8,16},{16,24},{1,9},{9,17},{17,25},{2,10},{10,18},{18,26},{... | collective-permute-start | bytes 798728 | tf_op jit(solution)/shard_map/ppermute | solution.py:25
  46.9 30.1 %copy-start.2 = (f32[1024,128]{1,0:T(8,128)}, f32[1024,128]{1,0:T(8,128)S(1)}, u32[]{:S(2)}) copy-start(f32[1024,128]{1,0:T(8,128)S(1)} %slice_convert_fusion) | copy-start | bytes 1572868
  53.6 23.4 %copy-start.4 = (bf16[1024,128]{1,0:T(8,128)(2,1)}, bf16[1024,128]{1,0:T(8,128)(2,1)S(1)}, u32[]{:S(2)}) copy-start(bf16[1024,128]{1,0:T(8,128)(2,1)S(1)} %slice.173) | copy-start | bytes 786436
  53.8 23.2 %collective-permute-start.4 = (bf16[16,64,128]{2,1,0:T(8,128)(2,1)S(1)}, bf16[16,64,128]{2,1,0:T(8,128)(2,1)S(1)}, u32[]{:S(2)}, u32[]{:S(2)}) collective-permute-start(bf16[16,64,128]{2,1,0:T(8,128)(2,1)S(1)} %fusion.42), channel_id=1, source_target_pairs={{0,16},{8,24},{1,17},{9,25},{2,18},{10,26},{3,19},{11,27},{4,20},{... | collective-permute-start | bytes 786440 | tf_op jit(solution)/shard_map/ppermute | solution.py:25
  66.4 10.6 %copy-start.10 = (f32[16]{0:T(128)S(1)}, f32[16]{0:T(128)}, u32[]{:S(2)}) copy-start(f32[16]{0:T(128)} %get-tuple-element.29) | copy-start | bytes 196
  77.0 5.7 %copy-start.13 = (f32[32]{0:T(128)S(1)}, f32[32]{0:T(128)}, u32[]{:S(2)}) copy-start(f32[32]{0:T(128)} %param.21) | copy-start | bytes 388
  77.0 5.9 %copy-start.11 = (bf16[2048]{0:T(1024)(128)(2,1)S(1)}, bf16[2048]{0:T(1024)(128)(2,1)}, u32[]{:S(2)}) copy-start(bf16[2048]{0:T(1024)(128)(2,1)} %param.22) | copy-start | bytes 12292
  77.0 1.1 copy-start.8
  78.1 8.3 %collective-permute-start.5 = (bf16[16,64,128]{2,1,0:T(8,128)(2,1)}, bf16[16,64,128]{2,1,0:T(8,128)(2,1)}, u32[]{:S(2)}, u32[]{:S(2)}) collective-permute-start(bf16[16,64,128]{2,1,0:T(8,128)(2,1)} %select_convert_fusion), channel_id=1, source_target_pairs={{0,4},{4,0},{1,5},{5,1},{2,6},{6,2},{3,7},{7,3},{8,12},{12,8},{9,1... | collective-permute-start | bytes 786440 | tf_op jit(solution)/shard_map/ppermute | solution.py:271
  82.9 6.1 %copy-start.3 = (f32[512,2,16,64]{0,3,2,1:T(8,128)S(1)}, f32[512,2,16,64]{0,3,2,1:T(8,128)}, u32[]{:S(2)}) copy-start(f32[512,2,16,64]{0,3,2,1:T(8,128)} %fusion.17) | copy-start | bytes 12582916
  82.9 6.1 %copy-start.5 = (bf16[512,1,256]{0,2,1:T(8,128)(2,1)S(1)}, bf16[512,1,256]{0,2,1:T(8,128)(2,1)}, u32[]{:S(2)}) copy-start(bf16[512,1,256]{0,2,1:T(8,128)(2,1)} %get-tuple-element.30) | copy-start | bytes 786436
  89.0 2.1 %copy-start.1 = (bf16[512,2048]{0,1:T(8,128)(2,1)S(1)}, bf16[512,2048]{0,1:T(8,128)(2,1)}, u32[]{:S(2)}) copy-start(bf16[512,2048]{0,1:T(8,128)(2,1)} %copy.50) | copy-start | bytes 6291460
  91.1 7.6 %slice-start = ((s8[16777216]{0:T(1024)(128)(4,1)}), s8[4194304]{0:T(1024)(128)(4,1)S(1)}, s32[]{:S(2)}) async-start(s8[16777216]{0:T(1024)(128)(4,1)} %bitcast.241), calls=%async_computation | async-start | bytes 8388608
  91.1 7.6 %slice-start.1 = ((s8[16777216]{0:T(1024)(128)(4,1)}), s8[4194304]{0:T(1024)(128)(4,1)S(1)}, s32[]{:S(2)}) async-start(s8[16777216]{0:T(1024)(128)(4,1)} %bitcast.241), calls=%async_computation.1 | async-start | bytes 8388608
  93.5 5.3 %slice-start.2 = ((s8[16777216]{0:T(1024)(128)(4,1)}), s8[4194304]{0:T(1024)(128)(4,1)S(1)}, s32[]{:S(2)}) async-start(s8[16777216]{0:T(1024)(128)(4,1)} %bitcast.241), calls=%async_computation.2 | async-start | bytes 8388608
  93.9 4.9 %slice-start.3 = ((s8[16777216]{0:T(1024)(128)(4,1)}), s8[4194304]{0:T(1024)(128)(4,1)S(1)}, s32[]{:S(2)}) async-start(s8[16777216]{0:T(1024)(128)(4,1)} %bitcast.241), calls=%async_computation.3 | async-start | bytes 8388608
  101.2 3.2 %collective-permute-start.6 = (bf16[2,128,1024]{2,1,0:T(8,128)(2,1)S(1)}, bf16[2,128,1024]{2,1,0:T(8,128)(2,1)S(1)}, u32[]{:S(2)}, u32[]{:S(2)}) collective-permute-start(bf16[2,128,1024]{2,1,0:T(8,128)(2,1)S(1)} %dynamic-slice_bitcast_fusion.3), channel_id=1, source_target_pairs={{0,1},{1,0},{2,3},{3,2},{4,5},{5,4},{6,7},{7,6},{8,9},{9,8},{10,11... | collective-permute-start | bytes 1572872 | tf_op jit(solution)/shard_map/ppermute | solution.py:271
  101.3 4.9 %collective-permute-start.8 = (bf16[2,128,1024]{2,1,0:T(8,128)(2,1)S(1)}, bf16[2,128,1024]{2,1,0:T(8,128)(2,1)S(1)}, u32[]{:S(2)}, u32[]{:S(2)}) collective-permute-start(bf16[2,128,1024]{2,1,0:T(8,128)(2,1)S(1)} %dynamic-slice_bitcast_fusion.2), channel_id=1, source_target_pairs={{0,1},{1,0},{2,3},{3,2},{4,5},{5,4},{6,7},{7,6},{8,9},{9,8},{10,11... | collective-permute-start | bytes 1572872 | tf_op jit(solution)/shard_map/ppermute | solution.py:271
  104.3 5.2 %collective-permute-start.10 = (bf16[2,128,1024]{2,1,0:T(8,128)(2,1)S(1)}, bf16[2,128,1024]{2,1,0:T(8,128)(2,1)S(1)}, u32[]{:S(2)}, u32[]{:S(2)}) collective-permute-start(bf16[2,128,1024]{2,1,0:T(8,128)(2,1)S(1)} %dynamic-slice_bitcast_fusion.1), channel_id=1, source_target_pairs={{0,1},{1,0},{2,3},{3,2},{4,5},{5,4},{6,7},{7,6},{8,9},{9,8},{10,11... | collective-permute-start | bytes 1572872 | tf_op jit(solution)/shard_map/ppermute | solution.py:271
  104.6 9.2 %collective-permute-start.7 = (bf16[128,1024]{1,0:T(8,128)(2,1)S(1)}, bf16[128,1024]{1,0:T(8,128)(2,1)S(1)}, u32[]{:S(2)}, u32[]{:S(2)}) collective-permute-start(bf16[128,1024]{1,0:T(8,128)(2,1)S(1)} %fusion.44), channel_id=1, source_target_pairs={{0,2},{2,0},{1,3},{3,1},{4,6},{6,4},{5,7},{7,5},{8,10},{10,8},{9,1... | collective-permute-start | bytes 786440 | tf_op jit(solution)/shard_map/ppermute | solution.py:271
  106.4 13.0 %collective-permute-start.9 = (bf16[128,1024]{1,0:T(8,128)(2,1)S(1)}, bf16[128,1024]{1,0:T(8,128)(2,1)S(1)}, u32[]{:S(2)}, u32[]{:S(2)}) collective-permute-start(bf16[128,1024]{1,0:T(8,128)(2,1)S(1)} %fusion.45), channel_id=1, source_target_pairs={{0,2},{2,0},{1,3},{3,1},{4,6},{6,4},{5,7},{7,5},{8,10},{10,8},{9,1... | collective-permute-start | bytes 786440 | tf_op jit(solution)/shard_map/ppermute | solution.py:271
  109.4 4.4 %collective-permute-start.12 = (bf16[2,128,1024]{2,1,0:T(8,128)(2,1)S(1)}, bf16[2,128,1024]{2,1,0:T(8,128)(2,1)S(1)}, u32[]{:S(2)}, u32[]{:S(2)}) collective-permute-start(bf16[2,128,1024]{2,1,0:T(8,128)(2,1)S(1)} %dynamic-slice_bitcast_fusion), channel_id=1, source_target_pairs={{0,1},{1,0},{2,3},{3,2},{4,5},{5,4},{6,7},{7,6},{8,9},{9,8},{10,11... | collective-permute-start | bytes 1572872 | tf_op jit(solution)/shard_map/ppermute | solution.py:271
  109.7 15.3 %collective-permute-start.11 = (bf16[128,1024]{1,0:T(8,128)(2,1)S(1)}, bf16[128,1024]{1,0:T(8,128)(2,1)S(1)}, u32[]{:S(2)}, u32[]{:S(2)}) collective-permute-start(bf16[128,1024]{1,0:T(8,128)(2,1)S(1)} %fusion.46), channel_id=1, source_target_pairs={{0,2},{2,0},{1,3},{3,1},{4,6},{6,4},{5,7},{7,5},{8,10},{10,8},{9,1... | collective-permute-start | bytes 786440 | tf_op jit(solution)/shard_map/ppermute | solution.py:271
  114.1 16.1 %collective-permute-start.13 = (bf16[128,1024]{1,0:T(8,128)(2,1)S(1)}, bf16[128,1024]{1,0:T(8,128)(2,1)S(1)}, u32[]{:S(2)}, u32[]{:S(2)}) collective-permute-start(bf16[128,1024]{1,0:T(8,128)(2,1)S(1)} %fusion.47), channel_id=1, source_target_pairs={{0,2},{2,0},{1,3},{3,1},{4,6},{6,4},{5,7},{7,5},{8,10},{10,8},{9,1... | collective-permute-start | bytes 786440 | tf_op jit(solution)/shard_map/ppermute | solution.py:271

commit v15 on v12

--- a/solution.py
+++ b/solution.py
@@ -34,11 +34,11 @@
     return lax.optimization_barrier(jax.nn.silu(summed).astype(jnp.bfloat16))
 
 
-def conv_kernel(halo_ref, x_ref, w_ref, b_ref, o_ref, pad_ref):
+def conv_kernel(halo_ref, x_ref, w_ref, o_ref, pad_ref):
     rows = x_ref.shape[0]
     pad_ref[0:8, :] = halo_ref[...].astype(jnp.float32)
     pad_ref[8 : 8 + rows, :] = x_ref[...].astype(jnp.float32)
-    summed = b_ref[...].astype(jnp.float32)
+    summed = halo_ref[0:1, :].astype(jnp.float32)
     for k in range(CONV):
         summed = summed + w_ref[k : k + 1, :].astype(jnp.float32) * pad_ref[8 - (CONV - 1) + k : 8 - (CONV - 1) + k + rows, :]
     o_ref[...] = jnp.transpose(jax.nn.silu(summed)).astype(o_ref.dtype)
@@ -46,7 +46,10 @@
 def conv_silu_kernel(halo, x, weight, bias):
     rows, width = x.shape
     block = 512 if width % 512 == 0 else width
-    halo8 = jnp.concatenate([jnp.zeros((8 - halo.shape[0], width), halo.dtype), halo], axis=0)
+    halo8 = jnp.concatenate(
+        [bias.reshape(1, width).astype(halo.dtype), jnp.zeros((7 - halo.shape[0], width), halo.dtype), halo],
+        axis=0,
+    )
     return pl.pallas_call(
         conv_kernel,
         grid=(width // block,),
@@ -54,12 +57,11 @@
             pl.BlockSpec((8, block), lambda j: (0, j)),
             pl.BlockSpec((rows, block), lambda j: (0, j)),
             pl.BlockSpec((CONV, block), lambda j: (0, j)),
-            pl.BlockSpec((1, block), lambda j: (0, j)),
         ],
         out_specs=pl.BlockSpec((block, rows), lambda j: (j, 0)),
         out_shape=jax.ShapeDtypeStruct((width, rows), jnp.bfloat16),
         scratch_shapes=[pltpu.VMEM((rows + 8, block), jnp.float32)],
-    )(halo8, x, weight, bias.reshape(1, width))
+    )(halo8, x, weight)
 
 def diagonal_of(inner_block, b_block, c_block, step_sizes, cumulative):
     length = inner_block.shape[0]

time: 132 us -> 132 us (level)
  no operation moved by 1% of the time
where the time goes in v15:
time: 132 us; the launch traced here: 131 us
  waiting for transfers between devices  32.4 us (25%)
  starting transfers between devices  32.3 us (24%)
  matrix products  28.3 us (21%)
  other arithmetic  20.5 us (16%)
  local copies, waits for them, and re-layouts  10.7 us (8%)
  Pallas kernels  5.99 us (5%)
    ppermute x10, waiting for transfers between devices, swap(): return lax.ppermute(value, axis, [(0, 1), (1, 0)])  25.8 us
    ppermute x4, starting transfers between devices, shifted(): return lax.ppermute(value, axis, pairs)  23.9 us
    dot_general x4, matrix products, reduce_rows(): jnp.dot(source, out_weight[:, c * step:(c + 1) * step], preferred_element...  11.9 us
    dot_general x1, matrix products, diagonal_of(): jnp.einsum('ghij,jghp->ighp', mixing, inner_block, preferred_element_type...  10.5 us
    ppermute x10, starting transfers between devices, swap(): return lax.ppermute(value, axis, [(0, 1), (1, 0)])  8.41 us
    unnamed x40, local copies, waits for them, and re-layouts  6.53 us
    ppermute x4, waiting for transfers between devices, shifted(): return lax.ppermute(value, axis, pairs)  6.52 us
    pallas_call x1, Pallas kernels, conv_silu_kernel(): pl.pallas_call(conv_kernel, grid=(width // block,), in_specs=[pl.BlockSpe...  5.99 us
  transfers between devices with their start and end apart: 14, of which 8 were waited for; matrix products, arithmetic and copies ran while one was open for 24% of the time, Pallas kernels for 0%

profile of v15, /device:TPU:0, one launch (start us, length us, event | category | flops | bytes accessed | tf_op | source)
XLA Modules:
  0.0 130.8 jit_solution(16728318815310335922)
XLA Ops:
  1.5 4.8 %collective-permute-start = (bf16[3,2560]{1,0:T(4,128)(2,1)S(1)}, bf16[3,2560]{1,0:T(4,128)(2,1)S(1)}, u32[]{:S(2)}, u32[]{:S(2)}) collective-permute-start(bf16[3,2560]{1,0:T(4,128)(2,1)S(1)} %pad_maximum_fusion.6), channel_id=1, source_target_pairs={{0,4},{4,8},{8,12},{12,16},{16,20},{20,24},{24,28},{1,5},{5,9},{9,... | collective-permute-start | bytes 46088 | tf_op jit(solution)/shard_map/ppermute | solution.py:25
  7.9 2.3 %reduce-window.6 = f32[16,2,4,128]{3,0,1,2:T(8,128)S(1)} reduce-window(f32[16,2,4,128]{3,0,1,2:T(8,128)S(1)} %bitcast.238, f32[]{:T(128)} %constant.68.clone.1), window={size=1x1x1x128 pad=0_0x0_0x0_0x127_0}, to_apply=%region_0.1 | reduce-window | flops 2080768 | bytes 131076 | tf_op jit(solution)/shard_map/reduce-window
  12.3 1.3 copy.44
  15.3 1.3 %multiply_convert_fusion.6 = bf16[512,2,256]{0,2,1:T(8,128)(2,1)S(1)} fusion(bf16[512,2,256]{0,2,1:T(8,128)(2,1)S(1)} %copy.44, bf16[3,2,256]{0,2,1:T(8,128)(2,1)S(1)} %bitcast.234, f32[2,256]{1,0:T(2,128)S(1)} %get-tuple-element.40, f32[2,256]{1,0:T(2,128)S(1)} %get-tuple-element.41, f32[2,256]{1,0:T(2,128)S(1)} %get-tuple-element.39, ...), kind=kLoop, calls=%fused_computation.39 | loop fusion | flops 6815744 | bytes 1061888 | tf_op jit(solution)/shard_map/convert_element_type | solution.py:34
  18.1 6.0 %shard_map.118 = bf16[2048,512]{1,0:T(8,128)(2,1)} custom-call(bf16[8,2048]{1,0:T(8,128)(2,1)} %pad_maximum_fusion.5.halo_ref, bf16[512,2048]{1,0:T(8,128)(2,1)} %x_ref.1, bf16[4,2048]{1,0:T(4,128)(2,1)} %w_ref.1), custom_call_target="tpu_custom_call" | custom-call | tf_op jit(solution)/shard_map/pallas_call | solution.py:53
  24.1 2.3 %fusion.18 = f32[2,16,64,128]{3,2,1,0:T(8,128)S(1)} fusion(bf16[512,2,128,1]{0,2,3,1:T(8,128)(2,1)S(1)} %bitcast.223, bf16[512,2,16,64]{0,3,2,1:T(8,128)(2,1)} %bitcast.210, f32[512,2,16]{0,2,1:T(8,128)S(1)} %get-tuple-element.33), kind=kOutput, calls=%fused_computation.26 | convolution fusion | flops 271581184 | bytes 3473408 | tf_op jit(solution)/shard_map/jghp,jgn->ghpn/dot_general | solution.py:83
  26.5 1.6 %collective-permute-start.1 = (bf16[1040,128]{1,0:T(8,128)(2,1)S(1)}, bf16[1040,128]{1,0:T(8,128)(2,1)S(1)}, u32[]{:S(2)}, u32[]{:S(2)}) collective-permute-start(bf16[1040,128]{1,0:T(8,128)(2,1)S(1)} %pad_maximum_fusion.3), channel_id=1, source_target_pairs={{0,4},{4,0},{1,5},{5,1},{2,6},{6,2},{3,7},{7,3},{8,12},{12,8},{9,1... | collective-permute-start | bytes 798728 | tf_op jit(solution)/shard_map/ppermute | solution.py:273
  29.0 5.5 %collective-permute-done.1 = bf16[1040,128]{1,0:T(8,128)(2,1)S(1)} collective-permute-done((bf16[1040,128]{1,0:T(8,128)(2,1)S(1)}, bf16[1040,128]{1,0:T(8,128)(2,1)S(1)}, u32[]{:S(2)}, u32[]{:S(2)}) %collective-permute-start.1) | collective-permute-done | bytes 266272 | tf_op jit(solution)/shard_map/ppermute | solution.py:273
  37.1 1.2 fusion.41
  38.4 4.5 %collective-permute-start.3 = (bf16[1040,128]{1,0:T(8,128)(2,1)S(1)}, bf16[1040,128]{1,0:T(8,128)(2,1)S(1)}, u32[]{:S(2)}, u32[]{:S(2)}) collective-permute-start(bf16[1040,128]{1,0:T(8,128)(2,1)S(1)} %pad_maximum_fusion.4), channel_id=1, source_target_pairs={{0,16},{8,24},{1,17},{9,25},{2,18},{10,26},{3,19},{11,27},{4,20},{... | collective-permute-start | bytes 798728 | tf_op jit(solution)/shard_map/ppermute | solution.py:25
  43.0 3.5 %collective-permute-start.2 = (bf16[1040,128]{1,0:T(8,128)(2,1)S(1)}, bf16[1040,128]{1,0:T(8,128)(2,1)S(1)}, u32[]{:S(2)}, u32[]{:S(2)}) collective-permute-start(bf16[1040,128]{1,0:T(8,128)(2,1)S(1)} %pad_maximum_fusion.4), channel_id=1, source_target_pairs={{0,8},{8,16},{16,24},{1,9},{9,17},{17,25},{2,10},{10,18},{18,26},{... | collective-permute-start | bytes 798728 | tf_op jit(solution)/shard_map/ppermute | solution.py:25
  46.6 3.2 %collective-permute-done.3 = bf16[1040,128]{1,0:T(8,128)(2,1)S(1)} collective-permute-done((bf16[1040,128]{1,0:T(8,128)(2,1)S(1)}, bf16[1040,128]{1,0:T(8,128)(2,1)S(1)}, u32[]{:S(2)}, u32[]{:S(2)}) %collective-permute-start.3) | collective-permute-done | bytes 266272 | tf_op jit(solution)/shard_map/ppermute | solution.py:25
  49.7 3.4 %collective-permute-done.2 = bf16[1040,128]{1,0:T(8,128)(2,1)S(1)} collective-permute-done((bf16[1040,128]{1,0:T(8,128)(2,1)S(1)}, bf16[1040,128]{1,0:T(8,128)(2,1)S(1)}, u32[]{:S(2)}, u32[]{:S(2)}) %collective-permute-start.2) | collective-permute-done | bytes 266272 | tf_op jit(solution)/shard_map/ppermute | solution.py:25
  53.4 11.0 %collective-permute-start.4 = (bf16[16,64,128]{2,1,0:T(8,128)(2,1)S(1)}, bf16[16,64,128]{2,1,0:T(8,128)(2,1)S(1)}, u32[]{:S(2)}, u32[]{:S(2)}) collective-permute-start(bf16[16,64,128]{2,1,0:T(8,128)(2,1)S(1)} %fusion.42), channel_id=1, source_target_pairs={{0,16},{8,24},{1,17},{9,25},{2,18},{10,26},{3,19},{11,27},{4,20},{... | collective-permute-start | bytes 786440 | tf_op jit(solution)/shard_map/ppermute | solution.py:25
  64.4 1.4 %fusion.68 = f32[2,512,512]{2,1,0:T(8,128)S(1)} fusion(bf16[512,2,128]{0,2,1:T(8,128)(2,1)} %bitcast.221, bf16[512,2,128]{0,2,1:T(8,128)(2,1)S(1)} %bitcast.224), kind=kOutput, calls=%fused_computation.135 | convolution fusion | flops 134217728 | bytes 2621440 | tf_op jit(solution)/shard_map/ign,jgn->gij/dot_general | solution.py:73
  65.9 10.5 %fusion.17 = f32[512,2,16,64]{0,3,2,1:T(8,128)} fusion(bf16[512,2,16,64]{0,3,2,1:T(8,128)(2,1)S(1)} %bitcast.211, f32[2,16,512]{2,1,0:T(8,128)S(1)} %bitcast.237, f32[2,512,512]{2,1,0:T(8,128)S(1)} %fusion.68, f32[2,16,512]{2,1,0:T(8,128)S(1)} %copy-done.9, pred[512,512]{1,0:T(8,128)(4,1)S(1)} %iota_compare_fusion), kind=kOutput, calls=%fused_computation.25 | convolution fusion | flops 1115684864 | bytes 8781824 | tf_op jit(solution)/shard_map/ghij,jghp->ighp/dot_general | solution.py:77
  78.2 3.9 %copy.50 = bf16[512,2048]{0,1:T(8,128)(2,1)} copy(bf16[512,2048]{1,0:T(8,128)(2,1)} %param.14) | data formatting | bytes 4194304 | tf_op args[2]
  82.3 3.5 %collective-permute-done.5 = bf16[16,64,128]{2,1,0:T(8,128)(2,1)} collective-permute-done((bf16[16,64,128]{2,1,0:T(8,128)(2,1)}, bf16[16,64,128]{2,1,0:T(8,128)(2,1)}, u32[]{:S(2)}, u32[]{:S(2)}) %collective-permute-start.5) | collective-permute-done | bytes 262176 | tf_op jit(solution)/shard_map/ppermute | solution.py:273
  85.8 1.5 %convert_select_fusion.1 = (f32[16,64,128]{2,1,0:T(8,128)S(1)}, f32[16,64,128]{2,1,0:T(8,128)S(1)}) fusion(bf16[16,64,128]{2,1,0:T(8,128)(2,1)} %collective-permute-done.5, pred[]{:T(512)S(6)} %eq.3, f32[16,64,128]{2,1,0:T(8,128)} %bitcast.213, f32[16]{0:T(128)S(1)} %copy-done.10, bf16[16,64,128]{2,1,0:T(8,128)(2,1)} %bitcast.220, ...), kind=kLoop, calls=%fused_computation.43 | loop fusion | flops 1835008 | bytes 3671232 | tf_op jit(solution)/shard_map/jit(_where)/select_n | solution.py:189
  88.4 2.1 %fusion.6 = f32[1,512,2,16,64]{1,4,3,2,0:T(8,128)S(1)} fusion(f32[512,2,16,64]{0,3,2,1:T(8,128)S(1)} %copy-done.3, f32[512,2,16]{0,2,1:T(8,128)S(1)} %get-tuple-element.32, f32[2,16,64,128]{3,2,1,0:T(8,128)S(1)} %bitcast.214, bf16[512,2,128,1]{0,2,3,1:T(8,128)(2,1)S(1)} %bitcast.222), kind=kOutput, calls=%fused_computation.10 | convolution fusion | flops 1612709888 | bytes 9764864 | tf_op jit(solution)/shard_map/vmap(ign,ghpn->ighp)/dot_general | solution.py:94
  90.6 2.2 %bitcast_reduce_fusion = (f32[512,2]{0,1:T(2,128)S(1)}, f32[512,2048]{0,1:T(8,128)S(1)}) fusion(bf16[512,2048]{0,1:T(8,128)(2,1)S(1)} %copy-done.1, bf16[2048,512]{1,0:T(8,128)(2,1)S(1)} %copy-done, f32[2048]{0:T(1024)S(1)} %mul.224, f32[1,512,2,16,64]{1,4,3,2,0:T(8,128)S(1)} %fusion.6), kind=kLoop, calls=%fused_computation.14 | loop fusion | flops 11533312 | bytes 12595200 | tf_op jit(solution)/shard_map/reduce_sum | solution.py:265
  93.3 4.9 %fusion.20 = bf16[512,1024]{1,0:T(8,128)(2,1)S(1)} fusion(bf16[512,2048]{0,1:T(8,128)(2,1)S(1)} %fusion.8, bf16[2048,4096]{1,0:T(8,128)(2,1)} %param.23), kind=kOutput, calls=%fused_computation.28 | convolution fusion | flops 2148007936 | bytes 7340032 | tf_op jit(solution)/shard_map/dot_general | solution.py:301
  98.2 2.3 %fusion.23 = bf16[512,1024]{1,0:T(8,128)(2,1)S(1)} fusion(bf16[512,2048]{0,1:T(8,128)(2,1)S(1)} %fusion.8, bf16[2048,4096]{1,0:T(8,128)(2,1)S(1)} %bitcast.242), kind=kOutput, calls=%fused_computation.29 | convolution fusion | flops 2148007936 | bytes 7340032 | tf_op jit(solution)/shard_map/dot_general | solution.py:301
  101.3 2.3 %fusion.26 = bf16[512,1024]{1,0:T(8,128)(2,1)S(1)} fusion(bf16[512,2048]{0,1:T(8,128)(2,1)S(1)} %fusion.8, bf16[2048,4096]{1,0:T(8,128)(2,1)S(1)} %bitcast.242), kind=kOutput, calls=%fused_computation.30 | convolution fusion | flops 2148007936 | bytes 7340032 | tf_op jit(solution)/shard_map/dot_general | solution.py:301
  104.0 1.6 %collective-permute-start.7 = (bf16[128,1024]{1,0:T(8,128)(2,1)S(1)}, bf16[128,1024]{1,0:T(8,128)(2,1)S(1)}, u32[]{:S(2)}, u32[]{:S(2)}) collective-permute-start(bf16[128,1024]{1,0:T(8,128)(2,1)S(1)} %fusion.44), channel_id=1, source_target_pairs={{0,2},{2,0},{1,3},{3,1},{4,6},{6,4},{5,7},{7,5},{8,10},{10,8},{9,1... | collective-permute-start | bytes 786440 | tf_op jit(solution)/shard_map/ppermute | solution.py:273
  106.4 2.3 %fusion.29 = bf16[512,1024]{1,0:T(8,128)(2,1)S(1)} fusion(bf16[512,2048]{0,1:T(8,128)(2,1)S(1)} %fusion.8, bf16[2048,4096]{1,0:T(8,128)(2,1)S(1)} %bitcast.242), kind=kOutput, calls=%fused_computation.31 | convolution fusion | flops 2148007936 | bytes 7340032 | tf_op jit(solution)/shard_map/dot_general | solution.py:301
  109.1 1.6 %collective-permute-start.11 = (bf16[128,1024]{1,0:T(8,128)(2,1)S(1)}, bf16[128,1024]{1,0:T(8,128)(2,1)S(1)}, u32[]{:S(2)}, u32[]{:S(2)}) collective-permute-start(bf16[128,1024]{1,0:T(8,128)(2,1)S(1)} %fusion.46), channel_id=1, source_target_pairs={{0,2},{2,0},{1,3},{3,1},{4,6},{6,4},{5,7},{7,5},{8,10},{10,8},{9,1... | collective-permute-start | bytes 786440 | tf_op jit(solution)/shard_map/ppermute | solution.py:273
  110.7 2.5 %collective-permute-done.7 = bf16[128,1024]{1,0:T(8,128)(2,1)S(1)} collective-permute-done((bf16[128,1024]{1,0:T(8,128)(2,1)S(1)}, bf16[128,1024]{1,0:T(8,128)(2,1)S(1)}, u32[]{:S(2)}, u32[]{:S(2)}) %collective-permute-start.7) | collective-permute-done | bytes 262176 | tf_op jit(solution)/shard_map/ppermute | solution.py:273
  113.5 1.6 %collective-permute-start.13 = (bf16[128,1024]{1,0:T(8,128)(2,1)S(1)}, bf16[128,1024]{1,0:T(8,128)(2,1)S(1)}, u32[]{:S(2)}, u32[]{:S(2)}) collective-permute-start(bf16[128,1024]{1,0:T(8,128)(2,1)S(1)} %fusion.47), channel_id=1, source_target_pairs={{0,2},{2,0},{1,3},{3,1},{4,6},{6,4},{5,7},{7,5},{8,10},{10,8},{9,1... | collective-permute-start | bytes 786440 | tf_op jit(solution)/shard_map/ppermute | solution.py:273
  115.1 3.7 %collective-permute-done.9 = bf16[128,1024]{1,0:T(8,128)(2,1)S(1)} collective-permute-done((bf16[128,1024]{1,0:T(8,128)(2,1)S(1)}, bf16[128,1024]{1,0:T(8,128)(2,1)S(1)}, u32[]{:S(2)}, u32[]{:S(2)}) %collective-permute-start.9) | collective-permute-done | bytes 262176 | tf_op jit(solution)/shard_map/ppermute | solution.py:273
  118.9 5.6 %collective-permute-done.11 = bf16[128,1024]{1,0:T(8,128)(2,1)S(1)} collective-permute-done((bf16[128,1024]{1,0:T(8,128)(2,1)S(1)}, bf16[128,1024]{1,0:T(8,128)(2,1)S(1)}, u32[]{:S(2)}, u32[]{:S(2)}) %collective-permute-start.11) | collective-permute-done | bytes 262176 | tf_op jit(solution)/shard_map/ppermute | solution.py:273
  124.5 5.1 %collective-permute-done.13 = bf16[128,1024]{1,0:T(8,128)(2,1)S(1)} collective-permute-done((bf16[128,1024]{1,0:T(8,128)(2,1)S(1)}, bf16[128,1024]{1,0:T(8,128)(2,1)S(1)}, u32[]{:S(2)}, u32[]{:S(2)}) %collective-permute-start.13) | collective-permute-done | bytes 262176 | tf_op jit(solution)/shard_map/ppermute | solution.py:273
  (121 shorter events, 19.4 us)
Async XLA Ops:
  1.5 13.6 %collective-permute-start = (bf16[3,2560]{1,0:T(4,128)(2,1)S(1)}, bf16[3,2560]{1,0:T(4,128)(2,1)S(1)}, u32[]{:S(2)}, u32[]{:S(2)}) collective-permute-start(bf16[3,2560]{1,0:T(4,128)(2,1)S(1)} %pad_maximum_fusion.6), channel_id=1, source_target_pairs={{0,4},{4,8},{8,12},{12,16},{16,20},{20,24},{24,28},{1,5},{5,9},{9,... | collective-permute-start | bytes 46088 | tf_op jit(solution)/shard_map/ppermute | solution.py:25
  17.4 9.1 %copy-start.6 = (bf16[512,1,256]{0,2,1:T(8,128)(2,1)}, bf16[512,1,256]{0,2,1:T(8,128)(2,1)S(1)}, u32[]{:S(2)}) copy-start(bf16[512,1,256]{0,2,1:T(8,128)(2,1)S(1)} %get-tuple-element.31) | copy-start | bytes 786436
  26.5 39.3 %copy-start = (bf16[2048,512]{1,0:T(8,128)(2,1)S(1)}, bf16[2048,512]{1,0:T(8,128)(2,1)}, u32[]{:S(2)}) copy-start(bf16[2048,512]{1,0:T(8,128)(2,1)} %shard_map.118) | copy-start | bytes 6291460
  26.5 7.9 %collective-permute-start.1 = (bf16[1040,128]{1,0:T(8,128)(2,1)S(1)}, bf16[1040,128]{1,0:T(8,128)(2,1)S(1)}, u32[]{:S(2)}, u32[]{:S(2)}) collective-permute-start(bf16[1040,128]{1,0:T(8,128)(2,1)S(1)} %pad_maximum_fusion.3), channel_id=1, source_target_pairs={{0,4},{4,0},{1,5},{5,1},{2,6},{6,2},{3,7},{7,3},{8,12},{12,8},{9,1... | collective-permute-start | bytes 798728 | tf_op jit(solution)/shard_map/ppermute | solution.py:273
  35.1 0.5 copy-start.12
  35.7 28.7 %copy-start.7 = (bf16[512,1,256]{0,2,1:T(8,128)(2,1)S(1)}, bf16[512,1,256]{0,2,1:T(8,128)(2,1)}, u32[]{:S(2)}) copy-start(bf16[512,1,256]{0,2,1:T(8,128)(2,1)} %copy-done.6) | copy-start | bytes 786436
  35.7 30.1 %copy-start.9 = (f32[2,16,512]{2,1,0:T(8,128)S(1)}, f32[2,16,512]{2,1,0:T(8,128)}, u32[]{:S(2)}) copy-start(f32[2,16,512]{2,1,0:T(8,128)} %get-tuple-element.34) | copy-start | bytes 196612
  38.4 11.3 %collective-permute-start.3 = (bf16[1040,128]{1,0:T(8,128)(2,1)S(1)}, bf16[1040,128]{1,0:T(8,128)(2,1)S(1)}, u32[]{:S(2)}, u32[]{:S(2)}) collective-permute-start(bf16[1040,128]{1,0:T(8,128)(2,1)S(1)} %pad_maximum_fusion.4), channel_id=1, source_target_pairs={{0,16},{8,24},{1,17},{9,25},{2,18},{10,26},{3,19},{11,27},{4,20},{... | collective-permute-start | bytes 798728 | tf_op jit(solution)/shard_map/ppermute | solution.py:25
  43.0 10.1 %collective-permute-start.2 = (bf16[1040,128]{1,0:T(8,128)(2,1)S(1)}, bf16[1040,128]{1,0:T(8,128)(2,1)S(1)}, u32[]{:S(2)}, u32[]{:S(2)}) collective-permute-start(bf16[1040,128]{1,0:T(8,128)(2,1)S(1)} %pad_maximum_fusion.4), channel_id=1, source_target_pairs={{0,8},{8,16},{16,24},{1,9},{9,17},{17,25},{2,10},{10,18},{18,26},{... | collective-permute-start | bytes 798728 | tf_op jit(solution)/shard_map/ppermute | solution.py:25
  46.5 29.9 %copy-start.2 = (f32[1024,128]{1,0:T(8,128)}, f32[1024,128]{1,0:T(8,128)S(1)}, u32[]{:S(2)}) copy-start(f32[1024,128]{1,0:T(8,128)S(1)} %slice_convert_fusion) | copy-start | bytes 1572868
  53.2 23.2 %copy-start.4 = (bf16[1024,128]{1,0:T(8,128)(2,1)}, bf16[1024,128]{1,0:T(8,128)(2,1)S(1)}, u32[]{:S(2)}) copy-start(bf16[1024,128]{1,0:T(8,128)(2,1)S(1)} %slice.173) | copy-start | bytes 786436
  53.4 23.0 %collective-permute-start.4 = (bf16[16,64,128]{2,1,0:T(8,128)(2,1)S(1)}, bf16[16,64,128]{2,1,0:T(8,128)(2,1)S(1)}, u32[]{:S(2)}, u32[]{:S(2)}) collective-permute-start(bf16[16,64,128]{2,1,0:T(8,128)(2,1)S(1)} %fusion.42), channel_id=1, source_target_pairs={{0,16},{8,24},{1,17},{9,25},{2,18},{10,26},{3,19},{11,27},{4,20},{... | collective-permute-start | bytes 786440 | tf_op jit(solution)/shard_map/ppermute | solution.py:25
  65.9 10.6 %copy-start.10 = (f32[16]{0:T(128)S(1)}, f32[16]{0:T(128)}, u32[]{:S(2)}) copy-start(f32[16]{0:T(128)} %get-tuple-element.29) | copy-start | bytes 196
  76.4 5.7 %copy-start.13 = (f32[32]{0:T(128)S(1)}, f32[32]{0:T(128)}, u32[]{:S(2)}) copy-start(f32[32]{0:T(128)} %param.21) | copy-start | bytes 388
  76.4 5.9 %copy-start.11 = (bf16[2048]{0:T(1024)(128)(2,1)S(1)}, bf16[2048]{0:T(1024)(128)(2,1)}, u32[]{:S(2)}) copy-start(bf16[2048]{0:T(1024)(128)(2,1)} %param.22) | copy-start | bytes 12292
  76.4 1.1 copy-start.8
  77.5 8.3 %collective-permute-start.5 = (bf16[16,64,128]{2,1,0:T(8,128)(2,1)}, bf16[16,64,128]{2,1,0:T(8,128)(2,1)}, u32[]{:S(2)}, u32[]{:S(2)}) collective-permute-start(bf16[16,64,128]{2,1,0:T(8,128)(2,1)} %select_convert_fusion), channel_id=1, source_target_pairs={{0,4},{4,0},{1,5},{5,1},{2,6},{6,2},{3,7},{7,3},{8,12},{12,8},{9,1... | collective-permute-start | bytes 786440 | tf_op jit(solution)/shard_map/ppermute | solution.py:273
  82.3 6.1 %copy-start.3 = (f32[512,2,16,64]{0,3,2,1:T(8,128)S(1)}, f32[512,2,16,64]{0,3,2,1:T(8,128)}, u32[]{:S(2)}) copy-start(f32[512,2,16,64]{0,3,2,1:T(8,128)} %fusion.17) | copy-start | bytes 12582916
  82.3 6.1 %copy-start.5 = (bf16[512,1,256]{0,2,1:T(8,128)(2,1)S(1)}, bf16[512,1,256]{0,2,1:T(8,128)(2,1)}, u32[]{:S(2)}) copy-start(bf16[512,1,256]{0,2,1:T(8,128)(2,1)} %get-tuple-element.30) | copy-start | bytes 786436
  88.4 2.1 %copy-start.1 = (bf16[512,2048]{0,1:T(8,128)(2,1)S(1)}, bf16[512,2048]{0,1:T(8,128)(2,1)}, u32[]{:S(2)}) copy-start(bf16[512,2048]{0,1:T(8,128)(2,1)} %copy.50) | copy-start | bytes 6291460
  90.5 7.6 %slice-start = ((s8[16777216]{0:T(1024)(128)(4,1)}), s8[4194304]{0:T(1024)(128)(4,1)S(1)}, s32[]{:S(2)}) async-start(s8[16777216]{0:T(1024)(128)(4,1)} %bitcast.241), calls=%async_computation | async-start | bytes 8388608
  90.6 7.6 %slice-start.1 = ((s8[16777216]{0:T(1024)(128)(4,1)}), s8[4194304]{0:T(1024)(128)(4,1)S(1)}, s32[]{:S(2)}) async-start(s8[16777216]{0:T(1024)(128)(4,1)} %bitcast.241), calls=%async_computation.1 | async-start | bytes 8388608
  92.8 5.4 %slice-start.2 = ((s8[16777216]{0:T(1024)(128)(4,1)}), s8[4194304]{0:T(1024)(128)(4,1)S(1)}, s32[]{:S(2)}) async-start(s8[16777216]{0:T(1024)(128)(4,1)} %bitcast.241), calls=%async_computation.2 | async-start | bytes 8388608
  93.3 4.9 %slice-start.3 = ((s8[16777216]{0:T(1024)(128)(4,1)}), s8[4194304]{0:T(1024)(128)(4,1)S(1)}, s32[]{:S(2)}) async-start(s8[16777216]{0:T(1024)(128)(4,1)} %bitcast.241), calls=%async_computation.3 | async-start | bytes 8388608
  100.6 3.2 %collective-permute-start.6 = (bf16[2,128,1024]{2,1,0:T(8,128)(2,1)S(1)}, bf16[2,128,1024]{2,1,0:T(8,128)(2,1)S(1)}, u32[]{:S(2)}, u32[]{:S(2)}) collective-permute-start(bf16[2,128,1024]{2,1,0:T(8,128)(2,1)S(1)} %dynamic-slice_bitcast_fusion.3), channel_id=1, source_target_pairs={{0,1},{1,0},{2,3},{3,2},{4,5},{5,4},{6,7},{7,6},{8,9},{9,8},{10,11... | collective-permute-start | bytes 1572872 | tf_op jit(solution)/shard_map/ppermute | solution.py:273
  100.8 4.9 %collective-permute-start.8 = (bf16[2,128,1024]{2,1,0:T(8,128)(2,1)S(1)}, bf16[2,128,1024]{2,1,0:T(8,128)(2,1)S(1)}, u32[]{:S(2)}, u32[]{:S(2)}) collective-permute-start(bf16[2,128,1024]{2,1,0:T(8,128)(2,1)S(1)} %dynamic-slice_bitcast_fusion.2), channel_id=1, source_target_pairs={{0,1},{1,0},{2,3},{3,2},{4,5},{5,4},{6,7},{7,6},{8,9},{9,8},{10,11... | collective-permute-start | bytes 1572872 | tf_op jit(solution)/shard_map/ppermute | solution.py:273
  103.7 5.2 %collective-permute-start.10 = (bf16[2,128,1024]{2,1,0:T(8,128)(2,1)S(1)}, bf16[2,128,1024]{2,1,0:T(8,128)(2,1)S(1)}, u32[]{:S(2)}, u32[]{:S(2)}) collective-permute-start(bf16[2,128,1024]{2,1,0:T(8,128)(2,1)S(1)} %dynamic-slice_bitcast_fusion.1), channel_id=1, source_target_pairs={{0,1},{1,0},{2,3},{3,2},{4,5},{5,4},{6,7},{7,6},{8,9},{9,8},{10,11... | collective-permute-start | bytes 1572872 | tf_op jit(solution)/shard_map/ppermute | solution.py:273
  104.0 9.2 %collective-permute-start.7 = (bf16[128,1024]{1,0:T(8,128)(2,1)S(1)}, bf16[128,1024]{1,0:T(8,128)(2,1)S(1)}, u32[]{:S(2)}, u32[]{:S(2)}) collective-permute-start(bf16[128,1024]{1,0:T(8,128)(2,1)S(1)} %fusion.44), channel_id=1, source_target_pairs={{0,2},{2,0},{1,3},{3,1},{4,6},{6,4},{5,7},{7,5},{8,10},{10,8},{9,1... | collective-permute-start | bytes 786440 | tf_op jit(solution)/shard_map/ppermute | solution.py:273
  105.9 13.0 %collective-permute-start.9 = (bf16[128,1024]{1,0:T(8,128)(2,1)S(1)}, bf16[128,1024]{1,0:T(8,128)(2,1)S(1)}, u32[]{:S(2)}, u32[]{:S(2)}) collective-permute-start(bf16[128,1024]{1,0:T(8,128)(2,1)S(1)} %fusion.45), channel_id=1, source_target_pairs={{0,2},{2,0},{1,3},{3,1},{4,6},{6,4},{5,7},{7,5},{8,10},{10,8},{9,1... | collective-permute-start | bytes 786440 | tf_op jit(solution)/shard_map/ppermute | solution.py:273
  108.8 4.4 %collective-permute-start.12 = (bf16[2,128,1024]{2,1,0:T(8,128)(2,1)S(1)}, bf16[2,128,1024]{2,1,0:T(8,128)(2,1)S(1)}, u32[]{:S(2)}, u32[]{:S(2)}) collective-permute-start(bf16[2,128,1024]{2,1,0:T(8,128)(2,1)S(1)} %dynamic-slice_bitcast_fusion), channel_id=1, source_target_pairs={{0,1},{1,0},{2,3},{3,2},{4,5},{5,4},{6,7},{7,6},{8,9},{9,8},{10,11... | collective-permute-start | bytes 1572872 | tf_op jit(solution)/shard_map/ppermute | solution.py:273
  109.1 15.3 %collective-permute-start.11 = (bf16[128,1024]{1,0:T(8,128)(2,1)S(1)}, bf16[128,1024]{1,0:T(8,128)(2,1)S(1)}, u32[]{:S(2)}, u32[]{:S(2)}) collective-permute-start(bf16[128,1024]{1,0:T(8,128)(2,1)S(1)} %fusion.46), channel_id=1, source_target_pairs={{0,2},{2,0},{1,3},{3,1},{4,6},{6,4},{5,7},{7,5},{8,10},{10,8},{9,1... | collective-permute-start | bytes 786440 | tf_op jit(solution)/shard_map/ppermute | solution.py:273
  113.5 16.1 %collective-permute-start.13 = (bf16[128,1024]{1,0:T(8,128)(2,1)S(1)}, bf16[128,1024]{1,0:T(8,128)(2,1)S(1)}, u32[]{:S(2)}, u32[]{:S(2)}) collective-permute-start(bf16[128,1024]{1,0:T(8,128)(2,1)S(1)} %fusion.47), channel_id=1, source_target_pairs={{0,2},{2,0},{1,3},{3,1},{4,6},{6,4},{5,7},{7,5},{8,10},{10,8},{9,1... | collective-permute-start | bytes 786440 | tf_op jit(solution)/shard_map/ppermute | solution.py:273
